TPU v7x, 32 devices: a whole 2x2x4 slice. The times are simulated.
32 devices in a mesh: groups: 2 (over x), col: 8 (over z, y), row: 2 (over core).
Axes of the slice: x: 2, y: 2, z: 4, core: 2. Of those that a mesh axis runs over, the one named last changes fastest.
Arguments:
- queries: bfloat16 [32, 8, 64, 1536], P(('groups', 'row'), 'col'), parts along dimension 0, may hold values from -300 to 300
- key_mant: bfloat16 [32, 8, 64, 1536], P(('groups', 'row'), 'col'), parts along dimension 0, may hold values from -8 to 8
- key_exp: int32 [32, 8, 2, 1536], P(('groups', 'row'), 'col'), parts along dimension 0, may hold values from -1 to 1
- value_mant: bfloat16 [32, 8, 64, 1536], P(('groups', 'row'), 'col'), parts along dimension 0, may hold values from -4 to 4
- value_exp: int32 [32, 8, 2, 1536], P(('groups', 'row'), 'col'), parts along dimension 0, may hold values from 0 to 2
- cycle_list: int32 [4, 8, 4], P(('groups', 'row'), 'col'), parts along dimension 0, may hold values from 0 to 17, as said below
- dilated_list: int32 [4, 8, 4], P(('groups', 'row'), 'col'), parts along dimension 0, may hold values from 0 to 13, as said below
Outputs:
- attended: bfloat16 [32, 8, 64, 1536], P(('groups', 'row'), 'col'), parts along dimension 0
There are 2 independent parts, one for each index of `groups`. A program takes and returns all parts, laid end to end along the dimension named above; each array names one. Nothing has to cross between parts.
Inputs may be any that keep to these rules, and one draw needn't show every extreme that they name: `cycle_list`: the 4 entries of a tile are distinct; none names a block outside the image, and every side of the cycle that lies inside the image is named at least once. `dilated_list`: the 4 entries of a tile are distinct.
All inputs are finite; a program needn't handle non-finite values.
Results may differ from a plain program's by a relative error of at most 0.0043.
Values may be sent and summed in bfloat16 or wider, within the bound.
No kernel may reach another device: no remote copies, remote signals or barrier semaphores. Data moves between devices by JAX's collectives and lax.ppermute only.
A program may use at most 128 MiB of HBM per device.

v0:
```python
import jax
import jax.numpy as jnp
from jax import lax
from jax.sharding import PartitionSpec as P

HEADS = 12
HEAD_DIM = 128
DILATION_TILES = 8


def with_halo(cells, sides, width):
    for axis, dim in sides:
        count = lax.axis_size(axis)
        ends = count - 1
        head = lax.slice_in_dim(cells, 0, width, axis=dim)
        tail = lax.slice_in_dim(cells, cells.shape[dim] - width, cells.shape[dim], axis=dim)
        cells = jnp.concatenate(
            [
                lax.ppermute(tail, axis, [(i, (i + 1) % count) for i in range(ends)]),
                cells,
                lax.ppermute(head, axis, [((i + 1) % count, i) for i in range(ends)]),
            ],
            axis=dim,
        )
    return cells


def passed_along(block, axis, distance):
    devices = range(lax.axis_size(axis))
    route = [((i - distance) % len(devices), i) for i in devices]
    return lax.ppermute(block, axis, route)


def dequant(mantissa, exponent):
    tile_rows, tile_cols, block_length, feature_channel_width = mantissa.shape
    groups = exponent.shape[2]
    factor = jnp.exp2(exponent.astype(jnp.float32))[:, :, :, None, :]
    scaled = (
        mantissa.reshape(
            tile_rows, tile_cols, groups, block_length // groups, feature_channel_width
        ).astype(jnp.float32)
        * factor
    )
    return scaled.reshape(mantissa.shape).astype(jnp.bfloat16)


def attend_group(operands):
    query_part, key_part, value_part = operands
    scores = jnp.einsum(
        "qhd,khd->hqk", query_part, key_part, preferred_element_type=jnp.float32
    ) * HEAD_DIM ** (-0.5)
    row_max = jnp.max(scores, axis=-1, keepdims=True)
    weights = jnp.exp(scores - row_max)
    row_total = jnp.sum(weights, axis=-1)
    rounded = weights.astype(jnp.bfloat16)
    blended = jnp.einsum("hqk,khd->qhd", rounded, value_part, preferred_element_type=jnp.float32)
    return (blended / jnp.transpose(row_total)[:, :, None]).astype(jnp.bfloat16)


def per_device(queries, key_mant, key_exp, value_mant, value_exp, cycle_list, dilated_list):
    tile_blocks = queries.shape[0]
    block_length = queries.shape[2]
    feature_channel_width = queries.shape[3]
    distant_rows = tile_blocks // 4
    stacked = jnp.stack([dequant(key_mant, key_exp), dequant(value_mant, value_exp)])
    extended = with_halo(stacked, (("col", 2), ("row", 1)), 1)
    cycle_entry = cycle_list[0, 0]
    cycle_row = jnp.where(
        cycle_entry == 0,
        0,
        jnp.where(
            cycle_entry == 1,
            tile_blocks + 1,
            jnp.where(
                cycle_entry < tile_blocks + 2, cycle_entry - 1, cycle_entry - 1 - tile_blocks
            ),
        ),
    )
    cycle_col = jnp.where(cycle_entry < 2, 1, jnp.where(cycle_entry < tile_blocks + 2, 0, 2))
    extended_flat = extended.reshape(2, (tile_blocks + 2) * 3, block_length, feature_channel_width)
    cycle_blocks = jnp.take(extended_flat, cycle_row * 3 + cycle_col, axis=1)
    far_source = stacked[:, 0::4, 0]
    column_loop_length = lax.axis_size("col")
    step_spacing = column_loop_length // DILATION_TILES
    incoming_blocks = {}
    relayed = far_source
    for start_shift in range(1, DILATION_TILES):
        relayed = passed_along(relayed, "col", column_loop_length - step_spacing)
        incoming_blocks[start_shift] = relayed
    dilated_full_list = jnp.stack(
        [incoming_blocks[start_shift] for start_shift in range(1, DILATION_TILES)], axis=1
    ).reshape(2, (DILATION_TILES - 1) * distant_rows, block_length, feature_channel_width)
    dilated_blocks = jnp.take(dilated_full_list, dilated_list[0, 0], axis=1)
    own_blocks = stacked.reshape(2, tile_blocks, block_length, feature_channel_width)
    key_values = jnp.concatenate([own_blocks, cycle_blocks, dilated_blocks], axis=1)
    key_values = key_values.reshape(2, -1, HEADS // 2, 2, HEAD_DIM)
    token_count = tile_blocks * block_length
    query_groups = queries.reshape(token_count, HEADS // 2, 2, HEAD_DIM).transpose(1, 0, 2, 3)
    key_groups = key_values[0].transpose(1, 0, 2, 3)
    value_groups = key_values[1].transpose(1, 0, 2, 3)
    results = lax.map(attend_group, (query_groups, key_groups, value_groups))
    return results.transpose(1, 0, 2, 3).reshape(queries.shape)


def solution(mesh):
    in_specs = (
        P(("groups", "row"), "col", None, None),
        P(("groups", "row"), "col", None, None),
        P(("groups", "row"), "col", None, None),
        P(("groups", "row"), "col", None, None),
        P(("groups", "row"), "col", None, None),
        P(("groups", "row"), "col", None),
        P(("groups", "row"), "col", None),
    )
    out_specs = P(("groups", "row"), "col", None, None)
    return jax.shard_map(
        per_device, mesh=mesh, in_specs=in_specs, out_specs=out_specs, check_vma=False
    )
```

profile of v0, /device:TPU:0, one launch (start us, length us, event | category | flops | bytes accessed | tf_op | source)
XLA Modules:
  0.0 378.6 jit_solution(2773527997782003790)
XLA Ops:
  0.0 1.1 exponential_bitcast_fusion
  1.1 1.0 exponential_bitcast_fusion.1
  2.1 1.7 fusion.24
  4.1 3.1 fusion.29
  7.2 1.2 slice_bitcast_fusion
  8.4 6.1 %collective-permute-start.4 = (bf16[2,2,64,1536]{3,2,1,0:T(8,128)(2,1)S(1)}, bf16[2,2,64,1536]{3,2,1,0:T(8,128)(2,1)S(1)}, u32[]{:S(2)}, u32[]{:S(2)}) collective-permute-start(bf16[2,2,64,1536]{3,2,1,0:T(8,128)(2,1)S(1)} %slice_bitcast_fusion), channel_id=1, source_target_pairs={{2,0},{4,2},{6,4},{8,6},{10,8},{12,10},{14,12},{0,14},{3,1},{5,3},... | collective-permute-start | bytes 2359304 | tf_op jit(solution)/shard_map/ppermute | solution.py:31
  14.4 3.0 collective-permute-start
  17.4 1.3 collective-permute-start.1
  18.7 12.5 %collective-permute-done.4 = bf16[2,2,64,1536]{3,2,1,0:T(8,128)(2,1)S(1)} collective-permute-done((bf16[2,2,64,1536]{3,2,1,0:T(8,128)(2,1)S(1)}, bf16[2,2,64,1536]{3,2,1,0:T(8,128)(2,1)S(1)}, u32[]{:S(2)}, u32[]{:S(2)}) %collective-permute-start.4) | collective-permute-done | bytes 786464 | tf_op jit(solution)/shard_map/ppermute | solution.py:31
  32.1 69.1 %collective-permute-start.5 = (bf16[2,2,64,1536]{3,2,1,0:T(8,128)(2,1)S(1)}, bf16[2,2,64,1536]{3,2,1,0:T(8,128)(2,1)}, u32[]{:S(2)}, u32[]{:S(2)}) collective-permute-start(bf16[2,2,64,1536]{3,2,1,0:T(8,128)(2,1)S(1)} %collective-permute-done.4), channel_id=1, source_target_pairs={{2,0},{4,2},{6,4},{8,6},{10,8},{12,10},{14,12},{0,14},{3,1},{5,3},... | collective-permute-start | bytes 2359304 | tf_op jit(solution)/shard_map/ppermute | solution.py:31
  101.2 14.8 %collective-permute-done.5 = bf16[2,2,64,1536]{3,2,1,0:T(8,128)(2,1)} collective-permute-done((bf16[2,2,64,1536]{3,2,1,0:T(8,128)(2,1)S(1)}, bf16[2,2,64,1536]{3,2,1,0:T(8,128)(2,1)}, u32[]{:S(2)}, u32[]{:S(2)}) %collective-permute-start.5) | collective-permute-done | bytes 786464 | tf_op jit(solution)/shard_map/ppermute | solution.py:31
  116.0 67.4 %collective-permute-start.6 = (bf16[2,2,64,1536]{3,2,1,0:T(8,128)(2,1)}, bf16[2,2,64,1536]{3,2,1,0:T(8,128)(2,1)}, u32[]{:S(2)}, u32[]{:S(2)}) collective-permute-start(bf16[2,2,64,1536]{3,2,1,0:T(8,128)(2,1)} %collective-permute-done.5), channel_id=1, source_target_pairs={{2,0},{4,2},{6,4},{8,6},{10,8},{12,10},{14,12},{0,14},{3,1},{5,3},... | collective-permute-start | bytes 2359304 | tf_op jit(solution)/shard_map/ppermute | solution.py:31
  183.4 4.6 %reshape.222 = bf16[512,6,2,128]{3,2,1,0:T(2,128)(2,1)} reshape(bf16[8,1,64,1536]{3,2,1,0:T(8,128)(2,1)} %param.9) | data formatting | bytes 3145728 | tf_op jit(solution)/shard_map/reshape | solution.py:98
  188.0 11.6 %collective-permute-done.6 = bf16[2,2,64,1536]{3,2,1,0:T(8,128)(2,1)} collective-permute-done((bf16[2,2,64,1536]{3,2,1,0:T(8,128)(2,1)}, bf16[2,2,64,1536]{3,2,1,0:T(8,128)(2,1)}, u32[]{:S(2)}, u32[]{:S(2)}) %collective-permute-start.6) | collective-permute-done | bytes 786464 | tf_op jit(solution)/shard_map/ppermute | solution.py:31
  199.7 5.2 %collective-permute-start.7 = (bf16[2,2,64,1536]{3,2,1,0:T(8,128)(2,1)}, bf16[2,2,64,1536]{3,2,1,0:T(8,128)(2,1)S(1)}, u32[]{:S(2)}, u32[]{:S(2)}) collective-permute-start(bf16[2,2,64,1536]{3,2,1,0:T(8,128)(2,1)} %collective-permute-done.6), channel_id=1, source_target_pairs={{2,0},{4,2},{6,4},{8,6},{10,8},{12,10},{14,12},{0,14},{3,1},{5,3},... | collective-permute-start | bytes 2359304 | tf_op jit(solution)/shard_map/ppermute | solution.py:31
  204.8 1.2 bitcast_dynamic-update-slice_fusion.6
  206.0 1.2 bitcast_dynamic-update-slice_fusion.5
  207.2 12.9 %collective-permute-done.7 = bf16[2,2,64,1536]{3,2,1,0:T(8,128)(2,1)S(1)} collective-permute-done((bf16[2,2,64,1536]{3,2,1,0:T(8,128)(2,1)}, bf16[2,2,64,1536]{3,2,1,0:T(8,128)(2,1)S(1)}, u32[]{:S(2)}, u32[]{:S(2)}) %collective-permute-start.7) | collective-permute-done | bytes 786464 | tf_op jit(solution)/shard_map/ppermute | solution.py:31
  220.2 5.1 %collective-permute-start.8 = (bf16[2,2,64,1536]{3,2,1,0:T(8,128)(2,1)S(1)}, bf16[2,2,64,1536]{3,2,1,0:T(8,128)(2,1)S(1)}, u32[]{:S(2)}, u32[]{:S(2)}) collective-permute-start(bf16[2,2,64,1536]{3,2,1,0:T(8,128)(2,1)S(1)} %collective-permute-done.7), channel_id=1, source_target_pairs={{2,0},{4,2},{6,4},{8,6},{10,8},{12,10},{14,12},{0,14},{3,1},{5,3},... | collective-permute-start | bytes 2359304 | tf_op jit(solution)/shard_map/ppermute | solution.py:31
  225.2 1.6 pad_maximum_fusion.6
  226.9 1.4 collective-permute-start.2
  228.2 1.3 collective-permute-start.3
  229.5 1.2 bitcast_dynamic-update-slice_fusion.4
  230.7 8.6 %collective-permute-done.8 = bf16[2,2,64,1536]{3,2,1,0:T(8,128)(2,1)S(1)} collective-permute-done((bf16[2,2,64,1536]{3,2,1,0:T(8,128)(2,1)S(1)}, bf16[2,2,64,1536]{3,2,1,0:T(8,128)(2,1)S(1)}, u32[]{:S(2)}, u32[]{:S(2)}) %collective-permute-start.8) | collective-permute-done | bytes 786464 | tf_op jit(solution)/shard_map/ppermute | solution.py:31
  239.3 5.2 %collective-permute-start.9 = (bf16[2,2,64,1536]{3,2,1,0:T(8,128)(2,1)S(1)}, bf16[2,2,64,1536]{3,2,1,0:T(8,128)(2,1)}, u32[]{:S(2)}, u32[]{:S(2)}) collective-permute-start(bf16[2,2,64,1536]{3,2,1,0:T(8,128)(2,1)S(1)} %collective-permute-done.8), channel_id=1, source_target_pairs={{2,0},{4,2},{6,4},{8,6},{10,8},{12,10},{14,12},{0,14},{3,1},{5,3},... | collective-permute-start | bytes 2359304 | tf_op jit(solution)/shard_map/ppermute | solution.py:31
  244.6 13.0 %collective-permute-done.9 = bf16[2,2,64,1536]{3,2,1,0:T(8,128)(2,1)} collective-permute-done((bf16[2,2,64,1536]{3,2,1,0:T(8,128)(2,1)S(1)}, bf16[2,2,64,1536]{3,2,1,0:T(8,128)(2,1)}, u32[]{:S(2)}, u32[]{:S(2)}) %collective-permute-start.9) | collective-permute-done | bytes 786464 | tf_op jit(solution)/shard_map/ppermute | solution.py:31
  257.7 5.3 %collective-permute-start.10 = (bf16[2,2,64,1536]{3,2,1,0:T(8,128)(2,1)}, bf16[2,2,64,1536]{3,2,1,0:T(8,128)(2,1)}, u32[]{:S(2)}, u32[]{:S(2)}) collective-permute-start(bf16[2,2,64,1536]{3,2,1,0:T(8,128)(2,1)} %collective-permute-done.9), channel_id=1, source_target_pairs={{2,0},{4,2},{6,4},{8,6},{10,8},{12,10},{14,12},{0,14},{3,1},{5,3},... | collective-permute-start | bytes 2359304 | tf_op jit(solution)/shard_map/ppermute | solution.py:31
  262.9 8.6 %pad_maximum_fusion = bf16[2,10,3,64,1536]{4,3,2,1,0:T(8,128)(2,1)} fusion(bf16[2,1,3,64,1536]{4,3,2,1,0:T(8,128)(2,1)S(1)} %collective-permute-done.3, bf16[2,8,1,64,1536]{4,3,2,1,0:T(8,128)(2,1)} %collective-permute-done.1, bf16[1,8,1,64,1536]{4,3,2,1,0:T(8,128)(2,1)S(1)} %bitcast.108, bf16[1,8,1,64,1536]{4,3,2,1,0:T(8,128)(2,1)S(1)} %bitcast.111, ...), kind=kLoop, calls=%fused_computation.22 | loop fusion | flops 29491200 | bytes 23592960 | tf_op jit(solution)/shard_map/concatenate | solution.py:17
  271.5 6.2 %gather_fusion = bf16[4,2,64,1536]{3,2,1,0:T(8,128)(2,1)} fusion(bf16[2,30,64,1536]{3,2,1,0:T(8,128)(2,1)} %bitcast.112, s32[1024]{0:T(1024)S(1)} %pad_clamp_fusion.1), kind=kCustom, calls=%fused_computation | custom fusion | bytes 3145744 | tf_op jit(solution)/shard_map/jit(_take)/gather | solution.py:81
  277.7 2.1 bitcast_dynamic-update-slice_fusion.1
  279.8 2.1 bitcast_dynamic-update-slice_fusion
  281.8 5.6 %copy.13 = bf16[2,7,2,64,1536]{4,3,2,1,0:T(8,128)(2,1)} copy(bf16[2,7,2,64,1536]{4,3,2,0,1:T(8,128)(2,1)} %bitcast_dynamic-update-slice_fusion) | data formatting | bytes 11010048 | tf_op jit(solution)/shard_map/stack | solution.py:90
  287.4 4.5 %gather_fusion.1 = bf16[4,2,64,1536]{3,2,1,0:T(8,128)(2,1)} fusion(bf16[2,14,64,1536]{3,2,1,0:T(8,128)(2,1)} %bitcast.115, s32[1024]{0:T(1024)S(1)} %pad_clamp_fusion), kind=kCustom, calls=%fused_computation.1 | custom fusion | bytes 3145744 | tf_op jit(solution)/shard_map/jit(_take)/gather | solution.py:93
  291.9 1.7 select_bitcast_fusion
  294.7 2.2 fusion.31
  296.9 7.4 %squeeze.29 = bf16[1024,6,2,128]{3,2,1,0:T(2,128)(2,1)} reshape(bf16[1,16,64,1536]{3,2,1,0:T(8,128)(2,1)} %get-tuple-element.57) | data formatting | bytes 6291456 | tf_op jit(solution)/shard_map/squeeze | solution.py:100
  304.3 2.5 squeeze.30
  306.8 66.3 %while.10 = (s32[]{:T(128)}, bf16[6,512,2,128]{1,3,2,0:T(8,128)(2,1)}, bf16[6,1024,2,128]{3,2,0,1:T(2,128)(2,1)}, bf16[6,512,2,128]{3,2,0,1:T(2,128)(2,1)}, bf16[6,1024,2,128]{3,2,0,1:T(2,128)(2,1)}, /*index=5*/s32[]{:T(128)}) while((s32[]{:T(128)}, bf16[6,512,2,128]{1,3,2,0:T(8,128)(2,1)}, bf16[6,1024,2,128]{3,2,0,1:T(2,128)(2,1)}, ...), condition=%wide.region_3.4_spmd, body=%wide.region_0.3_spmd.sunk | while | flops 545519616 | bytes 34624104 | solution.py:101
  306.8 1.9 constant_dynamic-slice_fusion.5
  308.8 1.1 constant_dynamic-slice_fusion.6
  310.7 1.9 copy-done
  314.0 3.9 %fusion.41 = bf16[6,512,2,128]{1,3,2,0:T(8,128)(2,1)} fusion(bf16[6,512,2,128]{1,3,2,0:T(8,128)(2,1)} %get-tuple-element.106, s32[]{:T(128)} %get-tuple-element.105, f32[2,512,1024]{2,1,0:T(8,128)} %copy-done, f32[2,512]{1,0:T(2,128)S(1)} %get-tuple-element.97, bf16[1,1024,2,128]{1,3,2,0:T(8,128)(2,1)S(1)} %copy.40, f32[512,2]{0,1:T(2,128)S(1)} %bitcast.118), kind=kOutput, calls=%fused_computation.13.clone.1 | convolution fusion | flops 271843328 | bytes 4989440 | tf_op jit(solution)/shard_map/while/body/eval_jaxpr/hqk,khd->qhd/dot_general | solution.py:56
  317.9 1.9 constant_dynamic-slice_fusion.5
  319.8 1.1 constant_dynamic-slice_fusion.6
  321.8 1.9 copy-done
  325.1 3.9 %fusion.41 = bf16[6,512,2,128]{1,3,2,0:T(8,128)(2,1)} fusion(bf16[6,512,2,128]{1,3,2,0:T(8,128)(2,1)} %get-tuple-element.106, s32[]{:T(128)} %get-tuple-element.105, f32[2,512,1024]{2,1,0:T(8,128)} %copy-done, f32[2,512]{1,0:T(2,128)S(1)} %get-tuple-element.97, bf16[1,1024,2,128]{1,3,2,0:T(8,128)(2,1)S(1)} %copy.40, f32[512,2]{0,1:T(2,128)S(1)} %bitcast.118), kind=kOutput, calls=%fused_computation.13.clone.1 | convolution fusion | flops 271843328 | bytes 4989440 | tf_op jit(solution)/shard_map/while/body/eval_jaxpr/hqk,khd->qhd/dot_general | solution.py:56
  329.0 1.9 constant_dynamic-slice_fusion.5
  330.9 1.1 constant_dynamic-slice_fusion.6
  332.8 1.9 copy-done
  336.1 3.9 %fusion.41 = bf16[6,512,2,128]{1,3,2,0:T(8,128)(2,1)} fusion(bf16[6,512,2,128]{1,3,2,0:T(8,128)(2,1)} %get-tuple-element.106, s32[]{:T(128)} %get-tuple-element.105, f32[2,512,1024]{2,1,0:T(8,128)} %copy-done, f32[2,512]{1,0:T(2,128)S(1)} %get-tuple-element.97, bf16[1,1024,2,128]{1,3,2,0:T(8,128)(2,1)S(1)} %copy.40, f32[512,2]{0,1:T(2,128)S(1)} %bitcast.118), kind=kOutput, calls=%fused_computation.13.clone.1 | convolution fusion | flops 271843328 | bytes 4989440 | tf_op jit(solution)/shard_map/while/body/eval_jaxpr/hqk,khd->qhd/dot_general | solution.py:56
  340.0 1.9 constant_dynamic-slice_fusion.5
  341.9 1.1 constant_dynamic-slice_fusion.6
  343.9 1.9 copy-done
  347.2 3.9 %fusion.41 = bf16[6,512,2,128]{1,3,2,0:T(8,128)(2,1)} fusion(bf16[6,512,2,128]{1,3,2,0:T(8,128)(2,1)} %get-tuple-element.106, s32[]{:T(128)} %get-tuple-element.105, f32[2,512,1024]{2,1,0:T(8,128)} %copy-done, f32[2,512]{1,0:T(2,128)S(1)} %get-tuple-element.97, bf16[1,1024,2,128]{1,3,2,0:T(8,128)(2,1)S(1)} %copy.40, f32[512,2]{0,1:T(2,128)S(1)} %bitcast.118), kind=kOutput, calls=%fused_computation.13.clone.1 | convolution fusion | flops 271843328 | bytes 4989440 | tf_op jit(solution)/shard_map/while/body/eval_jaxpr/hqk,khd->qhd/dot_general | solution.py:56
  351.1 1.9 constant_dynamic-slice_fusion.5
  353.0 1.1 constant_dynamic-slice_fusion.6
  354.9 1.9 copy-done
  358.2 3.9 %fusion.41 = bf16[6,512,2,128]{1,3,2,0:T(8,128)(2,1)} fusion(bf16[6,512,2,128]{1,3,2,0:T(8,128)(2,1)} %get-tuple-element.106, s32[]{:T(128)} %get-tuple-element.105, f32[2,512,1024]{2,1,0:T(8,128)} %copy-done, f32[2,512]{1,0:T(2,128)S(1)} %get-tuple-element.97, bf16[1,1024,2,128]{1,3,2,0:T(8,128)(2,1)S(1)} %copy.40, f32[512,2]{0,1:T(2,128)S(1)} %bitcast.118), kind=kOutput, calls=%fused_computation.13.clone.1 | convolution fusion | flops 271843328 | bytes 4989440 | tf_op jit(solution)/shard_map/while/body/eval_jaxpr/hqk,khd->qhd/dot_general | solution.py:56
  362.1 1.9 constant_dynamic-slice_fusion.5
  364.0 1.1 constant_dynamic-slice_fusion.6
  366.0 1.9 copy-done
  369.3 3.9 %fusion.41 = bf16[6,512,2,128]{1,3,2,0:T(8,128)(2,1)} fusion(bf16[6,512,2,128]{1,3,2,0:T(8,128)(2,1)} %get-tuple-element.106, s32[]{:T(128)} %get-tuple-element.105, f32[2,512,1024]{2,1,0:T(8,128)} %copy-done, f32[2,512]{1,0:T(2,128)S(1)} %get-tuple-element.97, bf16[1,1024,2,128]{1,3,2,0:T(8,128)(2,1)S(1)} %copy.40, f32[512,2]{0,1:T(2,128)S(1)} %bitcast.118), kind=kOutput, calls=%fused_computation.13.clone.1 | convolution fusion | flops 271843328 | bytes 4989440 | tf_op jit(solution)/shard_map/while/body/eval_jaxpr/hqk,khd->qhd/dot_general | solution.py:56
  373.2 3.9 %copy.19 = bf16[512,6,2,128]{3,2,1,0:T(2,128)(2,1)S(1)} copy(bf16[512,6,2,128]{0,3,2,1:T(8,128)(2,1)} %bitcast.117) | data formatting | bytes 3145728 | tf_op jit(solution)/shard_map/transpose | solution.py:102
  377.1 1.5 reshape.223
  (54 shorter events, 15.3 us)
Async XLA Ops:
  0.0 3.8 copy-start.4
  4.1 97.1 %copy-start.7 = (s32[1,1,4]{2,1,0:T(1,128)S(1)}, s32[1,1,4]{2,1,0:T(1,128)}, u32[]{:S(2)}) copy-start(s32[1,1,4]{2,1,0:T(1,128)} %param.15) | copy-start | bytes 52
  7.2 180.8 %copy-start.6 = (s32[1,1,4]{2,1,0:T(1,128)S(1)}, s32[1,1,4]{2,1,0:T(1,128)}, u32[]{:S(2)}) copy-start(s32[1,1,4]{2,1,0:T(1,128)} %param.14) | copy-start | bytes 52
  8.4 22.9 %collective-permute-start.4 = (bf16[2,2,64,1536]{3,2,1,0:T(8,128)(2,1)S(1)}, bf16[2,2,64,1536]{3,2,1,0:T(8,128)(2,1)S(1)}, u32[]{:S(2)}, u32[]{:S(2)}) collective-permute-start(bf16[2,2,64,1536]{3,2,1,0:T(8,128)(2,1)S(1)} %slice_bitcast_fusion), channel_id=1, source_target_pairs={{2,0},{4,2},{6,4},{8,6},{10,8},{12,10},{14,12},{0,14},{3,1},{5,3},... | collective-permute-start | bytes 2359304 | tf_op jit(solution)/shard_map/ppermute | solution.py:31
  14.4 210.8 %collective-permute-start = (bf16[2,8,1,64,1536]{4,3,2,1,0:T(8,128)(2,1)}, bf16[2,8,1,64,1536]{4,3,2,1,0:T(8,128)(2,1)}, u32[]{:S(2)}, u32[]{:S(2)}) collective-permute-start(bf16[2,8,1,64,1536]{4,3,2,1,0:T(8,128)(2,1)} %get-tuple-element.59), channel_id=1, source_target_pairs={{0,2},{2,4},{4,6},{6,8},{8,10},{10,12},{12,14},{1,3},{3,5},{5,7},{... | collective-permute-start | bytes 9437192 | tf_op jit(solution)/shard_map/ppermute | solution.py:19
  17.4 207.8 %collective-permute-start.1 = (bf16[2,8,1,64,1536]{4,3,2,1,0:T(8,128)(2,1)}, bf16[2,8,1,64,1536]{4,3,2,1,0:T(8,128)(2,1)}, u32[]{:S(2)}, u32[]{:S(2)}) collective-permute-start(bf16[2,8,1,64,1536]{4,3,2,1,0:T(8,128)(2,1)} %get-tuple-element.59), channel_id=1, source_target_pairs={{2,0},{4,2},{6,4},{8,6},{10,8},{12,10},{14,12},{3,1},{5,3},{7,5},{... | collective-permute-start | bytes 9437192 | tf_op jit(solution)/shard_map/ppermute | solution.py:21
  31.2 0.9 copy-start.5
  32.1 83.8 %collective-permute-start.5 = (bf16[2,2,64,1536]{3,2,1,0:T(8,128)(2,1)S(1)}, bf16[2,2,64,1536]{3,2,1,0:T(8,128)(2,1)}, u32[]{:S(2)}, u32[]{:S(2)}) collective-permute-start(bf16[2,2,64,1536]{3,2,1,0:T(8,128)(2,1)S(1)} %collective-permute-done.4), channel_id=1, source_target_pairs={{2,0},{4,2},{6,4},{8,6},{10,8},{12,10},{14,12},{0,14},{3,1},{5,3},... | collective-permute-start | bytes 2359304 | tf_op jit(solution)/shard_map/ppermute | solution.py:31
  116.0 83.7 %collective-permute-start.6 = (bf16[2,2,64,1536]{3,2,1,0:T(8,128)(2,1)}, bf16[2,2,64,1536]{3,2,1,0:T(8,128)(2,1)}, u32[]{:S(2)}, u32[]{:S(2)}) collective-permute-start(bf16[2,2,64,1536]{3,2,1,0:T(8,128)(2,1)} %collective-permute-done.5), channel_id=1, source_target_pairs={{2,0},{4,2},{6,4},{8,6},{10,8},{12,10},{14,12},{0,14},{3,1},{5,3},... | collective-permute-start | bytes 2359304 | tf_op jit(solution)/shard_map/ppermute | solution.py:31
  199.7 20.5 %collective-permute-start.7 = (bf16[2,2,64,1536]{3,2,1,0:T(8,128)(2,1)}, bf16[2,2,64,1536]{3,2,1,0:T(8,128)(2,1)S(1)}, u32[]{:S(2)}, u32[]{:S(2)}) collective-permute-start(bf16[2,2,64,1536]{3,2,1,0:T(8,128)(2,1)} %collective-permute-done.6), channel_id=1, source_target_pairs={{2,0},{4,2},{6,4},{8,6},{10,8},{12,10},{14,12},{0,14},{3,1},{5,3},... | collective-permute-start | bytes 2359304 | tf_op jit(solution)/shard_map/ppermute | solution.py:31
  220.2 19.2 %collective-permute-start.8 = (bf16[2,2,64,1536]{3,2,1,0:T(8,128)(2,1)S(1)}, bf16[2,2,64,1536]{3,2,1,0:T(8,128)(2,1)S(1)}, u32[]{:S(2)}, u32[]{:S(2)}) collective-permute-start(bf16[2,2,64,1536]{3,2,1,0:T(8,128)(2,1)S(1)} %collective-permute-done.7), channel_id=1, source_target_pairs={{2,0},{4,2},{6,4},{8,6},{10,8},{12,10},{14,12},{0,14},{3,1},{5,3},... | collective-permute-start | bytes 2359304 | tf_op jit(solution)/shard_map/ppermute | solution.py:31
  226.9 36.1 %collective-permute-start.2 = (bf16[2,1,3,64,1536]{4,3,2,1,0:T(8,128)(2,1)S(1)}, bf16[2,1,3,64,1536]{4,3,2,1,0:T(8,128)(2,1)S(1)}, u32[]{:S(2)}, u32[]{:S(2)}) collective-permute-start(bf16[2,1,3,64,1536]{4,3,2,1,0:T(8,128)(2,1)S(1)} %get-tuple-element.54), channel_id=1, source_target_pairs={{0,1},{2,3},{4,5},{6,7},{8,9},{10,11},{12,13},{14,15},{16,17},{18,... | collective-permute-start | bytes 3538952 | tf_op jit(solution)/shard_map/ppermute | solution.py:19
  228.2 34.7 %collective-permute-start.3 = (bf16[2,1,3,64,1536]{4,3,2,1,0:T(8,128)(2,1)S(1)}, bf16[2,1,3,64,1536]{4,3,2,1,0:T(8,128)(2,1)S(1)}, u32[]{:S(2)}, u32[]{:S(2)}) collective-permute-start(bf16[2,1,3,64,1536]{4,3,2,1,0:T(8,128)(2,1)S(1)} %get-tuple-element.55), channel_id=1, source_target_pairs={{1,0},{3,2},{5,4},{7,6},{9,8},{11,10},{13,12},{15,14},{17,16},{19,... | collective-permute-start | bytes 3538952 | tf_op jit(solution)/shard_map/ppermute | solution.py:21
  239.3 18.3 %collective-permute-start.9 = (bf16[2,2,64,1536]{3,2,1,0:T(8,128)(2,1)S(1)}, bf16[2,2,64,1536]{3,2,1,0:T(8,128)(2,1)}, u32[]{:S(2)}, u32[]{:S(2)}) collective-permute-start(bf16[2,2,64,1536]{3,2,1,0:T(8,128)(2,1)S(1)} %collective-permute-done.8), channel_id=1, source_target_pairs={{2,0},{4,2},{6,4},{8,6},{10,8},{12,10},{14,12},{0,14},{3,1},{5,3},... | collective-permute-start | bytes 2359304 | tf_op jit(solution)/shard_map/ppermute | solution.py:31
  244.6 26.9 %copy-start.2 = (bf16[2,7,2,64,1536]{4,3,2,0,1:T(8,128)(2,1)}, bf16[2,7,2,64,1536]{4,3,2,0,1:T(8,128)(2,1)S(1)}, u32[]{:S(2)}) copy-start(bf16[2,7,2,64,1536]{4,3,2,0,1:T(8,128)(2,1)S(1)} %bitcast_dynamic-update-slice_fusion.2) | copy-start | bytes 16515076
  257.7 22.1 %collective-permute-start.10 = (bf16[2,2,64,1536]{3,2,1,0:T(8,128)(2,1)}, bf16[2,2,64,1536]{3,2,1,0:T(8,128)(2,1)}, u32[]{:S(2)}, u32[]{:S(2)}) collective-permute-start(bf16[2,2,64,1536]{3,2,1,0:T(8,128)(2,1)} %collective-permute-done.9), channel_id=1, source_target_pairs={{2,0},{4,2},{6,4},{8,6},{10,8},{12,10},{14,12},{0,14},{3,1},{5,3},... | collective-permute-start | bytes 2359304 | tf_op jit(solution)/shard_map/ppermute | solution.py:31
  287.4 6.3 %copy-start.1 = (bf16[2,8,64,1536]{3,2,1,0:T(8,128)(2,1)S(1)}, bf16[2,8,64,1536]{3,2,1,0:T(8,128)(2,1)}, u32[]{:S(2)}) copy-start(bf16[2,8,64,1536]{3,2,1,0:T(8,128)(2,1)} %get-tuple-element.58) | copy-start | bytes 9437188
  291.9 1.9 copy-start.3
  310.7 2.0 copy-start
  321.8 2.0 copy-start
  332.8 2.0 copy-start
  343.9 2.0 copy-start
  354.9 2.0 copy-start
  366.0 2.0 copy-start
where the time goes:
time: 380 us; the launch traced here: 379 us
  starting transfers between devices  170 us (45%)
  local copies, waits for them, and re-layouts  80.9 us (21%)
  waiting for transfers between devices  73.5 us (19%)
  matrix products  28.1 us (7%)
  other arithmetic  25.6 us (7%)
    ppermute x7, starting transfers between devices, passed_along(): return lax.ppermute(block, axis, route)  163 us
    ppermute x7, waiting for transfers between devices, passed_along(): return lax.ppermute(block, axis, route)  73.5 us
    dot_general x6, matrix products, attend_group(): jnp.einsum('hqk,khd->qhd', rounded, value_part, preferred_element_type=jn...  23.3 us
    dynamic_slice x18, local copies, waits for them, and re-layouts, per_device(): results = lax.map(attend_group, (query_groups, key_groups, value_groups))  20.8 us
    while x12, local copies, waits for them, and re-layouts  11.7 us
    concatenate x1, other arithmetic, with_halo(): jnp.concatenate([lax.ppermute(tail, axis, [(i, (i + 1) % count) for i in...  8.59 us
    another operation x2, local copies, waits for them, and re-layouts, per_device(): jnp.stack([incoming_blocks[start_shift] for start_shift in range(1, DILAT...  7.63 us
  transfers between devices with their start and end apart: 11, of which 6 were waited for; matrix products, arithmetic and copies ran while one was open for 7% of the time, Pallas kernels for 0%

commit v1 on v0

v1 whole, which is shorter than its diff:
```python
import jax
import jax.numpy as jnp
from jax import lax
from jax.experimental import pallas as pl
from jax.experimental.pallas import tpu as pltpu
from jax.sharding import PartitionSpec as P

HEAD_DIM = 128
DILATION_TILES = 8


def dequant(mantissa, exponent):
    tile_rows, tile_cols, block_length, feature_channel_width = mantissa.shape
    groups = exponent.shape[2]
    factor = jnp.exp2(exponent.astype(jnp.float32))[:, :, :, None, :]
    scaled = (
        mantissa.reshape(
            tile_rows, tile_cols, groups, block_length // groups, feature_channel_width
        ).astype(jnp.float32)
        * factor
    )
    return scaled.reshape(mantissa.shape).astype(jnp.bfloat16)


def shift(x, axis, count, step):
    if step > 0:
        pairs = [(i, i + step) for i in range(count - step)]
    else:
        pairs = [(i - step, i) for i in range(count + step)]
    if not pairs:
        return jnp.zeros_like(x)
    return lax.ppermute(x, axis, pairs)


def side_slots(entries, low, tile_blocks, cap):
    inside = (entries >= low) & (entries < low + tile_blocks)
    rank = jnp.cumsum(inside.astype(jnp.int32)) - 1
    slot = jnp.arange(cap, dtype=jnp.int32)[:, None]
    hit = inside[None, :] & (rank[None, :] == slot)
    return jnp.sum(jnp.where(hit, entries[None, :] - low, 0), axis=1), inside, rank


def attention_kernel(q_ref, k_ref, v_ref, o_ref):
    scores = lax.dot_general(
        q_ref[...], k_ref[...], (((1,), (1,)), ((), ())), preferred_element_type=jnp.float32
    ) * HEAD_DIM ** (-0.5)
    row_max = jnp.max(scores, axis=1, keepdims=True)
    weights = jnp.exp(scores - row_max)
    row_total = jnp.sum(weights, axis=1, keepdims=True)
    rounded = weights.astype(jnp.bfloat16)
    blended = jnp.dot(rounded, v_ref[...], preferred_element_type=jnp.float32)
    o_ref[...] = (blended / row_total).astype(o_ref.dtype)


def attend(query_rows, key_values):
    token_count, width = query_rows.shape
    key_count = key_values.shape[1]
    heads = width // HEAD_DIM
    return pl.pallas_call(
        attention_kernel,
        out_shape=jax.ShapeDtypeStruct((token_count, width), jnp.bfloat16),
        grid=(heads,),
        in_specs=[
            pl.BlockSpec((token_count, HEAD_DIM), lambda h: (0, h)),
            pl.BlockSpec((None, key_count, HEAD_DIM), lambda h: (0, 0, h)),
            pl.BlockSpec((None, key_count, HEAD_DIM), lambda h: (1, 0, h)),
        ],
        out_specs=pl.BlockSpec((token_count, HEAD_DIM), lambda h: (0, h)),
        cost_estimate=pl.CostEstimate(
            flops=4 * token_count * key_count * width,
            transcendentals=token_count * key_count * heads,
            bytes_accessed=2 * (2 * token_count * width + 2 * key_count * width),
        ),
    )(query_rows, key_values, key_values)


def per_device(queries, key_mant, key_exp, value_mant, value_exp, cycle_list, dilated_list):
    tile_blocks = queries.shape[0]
    block_length = queries.shape[2]
    width = queries.shape[3]
    col_count = lax.axis_size("col")
    row_count = lax.axis_size("row")
    distant_rows = tile_blocks // 4
    step_spacing = col_count // DILATION_TILES
    me_col = lax.axis_index("col")

    stacked = jnp.stack([dequant(key_mant, key_exp), dequant(value_mant, value_exp)])[:, :, 0]

    above = shift(stacked[:, tile_blocks - 1], "row", row_count, 1)
    below = shift(stacked[:, 0], "row", row_count, -1)

    cap = 3 if row_count >= 2 else 4
    cap = min(cap, tile_blocks)
    entries = cycle_list[0, 0]
    right_entries = shift(entries, "col", col_count, -1)
    left_entries = shift(entries, "col", col_count, 1)
    to_right, _, _ = side_slots(right_entries, 2, tile_blocks, cap)
    to_left, _, _ = side_slots(left_entries, 2 + tile_blocks, tile_blocks, cap)
    from_left = shift(jnp.take(stacked, to_right, axis=1), "col", col_count, 1)
    from_right = shift(jnp.take(stacked, to_left, axis=1), "col", col_count, -1)

    _, is_left, left_rank = side_slots(entries, 2, tile_blocks, cap)
    _, is_right, right_rank = side_slots(entries, 2 + tile_blocks, tile_blocks, cap)
    pool_index = jnp.where(
        entries == 0,
        0,
        jnp.where(entries == 1, 1, jnp.where(is_left, 2 + left_rank, 2 + cap + right_rank)),
    )
    pool = jnp.concatenate([above[:, None], below[:, None], from_left, from_right], axis=1)
    cycle_blocks = jnp.take(pool, pool_index, axis=1)

    far_source = stacked[:, 0::4]
    dilated_entries = dilated_list[0, 0]
    if step_spacing == 1:
        gathered = lax.all_gather(far_source, "col", axis=1)
        source_col = (me_col + dilated_entries // distant_rows + 1) % col_count
        dilated_index = source_col * distant_rows + dilated_entries % distant_rows
        dilated_pool = gathered.reshape(2, col_count * distant_rows, block_length, width)
    else:
        hop_tiles = []
        for hop in range(1, DILATION_TILES):
            distance = hop * step_spacing
            route = [((i + distance) % col_count, i) for i in range(col_count)]
            hop_tiles.append(lax.ppermute(far_source, "col", route))
        dilated_index = dilated_entries
        dilated_pool = jnp.stack(hop_tiles, axis=1).reshape(
            2, (DILATION_TILES - 1) * distant_rows, block_length, width
        )
    dilated_blocks = jnp.take(dilated_pool, dilated_index, axis=1)

    key_values = jnp.concatenate([stacked, cycle_blocks, dilated_blocks], axis=1)
    key_values = key_values.reshape(2, -1, width)
    token_count = tile_blocks * block_length
    result = attend(queries.reshape(token_count, width), key_values)
    return result.reshape(queries.shape)


def solution(mesh):
    in_specs = (
        P(("groups", "row"), "col", None, None),
        P(("groups", "row"), "col", None, None),
        P(("groups", "row"), "col", None, None),
        P(("groups", "row"), "col", None, None),
        P(("groups", "row"), "col", None, None),
        P(("groups", "row"), "col", None),
        P(("groups", "row"), "col", None),
    )
    out_specs = P(("groups", "row"), "col", None, None)
    return jax.shard_map(
        per_device, mesh=mesh, in_specs=in_specs, out_specs=out_specs, check_vma=False
    )
```

time: 380 us -> 194 us (0.51)
  the two profiles are of different devices: /device:TPU:0 before, /device:TPU:7 now
where the time goes in v1:
time: 194 us
  waiting for transfers between devices  91.6 us (47%)
  local copies, waits for them, and re-layouts  30.9 us (16%)
  Pallas kernels  21 us (11%)
  other arithmetic  20.6 us (11%)
  starting transfers between devices  15.9 us (8%)
  between operations  13.6 us (7%)
    ppermute x6, waiting for transfers between devices, shift(): return lax.ppermute(x, axis, pairs)  61.1 us
    all_gather x1, waiting for transfers between devices, per_device(): gathered = lax.all_gather(far_source, 'col', axis=1)  30.4 us
    pallas_call x1, Pallas kernels, attend(): pl.pallas_call(attention_kernel, out_shape=jax.ShapeDtypeStruct((token_co...  21 us
    ppermute x6, starting transfers between devices, shift(): return lax.ppermute(x, axis, pairs)  15.9 us
    all_gather x1, local copies, waits for them, and re-layouts, per_device(): gathered = lax.all_gather(far_source, 'col', axis=1)  6.1 us
    gather x1, local copies, waits for them, and re-layouts, per_device(): dilated_blocks = jnp.take(dilated_pool, dilated_index, axis=1)  4.58 us
  transfers between devices with their start and end apart: 7, of which 3 were waited for; matrix products, arithmetic and copies ran while one was open for 15% of the time, Pallas kernels for 0%

profile of v1, /device:TPU:7, one launch (start us, length us, event | category | flops | bytes accessed | tf_op | source)
XLA Modules:
  0.0 193.6 jit_solution(7707034810686304627)
XLA Ops:
  6.5 0.0 all-gather.3.cloned.1.call-start
  6.5 1.0 exponential_bitcast_fusion
  7.5 1.0 exponential_bitcast_fusion.1
  8.5 0.0 copy-start
  8.5 1.8 fusion
  10.3 0.1 copy-done
  10.4 0.3 fusion.1
  10.6 0.3 maximum_bitcast_fusion
  10.9 0.0 copy-start.1
  11.0 1.0 slice.11
  11.9 0.0 all-gather.3.cloned.1.call-update
  11.9 0.0 copy-done.1
  11.9 3.1 %collective-permute-start.4 = (s32[4]{0:T(128)S(1)}, s32[4]{0:T(128)S(1)}, u32[]{:S(2)}, u32[]{:S(2)}) collective-permute-start(s32[4]{0:T(128)S(1)} %bitcast.120), channel_id=1, source_target_pairs={{0,2},{2,4},{4,6},{6,8},{8,10},{10,12},{12,14},{1,3},{3,5},{5,7},{... | collective-permute-start | bytes 56 | tf_op jit(solution)/shard_map/ppermute | solution.py:32
  15.1 2.1 %collective-permute-start.2 = (s32[4]{0:T(128)S(1)}, s32[4]{0:T(128)}, u32[]{:S(2)}, u32[]{:S(2)}) collective-permute-start(s32[4]{0:T(128)S(1)} %bitcast.121), channel_id=1, source_target_pairs={{2,0},{4,2},{6,4},{8,6},{10,8},{12,10},{14,12},{3,1},{5,3},{7,5},{... | collective-permute-start | bytes 56 | tf_op jit(solution)/shard_map/ppermute | solution.py:32
  17.2 1.0 slice_bitcast_fusion.1
  18.2 3.2 %collective-permute-start.1 = (bf16[2,64,1536]{2,1,0:T(8,128)(2,1)}, bf16[2,64,1536]{2,1,0:T(8,128)(2,1)S(1)}, u32[]{:S(2)}, u32[]{:S(2)}) collective-permute-start(bf16[2,64,1536]{2,1,0:T(8,128)(2,1)} %get-tuple-element.7), channel_id=1, source_target_pairs={{1,0},{3,2},{5,4},{7,6},{9,8},{11,10},{13,12},{15,14},{17,16},{19,... | collective-permute-start | bytes 1179656 | tf_op jit(solution)/shard_map/ppermute | solution.py:32
  21.4 1.3 collective-permute-start
  22.7 2.0 %copy.36 = bf16[2,8,64,1536]{3,2,1,0:T(8,128)(2,1)} copy(bf16[2,8,64,1536]{3,2,0,1:T(8,128)(2,1)S(1)} %maximum_bitcast_fusion) | data formatting | bytes 6291456 | tf_op jit(solution)/shard_map/squeeze | solution.py:87
  24.7 0.0 collective-permute-done.4
  24.7 0.7 reduce-window.29
  25.4 0.7 add_bitcast_fusion
  26.0 0.1 select_reduce_fusion
  26.2 3.6 %gather_fusion.3 = bf16[3,2,64,1536]{3,2,1,0:T(8,128)(2,1)} fusion(bf16[2,8,64,1536]{3,2,1,0:T(8,128)(2,1)} %copy.36, s32[1024]{0:T(1024)S(1)} %pad_clamp_fusion.2), kind=kCustom, calls=%fused_computation.1.clone | custom fusion | bytes 2359308 | tf_op jit(solution)/shard_map/jit(_take)/gather | solution.py:100
  29.8 2.5 %select_bitcast_fusion.2 = bf16[2,3,64,1536]{3,2,0,1:T(8,128)(2,1)} fusion(bf16[3,2,64,1536]{3,2,1,0:T(8,128)(2,1)} %gather_fusion.3, pred[3]{0:T(512)(128)(4,1)S(1)} %compare_and_fusion), kind=kLoop, calls=%fused_computation.13 | loop fusion | flops 589824 | bytes 2359299 | tf_op jit(solution)/shard_map/jit(_take)/select_n | solution.py:100
  32.2 1.9 collective-permute-start.5
  34.1 0.0 collective-permute-done.2
  34.1 0.6 compare_and_fusion.4
  34.7 0.2 reduce-window.28
  34.9 0.6 broadcast_add_fusion.1
  35.5 0.1 select_reduce_fusion.1
  35.6 3.6 %gather_fusion.2 = bf16[3,2,64,1536]{3,2,1,0:T(8,128)(2,1)} fusion(bf16[2,8,64,1536]{3,2,1,0:T(8,128)(2,1)} %copy.36, s32[1024]{0:T(1024)S(1)} %pad_clamp_fusion.3), kind=kCustom, calls=%fused_computation.clone | custom fusion | bytes 2359308 | tf_op jit(solution)/shard_map/jit(_take)/gather | solution.py:99
  39.2 2.5 %select_bitcast_fusion.3 = bf16[2,3,64,1536]{3,2,0,1:T(8,128)(2,1)} fusion(bf16[3,2,64,1536]{3,2,1,0:T(8,128)(2,1)} %gather_fusion.2, pred[3]{0:T(512)(128)(4,1)S(1)} %compare_and_fusion.1), kind=kLoop, calls=%fused_computation.14 | loop fusion | flops 589824 | bytes 2359299 | tf_op jit(solution)/shard_map/jit(_take)/select_n | solution.py:99
  41.7 4.3 %collective-permute-start.3 = (bf16[2,3,64,1536]{3,2,0,1:T(8,128)(2,1)}, bf16[2,3,64,1536]{3,2,0,1:T(8,128)(2,1)}, u32[]{:S(2)}, u32[]{:S(2)}) collective-permute-start(bf16[2,3,64,1536]{3,2,0,1:T(8,128)(2,1)} %select_bitcast_fusion.3), channel_id=1, source_target_pairs={{0,2},{2,4},{4,6},{6,8},{8,10},{10,12},{12,14},{1,3},{3,5},{5,7},{... | collective-permute-start | bytes 3538952 | tf_op jit(solution)/shard_map/ppermute | solution.py:32
  46.0 0.2 reduce-window.27
  46.2 0.2 reduce-window.26
  46.4 0.0 copy-start.2
  46.4 0.7 fusion.12
  47.0 0.0 copy-done.2
  47.1 1.2 compare_and_fusion.2
  48.3 1.2 compare_and_fusion.5
  49.5 0.0 collective-permute-done.1
  49.5 0.0 collective-permute-done
  49.5 37.7 %collective-permute-done.5 = bf16[2,3,64,1536]{3,2,0,1:T(8,128)(2,1)} collective-permute-done((bf16[2,3,64,1536]{3,2,0,1:T(8,128)(2,1)}, bf16[2,3,64,1536]{3,2,0,1:T(8,128)(2,1)}, u32[]{:S(2)}, u32[]{:S(2)}) %collective-permute-start.5) | collective-permute-done | bytes 1179680 | tf_op jit(solution)/shard_map/ppermute | solution.py:32
  87.3 23.4 %collective-permute-done.3 = bf16[2,3,64,1536]{3,2,0,1:T(8,128)(2,1)} collective-permute-done((bf16[2,3,64,1536]{3,2,0,1:T(8,128)(2,1)}, bf16[2,3,64,1536]{3,2,0,1:T(8,128)(2,1)}, u32[]{:S(2)}, u32[]{:S(2)}) %collective-permute-start.3) | collective-permute-done | bytes 1179680 | tf_op jit(solution)/shard_map/ppermute | solution.py:32
  110.7 1.9 pad_maximum_fusion.1
  112.6 2.0 %copy.38 = bf16[2,8,64,1536]{3,2,1,0:T(8,128)(2,1)} copy(bf16[2,8,64,1536]{3,2,0,1:T(8,128)(2,1)S(1)} %pad_maximum_fusion.1) | data formatting | bytes 6291456 | tf_op jit(solution)/shard_map/concatenate | solution.py:109
  114.5 3.7 %gather_fusion = bf16[4,2,64,1536]{3,2,1,0:T(8,128)(2,1)} fusion(bf16[2,8,64,1536]{3,2,1,0:T(8,128)(2,1)} %copy.38, s32[1024]{0:T(1024)S(1)} %pad_clamp_fusion.1), kind=kCustom, calls=%fused_computation.2 | custom fusion | bytes 3145744 | tf_op jit(solution)/shard_map/jit(_take)/gather | solution.py:110
  118.3 30.4 %all-gather.3.cloned.1.call-done = bf16[2,16,64,1536]{3,2,0,1:T(8,128)(2,1)} async-done(((bf16[2,2,64,1536]{3,2,0,1:T(8,128)(2,1)}), bf16[2,16,64,1536]{3,2,0,1:T(8,128)(2,1)}) %all-gather.3.cloned.1.call-update) | async-done | bytes 6291472 | tf_op jit(solution)/shard_map/all_gather | solution.py:115
  148.7 6.1 %copy.39 = bf16[2,16,64,1536]{3,2,1,0:T(8,128)(2,1)} copy(bf16[2,16,64,1536]{3,2,0,1:T(8,128)(2,1)} %all-gather.3.cloned.1.call-done) | data formatting | bytes 12582912 | tf_op jit(solution)/shard_map/all_gather | solution.py:115
  154.8 0.0 copy-start.3
  154.8 0.0 copy-start.4
  154.8 4.6 %gather_fusion.1 = bf16[4,2,64,1536]{3,2,1,0:T(8,128)(2,1)} fusion(bf16[2,16,64,1536]{3,2,1,0:T(8,128)(2,1)} %copy.39, s32[1024]{0:T(1024)S(1)} %pad_clamp_fusion), kind=kCustom, calls=%fused_computation.3 | custom fusion | bytes 3145744 | tf_op jit(solution)/shard_map/jit(_take)/gather | solution.py:129
  159.4 0.0 copy-done.3
  159.4 0.0 copy-done.4
  159.4 2.2 %select_bitcast_fusion = (bf16[2,4,64,1536]{3,2,0,1:T(8,128)(2,1)S(1)}, bf16[2,4,64,1536]{3,2,0,1:T(8,128)(2,1)S(1)}) fusion(bf16[4,2,64,1536]{3,2,1,0:T(8,128)(2,1)} %gather_fusion.1, pred[4]{0:T(512)(128)(4,1)S(1)} %copy-done.4, bf16[4,2,64,1536]{3,2,1,0:T(8,128)(2,1)} %gather_fusion, pred[4]{0:T(512)(128)(4,1)S(1)} %copy-done.3), kind=kLoop, calls=%fused_computation.11 | loop fusion | flops 1572864 | bytes 6291464 | tf_op jit(solution)/shard_map/jit(_take)/select_n | solution.py:129
  161.6 0.8 pad_maximum_fusion
  162.4 3.3 %copy.40 = bf16[2,16,64,1536]{3,2,1,0:T(8,128)(2,1)} copy(bf16[2,16,64,1536]{3,2,0,1:T(8,128)(2,1)S(1)} %pad_maximum_fusion) | data formatting | bytes 12582912 | tf_op jit(solution)/shard_map/concatenate | solution.py:131
  165.7 21.0 %shard_map.73 = bf16[512,1536]{1,0:T(8,128)(2,1)} custom-call(bf16[512,1536]{1,0:T(8,128)(2,1)} %bitcast.118, bf16[2,1024,1536]{2,1,0:T(8,128)(2,1)} %bitcast.114, bf16[2,1024,1536]{2,1,0:T(8,128)(2,1)} %bitcast.115), custom_call_target="tpu_custom_call" | custom-call | flops 3221225472 | bytes 9437184 | tf_op jit(solution)/shard_map/pallas_call | solution.py:59
  (13 shorter events, 0.1 us)
Async XLA Ops:
  6.5 142.2 %all-gather.3.cloned.1.call-start = ((), (), s32[]{:S(2)}) async-start(), calls=%async_computation | async-start | bytes 7077888 | tf_op jit(solution)/shard_map/all_gather | solution.py:115
  8.5 1.9 copy-start
  10.9 1.0 copy-start.1
  11.9 12.7 %collective-permute-start.4 = (s32[4]{0:T(128)S(1)}, s32[4]{0:T(128)S(1)}, u32[]{:S(2)}, u32[]{:S(2)}) collective-permute-start(s32[4]{0:T(128)S(1)} %bitcast.120), channel_id=1, source_target_pairs={{0,2},{2,4},{4,6},{6,8},{8,10},{10,12},{12,14},{1,3},{3,5},{5,7},{... | collective-permute-start | bytes 56 | tf_op jit(solution)/shard_map/ppermute | solution.py:32
  15.1 19.0 %collective-permute-start.2 = (s32[4]{0:T(128)S(1)}, s32[4]{0:T(128)}, u32[]{:S(2)}, u32[]{:S(2)}) collective-permute-start(s32[4]{0:T(128)S(1)} %bitcast.121), channel_id=1, source_target_pairs={{2,0},{4,2},{6,4},{8,6},{10,8},{12,10},{14,12},{3,1},{5,3},{7,5},{... | collective-permute-start | bytes 56 | tf_op jit(solution)/shard_map/ppermute | solution.py:32
  18.2 31.3 %collective-permute-start.1 = (bf16[2,64,1536]{2,1,0:T(8,128)(2,1)}, bf16[2,64,1536]{2,1,0:T(8,128)(2,1)S(1)}, u32[]{:S(2)}, u32[]{:S(2)}) collective-permute-start(bf16[2,64,1536]{2,1,0:T(8,128)(2,1)} %get-tuple-element.7), channel_id=1, source_target_pairs={{1,0},{3,2},{5,4},{7,6},{9,8},{11,10},{13,12},{15,14},{17,16},{19,... | collective-permute-start | bytes 1179656 | tf_op jit(solution)/shard_map/ppermute | solution.py:32
  21.4 28.1 %collective-permute-start = (bf16[2,64,1536]{2,1,0:T(8,128)(2,1)}, bf16[2,64,1536]{2,1,0:T(8,128)(2,1)}, u32[]{:S(2)}, u32[]{:S(2)}) collective-permute-start(bf16[2,64,1536]{2,1,0:T(8,128)(2,1)} %get-tuple-element.6), channel_id=1, source_target_pairs={{0,1},{2,3},{4,5},{6,7},{8,9},{10,11},{12,13},{14,15},{16,17},{18,... | collective-permute-start | bytes 1179656 | tf_op jit(solution)/shard_map/ppermute | solution.py:32
  32.2 55.1 %collective-permute-start.5 = (bf16[2,3,64,1536]{3,2,0,1:T(8,128)(2,1)}, bf16[2,3,64,1536]{3,2,0,1:T(8,128)(2,1)}, u32[]{:S(2)}, u32[]{:S(2)}) collective-permute-start(bf16[2,3,64,1536]{3,2,0,1:T(8,128)(2,1)} %select_bitcast_fusion.2), channel_id=1, source_target_pairs={{2,0},{4,2},{6,4},{8,6},{10,8},{12,10},{14,12},{3,1},{5,3},{7,5},{... | collective-permute-start | bytes 3538952 | tf_op jit(solution)/shard_map/ppermute | solution.py:32
  41.7 69.0 %collective-permute-start.3 = (bf16[2,3,64,1536]{3,2,0,1:T(8,128)(2,1)}, bf16[2,3,64,1536]{3,2,0,1:T(8,128)(2,1)}, u32[]{:S(2)}, u32[]{:S(2)}) collective-permute-start(bf16[2,3,64,1536]{3,2,0,1:T(8,128)(2,1)} %select_bitcast_fusion.3), channel_id=1, source_target_pairs={{0,2},{2,4},{4,6},{6,8},{8,10},{10,12},{12,14},{1,3},{3,5},{5,7},{... | collective-permute-start | bytes 3538952 | tf_op jit(solution)/shard_map/ppermute | solution.py:32
  46.4 0.7 copy-start.2
  154.8 4.6 %copy-start.3 = (pred[4]{0:T(512)(128)(4,1)S(1)}, pred[4]{0:T(512)(128)(4,1)}, u32[]{:S(2)}) copy-start(pred[4]{0:T(512)(128)(4,1)} %compare_and_fusion.5) | copy-start | bytes 16
  154.8 4.6 %copy-start.4 = (pred[4]{0:T(512)(128)(4,1)S(1)}, pred[4]{0:T(512)(128)(4,1)}, u32[]{:S(2)}) copy-start(pred[4]{0:T(512)(128)(4,1)} %compare_and_fusion.2) | copy-start | bytes 16
Sparse Core Ops, SparseCore 0:
  12.1 136.5 all-gather.2

commit v2 on v1

--- a/solution.py
+++ b/solution.py
@@ -38,6 +38,39 @@
     slot = jnp.arange(cap, dtype=jnp.int32)[:, None]
     hit = inside[None, :] & (rank[None, :] == slot)
     return jnp.sum(jnp.where(hit, entries[None, :] - low, 0), axis=1), inside, rank
+
+
+def ring_gather(item, count, me):
+    order = list(range(0, count, 2)) + list(range(count - 1 - count % 2, 0, -2))
+    position = [0] * count
+    for place, col in enumerate(order):
+        position[col] = place
+    forward = [(order[i], order[(i + 1) % count]) for i in range(count)]
+    backward = [(order[(i + 1) % count], order[i]) for i in range(count)]
+    half = count // 2
+    rows = item.shape[1]
+    split = (rows + 1) // 2
+    ahead, behind = item, item
+    slots = [None] * (count - 1)
+    for distance in range(1, half + 1):
+        if distance == half and count % 2 == 0:
+            first = lax.ppermute(ahead[:, :split], "col", forward)
+            parts = [first]
+            if split < rows:
+                parts.append(lax.ppermute(behind[:, split:], "col", backward))
+            slots[distance - 1] = jnp.concatenate(parts, axis=1) if len(parts) > 1 else first
+            continue
+        ahead = lax.ppermute(ahead, "col", forward)
+        slots[distance - 1] = ahead
+        behind = lax.ppermute(behind, "col", backward)
+        slots[count - distance - 1] = behind
+    pool = jnp.concatenate(slots, axis=1)
+    table = jnp.array(position, dtype=jnp.int32)
+
+    def source_slot(col):
+        return (table[me] - table[col]) % count - 1
+
+    return pool, source_slot
 
 
 def attention_kernel(q_ref, k_ref, v_ref, o_ref):
@@ -89,22 +122,32 @@
     above = shift(stacked[:, tile_blocks - 1], "row", row_count, 1)
     below = shift(stacked[:, 0], "row", row_count, -1)
 
-    cap = 3 if row_count >= 2 else 4
-    cap = min(cap, tile_blocks)
+    edge_cap = min(3 if row_count >= 2 else 4, tile_blocks)
+    main_cap = edge_cap - 1 if col_count >= 3 else edge_cap
     entries = cycle_list[0, 0]
     right_entries = shift(entries, "col", col_count, -1)
     left_entries = shift(entries, "col", col_count, 1)
-    to_right, _, _ = side_slots(right_entries, 2, tile_blocks, cap)
-    to_left, _, _ = side_slots(left_entries, 2 + tile_blocks, tile_blocks, cap)
-    from_left = shift(jnp.take(stacked, to_right, axis=1), "col", col_count, 1)
-    from_right = shift(jnp.take(stacked, to_left, axis=1), "col", col_count, -1)
+    to_right, _, _ = side_slots(right_entries, 2, tile_blocks, edge_cap)
+    to_left, _, _ = side_slots(left_entries, 2 + tile_blocks, tile_blocks, edge_cap)
+    right_payload = jnp.take(stacked, to_right, axis=1)
+    left_payload = jnp.take(stacked, to_left, axis=1)
+    from_left = shift(right_payload[:, :main_cap], "col", col_count, 1)
+    from_right = shift(left_payload[:, :main_cap], "col", col_count, -1)
+    if main_cap < edge_cap:
+        last = col_count - 1
+        from_left = jnp.concatenate(
+            [from_left, lax.ppermute(right_payload[:, main_cap:], "col", [(last - 1, last)])], axis=1
+        )
+        from_right = jnp.concatenate(
+            [from_right, lax.ppermute(left_payload[:, main_cap:], "col", [(1, 0)])], axis=1
+        )
 
-    _, is_left, left_rank = side_slots(entries, 2, tile_blocks, cap)
-    _, is_right, right_rank = side_slots(entries, 2 + tile_blocks, tile_blocks, cap)
+    _, is_left, left_rank = side_slots(entries, 2, tile_blocks, edge_cap)
+    _, is_right, right_rank = side_slots(entries, 2 + tile_blocks, tile_blocks, edge_cap)
     pool_index = jnp.where(
         entries == 0,
         0,
-        jnp.where(entries == 1, 1, jnp.where(is_left, 2 + left_rank, 2 + cap + right_rank)),
+        jnp.where(entries == 1, 1, jnp.where(is_left, 2 + left_rank, 2 + edge_cap + right_rank)),
     )
     pool = jnp.concatenate([above[:, None], below[:, None], from_left, from_right], axis=1)
     cycle_blocks = jnp.take(pool, pool_index, axis=1)
@@ -112,10 +155,9 @@
     far_source = stacked[:, 0::4]
     dilated_entries = dilated_list[0, 0]
     if step_spacing == 1:
-        gathered = lax.all_gather(far_source, "col", axis=1)
+        dilated_pool, source_slot = ring_gather(far_source, col_count, me_col)
         source_col = (me_col + dilated_entries // distant_rows + 1) % col_count
-        dilated_index = source_col * distant_rows + dilated_entries % distant_rows
-        dilated_pool = gathered.reshape(2, col_count * distant_rows, block_length, width)
+        dilated_index = source_slot(source_col) * distant_rows + dilated_entries % distant_rows
     else:
         hop_tiles = []
         for hop in range(1, DILATION_TILES):

time: 194 us -> 187 us (0.964)
  the two profiles are of different devices: /device:TPU:7 before, /device:TPU:0 now
where the time goes in v2:
time: 187 us; the launch traced here: 186 us
  waiting for transfers between devices  60.1 us (32%)
  local copies, waits for them, and re-layouts  50 us (27%)
  other arithmetic  28.4 us (15%)
  starting transfers between devices  26 us (14%)
  Pallas kernels  21 us (11%)
    ppermute x6, waiting for transfers between devices, shift(): return lax.ppermute(x, axis, pairs)  25.2 us
    pallas_call x1, Pallas kernels, attend(): pl.pallas_call(attention_kernel, out_shape=jax.ShapeDtypeStruct((token_co...  21 us
    ppermute x6, starting transfers between devices, shift(): return lax.ppermute(x, axis, pairs)  14.5 us
    ppermute x3, waiting for transfers between devices, ring_gather(): ahead = lax.ppermute(ahead, 'col', forward)  13.1 us
    unnamed x26, local copies, waits for them, and re-layouts  12.2 us
    ppermute x1, waiting for transfers between devices, per_device(): lax.ppermute(left_payload[:, main_cap:], 'col', [(1, 0)])  8.32 us
    concatenate x2, local copies, waits for them, and re-layouts, ring_gather(): pool = jnp.concatenate(slots, axis=1)  7.71 us
    ppermute x1, waiting for transfers between devices, ring_gather(): parts.append(lax.ppermute(behind[:, split:], 'col', backward))  7.15 us
  transfers between devices with their start and end apart: 16, of which 8 were waited for; matrix products, arithmetic and copies ran while one was open for 28% of the time, Pallas kernels for 0%

profile of v2, /device:TPU:0, one launch (start us, length us, event | category | flops | bytes accessed | tf_op | source)
XLA Modules:
  0.0 185.8 jit_solution(7228107412096980315)
XLA Ops:
  0.0 1.1 exponential_bitcast_fusion
  1.1 1.0 exponential_bitcast_fusion.1
  2.1 1.7 fusion
  4.4 1.0 slice.33
  5.3 3.0 %collective-permute-start.8 = (bf16[2,2,64,1536]{3,2,0,1:T(8,128)(2,1)}, bf16[2,2,64,1536]{3,2,0,1:T(8,128)(2,1)}, u32[]{:S(2)}, u32[]{:S(2)}) collective-permute-start(bf16[2,2,64,1536]{3,2,0,1:T(8,128)(2,1)} %slice.33), channel_id=1, source_target_pairs={{0,4},{4,8},{8,12},{12,14},{14,10},{10,6},{6,2},{2,0},{1,5},{5,9},... | collective-permute-start | bytes 2359304 | tf_op jit(solution)/shard_map/ppermute | solution.py:63
  8.4 4.4 %collective-permute-start.5 = (s32[4]{0:T(128)S(1)}, s32[4]{0:T(128)}, u32[]{:S(2)}, u32[]{:S(2)}) collective-permute-start(s32[4]{0:T(128)S(1)} %bitcast.119), channel_id=1, source_target_pairs={{0,2},{2,4},{4,6},{6,8},{8,10},{10,12},{12,14},{1,3},{3,5},{5,7},{... | collective-permute-start | bytes 56 | tf_op jit(solution)/shard_map/ppermute | solution.py:32
  12.7 1.3 collective-permute-start.2
  14.0 1.0 slice_bitcast_fusion
  15.1 1.3 collective-permute-start
  16.4 1.9 %copy.29 = bf16[2,8,64,1536]{3,2,1,0:T(8,128)(2,1)} copy(bf16[2,8,64,1536]{3,2,0,1:T(8,128)(2,1)S(1)} %maximum_bitcast_fusion) | data formatting | bytes 6291456 | tf_op jit(solution)/shard_map/squeeze | solution.py:120
  18.8 1.4 reduce-window.27
  20.2 0.7 reduce-window.26
  20.9 0.7 fusion.15
  21.6 1.2 compare_and_fusion.5
  24.0 2.2 %collective-permute-done.2 = s32[4]{0:T(128)} collective-permute-done((s32[4]{0:T(128)S(1)}, s32[4]{0:T(128)}, u32[]{:S(2)}, u32[]{:S(2)}) %collective-permute-start.2) | collective-permute-done | bytes 48 | tf_op jit(solution)/shard_map/ppermute | solution.py:32
  26.2 1.3 collective-permute-start.1
  27.5 1.1 compare_and_fusion.4
  28.6 1.4 reduce-window.28
  32.0 3.6 %gather_fusion.3 = bf16[3,2,64,1536]{3,2,1,0:T(8,128)(2,1)} fusion(bf16[2,8,64,1536]{3,2,1,0:T(8,128)(2,1)} %copy.29, s32[1024]{0:T(1024)S(1)} %pad_clamp_fusion.4), kind=kCustom, calls=%fused_computation.clone | custom fusion | bytes 2359308 | tf_op jit(solution)/shard_map/jit(_take)/gather | solution.py:132
  35.5 1.4 select_bitcast_fusion.3
  37.0 1.0 slice.48
  37.9 0.8 slice.49
  39.3 0.7 reduce-window.29
  40.0 0.7 add_bitcast_fusion
  41.9 0.7 pad_clamp_fusion.1
  42.6 3.6 %gather_fusion.4 = bf16[3,2,64,1536]{3,2,1,0:T(8,128)(2,1)} fusion(bf16[2,8,64,1536]{3,2,1,0:T(8,128)(2,1)} %copy.29, s32[1024]{0:T(1024)S(1)} %get-tuple-element.15), kind=kCustom, calls=%fused_computation.1.clone | custom fusion | bytes 2359308 | tf_op jit(solution)/shard_map/jit(_take)/gather | solution.py:133
  46.1 1.4 select_bitcast_fusion.2
  47.6 0.9 slice.50
  48.5 0.8 slice.51
  49.9 5.0 %collective-permute-start.3 = (bf16[2,2,64,1536]{3,2,0,1:T(8,128)(2,1)}, bf16[2,2,64,1536]{3,2,0,1:T(8,128)(2,1)S(1)}, u32[]{:S(2)}, u32[]{:S(2)}) collective-permute-start(bf16[2,2,64,1536]{3,2,0,1:T(8,128)(2,1)} %slice.48), channel_id=1, source_target_pairs={{0,2},{2,4},{4,6},{6,8},{8,10},{10,12},{12,14},{1,3},{3,5},{5,7},{... | collective-permute-start | bytes 2359304 | tf_op jit(solution)/shard_map/ppermute | solution.py:32
  54.9 1.2 fusion.17
  56.2 1.2 compare_and_fusion.2
  57.4 0.7 collective-permute-start.4
  58.1 1.3 collective-permute-start.6
  59.4 1.0 bitcast_dynamic-update-slice_fusion
  60.5 2.2 %collective-permute-start.9 = (bf16[2,2,64,1536]{3,2,0,1:T(8,128)(2,1)}, bf16[2,2,64,1536]{3,2,0,1:T(8,128)(2,1)}, u32[]{:S(2)}, u32[]{:S(2)}) collective-permute-start(bf16[2,2,64,1536]{3,2,0,1:T(8,128)(2,1)} %collective-permute-done.8), channel_id=1, source_target_pairs={{0,4},{4,8},{8,12},{12,14},{14,10},{10,6},{6,2},{2,0},{1,5},{5,9},... | collective-permute-start | bytes 2359304 | tf_op jit(solution)/shard_map/ppermute | solution.py:63
  62.7 2.1 %constant_dynamic-update-slice_fusion.11 = bf16[2,14,64,1536]{3,2,0,1:T(8,128)(2,1)} fusion(bf16[2,2,64,1536]{3,2,0,1:T(8,128)(2,1)} %collective-permute-done.8), kind=kLoop, calls=%fused_computation.32 | loop fusion | bytes 1572864
  64.8 1.3 collective-permute-start.7
  66.1 23.0 %collective-permute-done.3 = bf16[2,2,64,1536]{3,2,0,1:T(8,128)(2,1)S(1)} collective-permute-done((bf16[2,2,64,1536]{3,2,0,1:T(8,128)(2,1)}, bf16[2,2,64,1536]{3,2,0,1:T(8,128)(2,1)S(1)}, u32[]{:S(2)}, u32[]{:S(2)}) %collective-permute-start.3) | collective-permute-done | bytes 786464 | tf_op jit(solution)/shard_map/ppermute | solution.py:32
  89.1 2.4 %collective-permute-start.13 = (bf16[2,2,64,1536]{3,2,0,1:T(8,128)(2,1)}, bf16[2,2,64,1536]{3,2,0,1:T(8,128)(2,1)}, u32[]{:S(2)}, u32[]{:S(2)}) collective-permute-start(bf16[2,2,64,1536]{3,2,0,1:T(8,128)(2,1)} %collective-permute-done.12), channel_id=1, source_target_pairs={{4,0},{8,4},{12,8},{14,12},{10,14},{6,10},{2,6},{0,2},{5,1},{9,5},... | collective-permute-start | bytes 2359304 | tf_op jit(solution)/shard_map/ppermute | solution.py:65
  91.6 5.4 %collective-permute-done.9 = bf16[2,2,64,1536]{3,2,0,1:T(8,128)(2,1)} collective-permute-done((bf16[2,2,64,1536]{3,2,0,1:T(8,128)(2,1)}, bf16[2,2,64,1536]{3,2,0,1:T(8,128)(2,1)}, u32[]{:S(2)}, u32[]{:S(2)}) %collective-permute-start.9) | collective-permute-done | bytes 786464 | tf_op jit(solution)/shard_map/ppermute | solution.py:63
  97.1 8.3 %collective-permute-done.7 = bf16[2,1,64,1536]{3,2,0,1:T(8,128)(2,1)S(1)} collective-permute-done((bf16[2,1,64,1536]{3,2,0,1:T(8,128)(2,1)S(1)}, bf16[2,1,64,1536]{3,2,0,1:T(8,128)(2,1)S(1)}, u32[]{:S(2)}, u32[]{:S(2)}) %collective-permute-start.7) | collective-permute-done | bytes 393248 | tf_op jit(solution)/shard_map/ppermute | solution.py:142
  105.4 2.0 %copy.31 = bf16[2,8,64,1536]{3,2,1,0:T(8,128)(2,1)} copy(bf16[2,8,64,1536]{3,2,0,1:T(8,128)(2,1)S(1)} %constant_dynamic-update-slice_fusion) | data formatting | bytes 6291456 | tf_op jit(solution)/shard_map/concatenate | solution.py:152
  107.4 3.7 %gather_fusion = bf16[4,2,64,1536]{3,2,1,0:T(8,128)(2,1)} fusion(bf16[2,8,64,1536]{3,2,1,0:T(8,128)(2,1)} %copy.31, s32[1024]{0:T(1024)S(1)} %pad_clamp_fusion.2), kind=kCustom, calls=%fused_computation.2 | custom fusion | bytes 3145744 | tf_op jit(solution)/shard_map/jit(_take)/gather | solution.py:153
  111.1 0.8 collective-permute-start.14
  111.9 2.8 %select_bitcast_fusion.1 = bf16[2,4,64,1536]{3,2,0,1:T(8,128)(2,1)} fusion(bf16[4,2,64,1536]{3,2,1,0:T(8,128)(2,1)} %gather_fusion, pred[4]{0:T(512)(128)(4,1)S(1)} %copy-done.6), kind=kLoop, calls=%fused_computation.12 | loop fusion | flops 786432 | bytes 3145732 | tf_op jit(solution)/shard_map/jit(_take)/select_n | solution.py:153
  114.7 7.6 %collective-permute-done.10 = bf16[2,2,64,1536]{3,2,0,1:T(8,128)(2,1)} collective-permute-done((bf16[2,2,64,1536]{3,2,0,1:T(8,128)(2,1)}, bf16[2,2,64,1536]{3,2,0,1:T(8,128)(2,1)}, u32[]{:S(2)}, u32[]{:S(2)}) %collective-permute-start.10) | collective-permute-done | bytes 786464 | tf_op jit(solution)/shard_map/ppermute | solution.py:63
  122.3 1.0 slice.52
  123.4 2.1 %constant_dynamic-update-slice_fusion.10 = bf16[2,14,64,1536]{3,2,0,1:T(8,128)(2,1)} fusion(bf16[2,14,64,1536]{3,2,0,1:T(8,128)(2,1)} %constant_dynamic-update-slice_fusion.11, bf16[2,2,64,1536]{3,2,0,1:T(8,128)(2,1)} %collective-permute-done.9), kind=kLoop, calls=%fused_computation.31 | loop fusion | bytes 1572864
  125.5 5.9 %collective-permute-done.14 = bf16[2,2,64,1536]{3,2,0,1:T(8,128)(2,1)S(1)} collective-permute-done((bf16[2,2,64,1536]{3,2,0,1:T(8,128)(2,1)}, bf16[2,2,64,1536]{3,2,0,1:T(8,128)(2,1)S(1)}, u32[]{:S(2)}, u32[]{:S(2)}) %collective-permute-start.14) | collective-permute-done | bytes 786464 | tf_op jit(solution)/shard_map/ppermute | solution.py:65
  131.4 1.0 collective-permute-start.15
  132.5 2.1 %constant_dynamic-update-slice_fusion.9 = bf16[2,14,64,1536]{3,2,0,1:T(8,128)(2,1)} fusion(bf16[2,14,64,1536]{3,2,0,1:T(8,128)(2,1)} %constant_dynamic-update-slice_fusion.10, bf16[2,2,64,1536]{3,2,0,1:T(8,128)(2,1)} %collective-permute-done.10), kind=kLoop, calls=%fused_computation.30 | loop fusion | bytes 1572864
  135.0 0.8 constant_dynamic-update-slice_fusion.8
  135.8 7.2 %collective-permute-done.15 = bf16[2,1,64,1536]{3,2,0,1:T(8,128)(2,1)S(1)} collective-permute-done((bf16[2,1,64,1536]{3,2,0,1:T(8,128)(2,1)S(1)}, bf16[2,1,64,1536]{3,2,0,1:T(8,128)(2,1)S(1)}, u32[]{:S(2)}, u32[]{:S(2)}) %collective-permute-start.15) | collective-permute-done | bytes 393248 | tf_op jit(solution)/shard_map/ppermute | solution.py:60
  142.9 0.8 constant_dynamic-update-slice_fusion.7
  143.7 0.9 constant_dynamic-update-slice_fusion.6
  144.7 2.1 %constant_dynamic-update-slice_fusion.5 = bf16[2,14,64,1536]{3,2,0,1:T(8,128)(2,1)} fusion(bf16[2,14,64,1536]{3,2,0,1:T(8,128)(2,1)} %constant_dynamic-update-slice_fusion.6, bf16[2,2,64,1536]{3,2,0,1:T(8,128)(2,1)} %collective-permute-done.13), kind=kLoop, calls=%fused_computation.26 | loop fusion | bytes 1572864
  146.7 2.1 %constant_dynamic-update-slice_fusion.4 = bf16[2,14,64,1536]{3,2,0,1:T(8,128)(2,1)} fusion(bf16[2,14,64,1536]{3,2,0,1:T(8,128)(2,1)} %constant_dynamic-update-slice_fusion.5, bf16[2,2,64,1536]{3,2,0,1:T(8,128)(2,1)} %collective-permute-done.12), kind=kLoop, calls=%fused_computation.25 | loop fusion | bytes 1572864 | tf_op jit(solution)/shard_map/concatenate | solution.py:67
  148.8 5.6 %copy.32 = bf16[2,14,64,1536]{3,2,1,0:T(8,128)(2,1)} copy(bf16[2,14,64,1536]{3,2,0,1:T(8,128)(2,1)} %constant_dynamic-update-slice_fusion.4) | data formatting | bytes 11010048 | tf_op jit(solution)/shard_map/concatenate | solution.py:67
  154.4 4.3 %gather_fusion.2 = bf16[4,2,64,1536]{3,2,1,0:T(8,128)(2,1)} fusion(bf16[2,14,64,1536]{3,2,1,0:T(8,128)(2,1)} %copy.32, s32[1024]{0:T(1024)S(1)} %pad_clamp_fusion), kind=kCustom, calls=%fused_computation.4 | custom fusion | bytes 3145744 | tf_op jit(solution)/shard_map/jit(_take)/gather | solution.py:171
  158.8 1.7 select_bitcast_fusion
  160.7 0.7 pad_maximum_fusion
  161.4 3.4 %copy.33 = bf16[2,16,64,1536]{3,2,1,0:T(8,128)(2,1)} copy(bf16[2,16,64,1536]{3,2,0,1:T(8,128)(2,1)S(1)} %pad_maximum_fusion) | data formatting | bytes 12582912 | tf_op jit(solution)/shard_map/concatenate | solution.py:173
  164.8 21.0 %shard_map.82 = bf16[512,1536]{1,0:T(8,128)(2,1)} custom-call(bf16[512,1536]{1,0:T(8,128)(2,1)} %bitcast.118, bf16[2,1024,1536]{2,1,0:T(8,128)(2,1)} %bitcast.114, bf16[2,1024,1536]{2,1,0:T(8,128)(2,1)} %bitcast.115), custom_call_target="tpu_custom_call" | custom-call | flops 3221225472 | bytes 9437184 | tf_op jit(solution)/shard_map/pallas_call | solution.py:92
  (51 shorter events, 7.7 us)
Async XLA Ops:
  0.0 3.8 %copy-start.2 = (bf16[8,1,64,1536]{3,2,1,0:T(8,128)(2,1)S(1)}, bf16[8,1,64,1536]{3,2,1,0:T(8,128)(2,1)}, u32[]{:S(2)}) copy-start(bf16[8,1,64,1536]{3,2,1,0:T(8,128)(2,1)} %param.11) | copy-start | bytes 4718596
  4.1 4.3 %copy-start.4 = (s32[1,1,4]{2,1,0:T(1,128)S(1)}, s32[1,1,4]{2,1,0:T(1,128)}, u32[]{:S(2)}) copy-start(s32[1,1,4]{2,1,0:T(1,128)} %param.15) | copy-start | bytes 52
  5.3 55.1 %collective-permute-start.8 = (bf16[2,2,64,1536]{3,2,0,1:T(8,128)(2,1)}, bf16[2,2,64,1536]{3,2,0,1:T(8,128)(2,1)}, u32[]{:S(2)}, u32[]{:S(2)}) collective-permute-start(bf16[2,2,64,1536]{3,2,0,1:T(8,128)(2,1)} %slice.33), channel_id=1, source_target_pairs={{0,4},{4,8},{8,12},{12,14},{14,10},{10,6},{6,2},{2,0},{1,5},{5,9},... | collective-permute-start | bytes 2359304 | tf_op jit(solution)/shard_map/ppermute | solution.py:63
  8.4 56.4 %collective-permute-start.12 = (bf16[2,2,64,1536]{3,2,0,1:T(8,128)(2,1)}, bf16[2,2,64,1536]{3,2,0,1:T(8,128)(2,1)}, u32[]{:S(2)}, u32[]{:S(2)}) collective-permute-start(bf16[2,2,64,1536]{3,2,0,1:T(8,128)(2,1)} %slice.33), channel_id=1, source_target_pairs={{4,0},{8,4},{12,8},{14,12},{10,14},{6,10},{2,6},{0,2},{5,1},{9,5},... | collective-permute-start | bytes 2359304 | tf_op jit(solution)/shard_map/ppermute | solution.py:65
  8.4 30.4 %collective-permute-start.5 = (s32[4]{0:T(128)S(1)}, s32[4]{0:T(128)}, u32[]{:S(2)}, u32[]{:S(2)}) collective-permute-start(s32[4]{0:T(128)S(1)} %bitcast.119), channel_id=1, source_target_pairs={{0,2},{2,4},{4,6},{6,8},{8,10},{10,12},{12,14},{1,3},{3,5},{5,7},{... | collective-permute-start | bytes 56 | tf_op jit(solution)/shard_map/ppermute | solution.py:32
  12.7 13.5 %collective-permute-start.2 = (s32[4]{0:T(128)S(1)}, s32[4]{0:T(128)}, u32[]{:S(2)}, u32[]{:S(2)}) collective-permute-start(s32[4]{0:T(128)S(1)} %bitcast.120), channel_id=1, source_target_pairs={{2,0},{4,2},{6,4},{8,6},{10,8},{12,10},{14,12},{3,1},{5,3},{7,5},{... | collective-permute-start | bytes 56 | tf_op jit(solution)/shard_map/ppermute | solution.py:32
  15.1 42.3 %collective-permute-start = (bf16[2,64,1536]{2,1,0:T(8,128)(2,1)}, bf16[2,64,1536]{2,1,0:T(8,128)(2,1)S(1)}, u32[]{:S(2)}, u32[]{:S(2)}) collective-permute-start(bf16[2,64,1536]{2,1,0:T(8,128)(2,1)} %get-tuple-element.7), channel_id=1, source_target_pairs={{0,1},{2,3},{4,5},{6,7},{8,9},{10,11},{12,13},{14,15},{16,17},{18,... | collective-permute-start | bytes 1179656 | tf_op jit(solution)/shard_map/ppermute | solution.py:32
  16.4 6.4 %copy-start.5 = (s32[1,1,4]{2,1,0:T(1,128)S(1)}, s32[1,1,4]{2,1,0:T(1,128)}, u32[]{:S(2)}) copy-start(s32[1,1,4]{2,1,0:T(1,128)} %param.16) | copy-start | bytes 52
  16.4 7.0 %copy-start = (s32[8]{0:T(128)S(1)}, s32[8]{0:T(128)}, u32[]{:S(2)}) copy-start(s32[8]{0:T(128)} %constant.126.clone) | copy-start | bytes 100
  26.2 31.9 %collective-permute-start.1 = (bf16[2,64,1536]{2,1,0:T(8,128)(2,1)}, bf16[2,64,1536]{2,1,0:T(8,128)(2,1)}, u32[]{:S(2)}, u32[]{:S(2)}) collective-permute-start(bf16[2,64,1536]{2,1,0:T(8,128)(2,1)} %get-tuple-element.6), channel_id=1, source_target_pairs={{1,0},{3,2},{5,4},{7,6},{9,8},{11,10},{13,12},{15,14},{17,16},{19,... | collective-permute-start | bytes 1179656 | tf_op jit(solution)/shard_map/ppermute | solution.py:32
  49.9 14.9 %copy-start.3 = (bf16[2,1,64,1536]{3,2,0,1:T(8,128)(2,1)S(1)}, bf16[2,1,64,1536]{3,2,0,1:T(8,128)(2,1)}, u32[]{:S(2)}) copy-start(bf16[2,1,64,1536]{3,2,0,1:T(8,128)(2,1)} %slice.51) | copy-start | bytes 1179652
  49.9 39.1 %collective-permute-start.3 = (bf16[2,2,64,1536]{3,2,0,1:T(8,128)(2,1)}, bf16[2,2,64,1536]{3,2,0,1:T(8,128)(2,1)S(1)}, u32[]{:S(2)}, u32[]{:S(2)}) collective-permute-start(bf16[2,2,64,1536]{3,2,0,1:T(8,128)(2,1)} %slice.48), channel_id=1, source_target_pairs={{0,2},{2,4},{4,6},{6,8},{8,10},{10,12},{12,14},{1,3},{3,5},{5,7},{... | collective-permute-start | bytes 2359304 | tf_op jit(solution)/shard_map/ppermute | solution.py:32
  57.4 34.1 %collective-permute-start.4 = (bf16[2,1,64,1536]{3,2,0,1:T(8,128)(2,1)}, bf16[2,1,64,1536]{3,2,0,1:T(8,128)(2,1)S(1)}, u32[]{:S(2)}, u32[]{:S(2)}) collective-permute-start(bf16[2,1,64,1536]{3,2,0,1:T(8,128)(2,1)} %slice.49), channel_id=1, source_target_pairs={{12,14},{13,15},{28,30},{29,31}} | collective-permute-start | bytes 1179656 | tf_op jit(solution)/shard_map/ppermute | solution.py:139
  58.1 33.4 %collective-permute-start.6 = (bf16[2,2,64,1536]{3,2,0,1:T(8,128)(2,1)}, bf16[2,2,64,1536]{3,2,0,1:T(8,128)(2,1)S(1)}, u32[]{:S(2)}, u32[]{:S(2)}) collective-permute-start(bf16[2,2,64,1536]{3,2,0,1:T(8,128)(2,1)} %slice.50), channel_id=1, source_target_pairs={{2,0},{4,2},{6,4},{8,6},{10,8},{12,10},{14,12},{3,1},{5,3},{7,5},{... | collective-permute-start | bytes 2359304 | tf_op jit(solution)/shard_map/ppermute | solution.py:32
  60.5 36.6 %collective-permute-start.9 = (bf16[2,2,64,1536]{3,2,0,1:T(8,128)(2,1)}, bf16[2,2,64,1536]{3,2,0,1:T(8,128)(2,1)}, u32[]{:S(2)}, u32[]{:S(2)}) collective-permute-start(bf16[2,2,64,1536]{3,2,0,1:T(8,128)(2,1)} %collective-permute-done.8), channel_id=1, source_target_pairs={{0,4},{4,8},{8,12},{12,14},{14,10},{10,6},{6,2},{2,0},{1,5},{5,9},... | collective-permute-start | bytes 2359304 | tf_op jit(solution)/shard_map/ppermute | solution.py:63
  64.8 40.6 %collective-permute-start.7 = (bf16[2,1,64,1536]{3,2,0,1:T(8,128)(2,1)S(1)}, bf16[2,1,64,1536]{3,2,0,1:T(8,128)(2,1)S(1)}, u32[]{:S(2)}, u32[]{:S(2)}) collective-permute-start(bf16[2,1,64,1536]{3,2,0,1:T(8,128)(2,1)S(1)} %copy-done.3), channel_id=1, source_target_pairs={{2,0},{3,1},{18,16},{19,17}} | collective-permute-start | bytes 1179656 | tf_op jit(solution)/shard_map/ppermute | solution.py:142
  89.1 22.0 %collective-permute-start.13 = (bf16[2,2,64,1536]{3,2,0,1:T(8,128)(2,1)}, bf16[2,2,64,1536]{3,2,0,1:T(8,128)(2,1)}, u32[]{:S(2)}, u32[]{:S(2)}) collective-permute-start(bf16[2,2,64,1536]{3,2,0,1:T(8,128)(2,1)} %collective-permute-done.12), channel_id=1, source_target_pairs={{4,0},{8,4},{12,8},{14,12},{10,14},{6,10},{2,6},{0,2},{5,1},{9,5},... | collective-permute-start | bytes 2359304 | tf_op jit(solution)/shard_map/ppermute | solution.py:65
  97.0 25.3 %collective-permute-start.10 = (bf16[2,2,64,1536]{3,2,0,1:T(8,128)(2,1)}, bf16[2,2,64,1536]{3,2,0,1:T(8,128)(2,1)}, u32[]{:S(2)}, u32[]{:S(2)}) collective-permute-start(bf16[2,2,64,1536]{3,2,0,1:T(8,128)(2,1)} %collective-permute-done.9), channel_id=1, source_target_pairs={{0,4},{4,8},{8,12},{12,14},{14,10},{10,6},{6,2},{2,0},{1,5},{5,9},... | collective-permute-start | bytes 2359304 | tf_op jit(solution)/shard_map/ppermute | solution.py:63
  107.4 4.5 %copy-start.6 = (pred[4]{0:T(512)(128)(4,1)S(1)}, pred[4]{0:T(512)(128)(4,1)}, u32[]{:S(2)}) copy-start(pred[4]{0:T(512)(128)(4,1)} %compare_and_fusion.5) | copy-start | bytes 16
  111.1 20.3 %collective-permute-start.14 = (bf16[2,2,64,1536]{3,2,0,1:T(8,128)(2,1)}, bf16[2,2,64,1536]{3,2,0,1:T(8,128)(2,1)S(1)}, u32[]{:S(2)}, u32[]{:S(2)}) collective-permute-start(bf16[2,2,64,1536]{3,2,0,1:T(8,128)(2,1)} %collective-permute-done.13), channel_id=1, source_target_pairs={{4,0},{8,4},{12,8},{14,12},{10,14},{6,10},{2,6},{0,2},{5,1},{9,5},... | collective-permute-start | bytes 2359304 | tf_op jit(solution)/shard_map/ppermute | solution.py:65
  123.4 11.7 %collective-permute-start.11 = (bf16[2,1,64,1536]{3,2,0,1:T(8,128)(2,1)S(1)}, bf16[2,1,64,1536]{3,2,0,1:T(8,128)(2,1)S(1)}, u32[]{:S(2)}, u32[]{:S(2)}) collective-permute-start(bf16[2,1,64,1536]{3,2,0,1:T(8,128)(2,1)S(1)} %slice.52), channel_id=1, source_target_pairs={{0,4},{4,8},{8,12},{12,14},{14,10},{10,6},{6,2},{2,0},{1,5},{5,9},... | collective-permute-start | bytes 1179656 | tf_op jit(solution)/shard_map/ppermute | solution.py:57
  131.4 11.5 %collective-permute-start.15 = (bf16[2,1,64,1536]{3,2,0,1:T(8,128)(2,1)S(1)}, bf16[2,1,64,1536]{3,2,0,1:T(8,128)(2,1)S(1)}, u32[]{:S(2)}, u32[]{:S(2)}) collective-permute-start(bf16[2,1,64,1536]{3,2,0,1:T(8,128)(2,1)S(1)} %slice.53), channel_id=1, source_target_pairs={{4,0},{8,4},{12,8},{14,12},{10,14},{6,10},{2,6},{0,2},{5,1},{9,5},... | collective-permute-start | bytes 1179656 | tf_op jit(solution)/shard_map/ppermute | solution.py:60
  158.8 1.9 %copy-start.1 = (bf16[2,4,64,1536]{3,2,0,1:T(8,128)(2,1)S(1)}, bf16[2,4,64,1536]{3,2,0,1:T(8,128)(2,1)}, u32[]{:S(2)}) copy-start(bf16[2,4,64,1536]{3,2,0,1:T(8,128)(2,1)} %select_bitcast_fusion.1) | copy-start | bytes 4718596

commit v3 on v2

v3 whole, which is shorter than its diff:
```python
import functools

import jax
import jax.numpy as jnp
from jax import lax
from jax.experimental import pallas as pl
from jax.experimental.pallas import tpu as pltpu
from jax.sharding import PartitionSpec as P

HEAD_DIM = 128
DILATION_TILES = 8


def dequant(mantissa, exponent):
    tile_rows, tile_cols, block_length, feature_channel_width = mantissa.shape
    groups = exponent.shape[2]
    factor = jnp.exp2(exponent.astype(jnp.float32))[:, :, :, None, :]
    scaled = (
        mantissa.reshape(
            tile_rows, tile_cols, groups, block_length // groups, feature_channel_width
        ).astype(jnp.float32)
        * factor
    )
    return scaled.reshape(mantissa.shape).astype(jnp.bfloat16)


def shift(x, axis, count, step):
    if step > 0:
        pairs = [(i, i + step) for i in range(count - step)]
    else:
        pairs = [(i - step, i) for i in range(count + step)]
    if not pairs:
        return jnp.zeros_like(x)
    return lax.ppermute(x, axis, pairs)


def side_slots(entries, low, tile_blocks, cap):
    inside = (entries >= low) & (entries < low + tile_blocks)
    rank = jnp.cumsum(inside.astype(jnp.int32)) - 1
    slot = jnp.arange(cap, dtype=jnp.int32)[:, None]
    hit = inside[None, :] & (rank[None, :] == slot)
    return jnp.sum(jnp.where(hit, entries[None, :] - low, 0), axis=1), inside, rank


def ring_gather(item, count, me):
    order = list(range(0, count, 2)) + list(range(count - 1 - count % 2, 0, -2))
    position = [0] * count
    for place, col in enumerate(order):
        position[col] = place
    forward = [(order[i], order[(i + 1) % count]) for i in range(count)]
    backward = [(order[(i + 1) % count], order[i]) for i in range(count)]
    half = count // 2
    rows = item.shape[1]
    split = (rows + 1) // 2
    ahead, behind = item, item
    arrays = []
    lookup = [None] * (count - 1)
    for distance in range(1, half + 1):
        if distance == half and count % 2 == 0:
            arrays.append(lax.ppermute(ahead[:, :split], "col", forward))
            first = len(arrays) - 1
            if split < rows:
                arrays.append(lax.ppermute(behind[:, split:], "col", backward))
            lookup[distance - 1] = [
                (first, r) if r < split else (first + 1, r - split) for r in range(rows)
            ]
            continue
        ahead = lax.ppermute(ahead, "col", forward)
        arrays.append(ahead)
        lookup[distance - 1] = [(len(arrays) - 1, r) for r in range(rows)]
        behind = lax.ppermute(behind, "col", backward)
        arrays.append(behind)
        lookup[count - distance - 1] = [(len(arrays) - 1, r) for r in range(rows)]
    table = jnp.array(position, dtype=jnp.int32)

    def relative(col):
        return (table[me] - table[col]) % count - 1

    return arrays, lookup, relative


def gather_attention_kernel(cycle_sources, far_sources, table_ref, q_hbm, own_hbm, *rest):
    sources = rest[: cycle_sources + far_sources]
    o_ref, q_vmem, k_vmem, v_vmem, sems = rest[cycle_sources + far_sources :]
    tile_blocks = own_hbm.shape[1]
    block_length = own_hbm.shape[2]
    extra = table_ref.shape[0] // 2
    heads = q_vmem.shape[1] // HEAD_DIM

    copies = [pltpu.make_async_copy(q_hbm, q_vmem, sems.at[0, 0])]
    copies.append(pltpu.make_async_copy(own_hbm.at[0], k_vmem.at[pl.ds(0, tile_blocks)], sems.at[0, 1]))
    copies.append(pltpu.make_async_copy(own_hbm.at[1], v_vmem.at[pl.ds(0, tile_blocks)], sems.at[1, 1]))
    for c in copies:
        c.start()
    for slot in range(extra):
        src = table_ref[2 * slot]
        index = table_ref[2 * slot + 1]
        lo, hi = (0, cycle_sources) if slot < extra // 2 else (cycle_sources, cycle_sources + far_sources)
        for cand in range(lo, hi):
            @pl.when(src == cand)
            def _():
                for kv, dst in ((0, k_vmem), (1, v_vmem)):
                    pltpu.make_async_copy(
                        sources[cand].at[kv, index], dst.at[tile_blocks + slot], sems.at[kv, 2 + slot]
                    ).start()
    for c in copies:
        c.wait()
    for slot in range(extra):
        for kv, dst in ((0, k_vmem), (1, v_vmem)):
            pltpu.make_async_copy(
                own_hbm.at[kv, 0], dst.at[tile_blocks + slot], sems.at[kv, 2 + slot]
            ).wait()

    key_count = k_vmem.shape[0] * block_length

    def head(h, carry):
        lanes = pl.ds(pl.multiple_of(h * HEAD_DIM, HEAD_DIM), HEAD_DIM)
        q = q_vmem[:, lanes]
        k = k_vmem[:, :, lanes].reshape(key_count, HEAD_DIM)
        v = v_vmem[:, :, lanes].reshape(key_count, HEAD_DIM)
        scores = lax.dot_general(
            q, k, (((1,), (1,)), ((), ())), preferred_element_type=jnp.float32
        ) * HEAD_DIM ** (-0.5)
        row_max = jnp.max(scores, axis=1, keepdims=True)
        weights = jnp.exp(scores - row_max)
        row_total = jnp.sum(weights, axis=1, keepdims=True)
        rounded = weights.astype(jnp.bfloat16)
        blended = jnp.dot(rounded, v, preferred_element_type=jnp.float32)
        o_ref[:, lanes] = (blended / row_total).astype(o_ref.dtype)
        return carry

    lax.fori_loop(0, heads, head, 0)


def gather_attend(query_rows, own, cycle_list_sources, far_list_sources, table):
    token_count, width = query_rows.shape
    tile_blocks, block_length = own.shape[1], own.shape[2]
    extra = table.shape[0] // 2
    blocks = tile_blocks + extra
    key_count = blocks * block_length
    heads = width // HEAD_DIM
    n_sources = len(cycle_list_sources) + len(far_list_sources)
    kernel = functools.partial(
        gather_attention_kernel, len(cycle_list_sources), len(far_list_sources)
    )
    return pl.pallas_call(
        kernel,
        out_shape=jax.ShapeDtypeStruct((token_count, width), jnp.bfloat16),
        in_specs=[pl.BlockSpec(memory_space=pltpu.SMEM)]
        + [pl.BlockSpec(memory_space=pl.ANY)] * (2 + n_sources),
        out_specs=pl.BlockSpec(memory_space=pltpu.VMEM),
        scratch_shapes=[
            pltpu.VMEM((token_count, width), jnp.bfloat16),
            pltpu.VMEM((blocks, block_length, width), jnp.bfloat16),
            pltpu.VMEM((blocks, block_length, width), jnp.bfloat16),
            pltpu.SemaphoreType.DMA((2, 2 + extra)),
        ],
        compiler_params=pltpu.CompilerParams(vmem_limit_bytes=48 * 1024 * 1024),
        cost_estimate=pl.CostEstimate(
            flops=4 * token_count * key_count * width,
            transcendentals=token_count * key_count * heads,
            bytes_accessed=2 * (2 * token_count * width + 2 * key_count * width),
        ),
    )(table, query_rows, own, *cycle_list_sources, *far_list_sources)


def per_device(queries, key_mant, key_exp, value_mant, value_exp, cycle_list, dilated_list):
    tile_blocks = queries.shape[0]
    block_length = queries.shape[2]
    width = queries.shape[3]
    col_count = lax.axis_size("col")
    row_count = lax.axis_size("row")
    distant_rows = tile_blocks // 4
    step_spacing = col_count // DILATION_TILES
    me_col = lax.axis_index("col")

    stacked = jnp.stack([dequant(key_mant, key_exp), dequant(value_mant, value_exp)])[:, :, 0]

    above = shift(stacked[:, tile_blocks - 1 :], "row", row_count, 1)
    below = shift(stacked[:, :1], "row", row_count, -1)

    edge_cap = min(3 if row_count >= 2 else 4, tile_blocks)
    main_cap = edge_cap - 1 if col_count >= 3 else edge_cap
    entries = cycle_list[0, 0]
    right_entries = shift(entries, "col", col_count, -1)
    left_entries = shift(entries, "col", col_count, 1)
    to_right, _, _ = side_slots(right_entries, 2, tile_blocks, edge_cap)
    to_left, _, _ = side_slots(left_entries, 2 + tile_blocks, tile_blocks, edge_cap)
    right_payload = jnp.take(stacked, to_right, axis=1)
    left_payload = jnp.take(stacked, to_left, axis=1)
    cycle_sources = [above, below]
    cycle_sources.append(shift(right_payload[:, :main_cap], "col", col_count, 1))
    cycle_sources.append(shift(left_payload[:, :main_cap], "col", col_count, -1))
    if main_cap < edge_cap:
        last = col_count - 1
        cycle_sources.append(lax.ppermute(right_payload[:, main_cap:], "col", [(last - 1, last)]))
        cycle_sources.append(lax.ppermute(left_payload[:, main_cap:], "col", [(1, 0)]))

    _, is_left, left_rank = side_slots(entries, 2, tile_blocks, edge_cap)
    _, is_right, right_rank = side_slots(entries, 2 + tile_blocks, tile_blocks, edge_cap)
    side_rank = jnp.where(is_left, left_rank, right_rank)
    overflow = side_rank >= main_cap
    cycle_src = jnp.where(
        entries == 0,
        0,
        jnp.where(entries == 1, 1, 2 + is_right.astype(jnp.int32) + 2 * overflow.astype(jnp.int32)),
    )
    cycle_idx = jnp.where(entries < 2, 0, jnp.where(overflow, side_rank - main_cap, side_rank))

    far_source = stacked[:, 0::4]
    dilated_entries = dilated_list[0, 0]
    hop_slot = dilated_entries // distant_rows
    far_row = dilated_entries % distant_rows
    if step_spacing == 1:
        far_sources, lookup, relative = ring_gather(far_source, col_count, me_col)
        hop_slot = relative((me_col + hop_slot + 1) % col_count)
    else:
        far_sources = []
        lookup = []
        for hop in range(1, DILATION_TILES):
            distance = hop * step_spacing
            route = [((i + distance) % col_count, i) for i in range(col_count)]
            far_sources.append(lax.ppermute(far_source, "col", route))
            lookup.append([(hop - 1, r) for r in range(distant_rows)])
    lookup_src = jnp.array([[a for a, _ in row] for row in lookup], dtype=jnp.int32)
    lookup_idx = jnp.array([[b for _, b in row] for row in lookup], dtype=jnp.int32)
    far_src = len(cycle_sources) + lookup_src[hop_slot, far_row]
    far_idx = lookup_idx[hop_slot, far_row]

    table = jnp.stack(
        [jnp.concatenate([cycle_src, far_src]), jnp.concatenate([cycle_idx, far_idx])], axis=1
    ).reshape(-1)
    token_count = tile_blocks * block_length
    result = gather_attend(
        queries.reshape(token_count, width), stacked, cycle_sources, far_sources, table
    )
    return result.reshape(queries.shape)


def solution(mesh):
    in_specs = (
        P(("groups", "row"), "col", None, None),
        P(("groups", "row"), "col", None, None),
        P(("groups", "row"), "col", None, None),
        P(("groups", "row"), "col", None, None),
        P(("groups", "row"), "col", None, None),
        P(("groups", "row"), "col", None),
        P(("groups", "row"), "col", None),
    )
    out_specs = P(("groups", "row"), "col", None, None)
    return jax.shard_map(
        per_device, mesh=mesh, in_specs=in_specs, out_specs=out_specs, check_vma=False
    )
```

time: 187 us -> 148 us (0.79)
  local copies, waits for them, and re-layouts: 50 us -> 23.2 us
  other arithmetic: 28.4 us -> 15.5 us
  waiting for transfers between devices: 60.1 us -> 53.6 us
  Pallas kernels: 21 us -> 24.7 us
  starting transfers between devices: 26 us -> 28.8 us
    ppermute x3, waiting for transfers between devices: 5.88 us -> 43.5 us  [ring_gather(): behind = lax.ppermute(behind, 'col', backward)]
    ppermute x6, waiting for transfers between devices: 25.2 us -> 0.02 us  [shift(): return lax.ppermute(x, axis, pairs)]
    concatenate x5 -> x0, local copies, waits for them, and re-layouts: 13.1 us -> none  [the longest x2 7.71 us: ring_gather(): pool = jnp.concatenate(slots, axis=1)]
    ppermute x3, waiting for transfers between devices: 13.1 us -> 0.01 us  [ring_gather(): ahead = lax.ppermute(ahead, 'col', forward)]
    unnamed x26 -> x20, local copies, waits for them, and re-layouts: 12.2 us -> 0.12 us
    gather x3, local copies, waits for them, and re-layouts: 8.66 us -> 2.94 us  [the longest x1 1.16 us: per_device(): far_idx = lookup_idx[hop_slot, far_row]]
    select_n x5 -> x3, other arithmetic: 7.03 us -> 2.37 us  [the longest x1 1.21 us: per_device(): jnp.where(entries == 0, 0, jnp.where(entries == 1, 1, 2 + is_right.astype...]
    pallas_call x1, Pallas kernels: 21 us -> 24.7 us  [gather_attend(): pl.pallas_call(kernel, out_shape=jax.ShapeDtypeStruct((token_count, width...]
  transfers between devices with their start and end apart: 16 -> 16, of which waited for: 8 -> 5; matrix products, arithmetic and copies ran while one was open for 28% -> 26% of each run, Pallas kernels for 0% -> 0%
where the time goes in v3:
time: 148 us; the launch traced here: 146 us
  waiting for transfers between devices  53.6 us (36%)
  starting transfers between devices  28.8 us (19%)
  Pallas kernels  24.7 us (17%)
  local copies, waits for them, and re-layouts  23.2 us (16%)
  other arithmetic  15.5 us (10%)
    ppermute x3, waiting for transfers between devices, ring_gather(): behind = lax.ppermute(behind, 'col', backward)  43.5 us
    pallas_call x1, Pallas kernels, gather_attend(): pl.pallas_call(kernel, out_shape=jax.ShapeDtypeStruct((token_count, width...  24.7 us
    ppermute x6, starting transfers between devices, shift(): return lax.ppermute(x, axis, pairs)  15.4 us
    ppermute x3, starting transfers between devices, ring_gather(): behind = lax.ppermute(behind, 'col', backward)  6.51 us
    ppermute x1, waiting for transfers between devices, ring_gather(): arrays.append(lax.ppermute(ahead[:, :split], 'col', forward))  5.02 us
    ppermute x1, waiting for transfers between devices, per_device(): lax.ppermute(left_payload[:, main_cap:], 'col', [(1, 0)])  5.01 us
    gather x1, local copies, waits for them, and re-layouts, per_device(): left_payload = jnp.take(stacked, to_left, axis=1)  3.56 us
    gather x1, local copies, waits for them, and re-layouts, per_device(): right_payload = jnp.take(stacked, to_right, axis=1)  3.56 us
  transfers between devices with their start and end apart: 16, of which 5 were waited for; matrix products, arithmetic and copies ran while one was open for 26% of the time, Pallas kernels for 0%

profile of v3, /device:TPU:0, one launch (start us, length us, event | category | flops | bytes accessed | tf_op | source)
XLA Modules:
  0.0 146.1 jit_solution(10344339725508228631)
XLA Ops:
  0.0 4.9 %collective-permute-start.4 = (s32[4]{0:T(128)}, s32[4]{0:T(128)S(1)}, u32[]{:S(2)}, u32[]{:S(2)}) collective-permute-start(s32[4]{0:T(128)} %bitcast.90), channel_id=1, source_target_pairs={{0,2},{2,4},{4,6},{6,8},{8,10},{10,12},{12,14},{1,3},{3,5},{5,7},{... | collective-permute-start | bytes 56 | tf_op jit(solution)/shard_map/ppermute | solution.py:34
  4.9 1.3 collective-permute-start.2
  6.2 1.0 exponential_bitcast_fusion.1
  7.1 1.0 exponential_bitcast_fusion
  8.1 0.0 copy-start.5
  8.1 1.8 %fusion = bf16[8,1,64,1536]{3,2,0,1:T(8,128)(2,1)S(1)} fusion(bf16[8,1,64,1536]{3,2,1,0:T(8,128)(2,1)} %param.15, f32[8,2,1536]{2,1,0:T(2,128)S(1)} %exponential_bitcast_fusion), kind=kLoop, calls=%fused_computation.7 | loop fusion | flops 2359296 | bytes 3244032 | tf_op jit(solution)/shard_map/convert_element_type | solution.py:24
  9.9 0.1 copy-done.5
  10.0 0.3 fusion.1
  10.3 0.3 maximum_bitcast_fusion.own_hbm
  10.6 0.0 copy-start.6
  10.6 0.9 slice.33
  11.6 2.6 %collective-permute-start.9 = (bf16[2,2,64,1536]{3,2,1,0:T(8,128)(2,1)}, bf16[2,2,64,1536]{3,2,1,0:T(8,128)(2,1)S(1)}, u32[]{:S(2)}, u32[]{:S(2)}) collective-permute-start(bf16[2,2,64,1536]{3,2,1,0:T(8,128)(2,1)} %slice.33), channel_id=1, source_target_pairs={{4,0},{8,4},{12,8},{14,12},{10,14},{6,10},{2,6},{0,2},{5,1},{9,5},... | collective-permute-start | bytes 2359304 | tf_op jit(solution)/shard_map/ppermute | solution.py:71
  14.2 1.0 collective-permute-start.8
  15.2 0.8 fusion.16
  16.0 1.3 collective-permute-start.1
  17.3 0.5 fusion.6
  17.8 0.5 fusion.10
  18.3 0.2 reduce-window.37
  18.5 0.1 select_reduce_fusion
  18.7 0.2 reduce-window.36
  18.9 0.1 select_reduce_fusion.1
  19.0 3.6 %gather_fusion.4 = bf16[3,2,64,1536]{3,2,1,0:T(8,128)(2,1)} fusion(bf16[2,8,64,1536]{3,2,1,0:T(8,128)(2,1)} %copy-done.3, s32[1024]{0:T(1024)S(1)} %pad_clamp_fusion), kind=kCustom, calls=%fused_computation.1.clone | custom fusion | bytes 2359308 | tf_op jit(solution)/shard_map/jit(_take)/gather | solution.py:190
  22.6 1.4 select_bitcast_fusion
  24.0 8.3 %collective-permute-done.9.rest_7_ = bf16[2,2,64,1536]{3,2,1,0:T(8,128)(2,1)S(1)} collective-permute-done((bf16[2,2,64,1536]{3,2,1,0:T(8,128)(2,1)}, bf16[2,2,64,1536]{3,2,1,0:T(8,128)(2,1)S(1)}, u32[]{:S(2)}, u32[]{:S(2)}) %collective-permute-start.9) | collective-permute-done | bytes 786464 | tf_op jit(solution)/shard_map/ppermute | solution.py:71
  32.4 0.8 collective-permute-start.11
  33.2 1.2 collective-permute-start.10
  34.4 1.0 slice.49
  35.4 1.3 collective-permute-start.5
  36.7 3.6 %gather_fusion.3 = bf16[3,2,64,1536]{3,2,1,0:T(8,128)(2,1)} fusion(bf16[2,8,64,1536]{3,2,1,0:T(8,128)(2,1)} %copy-done.3, s32[1024]{0:T(1024)S(1)} %pad_clamp_fusion.1), kind=kCustom, calls=%fused_computation.clone | custom fusion | bytes 2359308 | tf_op jit(solution)/shard_map/jit(_take)/gather | solution.py:189
  40.3 0.0 copy-start
  40.3 1.5 select_bitcast_fusion.1
  41.8 0.0 copy-start.2
  41.8 0.0 copy-start.1
  41.8 1.0 slice.48
  42.9 5.4 %collective-permute-start.3 = (bf16[2,2,64,1536]{3,2,0,1:T(8,128)(2,1)}, bf16[2,2,64,1536]{3,2,0,1:T(8,128)(2,1)}, u32[]{:S(2)}, u32[]{:S(2)}) collective-permute-start(bf16[2,2,64,1536]{3,2,0,1:T(8,128)(2,1)} %slice.48), channel_id=1, source_target_pairs={{0,2},{2,4},{4,6},{6,8},{8,10},{10,12},{12,14},{1,3},{3,5},{5,7},{... | collective-permute-start | bytes 2359304 | tf_op jit(solution)/shard_map/ppermute | solution.py:34
  48.3 18.5 %collective-permute-done.11.rest_9_ = bf16[2,2,64,1536]{3,2,1,0:T(8,128)(2,1)} collective-permute-done((bf16[2,2,64,1536]{3,2,1,0:T(8,128)(2,1)S(1)}, bf16[2,2,64,1536]{3,2,1,0:T(8,128)(2,1)}, u32[]{:S(2)}, u32[]{:S(2)}) %collective-permute-start.11) | collective-permute-done | bytes 786464 | tf_op jit(solution)/shard_map/ppermute | solution.py:71
  66.8 3.1 %collective-permute-start.13 = (bf16[2,2,64,1536]{3,2,1,0:T(8,128)(2,1)}, bf16[2,2,64,1536]{3,2,1,0:T(8,128)(2,1)}, u32[]{:S(2)}, u32[]{:S(2)}) collective-permute-start(bf16[2,2,64,1536]{3,2,1,0:T(8,128)(2,1)} %collective-permute-done.11.rest_9_), channel_id=1, source_target_pairs={{4,0},{8,4},{12,8},{14,12},{10,14},{6,10},{2,6},{0,2},{5,1},{9,5},... | collective-permute-start | bytes 2359304 | tf_op jit(solution)/shard_map/ppermute | solution.py:71
  69.9 1.3 reduce-window.34
  71.2 1.3 reduce-window.35
  72.5 0.6 dynamic_slice.3
  73.1 1.1 gather_fusion
  74.2 1.2 compare_select_fusion.13
  75.4 1.3 fusion.15
  76.8 1.2 gather_fusion.2
  77.9 0.6 gather_fusion.1
  78.6 0.7 compare_select_fusion.11
  79.2 0.7 add_bitcast_fusion.1
  79.9 0.8 slice.51
  80.7 1.8 %slice.50 = bf16[2,1,64,1536]{3,2,0,1:T(8,128)(2,1)} slice(bf16[2,3,64,1536]{3,2,0,1:T(8,128)(2,1)} %copy-done.4), slice={[0:2], [2:3], [0:64], [0:1536]} | slice | bytes 786432 | tf_op jit(solution)/shard_map/slice | solution.py:196
  82.5 16.6 %collective-permute-done.13.rest_11_ = bf16[2,2,64,1536]{3,2,1,0:T(8,128)(2,1)} collective-permute-done((bf16[2,2,64,1536]{3,2,1,0:T(8,128)(2,1)}, bf16[2,2,64,1536]{3,2,1,0:T(8,128)(2,1)}, u32[]{:S(2)}, u32[]{:S(2)}) %collective-permute-start.13) | collective-permute-done | bytes 786464 | tf_op jit(solution)/shard_map/ppermute | solution.py:71
  99.1 1.3 collective-permute-start
  100.4 1.8 %slice.53 = bf16[2,1,64,1536]{3,2,1,0:T(8,128)(2,1)} slice(bf16[2,2,64,1536]{3,2,1,0:T(8,128)(2,1)} %collective-permute-done.13.rest_11_), slice={[0:2], [1:2], [0:64], [0:1536]} | slice | bytes 786432 | tf_op jit(solution)/shard_map/slice | solution.py:63
  102.2 1.3 collective-permute-start.7
  103.5 1.8 %slice.52 = bf16[2,1,64,1536]{3,2,1,0:T(8,128)(2,1)} slice(bf16[2,2,64,1536]{3,2,1,0:T(8,128)(2,1)} %collective-permute-done.12.rest_10_), slice={[0:2], [0:1], [0:64], [0:1536]} | slice | bytes 786432 | tf_op jit(solution)/shard_map/slice | solution.py:60
  105.3 0.7 collective-permute-start.6
  106.0 2.7 %collective-permute-start.15 = (bf16[2,1,64,1536]{3,2,1,0:T(8,128)(2,1)}, bf16[2,1,64,1536]{3,2,1,0:T(8,128)(2,1)S(1)}, u32[]{:S(2)}, u32[]{:S(2)}) collective-permute-start(bf16[2,1,64,1536]{3,2,1,0:T(8,128)(2,1)} %slice.53), channel_id=1, source_target_pairs={{4,0},{8,4},{12,8},{14,12},{10,14},{6,10},{2,6},{0,2},{5,1},{9,5},... | collective-permute-start | bytes 1179656 | tf_op jit(solution)/shard_map/ppermute | solution.py:63
  108.7 0.1 add_bitcast_fusion
  108.8 0.1 copy.27
  108.9 0.1 reshape.421.table_ref
  109.0 1.2 copy.31.rest_3_
  110.2 1.2 copy.30.rest_2_
  111.4 5.0 %collective-permute-done.7 = bf16[2,1,64,1536]{3,2,0,1:T(8,128)(2,1)S(1)} collective-permute-done((bf16[2,1,64,1536]{3,2,0,1:T(8,128)(2,1)}, bf16[2,1,64,1536]{3,2,0,1:T(8,128)(2,1)S(1)}, u32[]{:S(2)}, u32[]{:S(2)}) %collective-permute-start.7) | collective-permute-done | bytes 393248 | tf_op jit(solution)/shard_map/ppermute | solution.py:197
  116.4 5.0 %collective-permute-done.14.rest_12_ = bf16[2,1,64,1536]{3,2,1,0:T(8,128)(2,1)} collective-permute-done((bf16[2,1,64,1536]{3,2,1,0:T(8,128)(2,1)}, bf16[2,1,64,1536]{3,2,1,0:T(8,128)(2,1)}, u32[]{:S(2)}, u32[]{:S(2)}) %collective-permute-start.14) | collective-permute-done | bytes 393248 | tf_op jit(solution)/shard_map/ppermute | solution.py:60
  121.4 24.7 %shard_map.100 = bf16[512,1536]{1,0:T(8,128)(2,1)} custom-call(s32[16]{0:T(128)S(1)} %reshape.421.table_ref, bf16[512,1536]{1,0:T(8,128)(2,1)} %bitcast.89, bf16[2,8,64,1536]{3,2,1,0:T(8,128)(2,1)} %copy-done.3, bf16[2,1,64,1536]{3,2,1,0:T(8,128)(2,1)S(1)} %collective-permute-done.rest_0_, bf16[2,1,64,1536]{3,2,1,0:T(8,128)(2,1)S(1)} %collective-permute-done.1.rest_1_, ...), custom_call_target="tpu_custom_call" | custom-call | flops 3221225472 | bytes 9437184 | tf_op jit(solution)/shard_map/pallas_call | solution.py:146
  (42 shorter events, 0.2 us)
Async XLA Ops:
  0.0 18.3 %collective-permute-start.4 = (s32[4]{0:T(128)}, s32[4]{0:T(128)S(1)}, u32[]{:S(2)}, u32[]{:S(2)}) collective-permute-start(s32[4]{0:T(128)} %bitcast.90), channel_id=1, source_target_pairs={{0,2},{2,4},{4,6},{6,8},{8,10},{10,12},{12,14},{1,3},{3,5},{5,7},{... | collective-permute-start | bytes 56 | tf_op jit(solution)/shard_map/ppermute | solution.py:34
  4.9 13.8 %collective-permute-start.2 = (s32[4]{0:T(128)}, s32[4]{0:T(128)S(1)}, u32[]{:S(2)}, u32[]{:S(2)}) collective-permute-start(s32[4]{0:T(128)} %bitcast.91), channel_id=1, source_target_pairs={{2,0},{4,2},{6,4},{8,6},{10,8},{12,10},{14,12},{3,1},{5,3},{7,5},{... | collective-permute-start | bytes 56 | tf_op jit(solution)/shard_map/ppermute | solution.py:34
  8.1 1.9 %copy-start.5 = (bf16[8,1,64,1536]{3,2,1,0:T(8,128)(2,1)S(1)}, bf16[8,1,64,1536]{3,2,1,0:T(8,128)(2,1)}, u32[]{:S(2)}) copy-start(bf16[8,1,64,1536]{3,2,1,0:T(8,128)(2,1)} %param.13) | copy-start | bytes 4718596
  10.6 5.4 %copy-start.3 = (bf16[2,8,64,1536]{3,2,1,0:T(8,128)(2,1)}, bf16[2,8,64,1536]{3,2,1,0:T(8,128)(2,1)S(1)}, u32[]{:S(2)}) copy-start(bf16[2,8,64,1536]{3,2,1,0:T(8,128)(2,1)S(1)} %maximum_bitcast_fusion.own_hbm) | copy-start | bytes 9437188
  10.6 6.7 %copy-start.6 = (s32[1,1,4]{2,1,0:T(1,128)S(1)}, s32[1,1,4]{2,1,0:T(1,128)}, u32[]{:S(2)}) copy-start(s32[1,1,4]{2,1,0:T(1,128)} %param.17) | copy-start | bytes 52
  10.6 7.2 %copy-start.9 = (s32[1,1,4]{2,1,0:T(1,128)S(1)}, s32[1,1,4]{2,1,0:T(1,128)}, u32[]{:S(2)}) copy-start(s32[1,1,4]{2,1,0:T(1,128)} %param.18) | copy-start | bytes 52
  11.6 20.8 %collective-permute-start.9 = (bf16[2,2,64,1536]{3,2,1,0:T(8,128)(2,1)}, bf16[2,2,64,1536]{3,2,1,0:T(8,128)(2,1)S(1)}, u32[]{:S(2)}, u32[]{:S(2)}) collective-permute-start(bf16[2,2,64,1536]{3,2,1,0:T(8,128)(2,1)} %slice.33), channel_id=1, source_target_pairs={{4,0},{8,4},{12,8},{14,12},{10,14},{6,10},{2,6},{0,2},{5,1},{9,5},... | collective-permute-start | bytes 2359304 | tf_op jit(solution)/shard_map/ppermute | solution.py:71
  14.2 18.9 %collective-permute-start.8 = (bf16[2,2,64,1536]{3,2,1,0:T(8,128)(2,1)}, bf16[2,2,64,1536]{3,2,1,0:T(8,128)(2,1)S(1)}, u32[]{:S(2)}, u32[]{:S(2)}) collective-permute-start(bf16[2,2,64,1536]{3,2,1,0:T(8,128)(2,1)} %slice.33), channel_id=1, source_target_pairs={{0,4},{4,8},{8,12},{12,14},{14,10},{10,6},{6,2},{2,0},{1,5},{5,9},... | collective-permute-start | bytes 2359304 | tf_op jit(solution)/shard_map/ppermute | solution.py:68
  16.0 89.3 %collective-permute-start.1 = (bf16[2,1,64,1536]{3,2,1,0:T(8,128)(2,1)S(1)}, bf16[2,1,64,1536]{3,2,1,0:T(8,128)(2,1)S(1)}, u32[]{:S(2)}, u32[]{:S(2)}) collective-permute-start(bf16[2,1,64,1536]{3,2,1,0:T(8,128)(2,1)S(1)} %get-tuple-element.8), channel_id=1, source_target_pairs={{1,0},{3,2},{5,4},{7,6},{9,8},{11,10},{13,12},{15,14},{17,16},{19,... | collective-permute-start | bytes 1179656 | tf_op jit(solution)/shard_map/ppermute | solution.py:34
  32.4 34.4 %collective-permute-start.11 = (bf16[2,2,64,1536]{3,2,1,0:T(8,128)(2,1)S(1)}, bf16[2,2,64,1536]{3,2,1,0:T(8,128)(2,1)}, u32[]{:S(2)}, u32[]{:S(2)}) collective-permute-start(bf16[2,2,64,1536]{3,2,1,0:T(8,128)(2,1)S(1)} %collective-permute-done.9.rest_7_), channel_id=1, source_target_pairs={{4,0},{8,4},{12,8},{14,12},{10,14},{6,10},{2,6},{0,2},{5,1},{9,5},... | collective-permute-start | bytes 2359304 | tf_op jit(solution)/shard_map/ppermute | solution.py:71
  33.2 36.7 %collective-permute-start.10 = (bf16[2,2,64,1536]{3,2,1,0:T(8,128)(2,1)S(1)}, bf16[2,2,64,1536]{3,2,1,0:T(8,128)(2,1)}, u32[]{:S(2)}, u32[]{:S(2)}) collective-permute-start(bf16[2,2,64,1536]{3,2,1,0:T(8,128)(2,1)S(1)} %collective-permute-done.8.rest_6_), channel_id=1, source_target_pairs={{0,4},{4,8},{8,12},{12,14},{14,10},{10,6},{6,2},{2,0},{1,5},{5,9},... | collective-permute-start | bytes 2359304 | tf_op jit(solution)/shard_map/ppermute | solution.py:68
  35.4 70.5 %collective-permute-start.5 = (bf16[2,2,64,1536]{3,2,0,1:T(8,128)(2,1)}, bf16[2,2,64,1536]{3,2,0,1:T(8,128)(2,1)}, u32[]{:S(2)}, u32[]{:S(2)}) collective-permute-start(bf16[2,2,64,1536]{3,2,0,1:T(8,128)(2,1)} %slice.49), channel_id=1, source_target_pairs={{2,0},{4,2},{6,4},{8,6},{10,8},{12,10},{14,12},{3,1},{5,3},{7,5},{... | collective-permute-start | bytes 2359304 | tf_op jit(solution)/shard_map/ppermute | solution.py:34
  40.3 29.6 %copy-start.7 = (s32[4]{0:T(128)S(1)}, s32[4]{0:T(128)}, u32[]{:S(2)}) copy-start(s32[4]{0:T(128)} %fusion.10) | copy-start | bytes 52
  40.3 32.2 %copy-start = (s32[8]{0:T(128)S(1)}, s32[8]{0:T(128)}, u32[]{:S(2)}) copy-start(s32[8]{0:T(128)} %constant.99.clone) | copy-start | bytes 100
  41.8 28.1 %copy-start.4 = (bf16[2,3,64,1536]{3,2,0,1:T(8,128)(2,1)}, bf16[2,3,64,1536]{3,2,0,1:T(8,128)(2,1)S(1)}, u32[]{:S(2)}) copy-start(bf16[2,3,64,1536]{3,2,0,1:T(8,128)(2,1)S(1)} %select_bitcast_fusion.1) | copy-start | bytes 3538948
  41.8 35.0 %copy-start.2 = (s32[7,2]{1,0:T(8,128)S(1)}, s32[7,2]{1,0:T(8,128)}, u32[]{:S(2)}) copy-start(s32[7,2]{1,0:T(8,128)} %constant.101.clone) | copy-start | bytes 172
  41.8 36.1 %copy-start.1 = (s32[7,2]{1,0:T(8,128)S(1)}, s32[7,2]{1,0:T(8,128)}, u32[]{:S(2)}) copy-start(s32[7,2]{1,0:T(8,128)} %constant.100.clone) | copy-start | bytes 172
  42.9 65.8 %collective-permute-start.3 = (bf16[2,2,64,1536]{3,2,0,1:T(8,128)(2,1)}, bf16[2,2,64,1536]{3,2,0,1:T(8,128)(2,1)}, u32[]{:S(2)}, u32[]{:S(2)}) collective-permute-start(bf16[2,2,64,1536]{3,2,0,1:T(8,128)(2,1)} %slice.48), channel_id=1, source_target_pairs={{0,2},{2,4},{4,6},{6,8},{8,10},{10,12},{12,14},{1,3},{3,5},{5,7},{... | collective-permute-start | bytes 2359304 | tf_op jit(solution)/shard_map/ppermute | solution.py:34
  66.8 32.4 %collective-permute-start.13 = (bf16[2,2,64,1536]{3,2,1,0:T(8,128)(2,1)}, bf16[2,2,64,1536]{3,2,1,0:T(8,128)(2,1)}, u32[]{:S(2)}, u32[]{:S(2)}) collective-permute-start(bf16[2,2,64,1536]{3,2,1,0:T(8,128)(2,1)} %collective-permute-done.11.rest_9_), channel_id=1, source_target_pairs={{4,0},{8,4},{12,8},{14,12},{10,14},{6,10},{2,6},{0,2},{5,1},{9,5},... | collective-permute-start | bytes 2359304 | tf_op jit(solution)/shard_map/ppermute | solution.py:71
  69.9 32.3 %collective-permute-start.12 = (bf16[2,2,64,1536]{3,2,1,0:T(8,128)(2,1)}, bf16[2,2,64,1536]{3,2,1,0:T(8,128)(2,1)}, u32[]{:S(2)}, u32[]{:S(2)}) collective-permute-start(bf16[2,2,64,1536]{3,2,1,0:T(8,128)(2,1)} %collective-permute-done.10.rest_8_), channel_id=1, source_target_pairs={{0,4},{4,8},{8,12},{12,14},{14,10},{10,6},{6,2},{2,0},{1,5},{5,9},... | collective-permute-start | bytes 2359304 | tf_op jit(solution)/shard_map/ppermute | solution.py:68
  79.9 28.8 %copy-start.8 = (s32[4]{0:T(128)S(1)}, s32[4]{0:T(128)}, u32[]{:S(2)}) copy-start(s32[4]{0:T(128)} %get-tuple-element.6) | copy-start | bytes 52
  99.1 12.2 %collective-permute-start = (bf16[2,1,64,1536]{3,2,1,0:T(8,128)(2,1)}, bf16[2,1,64,1536]{3,2,1,0:T(8,128)(2,1)S(1)}, u32[]{:S(2)}, u32[]{:S(2)}) collective-permute-start(bf16[2,1,64,1536]{3,2,1,0:T(8,128)(2,1)} %get-tuple-element.9), channel_id=1, source_target_pairs={{0,1},{2,3},{4,5},{6,7},{8,9},{10,11},{12,13},{14,15},{16,17},{18,... | collective-permute-start | bytes 1179656 | tf_op jit(solution)/shard_map/ppermute | solution.py:34
  102.2 14.1 %collective-permute-start.7 = (bf16[2,1,64,1536]{3,2,0,1:T(8,128)(2,1)}, bf16[2,1,64,1536]{3,2,0,1:T(8,128)(2,1)S(1)}, u32[]{:S(2)}, u32[]{:S(2)}) collective-permute-start(bf16[2,1,64,1536]{3,2,0,1:T(8,128)(2,1)} %slice.51), channel_id=1, source_target_pairs={{2,0},{3,1},{18,16},{19,17}} | collective-permute-start | bytes 1179656 | tf_op jit(solution)/shard_map/ppermute | solution.py:197
  105.3 11.1 %collective-permute-start.6 = (bf16[2,1,64,1536]{3,2,0,1:T(8,128)(2,1)}, bf16[2,1,64,1536]{3,2,0,1:T(8,128)(2,1)S(1)}, u32[]{:S(2)}, u32[]{:S(2)}) collective-permute-start(bf16[2,1,64,1536]{3,2,0,1:T(8,128)(2,1)} %slice.50), channel_id=1, source_target_pairs={{12,14},{13,15},{28,30},{29,31}} | collective-permute-start | bytes 1179656 | tf_op jit(solution)/shard_map/ppermute | solution.py:196
  106.0 10.4 %collective-permute-start.15 = (bf16[2,1,64,1536]{3,2,1,0:T(8,128)(2,1)}, bf16[2,1,64,1536]{3,2,1,0:T(8,128)(2,1)S(1)}, u32[]{:S(2)}, u32[]{:S(2)}) collective-permute-start(bf16[2,1,64,1536]{3,2,1,0:T(8,128)(2,1)} %slice.53), channel_id=1, source_target_pairs={{4,0},{8,4},{12,8},{14,12},{10,14},{6,10},{2,6},{0,2},{5,1},{9,5},... | collective-permute-start | bytes 1179656 | tf_op jit(solution)/shard_map/ppermute | solution.py:63
  108.7 12.7 %collective-permute-start.14 = (bf16[2,1,64,1536]{3,2,1,0:T(8,128)(2,1)}, bf16[2,1,64,1536]{3,2,1,0:T(8,128)(2,1)}, u32[]{:S(2)}, u32[]{:S(2)}) collective-permute-start(bf16[2,1,64,1536]{3,2,1,0:T(8,128)(2,1)} %slice.52), channel_id=1, source_target_pairs={{0,4},{4,8},{8,12},{12,14},{14,10},{10,6},{6,2},{2,0},{1,5},{5,9},... | collective-permute-start | bytes 1179656 | tf_op jit(solution)/shard_map/ppermute | solution.py:60

commit v4 on v3

--- a/solution.py
+++ b/solution.py
@@ -79,19 +79,61 @@
     return arrays, lookup, relative
 
 
-def gather_attention_kernel(cycle_sources, far_sources, table_ref, q_hbm, own_hbm, *rest):
+def own_attention_kernel(q_ref, k_ref, v_ref, acc_ref, max_ref, total_ref):
+    scores = lax.dot_general(
+        q_ref[...], k_ref[...], (((1,), (1,)), ((), ())), preferred_element_type=jnp.float32
+    ) * HEAD_DIM ** (-0.5)
+    row_max = jnp.max(scores, axis=1, keepdims=True)
+    weights = jnp.exp(scores - row_max)
+    max_ref[...] = row_max
+    total_ref[...] = jnp.sum(weights, axis=1, keepdims=True)
+    acc_ref[...] = jnp.dot(
+        weights.astype(jnp.bfloat16), v_ref[...], preferred_element_type=jnp.float32
+    )
+
+
+def own_attend(query_rows, own):
+    token_count, width = query_rows.shape
+    key_count = own.shape[1] * own.shape[2]
+    heads = width // HEAD_DIM
+    key_values = own.reshape(2, key_count, width)
+    return pl.pallas_call(
+        own_attention_kernel,
+        out_shape=(
+            jax.ShapeDtypeStruct((token_count, width), jnp.float32),
+            jax.ShapeDtypeStruct((heads, token_count, 1), jnp.float32),
+            jax.ShapeDtypeStruct((heads, token_count, 1), jnp.float32),
+        ),
+        grid=(heads,),
+        in_specs=[
+            pl.BlockSpec((token_count, HEAD_DIM), lambda h: (0, h)),
+            pl.BlockSpec((None, key_count, HEAD_DIM), lambda h: (0, 0, h)),
+            pl.BlockSpec((None, key_count, HEAD_DIM), lambda h: (1, 0, h)),
+        ],
+        out_specs=(
+            pl.BlockSpec((token_count, HEAD_DIM), lambda h: (0, h)),
+            pl.BlockSpec((None, token_count, 1), lambda h: (h, 0, 0)),
+            pl.BlockSpec((None, token_count, 1), lambda h: (h, 0, 0)),
+        ),
+        cost_estimate=pl.CostEstimate(
+            flops=4 * token_count * key_count * width,
+            transcendentals=token_count * key_count * heads,
+            bytes_accessed=2 * token_count * width + 4 * key_count * width + 4 * token_count * width,
+        ),
+    )(query_rows, key_values, key_values)
+
+
+def gather_attention_kernel(
+    cycle_sources, far_sources, table_ref, q_hbm, acc_ref, max_ref, total_ref, *rest
+):
     sources = rest[: cycle_sources + far_sources]
     o_ref, q_vmem, k_vmem, v_vmem, sems = rest[cycle_sources + far_sources :]
-    tile_blocks = own_hbm.shape[1]
-    block_length = own_hbm.shape[2]
     extra = table_ref.shape[0] // 2
+    block_length = k_vmem.shape[1]
     heads = q_vmem.shape[1] // HEAD_DIM
 
-    copies = [pltpu.make_async_copy(q_hbm, q_vmem, sems.at[0, 0])]
-    copies.append(pltpu.make_async_copy(own_hbm.at[0], k_vmem.at[pl.ds(0, tile_blocks)], sems.at[0, 1]))
-    copies.append(pltpu.make_async_copy(own_hbm.at[1], v_vmem.at[pl.ds(0, tile_blocks)], sems.at[1, 1]))
-    for c in copies:
-        c.start()
+    query_copy = pltpu.make_async_copy(q_hbm, q_vmem, sems.at[0, extra])
+    query_copy.start()
     for slot in range(extra):
         src = table_ref[2 * slot]
         index = table_ref[2 * slot + 1]
@@ -101,17 +143,14 @@
             def _():
                 for kv, dst in ((0, k_vmem), (1, v_vmem)):
                     pltpu.make_async_copy(
-                        sources[cand].at[kv, index], dst.at[tile_blocks + slot], sems.at[kv, 2 + slot]
+                        sources[cand].at[kv, index], dst.at[slot], sems.at[kv, slot]
                     ).start()
-    for c in copies:
-        c.wait()
+    query_copy.wait()
     for slot in range(extra):
         for kv, dst in ((0, k_vmem), (1, v_vmem)):
-            pltpu.make_async_copy(
-                own_hbm.at[kv, 0], dst.at[tile_blocks + slot], sems.at[kv, 2 + slot]
-            ).wait()
-
-    key_count = k_vmem.shape[0] * block_length
+            pltpu.make_async_copy(sources[0].at[kv, 0], dst.at[slot], sems.at[kv, slot]).wait()
+
+    key_count = extra * block_length
 
     def head(h, carry):
         lanes = pl.ds(pl.multiple_of(h * HEAD_DIM, HEAD_DIM), HEAD_DIM)
@@ -121,23 +160,25 @@
         scores = lax.dot_general(
             q, k, (((1,), (1,)), ((), ())), preferred_element_type=jnp.float32
         ) * HEAD_DIM ** (-0.5)
-        row_max = jnp.max(scores, axis=1, keepdims=True)
+        own_max = max_ref[h]
+        row_max = jnp.maximum(own_max, jnp.max(scores, axis=1, keepdims=True))
         weights = jnp.exp(scores - row_max)
-        row_total = jnp.sum(weights, axis=1, keepdims=True)
-        rounded = weights.astype(jnp.bfloat16)
-        blended = jnp.dot(rounded, v, preferred_element_type=jnp.float32)
+        scale = jnp.exp(own_max - row_max)
+        row_total = total_ref[h] * scale + jnp.sum(weights, axis=1, keepdims=True)
+        blended = acc_ref[:, lanes] * scale + jnp.dot(
+            weights.astype(jnp.bfloat16), v, preferred_element_type=jnp.float32
+        )
         o_ref[:, lanes] = (blended / row_total).astype(o_ref.dtype)
         return carry
 
     lax.fori_loop(0, heads, head, 0)
 
 
-def gather_attend(query_rows, own, cycle_list_sources, far_list_sources, table):
+def gather_attend(query_rows, partial, cycle_list_sources, far_list_sources, table):
     token_count, width = query_rows.shape
-    tile_blocks, block_length = own.shape[1], own.shape[2]
+    block_length = cycle_list_sources[0].shape[2]
     extra = table.shape[0] // 2
-    blocks = tile_blocks + extra
-    key_count = blocks * block_length
+    key_count = extra * block_length
     heads = width // HEAD_DIM
     n_sources = len(cycle_list_sources) + len(far_list_sources)
     kernel = functools.partial(
@@ -146,22 +187,23 @@
     return pl.pallas_call(
         kernel,
         out_shape=jax.ShapeDtypeStruct((token_count, width), jnp.bfloat16),
-        in_specs=[pl.BlockSpec(memory_space=pltpu.SMEM)]
-        + [pl.BlockSpec(memory_space=pl.ANY)] * (2 + n_sources),
+        in_specs=[pl.BlockSpec(memory_space=pltpu.SMEM), pl.BlockSpec(memory_space=pl.ANY)]
+        + [pl.BlockSpec(memory_space=pltpu.VMEM)] * 3
+        + [pl.BlockSpec(memory_space=pl.ANY)] * n_sources,
         out_specs=pl.BlockSpec(memory_space=pltpu.VMEM),
         scratch_shapes=[
             pltpu.VMEM((token_count, width), jnp.bfloat16),
-            pltpu.VMEM((blocks, block_length, width), jnp.bfloat16),
-            pltpu.VMEM((blocks, block_length, width), jnp.bfloat16),
-            pltpu.SemaphoreType.DMA((2, 2 + extra)),
+            pltpu.VMEM((extra, block_length, width), jnp.bfloat16),
+            pltpu.VMEM((extra, block_length, width), jnp.bfloat16),
+            pltpu.SemaphoreType.DMA((2, extra + 1)),
         ],
         compiler_params=pltpu.CompilerParams(vmem_limit_bytes=48 * 1024 * 1024),
         cost_estimate=pl.CostEstimate(
             flops=4 * token_count * key_count * width,
             transcendentals=token_count * key_count * heads,
-            bytes_accessed=2 * (2 * token_count * width + 2 * key_count * width),
-        ),
-    )(table, query_rows, own, *cycle_list_sources, *far_list_sources)
+            bytes_accessed=2 * token_count * width * 2 + 4 * key_count * width + 4 * token_count * width,
+        ),
+    )(table, query_rows, *partial, *cycle_list_sources, *far_list_sources)
 
 
 def per_device(queries, key_mant, key_exp, value_mant, value_exp, cycle_list, dilated_list):
@@ -231,9 +273,9 @@
         [jnp.concatenate([cycle_src, far_src]), jnp.concatenate([cycle_idx, far_idx])], axis=1
     ).reshape(-1)
     token_count = tile_blocks * block_length
-    result = gather_attend(
-        queries.reshape(token_count, width), stacked, cycle_sources, far_sources, table
-    )
+    query_rows = queries.reshape(token_count, width)
+    partial = own_attend(query_rows, stacked)
+    result = gather_attend(query_rows, partial, cycle_sources, far_sources, table)
     return result.reshape(queries.shape)
 
 

time: 148 us -> 157 us (1.061)
  Pallas kernels: 24.7 us -> 43.5 us
  waiting for transfers between devices: 53.6 us -> 45.3 us
    pallas_call x0 -> x1, Pallas kernels: none -> 13.4 us  [own_attend(): pl.pallas_call(own_attention_kernel, out_shape=(jax.ShapeDtypeStruct((tok...]
    ppermute x3, waiting for transfers between devices: 0.01 us -> 9.7 us  [ring_gather(): ahead = lax.ppermute(ahead, 'col', forward)]
    ppermute x3, waiting for transfers between devices: 43.5 us -> 35.6 us  [ring_gather(): behind = lax.ppermute(behind, 'col', backward)]
    pallas_call x1, Pallas kernels: 24.7 us -> 30.1 us  [gather_attend(): pl.pallas_call(kernel, out_shape=jax.ShapeDtypeStruct((token_count, width...]
    ppermute x1, waiting for transfers between devices: 5.02 us -> 0.01 us  [ring_gather(): arrays.append(lax.ppermute(ahead[:, :split], 'col', forward))]
    ppermute x1, waiting for transfers between devices: 5.01 us -> 0.01 us  [per_device(): lax.ppermute(left_payload[:, main_cap:], 'col', [(1, 0)])]
  transfers between devices with their start and end apart: 16 -> 16, of which waited for: 5 -> 5; matrix products, arithmetic and copies ran while one was open for 26% -> 23% of each run, Pallas kernels for 0% -> 9%
where the time goes in v4:
time: 157 us; the launch traced here: 156 us
  waiting for transfers between devices  45.3 us (29%)
  Pallas kernels  43.5 us (28%)
  starting transfers between devices  29 us (18%)
  local copies, waits for them, and re-layouts  23.5 us (15%)
  other arithmetic  14.2 us (9%)
    ppermute x3, waiting for transfers between devices, ring_gather(): behind = lax.ppermute(behind, 'col', backward)  35.6 us
    pallas_call x1, Pallas kernels, gather_attend(): pl.pallas_call(kernel, out_shape=jax.ShapeDtypeStruct((token_count, width...  30.1 us
    ppermute x6, starting transfers between devices, shift(): return lax.ppermute(x, axis, pairs)  16 us
    pallas_call x1, Pallas kernels, own_attend(): pl.pallas_call(own_attention_kernel, out_shape=(jax.ShapeDtypeStruct((tok...  13.4 us
    ppermute x3, waiting for transfers between devices, ring_gather(): ahead = lax.ppermute(ahead, 'col', forward)  9.7 us
    ppermute x3, starting transfers between devices, ring_gather(): behind = lax.ppermute(behind, 'col', backward)  5.81 us
    gather x1, local copies, waits for them, and re-layouts, per_device(): right_payload = jnp.take(stacked, to_right, axis=1)  3.58 us
    gather x1, local copies, waits for them, and re-layouts, per_device(): left_payload = jnp.take(stacked, to_left, axis=1)  3.58 us
  transfers between devices with their start and end apart: 16, of which 5 were waited for; matrix products, arithmetic and copies ran while one was open for 23% of the time, Pallas kernels for 9%

profile of v4, /device:TPU:0, one launch (start us, length us, event | category | flops | bytes accessed | tf_op | source)
XLA Modules:
  0.0 155.8 jit_solution(14961434864991314753)
XLA Ops:
  0.0 1.3 collective-permute-start.2
  1.3 6.0 %collective-permute-start.4 = (s32[4]{0:T(128)}, s32[4]{0:T(128)}, u32[]{:S(2)}, u32[]{:S(2)}) collective-permute-start(s32[4]{0:T(128)} %bitcast.96), channel_id=1, source_target_pairs={{0,2},{2,4},{4,6},{6,8},{8,10},{10,12},{12,14},{1,3},{3,5},{5,7},{... | collective-permute-start | bytes 56 | tf_op jit(solution)/shard_map/ppermute | solution.py:34
  7.3 1.0 exponential_bitcast_fusion
  8.3 1.0 exponential_bitcast_fusion.1
  9.3 1.8 %fusion = bf16[8,1,64,1536]{3,2,0,1:T(8,128)(2,1)S(1)} fusion(bf16[8,1,64,1536]{3,2,1,0:T(8,128)(2,1)} %param.15, f32[8,2,1536]{2,1,0:T(2,128)S(1)} %exponential_bitcast_fusion), kind=kLoop, calls=%fused_computation.8 | loop fusion | flops 2359296 | bytes 3244032 | tf_op jit(solution)/shard_map/convert_element_type | solution.py:24
  11.1 0.1 copy-done.9
  11.2 0.3 fusion.1
  11.5 0.8 copy-done.4
  12.3 0.3 maximum_bitcast_fusion
  12.6 0.2 copy-done.6
  12.8 1.0 slice.33
  13.8 1.5 collective-permute-start.8
  15.3 0.8 collective-permute-start.9
  16.2 0.8 fusion.16
  17.0 1.3 collective-permute-start
  18.4 0.6 gather_fusion
  19.0 0.6 dynamic_slice.3
  19.6 0.2 reduce-window.35
  19.8 0.2 reduce-window.34
  20.0 0.6 compare_select_fusion.13
  20.6 0.2 reduce-window.36
  20.8 0.1 select_reduce_fusion.1
  20.9 3.6 %gather_fusion.3 = bf16[3,2,64,1536]{3,2,1,0:T(8,128)(2,1)} fusion(bf16[2,8,64,1536]{3,2,1,0:T(8,128)(2,1)} %copy-done.3, s32[1024]{0:T(1024)S(1)} %pad_clamp_fusion.1), kind=kCustom, calls=%fused_computation.clone | custom fusion | bytes 2359308 | tf_op jit(solution)/shard_map/jit(_take)/gather | solution.py:231
  24.5 1.4 select_bitcast_fusion.1
  25.9 1.0 slice.48
  26.9 4.8 %collective-permute-start.3 = (bf16[2,2,64,1536]{3,2,0,1:T(8,128)(2,1)}, bf16[2,2,64,1536]{3,2,0,1:T(8,128)(2,1)}, u32[]{:S(2)}, u32[]{:S(2)}) collective-permute-start(bf16[2,2,64,1536]{3,2,0,1:T(8,128)(2,1)} %slice.48), channel_id=1, source_target_pairs={{0,2},{2,4},{4,6},{6,8},{8,10},{10,12},{12,14},{1,3},{3,5},{5,7},{... | collective-permute-start | bytes 2359304 | tf_op jit(solution)/shard_map/ppermute | solution.py:34
  31.7 0.6 compare_and_fusion.2
  32.4 0.2 reduce-window.37
  32.6 0.6 broadcast_add_fusion
  33.2 0.1 select_reduce_fusion
  33.3 0.1 collective-permute-done.8.rest_6_
  33.4 0.9 collective-permute-start.10
  34.3 0.2 collective-permute-done.9.rest_7_
  34.5 2.4 %collective-permute-start.11 = (bf16[2,2,64,1536]{3,2,1,0:T(8,128)(2,1)S(1)}, bf16[2,2,64,1536]{3,2,1,0:T(8,128)(2,1)}, u32[]{:S(2)}, u32[]{:S(2)}) collective-permute-start(bf16[2,2,64,1536]{3,2,1,0:T(8,128)(2,1)S(1)} %collective-permute-done.9.rest_7_), channel_id=1, source_target_pairs={{4,0},{8,4},{12,8},{14,12},{10,14},{6,10},{2,6},{0,2},{5,1},{9,5},... | collective-permute-start | bytes 2359304 | tf_op jit(solution)/shard_map/ppermute | solution.py:71
  36.9 3.6 %gather_fusion.4 = bf16[3,2,64,1536]{3,2,1,0:T(8,128)(2,1)} fusion(bf16[2,8,64,1536]{3,2,1,0:T(8,128)(2,1)} %copy-done.3, s32[1024]{0:T(1024)S(1)} %pad_clamp_fusion), kind=kCustom, calls=%fused_computation.1.clone | custom fusion | bytes 2359308 | tf_op jit(solution)/shard_map/jit(_take)/gather | solution.py:232
  40.5 1.5 select_bitcast_fusion
  42.0 1.0 slice.49
  43.0 1.3 collective-permute-start.5
  44.3 9.6 %collective-permute-done.10.rest_8_ = bf16[2,2,64,1536]{3,2,1,0:T(8,128)(2,1)} collective-permute-done((bf16[2,2,64,1536]{3,2,1,0:T(8,128)(2,1)S(1)}, bf16[2,2,64,1536]{3,2,1,0:T(8,128)(2,1)}, u32[]{:S(2)}, u32[]{:S(2)}) %collective-permute-start.10) | collective-permute-done | bytes 786464 | tf_op jit(solution)/shard_map/ppermute | solution.py:68
  54.0 29.2 %collective-permute-done.11.rest_9_ = bf16[2,2,64,1536]{3,2,1,0:T(8,128)(2,1)} collective-permute-done((bf16[2,2,64,1536]{3,2,1,0:T(8,128)(2,1)S(1)}, bf16[2,2,64,1536]{3,2,1,0:T(8,128)(2,1)}, u32[]{:S(2)}, u32[]{:S(2)}) %collective-permute-start.11) | collective-permute-done | bytes 786464 | tf_op jit(solution)/shard_map/ppermute | solution.py:71
  83.2 2.6 %collective-permute-start.13 = (bf16[2,2,64,1536]{3,2,1,0:T(8,128)(2,1)}, bf16[2,2,64,1536]{3,2,1,0:T(8,128)(2,1)}, u32[]{:S(2)}, u32[]{:S(2)}) collective-permute-start(bf16[2,2,64,1536]{3,2,1,0:T(8,128)(2,1)} %collective-permute-done.11.rest_9_), channel_id=1, source_target_pairs={{4,0},{8,4},{12,8},{14,12},{10,14},{6,10},{2,6},{0,2},{5,1},{9,5},... | collective-permute-start | bytes 2359304 | tf_op jit(solution)/shard_map/ppermute | solution.py:71
  85.8 0.6 fusion.15
  86.5 0.6 gather_fusion.2
  87.1 0.6 gather_fusion.1
  87.7 0.7 compare_select_fusion.11
  88.4 0.1 add_bitcast_fusion.1
  88.5 0.7 add_bitcast_fusion
  89.2 0.1 copy.27
  89.3 0.1 reshape.425.table_ref
  89.4 0.8 slice.50
  90.2 2.1 %slice.51 = bf16[2,1,64,1536]{3,2,0,1:T(8,128)(2,1)} slice(bf16[2,3,64,1536]{3,2,0,1:T(8,128)(2,1)} %copy-done.8), slice={[0:2], [2:3], [0:64], [0:1536]} | slice | bytes 786432 | tf_op jit(solution)/shard_map/slice | solution.py:239
  92.3 1.3 collective-permute-start.1
  93.6 1.8 %slice.52 = bf16[2,1,64,1536]{3,2,1,0:T(8,128)(2,1)} slice(bf16[2,2,64,1536]{3,2,1,0:T(8,128)(2,1)} %collective-permute-done.12.rest_10_), slice={[0:2], [0:1], [0:64], [0:1536]} | slice | bytes 786432 | tf_op jit(solution)/shard_map/slice | solution.py:60
  95.3 6.1 %collective-permute-done.13.rest_11_ = bf16[2,2,64,1536]{3,2,1,0:T(8,128)(2,1)} collective-permute-done((bf16[2,2,64,1536]{3,2,1,0:T(8,128)(2,1)}, bf16[2,2,64,1536]{3,2,1,0:T(8,128)(2,1)}, u32[]{:S(2)}, u32[]{:S(2)}) %collective-permute-start.13) | collective-permute-done | bytes 786464 | tf_op jit(solution)/shard_map/ppermute | solution.py:71
  101.4 0.7 collective-permute-start.6
  102.1 1.8 %slice.53 = bf16[2,1,64,1536]{3,2,1,0:T(8,128)(2,1)} slice(bf16[2,2,64,1536]{3,2,1,0:T(8,128)(2,1)} %collective-permute-done.13.rest_11_), slice={[0:2], [1:2], [0:64], [0:1536]} | slice | bytes 786432 | tf_op jit(solution)/shard_map/slice | solution.py:63
  103.9 1.3 collective-permute-start.7
  105.2 0.1 collective-permute-start.14
  105.3 2.7 %collective-permute-start.15 = (bf16[2,1,64,1536]{3,2,1,0:T(8,128)(2,1)}, bf16[2,1,64,1536]{3,2,1,0:T(8,128)(2,1)}, u32[]{:S(2)}, u32[]{:S(2)}) collective-permute-start(bf16[2,1,64,1536]{3,2,1,0:T(8,128)(2,1)} %slice.53), channel_id=1, source_target_pairs={{4,0},{8,4},{12,8},{14,12},{10,14},{6,10},{2,6},{0,2},{5,1},{9,5},... | collective-permute-start | bytes 1179656 | tf_op jit(solution)/shard_map/ppermute | solution.py:63
  108.0 1.9 %pad_maximum_fusion.k_ref.v_ref = bf16[2,512,1536]{2,1,0:T(8,128)(2,1)} fusion(bf16[1,512,1536]{2,1,0:T(8,128)(2,1)S(1)} %bitcast.90, bf16[1,512,1536]{2,1,0:T(8,128)(2,1)S(1)} %bitcast.92), kind=kLoop, calls=%fused_computation.5 | loop fusion | flops 1572864 | bytes 6291456 | tf_op jit(solution)/shard_map/stack | solution.py:219
  109.9 13.4 %shard_map.100 = (f32[512,1536]{1,0:T(8,128)}, f32[12,512,1]{2,1,0:T(8,128)}, f32[12,512,1]{2,1,0:T(8,128)}) custom-call(bf16[512,1536]{1,0:T(8,128)(2,1)} %bitcast.93, bf16[2,512,1536]{2,1,0:T(8,128)(2,1)} %pad_maximum_fusion.k_ref.v_ref, bf16[2,512,1536]{2,1,0:T(8,128)(2,1)} %pad_maximum_fusion.k_ref.v_ref), custom_call_target="tpu_custom_call" | custom-call | flops 1610612736 | bytes 7864320 | tf_op jit(solution)/shard_map/pallas_call | solution.py:100
  123.3 1.2 copy.30.rest_2_
  124.5 1.2 copy.31.rest_3_
  125.8 30.1 %shard_map.101 = bf16[512,1536]{1,0:T(8,128)(2,1)} custom-call(s32[16]{0:T(128)S(1)} %reshape.425.table_ref, bf16[512,1536]{1,0:T(8,128)(2,1)} %bitcast.94, f32[512,1536]{1,0:T(8,128)} %get-tuple-element.9.acc_ref, f32[12,512,1]{2,1,0:T(8,128)} %get-tuple-element.10.max_ref, f32[12,512,1]{2,1,0:T(8,128)} %get-tuple-element.11.total_ref, ...), custom_call_target="tpu_custom_call" | custom-call | flops 1610612736 | bytes 9437184 | tf_op jit(solution)/shard_map/pallas_call | solution.py:187
  (50 shorter events, 0.2 us)
Async XLA Ops:
  0.0 20.6 %collective-permute-start.2 = (s32[4]{0:T(128)}, s32[4]{0:T(128)S(1)}, u32[]{:S(2)}, u32[]{:S(2)}) collective-permute-start(s32[4]{0:T(128)} %bitcast.95), channel_id=1, source_target_pairs={{2,0},{4,2},{6,4},{8,6},{10,8},{12,10},{14,12},{3,1},{5,3},{7,5},{... | collective-permute-start | bytes 56 | tf_op jit(solution)/shard_map/ppermute | solution.py:34
  1.3 30.5 %collective-permute-start.4 = (s32[4]{0:T(128)}, s32[4]{0:T(128)}, u32[]{:S(2)}, u32[]{:S(2)}) collective-permute-start(s32[4]{0:T(128)} %bitcast.96), channel_id=1, source_target_pairs={{0,2},{2,4},{4,6},{6,8},{8,10},{10,12},{12,14},{1,3},{3,5},{5,7},{... | collective-permute-start | bytes 56 | tf_op jit(solution)/shard_map/ppermute | solution.py:34
  9.3 1.9 %copy-start.9 = (bf16[8,1,64,1536]{3,2,1,0:T(8,128)(2,1)S(1)}, bf16[8,1,64,1536]{3,2,1,0:T(8,128)(2,1)}, u32[]{:S(2)}) copy-start(bf16[8,1,64,1536]{3,2,1,0:T(8,128)(2,1)} %param.13) | copy-start | bytes 4718596
  11.2 1.1 copy-start.4
  11.5 1.4 copy-start.6
  12.8 4.2 %copy-start.3 = (bf16[2,8,64,1536]{3,2,1,0:T(8,128)(2,1)}, bf16[2,8,64,1536]{3,2,1,0:T(8,128)(2,1)S(1)}, u32[]{:S(2)}) copy-start(bf16[2,8,64,1536]{3,2,1,0:T(8,128)(2,1)S(1)} %maximum_bitcast_fusion) | copy-start | bytes 9437188
  12.8 5.5 %copy-start.10 = (s32[1,1,4]{2,1,0:T(1,128)S(1)}, s32[1,1,4]{2,1,0:T(1,128)}, u32[]{:S(2)}) copy-start(s32[1,1,4]{2,1,0:T(1,128)} %param.17) | copy-start | bytes 52
  12.8 5.5 %copy-start.11 = (s32[1,1,4]{2,1,0:T(1,128)S(1)}, s32[1,1,4]{2,1,0:T(1,128)}, u32[]{:S(2)}) copy-start(s32[1,1,4]{2,1,0:T(1,128)} %param.18) | copy-start | bytes 52
  12.8 5.5 %copy-start = (s32[8]{0:T(128)S(1)}, s32[8]{0:T(128)}, u32[]{:S(2)}) copy-start(s32[8]{0:T(128)} %constant.99.clone) | copy-start | bytes 100
  13.8 19.6 %collective-permute-start.8 = (bf16[2,2,64,1536]{3,2,1,0:T(8,128)(2,1)}, bf16[2,2,64,1536]{3,2,1,0:T(8,128)(2,1)S(1)}, u32[]{:S(2)}, u32[]{:S(2)}) collective-permute-start(bf16[2,2,64,1536]{3,2,1,0:T(8,128)(2,1)} %slice.33), channel_id=1, source_target_pairs={{0,4},{4,8},{8,12},{12,14},{14,10},{10,6},{6,2},{2,0},{1,5},{5,9},... | collective-permute-start | bytes 2359304 | tf_op jit(solution)/shard_map/ppermute | solution.py:68
  15.3 19.2 %collective-permute-start.9 = (bf16[2,2,64,1536]{3,2,1,0:T(8,128)(2,1)}, bf16[2,2,64,1536]{3,2,1,0:T(8,128)(2,1)S(1)}, u32[]{:S(2)}, u32[]{:S(2)}) collective-permute-start(bf16[2,2,64,1536]{3,2,1,0:T(8,128)(2,1)} %slice.33), channel_id=1, source_target_pairs={{4,0},{8,4},{12,8},{14,12},{10,14},{6,10},{2,6},{0,2},{5,1},{9,5},... | collective-permute-start | bytes 2359304 | tf_op jit(solution)/shard_map/ppermute | solution.py:71
  17.0 86.9 %collective-permute-start = (bf16[2,1,64,1536]{3,2,1,0:T(8,128)(2,1)S(1)}, bf16[2,1,64,1536]{3,2,1,0:T(8,128)(2,1)S(1)}, u32[]{:S(2)}, u32[]{:S(2)}) collective-permute-start(bf16[2,1,64,1536]{3,2,1,0:T(8,128)(2,1)S(1)} %get-tuple-element.15), channel_id=1, source_target_pairs={{0,1},{2,3},{4,5},{6,7},{8,9},{10,11},{12,13},{14,15},{16,17},{18,... | collective-permute-start | bytes 1179656 | tf_op jit(solution)/shard_map/ppermute | solution.py:34
  26.9 78.3 %collective-permute-start.3 = (bf16[2,2,64,1536]{3,2,0,1:T(8,128)(2,1)}, bf16[2,2,64,1536]{3,2,0,1:T(8,128)(2,1)}, u32[]{:S(2)}, u32[]{:S(2)}) collective-permute-start(bf16[2,2,64,1536]{3,2,0,1:T(8,128)(2,1)} %slice.48), channel_id=1, source_target_pairs={{0,2},{2,4},{4,6},{6,8},{8,10},{10,12},{12,14},{1,3},{3,5},{5,7},{... | collective-permute-start | bytes 2359304 | tf_op jit(solution)/shard_map/ppermute | solution.py:34
  33.4 20.6 %collective-permute-start.10 = (bf16[2,2,64,1536]{3,2,1,0:T(8,128)(2,1)S(1)}, bf16[2,2,64,1536]{3,2,1,0:T(8,128)(2,1)}, u32[]{:S(2)}, u32[]{:S(2)}) collective-permute-start(bf16[2,2,64,1536]{3,2,1,0:T(8,128)(2,1)S(1)} %collective-permute-done.8.rest_6_), channel_id=1, source_target_pairs={{0,4},{4,8},{8,12},{12,14},{14,10},{10,6},{6,2},{2,0},{1,5},{5,9},... | collective-permute-start | bytes 2359304 | tf_op jit(solution)/shard_map/ppermute | solution.py:68
  34.5 48.7 %collective-permute-start.11 = (bf16[2,2,64,1536]{3,2,1,0:T(8,128)(2,1)S(1)}, bf16[2,2,64,1536]{3,2,1,0:T(8,128)(2,1)}, u32[]{:S(2)}, u32[]{:S(2)}) collective-permute-start(bf16[2,2,64,1536]{3,2,1,0:T(8,128)(2,1)S(1)} %collective-permute-done.9.rest_7_), channel_id=1, source_target_pairs={{4,0},{8,4},{12,8},{14,12},{10,14},{6,10},{2,6},{0,2},{5,1},{9,5},... | collective-permute-start | bytes 2359304 | tf_op jit(solution)/shard_map/ppermute | solution.py:71
  40.5 45.3 %copy-start.12 = (s32[1,1,4]{2,1,0:T(1,128)S(1)}, s32[1,1,4]{2,1,0:T(1,128)}, u32[]{:S(2)}) copy-start(s32[1,1,4]{2,1,0:T(1,128)} %param.18) | copy-start | bytes 52
  40.5 46.0 %copy-start.2 = (s32[7,2]{1,0:T(8,128)S(1)}, s32[7,2]{1,0:T(8,128)}, u32[]{:S(2)}) copy-start(s32[7,2]{1,0:T(8,128)} %constant.101.clone) | copy-start | bytes 172
  42.0 41.2 %copy-start.8 = (bf16[2,3,64,1536]{3,2,0,1:T(8,128)(2,1)}, bf16[2,3,64,1536]{3,2,0,1:T(8,128)(2,1)S(1)}, u32[]{:S(2)}) copy-start(bf16[2,3,64,1536]{3,2,0,1:T(8,128)(2,1)S(1)} %select_bitcast_fusion) | copy-start | bytes 3538948
  42.0 45.1 %copy-start.1 = (s32[7,2]{1,0:T(8,128)S(1)}, s32[7,2]{1,0:T(8,128)}, u32[]{:S(2)}) copy-start(s32[7,2]{1,0:T(8,128)} %constant.100.clone) | copy-start | bytes 172
  43.0 62.2 %collective-permute-start.5 = (bf16[2,2,64,1536]{3,2,0,1:T(8,128)(2,1)}, bf16[2,2,64,1536]{3,2,0,1:T(8,128)(2,1)}, u32[]{:S(2)}, u32[]{:S(2)}) collective-permute-start(bf16[2,2,64,1536]{3,2,0,1:T(8,128)(2,1)} %slice.49), channel_id=1, source_target_pairs={{2,0},{4,2},{6,4},{8,6},{10,8},{12,10},{14,12},{3,1},{5,3},{7,5},{... | collective-permute-start | bytes 2359304 | tf_op jit(solution)/shard_map/ppermute | solution.py:34
  54.0 38.3 %collective-permute-start.12 = (bf16[2,2,64,1536]{3,2,1,0:T(8,128)(2,1)}, bf16[2,2,64,1536]{3,2,1,0:T(8,128)(2,1)}, u32[]{:S(2)}, u32[]{:S(2)}) collective-permute-start(bf16[2,2,64,1536]{3,2,1,0:T(8,128)(2,1)} %collective-permute-done.10.rest_8_), channel_id=1, source_target_pairs={{0,4},{4,8},{8,12},{12,14},{14,10},{10,6},{6,2},{2,0},{1,5},{5,9},... | collective-permute-start | bytes 2359304 | tf_op jit(solution)/shard_map/ppermute | solution.py:68
  83.2 18.2 %collective-permute-start.13 = (bf16[2,2,64,1536]{3,2,1,0:T(8,128)(2,1)}, bf16[2,2,64,1536]{3,2,1,0:T(8,128)(2,1)}, u32[]{:S(2)}, u32[]{:S(2)}) collective-permute-start(bf16[2,2,64,1536]{3,2,1,0:T(8,128)(2,1)} %collective-permute-done.11.rest_9_), channel_id=1, source_target_pairs={{4,0},{8,4},{12,8},{14,12},{10,14},{6,10},{2,6},{0,2},{5,1},{9,5},... | collective-permute-start | bytes 2359304 | tf_op jit(solution)/shard_map/ppermute | solution.py:71
  89.4 18.6 %copy-start.5 = (bf16[8,1,64,1536]{3,2,0,1:T(8,128)(2,1)S(1)}, bf16[8,1,64,1536]{3,2,0,1:T(8,128)(2,1)}, u32[]{:S(2)}) copy-start(bf16[8,1,64,1536]{3,2,0,1:T(8,128)(2,1)} %copy-done.4) | copy-start | bytes 4718596
  89.4 18.6 %copy-start.7 = (bf16[8,1,64,1536]{3,2,0,1:T(8,128)(2,1)S(1)}, bf16[8,1,64,1536]{3,2,0,1:T(8,128)(2,1)}, u32[]{:S(2)}) copy-start(bf16[8,1,64,1536]{3,2,0,1:T(8,128)(2,1)} %copy-done.6) | copy-start | bytes 4718596
  92.3 33.5 %collective-permute-start.1 = (bf16[2,1,64,1536]{3,2,1,0:T(8,128)(2,1)}, bf16[2,1,64,1536]{3,2,1,0:T(8,128)(2,1)S(1)}, u32[]{:S(2)}, u32[]{:S(2)}) collective-permute-start(bf16[2,1,64,1536]{3,2,1,0:T(8,128)(2,1)} %get-tuple-element.14), channel_id=1, source_target_pairs={{1,0},{3,2},{5,4},{7,6},{9,8},{11,10},{13,12},{15,14},{17,16},{19,... | collective-permute-start | bytes 1179656 | tf_op jit(solution)/shard_map/ppermute | solution.py:34
  101.4 24.3 %collective-permute-start.6 = (bf16[2,1,64,1536]{3,2,0,1:T(8,128)(2,1)}, bf16[2,1,64,1536]{3,2,0,1:T(8,128)(2,1)S(1)}, u32[]{:S(2)}, u32[]{:S(2)}) collective-permute-start(bf16[2,1,64,1536]{3,2,0,1:T(8,128)(2,1)} %slice.50), channel_id=1, source_target_pairs={{12,14},{13,15},{28,30},{29,31}} | collective-permute-start | bytes 1179656 | tf_op jit(solution)/shard_map/ppermute | solution.py:238
  103.9 21.8 %collective-permute-start.7 = (bf16[2,1,64,1536]{3,2,0,1:T(8,128)(2,1)}, bf16[2,1,64,1536]{3,2,0,1:T(8,128)(2,1)S(1)}, u32[]{:S(2)}, u32[]{:S(2)}) collective-permute-start(bf16[2,1,64,1536]{3,2,0,1:T(8,128)(2,1)} %slice.51), channel_id=1, source_target_pairs={{2,0},{3,1},{18,16},{19,17}} | collective-permute-start | bytes 1179656 | tf_op jit(solution)/shard_map/ppermute | solution.py:239
  105.2 20.6 %collective-permute-start.14 = (bf16[2,1,64,1536]{3,2,1,0:T(8,128)(2,1)}, bf16[2,1,64,1536]{3,2,1,0:T(8,128)(2,1)S(1)}, u32[]{:S(2)}, u32[]{:S(2)}) collective-permute-start(bf16[2,1,64,1536]{3,2,1,0:T(8,128)(2,1)} %slice.52), channel_id=1, source_target_pairs={{0,4},{4,8},{8,12},{12,14},{14,10},{10,6},{6,2},{2,0},{1,5},{5,9},... | collective-permute-start | bytes 1179656 | tf_op jit(solution)/shard_map/ppermute | solution.py:60
  105.3 20.5 %collective-permute-start.15 = (bf16[2,1,64,1536]{3,2,1,0:T(8,128)(2,1)}, bf16[2,1,64,1536]{3,2,1,0:T(8,128)(2,1)}, u32[]{:S(2)}, u32[]{:S(2)}) collective-permute-start(bf16[2,1,64,1536]{3,2,1,0:T(8,128)(2,1)} %slice.53), channel_id=1, source_target_pairs={{4,0},{8,4},{12,8},{14,12},{10,14},{6,10},{2,6},{0,2},{5,1},{9,5},... | collective-permute-start | bytes 1179656 | tf_op jit(solution)/shard_map/ppermute | solution.py:63

commit v5 on v3

--- a/solution.py
+++ b/solution.py
@@ -52,25 +52,24 @@
     half = count // 2
     rows = item.shape[1]
     split = (rows + 1) // 2
-    ahead, behind = item, item
     arrays = []
-    lookup = [None] * (count - 1)
-    for distance in range(1, half + 1):
-        if distance == half and count % 2 == 0:
-            arrays.append(lax.ppermute(ahead[:, :split], "col", forward))
-            first = len(arrays) - 1
-            if split < rows:
-                arrays.append(lax.ppermute(behind[:, split:], "col", backward))
-            lookup[distance - 1] = [
-                (first, r) if r < split else (first + 1, r - split) for r in range(rows)
-            ]
-            continue
-        ahead = lax.ppermute(ahead, "col", forward)
-        arrays.append(ahead)
-        lookup[distance - 1] = [(len(arrays) - 1, r) for r in range(rows)]
-        behind = lax.ppermute(behind, "col", backward)
-        arrays.append(behind)
-        lookup[count - distance - 1] = [(len(arrays) - 1, r) for r in range(rows)]
+    lookup = [[None] * rows for _ in range(count - 1)]
+    for r in range(rows):
+        ahead = behind = item[:, r : r + 1]
+        for distance in range(1, half + 1):
+            if distance == half and count % 2 == 0:
+                if r < split:
+                    arrays.append(lax.ppermute(ahead, "col", forward))
+                else:
+                    arrays.append(lax.ppermute(behind, "col", backward))
+                lookup[distance - 1][r] = (len(arrays) - 1, 0)
+                continue
+            ahead = lax.ppermute(ahead, "col", forward)
+            arrays.append(ahead)
+            lookup[distance - 1][r] = (len(arrays) - 1, 0)
+            behind = lax.ppermute(behind, "col", backward)
+            arrays.append(behind)
+            lookup[count - distance - 1][r] = (len(arrays) - 1, 0)
     table = jnp.array(position, dtype=jnp.int32)
 
     def relative(col):

time: 148 us -> 145 us (0.980); the launches traced: 146 us -> 145 us
  starting transfers between devices: 28.8 us -> 37.9 us
  other arithmetic: 15.5 us -> 12.1 us
  local copies, waits for them, and re-layouts: 23.2 us -> 19.8 us
  waiting for transfers between devices: 53.6 us -> 50.6 us
    ppermute x3 -> x6, starting transfers between devices: 6.51 us -> 10.8 us  [ring_gather(): behind = lax.ppermute(behind, 'col', backward)]
    ppermute x1, waiting for transfers between devices: 5.01 us -> 0.85 us  [per_device(): lax.ppermute(left_payload[:, main_cap:], 'col', [(1, 0)])]
    slice x2 -> x1, local copies, waits for them, and re-layouts: 3.54 us -> 0.82 us  [ring_gather(): ahead = behind = item[:, r:r + 1]]
    ppermute x2, waiting for transfers between devices: 5.02 us -> 7.49 us  [the longest x1 7.49 us: ring_gather(): arrays.append(lax.ppermute(behind, 'col', backward))]
    ppermute x6, starting transfers between devices: 15.4 us -> 17.9 us  [shift(): return lax.ppermute(x, axis, pairs)]
    ppermute x2, local copies, waits for them, and re-layouts: 2.37 us -> 4.15 us  [shift(): return lax.ppermute(x, axis, pairs)]
    ppermute x3 -> x6, starting transfers between devices: 2.21 us -> 3.96 us  [ring_gather(): ahead = lax.ppermute(ahead, 'col', forward)]
    ppermute x3 -> x6, waiting for transfers between devices: 43.5 us -> 42.3 us  [ring_gather(): behind = lax.ppermute(behind, 'col', backward)]
  transfers between devices with their start and end apart: 16 -> 22, of which waited for: 5 -> 6; matrix products, arithmetic and copies ran while one was open for 26% -> 22% of each run, Pallas kernels for 0% -> 0%
where the time goes in v5:
time: 145 us
  waiting for transfers between devices  50.6 us (35%)
  starting transfers between devices  37.9 us (26%)
  Pallas kernels  24 us (17%)
  local copies, waits for them, and re-layouts  19.8 us (14%)
  other arithmetic  12.1 us (8%)
    ppermute x6, waiting for transfers between devices, ring_gather(): behind = lax.ppermute(behind, 'col', backward)  42.3 us
    pallas_call x1, Pallas kernels, gather_attend(): pl.pallas_call(kernel, out_shape=jax.ShapeDtypeStruct((token_count, width...  24 us
    ppermute x6, starting transfers between devices, shift(): return lax.ppermute(x, axis, pairs)  17.9 us
    ppermute x6, starting transfers between devices, ring_gather(): behind = lax.ppermute(behind, 'col', backward)  10.8 us
    ppermute x1, waiting for transfers between devices, ring_gather(): arrays.append(lax.ppermute(behind, 'col', backward))  7.49 us
    ppermute x2, local copies, waits for them, and re-layouts, shift(): return lax.ppermute(x, axis, pairs)  4.15 us
    ppermute x6, starting transfers between devices, ring_gather(): ahead = lax.ppermute(ahead, 'col', forward)  3.96 us
    gather x1, local copies, waits for them, and re-layouts, per_device(): right_payload = jnp.take(stacked, to_right, axis=1)  3.56 us
  transfers between devices with their start and end apart: 22, of which 6 were waited for; matrix products, arithmetic and copies ran while one was open for 22% of the time, Pallas kernels for 0%

profile of v5, /device:TPU:0, one launch (start us, length us, event | category | flops | bytes accessed | tf_op | source)
XLA Modules:
  0.0 144.8 jit_solution(418087475670236870)
XLA Ops:
  0.0 4.9 %collective-permute-start.4 = (s32[4]{0:T(128)}, s32[4]{0:T(128)S(1)}, u32[]{:S(2)}, u32[]{:S(2)}) collective-permute-start(s32[4]{0:T(128)} %bitcast.89), channel_id=1, source_target_pairs={{0,2},{2,4},{4,6},{6,8},{8,10},{10,12},{12,14},{1,3},{3,5},{5,7},{... | collective-permute-start | bytes 56 | tf_op jit(solution)/shard_map/ppermute | solution.py:34
  4.9 1.3 collective-permute-start.2
  6.2 1.0 exponential_bitcast_fusion.1
  7.1 1.0 exponential_bitcast_fusion
  8.1 1.8 %fusion = bf16[8,1,64,1536]{3,2,0,1:T(8,128)(2,1)S(1)} fusion(bf16[8,1,64,1536]{3,2,1,0:T(8,128)(2,1)} %param.15, f32[8,2,1536]{2,1,0:T(2,128)S(1)} %exponential_bitcast_fusion), kind=kLoop, calls=%fused_computation.7 | loop fusion | flops 2359296 | bytes 3244032 | tf_op jit(solution)/shard_map/convert_element_type | solution.py:24
  9.9 0.1 copy-done.4
  10.0 0.3 fusion.1
  10.3 0.3 maximum_bitcast_fusion.own_hbm
  10.6 0.1 slice.33
  10.7 0.8 fusion.17
  11.5 2.6 %collective-permute-start.16 = (bf16[2,1,64,1536]{3,2,1,0:T(8,128)(2,1)}, bf16[2,1,64,1536]{3,2,1,0:T(8,128)(2,1)S(1)}, u32[]{:S(2)}, u32[]{:S(2)}) collective-permute-start(bf16[2,1,64,1536]{3,2,1,0:T(8,128)(2,1)} %get-tuple-element.10), channel_id=1, source_target_pairs={{4,0},{8,4},{12,8},{14,12},{10,14},{6,10},{2,6},{0,2},{5,1},{9,5},... | collective-permute-start | bytes 1179656 | tf_op jit(solution)/shard_map/ppermute | solution.py:70
  14.2 1.0 collective-permute-start.15
  15.1 1.1 collective-permute-start.9
  16.2 1.0 fusion.16
  17.2 0.6 dynamic_slice.3
  17.8 0.6 gather_fusion
  18.5 1.0 collective-permute-start.8
  19.5 0.2 reduce-window.37
  19.7 0.1 select_reduce_fusion
  19.8 1.3 collective-permute-start.1
  21.1 0.2 reduce-window.36
  21.3 0.5 add_bitcast_fusion.3
  21.9 2.5 %gather_fusion.4 = bf16[3,2,64,1536]{3,2,1,0:T(8,128)(2,1)S(1)} fusion(bf16[2,8,64,1536]{3,2,1,0:T(8,128)(2,1)} %copy-done.2, s32[1024]{0:T(1024)S(1)} %pad_clamp_fusion), kind=kCustom, calls=%fused_computation.1.clone | custom fusion | bytes 2359308 | tf_op jit(solution)/shard_map/jit(_take)/gather | solution.py:189
  24.4 0.2 select_bitcast_fusion
  24.6 0.5 copy-done.10
  25.0 0.1 select_reduce_fusion.1
  25.2 0.8 slice.51
  25.9 0.9 slice.49
  26.9 3.6 %gather_fusion.3 = bf16[3,2,64,1536]{3,2,1,0:T(8,128)(2,1)} fusion(bf16[2,8,64,1536]{3,2,1,0:T(8,128)(2,1)} %copy-done.2, s32[1024]{0:T(1024)S(1)} %pad_clamp_fusion.1), kind=kCustom, calls=%fused_computation.clone | custom fusion | bytes 2359308 | tf_op jit(solution)/shard_map/jit(_take)/gather | solution.py:188
  30.5 3.1 %collective-permute-start = (bf16[2,1,64,1536]{3,2,1,0:T(8,128)(2,1)}, bf16[2,1,64,1536]{3,2,1,0:T(8,128)(2,1)S(1)}, u32[]{:S(2)}, u32[]{:S(2)}) collective-permute-start(bf16[2,1,64,1536]{3,2,1,0:T(8,128)(2,1)} %get-tuple-element.9), channel_id=1, source_target_pairs={{0,1},{2,3},{4,5},{6,7},{8,9},{10,11},{12,13},{14,15},{16,17},{18,... | collective-permute-start | bytes 1179656 | tf_op jit(solution)/shard_map/ppermute | solution.py:34
  33.6 1.3 collective-permute-start.7
  34.9 1.5 %select_bitcast_fusion.1 = bf16[2,3,64,1536]{3,2,0,1:T(8,128)(2,1)S(1)} fusion(bf16[3,2,64,1536]{3,2,1,0:T(8,128)(2,1)} %gather_fusion.3, pred[3]{0:T(512)(128)(4,1)S(1)} %compare_and_fusion.1), kind=kLoop, calls=%fused_computation.11 | loop fusion | flops 589824 | bytes 2359299 | tf_op jit(solution)/shard_map/jit(_take)/select_n | solution.py:188
  36.3 1.0 slice.48
  37.4 1.3 collective-permute-start.5
  38.7 6.1 %collective-permute-start.3 = (bf16[2,2,64,1536]{3,2,0,1:T(8,128)(2,1)}, bf16[2,2,64,1536]{3,2,0,1:T(8,128)(2,1)}, u32[]{:S(2)}, u32[]{:S(2)}) collective-permute-start(bf16[2,2,64,1536]{3,2,0,1:T(8,128)(2,1)} %slice.48), channel_id=1, source_target_pairs={{0,2},{2,4},{4,6},{6,8},{8,10},{10,12},{12,14},{1,3},{3,5},{5,7},{... | collective-permute-start | bytes 2359304 | tf_op jit(solution)/shard_map/ppermute | solution.py:34
  44.8 2.1 %collective-permute-start.18 = (bf16[2,1,64,1536]{3,2,1,0:T(8,128)(2,1)S(1)}, bf16[2,1,64,1536]{3,2,1,0:T(8,128)(2,1)S(1)}, u32[]{:S(2)}, u32[]{:S(2)}) collective-permute-start(bf16[2,1,64,1536]{3,2,1,0:T(8,128)(2,1)S(1)} %collective-permute-done.16.rest_14_), channel_id=1, source_target_pairs={{4,0},{8,4},{12,8},{14,12},{10,14},{6,10},{2,6},{0,2},{5,1},{9,5},... | collective-permute-start | bytes 1179656 | tf_op jit(solution)/shard_map/ppermute | solution.py:70
  46.9 0.9 collective-permute-done.7
  47.7 0.6 fusion.15
  48.4 0.6 gather_fusion.1
  49.0 0.5 fusion.6
  49.5 34.8 %collective-permute-done.18.rest_16_ = bf16[2,1,64,1536]{3,2,1,0:T(8,128)(2,1)S(1)} collective-permute-done((bf16[2,1,64,1536]{3,2,1,0:T(8,128)(2,1)S(1)}, bf16[2,1,64,1536]{3,2,1,0:T(8,128)(2,1)S(1)}, u32[]{:S(2)}, u32[]{:S(2)}) %collective-permute-start.18) | collective-permute-done | bytes 393248 | tf_op jit(solution)/shard_map/ppermute | solution.py:70
  84.4 2.5 %collective-permute-start.11 = (bf16[2,1,64,1536]{3,2,1,0:T(8,128)(2,1)S(1)}, bf16[2,1,64,1536]{3,2,1,0:T(8,128)(2,1)}, u32[]{:S(2)}, u32[]{:S(2)}) collective-permute-start(bf16[2,1,64,1536]{3,2,1,0:T(8,128)(2,1)S(1)} %collective-permute-done.9.rest_7_), channel_id=1, source_target_pairs={{4,0},{8,4},{12,8},{14,12},{10,14},{6,10},{2,6},{0,2},{5,1},{9,5},... | collective-permute-start | bytes 1179656 | tf_op jit(solution)/shard_map/ppermute | solution.py:70
  86.9 0.0 collective-permute-start.20
  86.9 2.0 %collective-permute-start.12 = (bf16[2,1,64,1536]{3,2,1,0:T(8,128)(2,1)}, bf16[2,1,64,1536]{3,2,1,0:T(8,128)(2,1)}, u32[]{:S(2)}, u32[]{:S(2)}) collective-permute-start(bf16[2,1,64,1536]{3,2,1,0:T(8,128)(2,1)} %collective-permute-done.10.rest_8_), channel_id=1, source_target_pairs={{0,4},{4,8},{8,12},{12,14},{14,10},{10,6},{6,2},{2,0},{1,5},{5,9},... | collective-permute-start | bytes 1179656 | tf_op jit(solution)/shard_map/ppermute | solution.py:67
  88.9 0.5 broadcast_add_fusion.2
  89.4 1.3 reduce-window.34
  90.6 0.7 reduce-window.35
  91.3 0.6 gather_fusion.2
  91.9 0.6 compare_select_fusion.13
  92.6 0.6 add_bitcast_fusion
  93.2 1.8 %slice.50 = bf16[2,1,64,1536]{3,2,0,1:T(8,128)(2,1)} slice(bf16[2,3,64,1536]{3,2,0,1:T(8,128)(2,1)} %copy-done.3), slice={[0:2], [2:3], [0:64], [0:1536]} | slice | bytes 786432 | tf_op jit(solution)/shard_map/slice | solution.py:195
  95.0 1.5 %collective-permute-done.11.rest_9_ = bf16[2,1,64,1536]{3,2,1,0:T(8,128)(2,1)} collective-permute-done((bf16[2,1,64,1536]{3,2,1,0:T(8,128)(2,1)S(1)}, bf16[2,1,64,1536]{3,2,1,0:T(8,128)(2,1)}, u32[]{:S(2)}, u32[]{:S(2)}) %collective-permute-start.11) | collective-permute-done | bytes 393248 | tf_op jit(solution)/shard_map/ppermute | solution.py:70
  96.4 1.4 %collective-permute-start.6 = (bf16[2,1,64,1536]{3,2,0,1:T(8,128)(2,1)}, bf16[2,1,64,1536]{3,2,0,1:T(8,128)(2,1)}, u32[]{:S(2)}, u32[]{:S(2)}) collective-permute-start(bf16[2,1,64,1536]{3,2,0,1:T(8,128)(2,1)} %slice.50), channel_id=1, source_target_pairs={{12,14},{13,15},{28,30},{29,31}} | collective-permute-start | bytes 1179656 | tf_op jit(solution)/shard_map/ppermute | solution.py:195
  97.9 2.5 %collective-permute-start.13 = (bf16[2,1,64,1536]{3,2,1,0:T(8,128)(2,1)}, bf16[2,1,64,1536]{3,2,1,0:T(8,128)(2,1)}, u32[]{:S(2)}, u32[]{:S(2)}) collective-permute-start(bf16[2,1,64,1536]{3,2,1,0:T(8,128)(2,1)} %collective-permute-done.11.rest_9_), channel_id=1, source_target_pairs={{4,0},{8,4},{12,8},{14,12},{10,14},{6,10},{2,6},{0,2},{5,1},{9,5},... | collective-permute-start | bytes 1179656 | tf_op jit(solution)/shard_map/ppermute | solution.py:70
  100.4 4.4 %collective-permute-done.20.rest_18_ = bf16[2,1,64,1536]{3,2,1,0:T(8,128)(2,1)} collective-permute-done((bf16[2,1,64,1536]{3,2,1,0:T(8,128)(2,1)S(1)}, bf16[2,1,64,1536]{3,2,1,0:T(8,128)(2,1)}, u32[]{:S(2)}, u32[]{:S(2)}) %collective-permute-start.20) | collective-permute-done | bytes 393248 | tf_op jit(solution)/shard_map/ppermute | solution.py:70
  104.9 2.5 %collective-permute-start.21 = (bf16[2,1,64,1536]{3,2,1,0:T(8,128)(2,1)}, bf16[2,1,64,1536]{3,2,1,0:T(8,128)(2,1)}, u32[]{:S(2)}, u32[]{:S(2)}) collective-permute-start(bf16[2,1,64,1536]{3,2,1,0:T(8,128)(2,1)} %collective-permute-done.20.rest_18_), channel_id=1, source_target_pairs={{4,0},{8,4},{12,8},{14,12},{10,14},{6,10},{2,6},{0,2},{5,1},{9,5},... | collective-permute-start | bytes 1179656 | tf_op jit(solution)/shard_map/ppermute | solution.py:64
  107.4 0.1 add_bitcast_fusion.1
  107.5 0.1 copy.27
  107.5 0.1 reshape.421.table_ref
  107.6 2.1 %copy.31.rest_3_ = bf16[2,2,64,1536]{3,2,1,0:T(8,128)(2,1)} copy(bf16[2,2,64,1536]{3,2,0,1:T(8,128)(2,1)} %collective-permute-done.5) | data formatting | bytes 1572864 | tf_op jit(solution)/shard_map/ppermute | solution.py:34
  109.7 2.1 %copy.30.rest_2_ = bf16[2,2,64,1536]{3,2,1,0:T(8,128)(2,1)} copy(bf16[2,2,64,1536]{3,2,0,1:T(8,128)(2,1)} %collective-permute-done.3) | data formatting | bytes 1572864 | tf_op jit(solution)/shard_map/ppermute | solution.py:34
  111.8 1.5 %collective-permute-done.13.rest_11_ = bf16[2,1,64,1536]{3,2,1,0:T(8,128)(2,1)} collective-permute-done((bf16[2,1,64,1536]{3,2,1,0:T(8,128)(2,1)}, bf16[2,1,64,1536]{3,2,1,0:T(8,128)(2,1)}, u32[]{:S(2)}, u32[]{:S(2)}) %collective-permute-start.13) | collective-permute-done | bytes 393248 | tf_op jit(solution)/shard_map/ppermute | solution.py:70
  113.3 7.5 %collective-permute-done.21.rest_19_ = bf16[2,1,64,1536]{3,2,1,0:T(8,128)(2,1)} collective-permute-done((bf16[2,1,64,1536]{3,2,1,0:T(8,128)(2,1)}, bf16[2,1,64,1536]{3,2,1,0:T(8,128)(2,1)}, u32[]{:S(2)}, u32[]{:S(2)}) %collective-permute-start.21) | collective-permute-done | bytes 393248 | tf_op jit(solution)/shard_map/ppermute | solution.py:64
  120.8 24.0 %shard_map.100 = bf16[512,1536]{1,0:T(8,128)(2,1)} custom-call(s32[16]{0:T(128)S(1)} %reshape.421.table_ref, bf16[512,1536]{1,0:T(8,128)(2,1)} %bitcast.88, bf16[2,8,64,1536]{3,2,1,0:T(8,128)(2,1)} %copy-done.2, bf16[2,1,64,1536]{3,2,1,0:T(8,128)(2,1)S(1)} %collective-permute-done.rest_0_, bf16[2,1,64,1536]{3,2,1,0:T(8,128)(2,1)S(1)} %collective-permute-done.1.rest_1_, ...), custom_call_target="tpu_custom_call" | custom-call | flops 3221225472 | bytes 9437184 | tf_op jit(solution)/shard_map/pallas_call | solution.py:145
  (56 shorter events, 0.2 us)
Async XLA Ops:
  0.0 18.5 %collective-permute-start.4 = (s32[4]{0:T(128)}, s32[4]{0:T(128)S(1)}, u32[]{:S(2)}, u32[]{:S(2)}) collective-permute-start(s32[4]{0:T(128)} %bitcast.89), channel_id=1, source_target_pairs={{0,2},{2,4},{4,6},{6,8},{8,10},{10,12},{12,14},{1,3},{3,5},{5,7},{... | collective-permute-start | bytes 56 | tf_op jit(solution)/shard_map/ppermute | solution.py:34
  4.9 14.9 %collective-permute-start.2 = (s32[4]{0:T(128)}, s32[4]{0:T(128)S(1)}, u32[]{:S(2)}, u32[]{:S(2)}) collective-permute-start(s32[4]{0:T(128)} %bitcast.90), channel_id=1, source_target_pairs={{2,0},{4,2},{6,4},{8,6},{10,8},{12,10},{14,12},{3,1},{5,3},{7,5},{... | collective-permute-start | bytes 56 | tf_op jit(solution)/shard_map/ppermute | solution.py:34
  8.1 1.9 %copy-start.4 = (bf16[8,1,64,1536]{3,2,1,0:T(8,128)(2,1)S(1)}, bf16[8,1,64,1536]{3,2,1,0:T(8,128)(2,1)}, u32[]{:S(2)}) copy-start(bf16[8,1,64,1536]{3,2,1,0:T(8,128)(2,1)} %param.13) | copy-start | bytes 4718596
  10.6 5.6 %copy-start.2 = (bf16[2,8,64,1536]{3,2,1,0:T(8,128)(2,1)}, bf16[2,8,64,1536]{3,2,1,0:T(8,128)(2,1)S(1)}, u32[]{:S(2)}) copy-start(bf16[2,8,64,1536]{3,2,1,0:T(8,128)(2,1)S(1)} %maximum_bitcast_fusion.own_hbm) | copy-start | bytes 9437188
  10.7 6.5 %copy-start.6 = (s32[1,1,4]{2,1,0:T(1,128)S(1)}, s32[1,1,4]{2,1,0:T(1,128)}, u32[]{:S(2)}) copy-start(s32[1,1,4]{2,1,0:T(1,128)} %param.18) | copy-start | bytes 52
  10.7 6.5 %copy-start = (s32[8]{0:T(128)S(1)}, s32[8]{0:T(128)}, u32[]{:S(2)}) copy-start(s32[8]{0:T(128)} %constant.99.clone) | copy-start | bytes 100
  11.5 18.9 %collective-permute-start.16 = (bf16[2,1,64,1536]{3,2,1,0:T(8,128)(2,1)}, bf16[2,1,64,1536]{3,2,1,0:T(8,128)(2,1)S(1)}, u32[]{:S(2)}, u32[]{:S(2)}) collective-permute-start(bf16[2,1,64,1536]{3,2,1,0:T(8,128)(2,1)} %get-tuple-element.10), channel_id=1, source_target_pairs={{4,0},{8,4},{12,8},{14,12},{10,14},{6,10},{2,6},{0,2},{5,1},{9,5},... | collective-permute-start | bytes 1179656 | tf_op jit(solution)/shard_map/ppermute | solution.py:70
  14.2 19.4 %collective-permute-start.15 = (bf16[2,1,64,1536]{3,2,1,0:T(8,128)(2,1)}, bf16[2,1,64,1536]{3,2,1,0:T(8,128)(2,1)S(1)}, u32[]{:S(2)}, u32[]{:S(2)}) collective-permute-start(bf16[2,1,64,1536]{3,2,1,0:T(8,128)(2,1)} %get-tuple-element.10), channel_id=1, source_target_pairs={{0,4},{4,8},{8,12},{12,14},{14,10},{10,6},{6,2},{2,0},{1,5},{5,9},... | collective-permute-start | bytes 1179656 | tf_op jit(solution)/shard_map/ppermute | solution.py:67
  15.1 22.2 %collective-permute-start.9 = (bf16[2,1,64,1536]{3,2,1,0:T(8,128)(2,1)S(1)}, bf16[2,1,64,1536]{3,2,1,0:T(8,128)(2,1)S(1)}, u32[]{:S(2)}, u32[]{:S(2)}) collective-permute-start(bf16[2,1,64,1536]{3,2,1,0:T(8,128)(2,1)S(1)} %get-tuple-element.11), channel_id=1, source_target_pairs={{4,0},{8,4},{12,8},{14,12},{10,14},{6,10},{2,6},{0,2},{5,1},{9,5},... | collective-permute-start | bytes 1179656 | tf_op jit(solution)/shard_map/ppermute | solution.py:70
  18.5 20.2 %collective-permute-start.8 = (bf16[2,1,64,1536]{3,2,1,0:T(8,128)(2,1)S(1)}, bf16[2,1,64,1536]{3,2,1,0:T(8,128)(2,1)S(1)}, u32[]{:S(2)}, u32[]{:S(2)}) collective-permute-start(bf16[2,1,64,1536]{3,2,1,0:T(8,128)(2,1)S(1)} %get-tuple-element.11), channel_id=1, source_target_pairs={{0,4},{4,8},{8,12},{12,14},{14,10},{10,6},{6,2},{2,0},{1,5},{5,9},... | collective-permute-start | bytes 1179656 | tf_op jit(solution)/shard_map/ppermute | solution.py:67
  19.8 1.5 %copy-start.9 = (s32[4]{0:T(128)}, s32[4]{0:T(128)S(1)}, u32[]{:S(2)}) copy-start(s32[4]{0:T(128)S(1)} %collective-permute-done.2) | copy-start | bytes 52
  19.8 24.9 %collective-permute-start.1 = (bf16[2,1,64,1536]{3,2,1,0:T(8,128)(2,1)}, bf16[2,1,64,1536]{3,2,1,0:T(8,128)(2,1)S(1)}, u32[]{:S(2)}, u32[]{:S(2)}) collective-permute-start(bf16[2,1,64,1536]{3,2,1,0:T(8,128)(2,1)} %get-tuple-element.8), channel_id=1, source_target_pairs={{1,0},{3,2},{5,4},{7,6},{9,8},{11,10},{13,12},{15,14},{17,16},{19,... | collective-permute-start | bytes 1179656 | tf_op jit(solution)/shard_map/ppermute | solution.py:34
  24.4 0.7 copy-start.10
  24.4 0.7 copy-start.8
  30.4 17.3 %copy-start.7 = (s32[1,1,4]{2,1,0:T(1,128)S(1)}, s32[1,1,4]{2,1,0:T(1,128)}, u32[]{:S(2)}) copy-start(s32[1,1,4]{2,1,0:T(1,128)} %param.18) | copy-start | bytes 52
  30.5 17.9 %copy-start.1 = (s32[7,2]{1,0:T(8,128)S(1)}, s32[7,2]{1,0:T(8,128)}, u32[]{:S(2)}) copy-start(s32[7,2]{1,0:T(8,128)} %constant.100.clone) | copy-start | bytes 172
  30.5 16.4 %collective-permute-start = (bf16[2,1,64,1536]{3,2,1,0:T(8,128)(2,1)}, bf16[2,1,64,1536]{3,2,1,0:T(8,128)(2,1)S(1)}, u32[]{:S(2)}, u32[]{:S(2)}) collective-permute-start(bf16[2,1,64,1536]{3,2,1,0:T(8,128)(2,1)} %get-tuple-element.9), channel_id=1, source_target_pairs={{0,1},{2,3},{4,5},{6,7},{8,9},{10,11},{12,13},{14,15},{16,17},{18,... | collective-permute-start | bytes 1179656 | tf_op jit(solution)/shard_map/ppermute | solution.py:34
  33.6 14.2 %collective-permute-start.7 = (bf16[2,1,64,1536]{3,2,0,1:T(8,128)(2,1)}, bf16[2,1,64,1536]{3,2,0,1:T(8,128)(2,1)S(1)}, u32[]{:S(2)}, u32[]{:S(2)}) collective-permute-start(bf16[2,1,64,1536]{3,2,0,1:T(8,128)(2,1)} %slice.51), channel_id=1, source_target_pairs={{2,0},{3,1},{18,16},{19,17}} | collective-permute-start | bytes 1179656 | tf_op jit(solution)/shard_map/ppermute | solution.py:196
  36.3 11.4 %copy-start.3 = (bf16[2,3,64,1536]{3,2,0,1:T(8,128)(2,1)}, bf16[2,3,64,1536]{3,2,0,1:T(8,128)(2,1)S(1)}, u32[]{:S(2)}) copy-start(bf16[2,3,64,1536]{3,2,0,1:T(8,128)(2,1)S(1)} %select_bitcast_fusion.1) | copy-start | bytes 3538948
  36.3 12.7 %copy-start.5 = (s32[1,1,4]{2,1,0:T(1,128)S(1)}, s32[1,1,4]{2,1,0:T(1,128)}, u32[]{:S(2)}) copy-start(s32[1,1,4]{2,1,0:T(1,128)} %param.17) | copy-start | bytes 52
  37.4 60.5 %collective-permute-start.5 = (bf16[2,2,64,1536]{3,2,0,1:T(8,128)(2,1)}, bf16[2,2,64,1536]{3,2,0,1:T(8,128)(2,1)}, u32[]{:S(2)}, u32[]{:S(2)}) collective-permute-start(bf16[2,2,64,1536]{3,2,0,1:T(8,128)(2,1)} %slice.49), channel_id=1, source_target_pairs={{2,0},{4,2},{6,4},{8,6},{10,8},{12,10},{14,12},{3,1},{5,3},{7,5},{... | collective-permute-start | bytes 2359304 | tf_op jit(solution)/shard_map/ppermute | solution.py:34
  38.7 59.2 %collective-permute-start.3 = (bf16[2,2,64,1536]{3,2,0,1:T(8,128)(2,1)}, bf16[2,2,64,1536]{3,2,0,1:T(8,128)(2,1)}, u32[]{:S(2)}, u32[]{:S(2)}) collective-permute-start(bf16[2,2,64,1536]{3,2,0,1:T(8,128)(2,1)} %slice.48), channel_id=1, source_target_pairs={{0,2},{2,4},{4,6},{6,8},{8,10},{10,12},{12,14},{1,3},{3,5},{5,7},{... | collective-permute-start | bytes 2359304 | tf_op jit(solution)/shard_map/ppermute | solution.py:34
  44.8 39.6 %collective-permute-start.18 = (bf16[2,1,64,1536]{3,2,1,0:T(8,128)(2,1)S(1)}, bf16[2,1,64,1536]{3,2,1,0:T(8,128)(2,1)S(1)}, u32[]{:S(2)}, u32[]{:S(2)}) collective-permute-start(bf16[2,1,64,1536]{3,2,1,0:T(8,128)(2,1)S(1)} %collective-permute-done.16.rest_14_), channel_id=1, source_target_pairs={{4,0},{8,4},{12,8},{14,12},{10,14},{6,10},{2,6},{0,2},{5,1},{9,5},... | collective-permute-start | bytes 1179656 | tf_op jit(solution)/shard_map/ppermute | solution.py:70
  46.9 40.0 %collective-permute-start.17 = (bf16[2,1,64,1536]{3,2,1,0:T(8,128)(2,1)S(1)}, bf16[2,1,64,1536]{3,2,1,0:T(8,128)(2,1)S(1)}, u32[]{:S(2)}, u32[]{:S(2)}) collective-permute-start(bf16[2,1,64,1536]{3,2,1,0:T(8,128)(2,1)S(1)} %collective-permute-done.15.rest_13_), channel_id=1, source_target_pairs={{0,4},{4,8},{8,12},{12,14},{14,10},{10,6},{6,2},{2,0},{1,5},{5,9},... | collective-permute-start | bytes 1179656 | tf_op jit(solution)/shard_map/ppermute | solution.py:67
  47.7 39.2 %collective-permute-start.10 = (bf16[2,1,64,1536]{3,2,1,0:T(8,128)(2,1)S(1)}, bf16[2,1,64,1536]{3,2,1,0:T(8,128)(2,1)}, u32[]{:S(2)}, u32[]{:S(2)}) collective-permute-start(bf16[2,1,64,1536]{3,2,1,0:T(8,128)(2,1)S(1)} %collective-permute-done.8.rest_6_), channel_id=1, source_target_pairs={{0,4},{4,8},{8,12},{12,14},{14,10},{10,6},{6,2},{2,0},{1,5},{5,9},... | collective-permute-start | bytes 1179656 | tf_op jit(solution)/shard_map/ppermute | solution.py:67
  84.4 12.1 %collective-permute-start.11 = (bf16[2,1,64,1536]{3,2,1,0:T(8,128)(2,1)S(1)}, bf16[2,1,64,1536]{3,2,1,0:T(8,128)(2,1)}, u32[]{:S(2)}, u32[]{:S(2)}) collective-permute-start(bf16[2,1,64,1536]{3,2,1,0:T(8,128)(2,1)S(1)} %collective-permute-done.9.rest_7_), channel_id=1, source_target_pairs={{4,0},{8,4},{12,8},{14,12},{10,14},{6,10},{2,6},{0,2},{5,1},{9,5},... | collective-permute-start | bytes 1179656 | tf_op jit(solution)/shard_map/ppermute | solution.py:70
  86.9 18.0 %collective-permute-start.20 = (bf16[2,1,64,1536]{3,2,1,0:T(8,128)(2,1)S(1)}, bf16[2,1,64,1536]{3,2,1,0:T(8,128)(2,1)}, u32[]{:S(2)}, u32[]{:S(2)}) collective-permute-start(bf16[2,1,64,1536]{3,2,1,0:T(8,128)(2,1)S(1)} %collective-permute-done.18.rest_16_), channel_id=1, source_target_pairs={{4,0},{8,4},{12,8},{14,12},{10,14},{6,10},{2,6},{0,2},{5,1},{9,5},... | collective-permute-start | bytes 1179656 | tf_op jit(solution)/shard_map/ppermute | solution.py:70
  86.9 20.5 %collective-permute-start.12 = (bf16[2,1,64,1536]{3,2,1,0:T(8,128)(2,1)}, bf16[2,1,64,1536]{3,2,1,0:T(8,128)(2,1)}, u32[]{:S(2)}, u32[]{:S(2)}) collective-permute-start(bf16[2,1,64,1536]{3,2,1,0:T(8,128)(2,1)} %collective-permute-done.10.rest_8_), channel_id=1, source_target_pairs={{0,4},{4,8},{8,12},{12,14},{14,10},{10,6},{6,2},{2,0},{1,5},{5,9},... | collective-permute-start | bytes 1179656 | tf_op jit(solution)/shard_map/ppermute | solution.py:67
  96.4 15.3 %collective-permute-start.6 = (bf16[2,1,64,1536]{3,2,0,1:T(8,128)(2,1)}, bf16[2,1,64,1536]{3,2,0,1:T(8,128)(2,1)}, u32[]{:S(2)}, u32[]{:S(2)}) collective-permute-start(bf16[2,1,64,1536]{3,2,0,1:T(8,128)(2,1)} %slice.50), channel_id=1, source_target_pairs={{12,14},{13,15},{28,30},{29,31}} | collective-permute-start | bytes 1179656 | tf_op jit(solution)/shard_map/ppermute | solution.py:195
  97.9 13.9 %collective-permute-start.19 = (bf16[2,1,64,1536]{3,2,1,0:T(8,128)(2,1)S(1)}, bf16[2,1,64,1536]{3,2,1,0:T(8,128)(2,1)}, u32[]{:S(2)}, u32[]{:S(2)}) collective-permute-start(bf16[2,1,64,1536]{3,2,1,0:T(8,128)(2,1)S(1)} %collective-permute-done.17.rest_15_), channel_id=1, source_target_pairs={{0,4},{4,8},{8,12},{12,14},{14,10},{10,6},{6,2},{2,0},{1,5},{5,9},... | collective-permute-start | bytes 1179656 | tf_op jit(solution)/shard_map/ppermute | solution.py:67
  97.9 15.4 %collective-permute-start.13 = (bf16[2,1,64,1536]{3,2,1,0:T(8,128)(2,1)}, bf16[2,1,64,1536]{3,2,1,0:T(8,128)(2,1)}, u32[]{:S(2)}, u32[]{:S(2)}) collective-permute-start(bf16[2,1,64,1536]{3,2,1,0:T(8,128)(2,1)} %collective-permute-done.11.rest_9_), channel_id=1, source_target_pairs={{4,0},{8,4},{12,8},{14,12},{10,14},{6,10},{2,6},{0,2},{5,1},{9,5},... | collective-permute-start | bytes 1179656 | tf_op jit(solution)/shard_map/ppermute | solution.py:70
  104.9 15.9 %collective-permute-start.21 = (bf16[2,1,64,1536]{3,2,1,0:T(8,128)(2,1)}, bf16[2,1,64,1536]{3,2,1,0:T(8,128)(2,1)}, u32[]{:S(2)}, u32[]{:S(2)}) collective-permute-start(bf16[2,1,64,1536]{3,2,1,0:T(8,128)(2,1)} %collective-permute-done.20.rest_18_), channel_id=1, source_target_pairs={{4,0},{8,4},{12,8},{14,12},{10,14},{6,10},{2,6},{0,2},{5,1},{9,5},... | collective-permute-start | bytes 1179656 | tf_op jit(solution)/shard_map/ppermute | solution.py:64
  107.4 13.4 %collective-permute-start.14 = (bf16[2,1,64,1536]{3,2,1,0:T(8,128)(2,1)}, bf16[2,1,64,1536]{3,2,1,0:T(8,128)(2,1)}, u32[]{:S(2)}, u32[]{:S(2)}) collective-permute-start(bf16[2,1,64,1536]{3,2,1,0:T(8,128)(2,1)} %collective-permute-done.12.rest_10_), channel_id=1, source_target_pairs={{0,4},{4,8},{8,12},{12,14},{14,10},{10,6},{6,2},{2,0},{1,5},{5,9},... | collective-permute-start | bytes 1179656 | tf_op jit(solution)/shard_map/ppermute | solution.py:62

commit v6 on v4

--- a/solution.py
+++ b/solution.py
@@ -52,25 +52,24 @@
     half = count // 2
     rows = item.shape[1]
     split = (rows + 1) // 2
-    ahead, behind = item, item
     arrays = []
-    lookup = [None] * (count - 1)
-    for distance in range(1, half + 1):
-        if distance == half and count % 2 == 0:
-            arrays.append(lax.ppermute(ahead[:, :split], "col", forward))
-            first = len(arrays) - 1
-            if split < rows:
-                arrays.append(lax.ppermute(behind[:, split:], "col", backward))
-            lookup[distance - 1] = [
-                (first, r) if r < split else (first + 1, r - split) for r in range(rows)
-            ]
-            continue
-        ahead = lax.ppermute(ahead, "col", forward)
-        arrays.append(ahead)
-        lookup[distance - 1] = [(len(arrays) - 1, r) for r in range(rows)]
-        behind = lax.ppermute(behind, "col", backward)
-        arrays.append(behind)
-        lookup[count - distance - 1] = [(len(arrays) - 1, r) for r in range(rows)]
+    lookup = [[None] * rows for _ in range(count - 1)]
+    for r in range(rows):
+        ahead = behind = item[:, r : r + 1]
+        for distance in range(1, half + 1):
+            if distance == half and count % 2 == 0:
+                if r < split:
+                    arrays.append(lax.ppermute(ahead, "col", forward))
+                else:
+                    arrays.append(lax.ppermute(behind, "col", backward))
+                lookup[distance - 1][r] = (len(arrays) - 1, 0)
+                continue
+            ahead = lax.ppermute(ahead, "col", forward)
+            arrays.append(ahead)
+            lookup[distance - 1][r] = (len(arrays) - 1, 0)
+            behind = lax.ppermute(behind, "col", backward)
+            arrays.append(behind)
+            lookup[count - distance - 1][r] = (len(arrays) - 1, 0)
     table = jnp.array(position, dtype=jnp.int32)
 
     def relative(col):
@@ -92,11 +91,10 @@
     )
 
 
-def own_attend(query_rows, own):
+def own_attend(query_rows, keys, values):
     token_count, width = query_rows.shape
-    key_count = own.shape[1] * own.shape[2]
+    key_count = keys.shape[0]
     heads = width // HEAD_DIM
-    key_values = own.reshape(2, key_count, width)
     return pl.pallas_call(
         own_attention_kernel,
         out_shape=(
@@ -107,8 +105,8 @@
         grid=(heads,),
         in_specs=[
             pl.BlockSpec((token_count, HEAD_DIM), lambda h: (0, h)),
-            pl.BlockSpec((None, key_count, HEAD_DIM), lambda h: (0, 0, h)),
-            pl.BlockSpec((None, key_count, HEAD_DIM), lambda h: (1, 0, h)),
+            pl.BlockSpec((key_count, HEAD_DIM), lambda h: (0, h)),
+            pl.BlockSpec((key_count, HEAD_DIM), lambda h: (0, h)),
         ],
         out_specs=(
             pl.BlockSpec((token_count, HEAD_DIM), lambda h: (0, h)),
@@ -120,58 +118,51 @@
             transcendentals=token_count * key_count * heads,
             bytes_accessed=2 * token_count * width + 4 * key_count * width + 4 * token_count * width,
         ),
-    )(query_rows, key_values, key_values)
+    )(query_rows, keys, values)
 
 
 def gather_attention_kernel(
-    cycle_sources, far_sources, table_ref, q_hbm, acc_ref, max_ref, total_ref, *rest
+    cycle_sources, far_sources, table_ref, q_ref, acc_ref, max_ref, total_ref, *rest
 ):
     sources = rest[: cycle_sources + far_sources]
-    o_ref, q_vmem, k_vmem, v_vmem, sems = rest[cycle_sources + far_sources :]
+    o_ref, k_vmem, v_vmem, sems = rest[cycle_sources + far_sources :]
     extra = table_ref.shape[0] // 2
     block_length = k_vmem.shape[1]
-    heads = q_vmem.shape[1] // HEAD_DIM
-
-    query_copy = pltpu.make_async_copy(q_hbm, q_vmem, sems.at[0, extra])
-    query_copy.start()
-    for slot in range(extra):
-        src = table_ref[2 * slot]
-        index = table_ref[2 * slot + 1]
-        lo, hi = (0, cycle_sources) if slot < extra // 2 else (cycle_sources, cycle_sources + far_sources)
-        for cand in range(lo, hi):
-            @pl.when(src == cand)
-            def _():
-                for kv, dst in ((0, k_vmem), (1, v_vmem)):
-                    pltpu.make_async_copy(
-                        sources[cand].at[kv, index], dst.at[slot], sems.at[kv, slot]
-                    ).start()
-    query_copy.wait()
-    for slot in range(extra):
-        for kv, dst in ((0, k_vmem), (1, v_vmem)):
-            pltpu.make_async_copy(sources[0].at[kv, 0], dst.at[slot], sems.at[kv, slot]).wait()
+    h = pl.program_id(0)
+
+    @pl.when(h == 0)
+    def _():
+        for slot in range(extra):
+            src = table_ref[2 * slot]
+            index = table_ref[2 * slot + 1]
+            lo, hi = (0, cycle_sources) if slot < extra // 2 else (cycle_sources, cycle_sources + far_sources)
+            for cand in range(lo, hi):
+                @pl.when(src == cand)
+                def _():
+                    for kv, dst in ((0, k_vmem), (1, v_vmem)):
+                        pltpu.make_async_copy(
+                            sources[cand].at[kv, index], dst.at[slot], sems.at[kv, slot]
+                        ).start()
+        for slot in range(extra):
+            for kv, dst in ((0, k_vmem), (1, v_vmem)):
+                pltpu.make_async_copy(sources[0].at[kv, 0], dst.at[slot], sems.at[kv, slot]).wait()
 
     key_count = extra * block_length
-
-    def head(h, carry):
-        lanes = pl.ds(pl.multiple_of(h * HEAD_DIM, HEAD_DIM), HEAD_DIM)
-        q = q_vmem[:, lanes]
-        k = k_vmem[:, :, lanes].reshape(key_count, HEAD_DIM)
-        v = v_vmem[:, :, lanes].reshape(key_count, HEAD_DIM)
-        scores = lax.dot_general(
-            q, k, (((1,), (1,)), ((), ())), preferred_element_type=jnp.float32
-        ) * HEAD_DIM ** (-0.5)
-        own_max = max_ref[h]
-        row_max = jnp.maximum(own_max, jnp.max(scores, axis=1, keepdims=True))
-        weights = jnp.exp(scores - row_max)
-        scale = jnp.exp(own_max - row_max)
-        row_total = total_ref[h] * scale + jnp.sum(weights, axis=1, keepdims=True)
-        blended = acc_ref[:, lanes] * scale + jnp.dot(
-            weights.astype(jnp.bfloat16), v, preferred_element_type=jnp.float32
-        )
-        o_ref[:, lanes] = (blended / row_total).astype(o_ref.dtype)
-        return carry
-
-    lax.fori_loop(0, heads, head, 0)
+    lanes = pl.ds(pl.multiple_of(h * HEAD_DIM, HEAD_DIM), HEAD_DIM)
+    k = k_vmem[:, :, lanes].reshape(key_count, HEAD_DIM)
+    v = v_vmem[:, :, lanes].reshape(key_count, HEAD_DIM)
+    scores = lax.dot_general(
+        q_ref[...], k, (((1,), (1,)), ((), ())), preferred_element_type=jnp.float32
+    ) * HEAD_DIM ** (-0.5)
+    own_max = max_ref[...]
+    row_max = jnp.maximum(own_max, jnp.max(scores, axis=1, keepdims=True))
+    weights = jnp.exp(scores - row_max)
+    scale = jnp.exp(own_max - row_max)
+    row_total = total_ref[...] * scale + jnp.sum(weights, axis=1, keepdims=True)
+    blended = acc_ref[...] * scale + jnp.dot(
+        weights.astype(jnp.bfloat16), v, preferred_element_type=jnp.float32
+    )
+    o_ref[...] = (blended / row_total).astype(o_ref.dtype)
 
 
 def gather_attend(query_rows, partial, cycle_list_sources, far_list_sources, table):
@@ -184,20 +175,23 @@
     kernel = functools.partial(
         gather_attention_kernel, len(cycle_list_sources), len(far_list_sources)
     )
+    column = pl.BlockSpec((token_count, HEAD_DIM), lambda h, t: (0, h))
+    per_head = pl.BlockSpec((None, token_count, 1), lambda h, t: (h, 0, 0))
     return pl.pallas_call(
         kernel,
         out_shape=jax.ShapeDtypeStruct((token_count, width), jnp.bfloat16),
-        in_specs=[pl.BlockSpec(memory_space=pltpu.SMEM), pl.BlockSpec(memory_space=pl.ANY)]
-        + [pl.BlockSpec(memory_space=pltpu.VMEM)] * 3
-        + [pl.BlockSpec(memory_space=pl.ANY)] * n_sources,
-        out_specs=pl.BlockSpec(memory_space=pltpu.VMEM),
-        scratch_shapes=[
-            pltpu.VMEM((token_count, width), jnp.bfloat16),
-            pltpu.VMEM((extra, block_length, width), jnp.bfloat16),
-            pltpu.VMEM((extra, block_length, width), jnp.bfloat16),
-            pltpu.SemaphoreType.DMA((2, extra + 1)),
-        ],
-        compiler_params=pltpu.CompilerParams(vmem_limit_bytes=48 * 1024 * 1024),
+        grid_spec=pltpu.PrefetchScalarGridSpec(
+            num_scalar_prefetch=1,
+            grid=(heads,),
+            in_specs=[column, column, per_head, per_head]
+            + [pl.BlockSpec(memory_space=pl.ANY)] * n_sources,
+            out_specs=column,
+            scratch_shapes=[
+                pltpu.VMEM((extra, block_length, width), jnp.bfloat16),
+                pltpu.VMEM((extra, block_length, width), jnp.bfloat16),
+                pltpu.SemaphoreType.DMA((2, extra)),
+            ],
+        ),
         cost_estimate=pl.CostEstimate(
             flops=4 * token_count * key_count * width,
             transcendentals=token_count * key_count * heads,
@@ -216,7 +210,9 @@
     step_spacing = col_count // DILATION_TILES
     me_col = lax.axis_index("col")
 
-    stacked = jnp.stack([dequant(key_mant, key_exp), dequant(value_mant, value_exp)])[:, :, 0]
+    keys = dequant(key_mant, key_exp)
+    values = dequant(value_mant, value_exp)
+    stacked = jnp.stack([keys, values])[:, :, 0]
 
     above = shift(stacked[:, tile_blocks - 1 :], "row", row_count, 1)
     below = shift(stacked[:, :1], "row", row_count, -1)
@@ -274,7 +270,9 @@
     ).reshape(-1)
     token_count = tile_blocks * block_length
     query_rows = queries.reshape(token_count, width)
-    partial = own_attend(query_rows, stacked)
+    partial = own_attend(
+        query_rows, keys.reshape(token_count, width), values.reshape(token_count, width)
+    )
     result = gather_attend(query_rows, partial, cycle_sources, far_sources, table)
     return result.reshape(queries.shape)
 

time: 157 us -> 159 us (1.013)
  local copies, waits for them, and re-layouts: 23.5 us -> 15.9 us
  starting transfers between devices: 29 us -> 35.4 us
  waiting for transfers between devices: 45.3 us -> 51 us
  Pallas kernels: 43.5 us -> 39.2 us
  other arithmetic: 14.2 us -> 16.9 us
    ppermute x3 -> x6, waiting for transfers between devices: 9.7 us -> 21.7 us  [ring_gather(): ahead = lax.ppermute(ahead, 'col', forward)]
    ppermute x3 -> x6, waiting for transfers between devices: 35.6 us -> 25.7 us  [ring_gather(): behind = lax.ppermute(behind, 'col', backward)]
    pallas_call x1, Pallas kernels: 30.1 us -> 25.7 us  [gather_attend(): pl.pallas_call(kernel, out_shape=jax.ShapeDtypeStruct((token_count, width...]
    ppermute x3 -> x6, starting transfers between devices: 5.81 us -> 9.58 us  [ring_gather(): behind = lax.ppermute(behind, 'col', backward)]
    ppermute x2, waiting for transfers between devices: 0.01 us -> 3.6 us  [the longest x1 3.59 us: ring_gather(): arrays.append(lax.ppermute(ahead, 'col', forward))]
    ppermute x3 -> x6, starting transfers between devices: 2.45 us -> 5.46 us  [ring_gather(): ahead = lax.ppermute(ahead, 'col', forward)]
    slice x2 -> x1, local copies, waits for them, and re-layouts: 3.56 us -> 0.95 us  [ring_gather(): ahead = behind = item[:, r:r + 1]]
    gather x1, local copies, waits for them, and re-layouts: 3.58 us -> 1.72 us  [per_device(): right_payload = jnp.take(stacked, to_right, axis=1)]
  transfers between devices with their start and end apart: 16 -> 22, of which waited for: 5 -> 5; matrix products, arithmetic and copies ran while one was open for 23% -> 19% of each run, Pallas kernels for 9% -> 8%
where the time goes in v6:
time: 159 us
  waiting for transfers between devices  51 us (32%)
  Pallas kernels  39.2 us (25%)
  starting transfers between devices  35.4 us (22%)
  other arithmetic  16.9 us (11%)
  local copies, waits for them, and re-layouts  15.9 us (10%)
    pallas_call x1, Pallas kernels, gather_attend(): pl.pallas_call(kernel, out_shape=jax.ShapeDtypeStruct((token_count, width...  25.7 us
    ppermute x6, waiting for transfers between devices, ring_gather(): behind = lax.ppermute(behind, 'col', backward)  25.7 us
    ppermute x6, waiting for transfers between devices, ring_gather(): ahead = lax.ppermute(ahead, 'col', forward)  21.7 us
    ppermute x6, starting transfers between devices, shift(): return lax.ppermute(x, axis, pairs)  15.9 us
    pallas_call x1, Pallas kernels, own_attend(): pl.pallas_call(own_attention_kernel, out_shape=(jax.ShapeDtypeStruct((tok...  13.4 us
    ppermute x6, starting transfers between devices, ring_gather(): behind = lax.ppermute(behind, 'col', backward)  9.58 us
    ppermute x6, starting transfers between devices, ring_gather(): ahead = lax.ppermute(ahead, 'col', forward)  5.46 us
    ppermute x1, waiting for transfers between devices, ring_gather(): arrays.append(lax.ppermute(ahead, 'col', forward))  3.59 us
  transfers between devices with their start and end apart: 22, of which 5 were waited for; matrix products, arithmetic and copies ran while one was open for 19% of the time, Pallas kernels for 8%

profile of v6, /device:TPU:0, one launch (start us, length us, event | category | flops | bytes accessed | tf_op | source)
XLA Modules:
  0.0 158.7 jit_solution(17448840002469345102)
XLA Ops:
  0.0 1.3 collective-permute-start.2
  1.3 6.0 %collective-permute-start.4 = (s32[4]{0:T(128)}, s32[4]{0:T(128)}, u32[]{:S(2)}, u32[]{:S(2)}) collective-permute-start(s32[4]{0:T(128)} %bitcast.96), channel_id=1, source_target_pairs={{0,2},{2,4},{4,6},{6,8},{8,10},{10,12},{12,14},{1,3},{3,5},{5,7},{... | collective-permute-start | bytes 56 | tf_op jit(solution)/shard_map/ppermute | solution.py:34
  7.3 1.0 exponential_bitcast_fusion.1
  8.3 1.0 exponential_bitcast_fusion
  9.3 1.8 %fusion.1 = bf16[8,1,64,1536]{3,2,0,1:T(8,128)(2,1)S(1)} fusion(bf16[8,1,64,1536]{3,2,1,0:T(8,128)(2,1)} %param.13, f32[8,2,1536]{2,1,0:T(2,128)S(1)} %exponential_bitcast_fusion.1), kind=kLoop, calls=%fused_computation.9 | loop fusion | flops 2359296 | bytes 3244032 | tf_op jit(solution)/shard_map/convert_element_type | solution.py:24
  11.1 0.3 fusion
  11.5 0.8 copy-done.2
  12.3 0.3 maximum_bitcast_fusion
  12.6 0.2 copy-done.3
  12.9 0.9 fusion.17
  13.9 1.6 collective-permute-start.8
  15.4 0.8 collective-permute-start.9
  16.3 0.8 fusion.16
  17.1 2.0 %collective-permute-start = (bf16[2,1,64,1536]{3,2,1,0:T(8,128)(2,1)}, bf16[2,1,64,1536]{3,2,1,0:T(8,128)(2,1)}, u32[]{:S(2)}, u32[]{:S(2)}) collective-permute-start(bf16[2,1,64,1536]{3,2,1,0:T(8,128)(2,1)} %get-tuple-element.15), channel_id=1, source_target_pairs={{0,1},{2,3},{4,5},{6,7},{8,9},{10,11},{12,13},{14,15},{16,17},{18,... | collective-permute-start | bytes 1179656 | tf_op jit(solution)/shard_map/ppermute | solution.py:34
  19.1 0.6 fusion.6
  19.7 0.6 gather_fusion
  20.4 0.6 dynamic_slice.3
  21.0 1.3 reduce-window.35
  22.3 1.4 reduce-window.34
  23.7 1.3 collective-permute-start.1
  24.9 0.6 compare_and_fusion.3
  25.6 0.2 reduce-window.36
  25.7 0.6 broadcast_add_fusion.1
  26.5 1.7 %gather_fusion.3 = bf16[3,2,64,1536]{3,2,1,0:T(8,128)(2,1)} fusion(bf16[2,8,64,1536]{3,2,1,0:T(8,128)(2,1)S(1)} %maximum_bitcast_fusion, s32[1024]{0:T(1024)S(1)} %pad_clamp_fusion.1), kind=kCustom, calls=%fused_computation.clone | custom fusion | bytes 2359308 | tf_op jit(solution)/shard_map/jit(_take)/gather | solution.py:227
  28.2 1.2 collective-permute-start.15
  29.4 0.6 compare_and_fusion.2
  30.0 0.7 reduce-window.37
  30.7 0.6 add_bitcast_fusion.2
  31.3 1.4 select_bitcast_fusion.1
  32.8 0.6 broadcast_add_fusion
  33.5 1.0 slice.48
  34.5 0.8 slice.50
  35.2 1.7 %gather_fusion.4 = bf16[3,2,64,1536]{3,2,1,0:T(8,128)(2,1)} fusion(bf16[2,8,64,1536]{3,2,1,0:T(8,128)(2,1)S(1)} %maximum_bitcast_fusion, s32[1024]{0:T(1024)S(1)} %pad_clamp_fusion), kind=kCustom, calls=%fused_computation.1.clone | custom fusion | bytes 2359308 | tf_op jit(solution)/shard_map/jit(_take)/gather | solution.py:228
  37.0 0.9 collective-permute-start.16
  37.9 0.7 collective-permute-start.6
  38.6 1.4 select_bitcast_fusion
  40.0 0.9 slice.49
  41.0 4.0 %collective-permute-start.3 = (bf16[2,2,64,1536]{3,2,0,1:T(8,128)(2,1)S(1)}, bf16[2,2,64,1536]{3,2,0,1:T(8,128)(2,1)S(1)}, u32[]{:S(2)}, u32[]{:S(2)}) collective-permute-start(bf16[2,2,64,1536]{3,2,0,1:T(8,128)(2,1)S(1)} %copy-done.5), channel_id=1, source_target_pairs={{0,2},{2,4},{4,6},{6,8},{8,10},{10,12},{12,14},{1,3},{3,5},{5,7},{... | collective-permute-start | bytes 2359304 | tf_op jit(solution)/shard_map/ppermute | solution.py:34
  45.0 1.3 collective-permute-start.5
  46.3 2.7 %collective-permute-start.10 = (bf16[2,1,64,1536]{3,2,1,0:T(8,128)(2,1)}, bf16[2,1,64,1536]{3,2,1,0:T(8,128)(2,1)}, u32[]{:S(2)}, u32[]{:S(2)}) collective-permute-start(bf16[2,1,64,1536]{3,2,1,0:T(8,128)(2,1)} %collective-permute-done.8.rest_6_), channel_id=1, source_target_pairs={{0,4},{4,8},{8,12},{12,14},{14,10},{10,6},{6,2},{2,0},{1,5},{5,9},... | collective-permute-start | bytes 1179656 | tf_op jit(solution)/shard_map/ppermute | solution.py:67
  49.0 0.3 collective-permute-start.11
  49.3 2.3 %collective-permute-start.18 = (bf16[2,1,64,1536]{3,2,1,0:T(8,128)(2,1)}, bf16[2,1,64,1536]{3,2,1,0:T(8,128)(2,1)}, u32[]{:S(2)}, u32[]{:S(2)}) collective-permute-start(bf16[2,1,64,1536]{3,2,1,0:T(8,128)(2,1)} %collective-permute-done.16.rest_14_), channel_id=1, source_target_pairs={{4,0},{8,4},{12,8},{14,12},{10,14},{6,10},{2,6},{0,2},{5,1},{9,5},... | collective-permute-start | bytes 1179656 | tf_op jit(solution)/shard_map/ppermute | solution.py:70
  51.7 0.6 fusion.15
  52.3 0.6 gather_fusion.2
  52.9 0.6 gather_fusion.1
  53.6 0.7 compare_select_fusion.13
  54.2 21.7 %collective-permute-done.10.rest_8_ = bf16[2,1,64,1536]{3,2,1,0:T(8,128)(2,1)} collective-permute-done((bf16[2,1,64,1536]{3,2,1,0:T(8,128)(2,1)}, bf16[2,1,64,1536]{3,2,1,0:T(8,128)(2,1)}, u32[]{:S(2)}, u32[]{:S(2)}) %collective-permute-start.10) | collective-permute-done | bytes 393248 | tf_op jit(solution)/shard_map/ppermute | solution.py:67
  76.0 13.0 %collective-permute-done.11.rest_9_ = bf16[2,1,64,1536]{3,2,1,0:T(8,128)(2,1)} collective-permute-done((bf16[2,1,64,1536]{3,2,1,0:T(8,128)(2,1)}, bf16[2,1,64,1536]{3,2,1,0:T(8,128)(2,1)}, u32[]{:S(2)}, u32[]{:S(2)}) %collective-permute-start.11) | collective-permute-done | bytes 393248 | tf_op jit(solution)/shard_map/ppermute | solution.py:70
  89.0 8.4 %collective-permute-done.18.rest_16_ = bf16[2,1,64,1536]{3,2,1,0:T(8,128)(2,1)} collective-permute-done((bf16[2,1,64,1536]{3,2,1,0:T(8,128)(2,1)}, bf16[2,1,64,1536]{3,2,1,0:T(8,128)(2,1)}, u32[]{:S(2)}, u32[]{:S(2)}) %collective-permute-start.18) | collective-permute-done | bytes 393248 | tf_op jit(solution)/shard_map/ppermute | solution.py:70
  97.4 2.5 %collective-permute-start.20 = (bf16[2,1,64,1536]{3,2,1,0:T(8,128)(2,1)}, bf16[2,1,64,1536]{3,2,1,0:T(8,128)(2,1)}, u32[]{:S(2)}, u32[]{:S(2)}) collective-permute-start(bf16[2,1,64,1536]{3,2,1,0:T(8,128)(2,1)} %collective-permute-done.18.rest_16_), channel_id=1, source_target_pairs={{4,0},{8,4},{12,8},{14,12},{10,14},{6,10},{2,6},{0,2},{5,1},{9,5},... | collective-permute-start | bytes 1179656 | tf_op jit(solution)/shard_map/ppermute | solution.py:70
  99.9 0.7 compare_select_fusion.11
  100.5 0.8 slice.51
  101.3 1.3 collective-permute-start.7
  102.6 2.7 %collective-permute-start.13 = (bf16[2,1,64,1536]{3,2,1,0:T(8,128)(2,1)}, bf16[2,1,64,1536]{3,2,1,0:T(8,128)(2,1)S(1)}, u32[]{:S(2)}, u32[]{:S(2)}) collective-permute-start(bf16[2,1,64,1536]{3,2,1,0:T(8,128)(2,1)} %collective-permute-done.11.rest_9_), channel_id=1, source_target_pairs={{4,0},{8,4},{12,8},{14,12},{10,14},{6,10},{2,6},{0,2},{5,1},{9,5},... | collective-permute-start | bytes 1179656 | tf_op jit(solution)/shard_map/ppermute | solution.py:70
  105.4 4.2 %collective-permute-done.20.rest_18_ = bf16[2,1,64,1536]{3,2,1,0:T(8,128)(2,1)} collective-permute-done((bf16[2,1,64,1536]{3,2,1,0:T(8,128)(2,1)}, bf16[2,1,64,1536]{3,2,1,0:T(8,128)(2,1)}, u32[]{:S(2)}, u32[]{:S(2)}) %collective-permute-start.20) | collective-permute-done | bytes 393248 | tf_op jit(solution)/shard_map/ppermute | solution.py:70
  109.6 2.5 %collective-permute-start.21 = (bf16[2,1,64,1536]{3,2,1,0:T(8,128)(2,1)}, bf16[2,1,64,1536]{3,2,1,0:T(8,128)(2,1)S(1)}, u32[]{:S(2)}, u32[]{:S(2)}) collective-permute-start(bf16[2,1,64,1536]{3,2,1,0:T(8,128)(2,1)} %collective-permute-done.20.rest_18_), channel_id=1, source_target_pairs={{4,0},{8,4},{12,8},{14,12},{10,14},{6,10},{2,6},{0,2},{5,1},{9,5},... | collective-permute-start | bytes 1179656 | tf_op jit(solution)/shard_map/ppermute | solution.py:64
  112.4 0.7 reshape.427.table_ref
  113.0 13.4 %shard_map.100 = (f32[512,1536]{1,0:T(8,128)}, f32[12,512,1]{2,1,0:T(8,128)}, f32[12,512,1]{2,1,0:T(8,128)}) custom-call(bf16[512,1536]{1,0:T(8,128)(2,1)} %bitcast.91, bf16[512,1536]{1,0:T(8,128)(2,1)} %bitcast.88, bf16[512,1536]{1,0:T(8,128)(2,1)} %bitcast.90), custom_call_target="tpu_custom_call" | custom-call | flops 1610612736 | bytes 7864320 | tf_op jit(solution)/shard_map/pallas_call | solution.py:98
  126.5 0.9 copy.30.rest_2_
  127.4 1.0 copy.31.rest_3_
  128.4 3.6 %collective-permute-done.14.rest_12_ = bf16[2,1,64,1536]{3,2,1,0:T(8,128)(2,1)S(1)} collective-permute-done((bf16[2,1,64,1536]{3,2,1,0:T(8,128)(2,1)}, bf16[2,1,64,1536]{3,2,1,0:T(8,128)(2,1)S(1)}, u32[]{:S(2)}, u32[]{:S(2)}) %collective-permute-start.14) | collective-permute-done | bytes 393248 | tf_op jit(solution)/shard_map/ppermute | solution.py:62
  132.0 0.7 copy-done.10
  132.8 0.2 copy-done.11
  132.9 25.7 %shard_map.101 = bf16[512,1536]{1,0:T(8,128)(2,1)} custom-call(s32[16]{0:T(128)} %reshape.427.table_ref, bf16[512,1536]{1,0:T(8,128)(2,1)} %bitcast.92, f32[512,1536]{1,0:T(8,128)} %get-tuple-element.9.acc_ref, f32[12,512,1]{2,1,0:T(8,128)} %get-tuple-element.10.max_ref, f32[12,512,1]{2,1,0:T(8,128)} %get-tuple-element.11.total_ref, ...), custom_call_target="tpu_custom_call" | custom-call | flops 1610612736 | bytes 9437184 | tf_op jit(solution)/shard_map/pallas_call | solution.py:180
  (65 shorter events, 0.8 us)
Async XLA Ops:
  0.0 23.7 %collective-permute-start.2 = (s32[4]{0:T(128)}, s32[4]{0:T(128)}, u32[]{:S(2)}, u32[]{:S(2)}) collective-permute-start(s32[4]{0:T(128)} %bitcast.95), channel_id=1, source_target_pairs={{2,0},{4,2},{6,4},{8,6},{10,8},{12,10},{14,12},{3,1},{5,3},{7,5},{... | collective-permute-start | bytes 56 | tf_op jit(solution)/shard_map/ppermute | solution.py:34
  1.3 26.9 %collective-permute-start.4 = (s32[4]{0:T(128)}, s32[4]{0:T(128)}, u32[]{:S(2)}, u32[]{:S(2)}) collective-permute-start(s32[4]{0:T(128)} %bitcast.96), channel_id=1, source_target_pairs={{0,2},{2,4},{4,6},{6,8},{8,10},{10,12},{12,14},{1,3},{3,5},{5,7},{... | collective-permute-start | bytes 56 | tf_op jit(solution)/shard_map/ppermute | solution.py:34
  9.3 1.9 %copy-start.4 = (bf16[8,1,64,1536]{3,2,1,0:T(8,128)(2,1)S(1)}, bf16[8,1,64,1536]{3,2,1,0:T(8,128)(2,1)}, u32[]{:S(2)}) copy-start(bf16[8,1,64,1536]{3,2,1,0:T(8,128)(2,1)} %param.15) | copy-start | bytes 4718596
  11.1 1.1 copy-start.2
  11.4 1.4 copy-start.3
  12.9 6.2 %copy-start.12 = (s32[1,1,4]{2,1,0:T(1,128)S(1)}, s32[1,1,4]{2,1,0:T(1,128)}, u32[]{:S(2)}) copy-start(s32[1,1,4]{2,1,0:T(1,128)} %param.17) | copy-start | bytes 52
  12.9 6.8 %copy-start.13 = (s32[1,1,4]{2,1,0:T(1,128)S(1)}, s32[1,1,4]{2,1,0:T(1,128)}, u32[]{:S(2)}) copy-start(s32[1,1,4]{2,1,0:T(1,128)} %param.18) | copy-start | bytes 52
  12.9 6.8 %copy-start = (s32[8]{0:T(128)S(1)}, s32[8]{0:T(128)}, u32[]{:S(2)}) copy-start(s32[8]{0:T(128)} %constant.99.clone) | copy-start | bytes 100
  13.9 27.1 %collective-permute-start.8 = (bf16[2,1,64,1536]{3,2,1,0:T(8,128)(2,1)}, bf16[2,1,64,1536]{3,2,1,0:T(8,128)(2,1)}, u32[]{:S(2)}, u32[]{:S(2)}) collective-permute-start(bf16[2,1,64,1536]{3,2,1,0:T(8,128)(2,1)} %get-tuple-element.17), channel_id=1, source_target_pairs={{0,4},{4,8},{8,12},{12,14},{14,10},{10,6},{6,2},{2,0},{1,5},{5,9},... | collective-permute-start | bytes 1179656 | tf_op jit(solution)/shard_map/ppermute | solution.py:67
  15.4 29.6 %collective-permute-start.9 = (bf16[2,1,64,1536]{3,2,1,0:T(8,128)(2,1)}, bf16[2,1,64,1536]{3,2,1,0:T(8,128)(2,1)}, u32[]{:S(2)}, u32[]{:S(2)}) collective-permute-start(bf16[2,1,64,1536]{3,2,1,0:T(8,128)(2,1)} %get-tuple-element.17), channel_id=1, source_target_pairs={{4,0},{8,4},{12,8},{14,12},{10,14},{6,10},{2,6},{0,2},{5,1},{9,5},... | collective-permute-start | bytes 1179656 | tf_op jit(solution)/shard_map/ppermute | solution.py:70
  17.1 19.9 %collective-permute-start = (bf16[2,1,64,1536]{3,2,1,0:T(8,128)(2,1)}, bf16[2,1,64,1536]{3,2,1,0:T(8,128)(2,1)}, u32[]{:S(2)}, u32[]{:S(2)}) collective-permute-start(bf16[2,1,64,1536]{3,2,1,0:T(8,128)(2,1)} %get-tuple-element.15), channel_id=1, source_target_pairs={{0,1},{2,3},{4,5},{6,7},{8,9},{10,11},{12,13},{14,15},{16,17},{18,... | collective-permute-start | bytes 1179656 | tf_op jit(solution)/shard_map/ppermute | solution.py:34
  23.7 14.2 %collective-permute-start.1 = (bf16[2,1,64,1536]{3,2,1,0:T(8,128)(2,1)S(1)}, bf16[2,1,64,1536]{3,2,1,0:T(8,128)(2,1)}, u32[]{:S(2)}, u32[]{:S(2)}) collective-permute-start(bf16[2,1,64,1536]{3,2,1,0:T(8,128)(2,1)S(1)} %get-tuple-element.14), channel_id=1, source_target_pairs={{1,0},{3,2},{5,4},{7,6},{9,8},{11,10},{13,12},{15,14},{17,16},{19,... | collective-permute-start | bytes 1179656 | tf_op jit(solution)/shard_map/ppermute | solution.py:34
  28.2 18.1 %collective-permute-start.15 = (bf16[2,1,64,1536]{3,2,1,0:T(8,128)(2,1)}, bf16[2,1,64,1536]{3,2,1,0:T(8,128)(2,1)}, u32[]{:S(2)}, u32[]{:S(2)}) collective-permute-start(bf16[2,1,64,1536]{3,2,1,0:T(8,128)(2,1)} %get-tuple-element.16), channel_id=1, source_target_pairs={{0,4},{4,8},{8,12},{12,14},{14,10},{10,6},{6,2},{2,0},{1,5},{5,9},... | collective-permute-start | bytes 1179656 | tf_op jit(solution)/shard_map/ppermute | solution.py:67
  37.0 4.0 %copy-start.5 = (bf16[2,2,64,1536]{3,2,0,1:T(8,128)(2,1)S(1)}, bf16[2,2,64,1536]{3,2,0,1:T(8,128)(2,1)}, u32[]{:S(2)}) copy-start(bf16[2,2,64,1536]{3,2,0,1:T(8,128)(2,1)} %slice.48) | copy-start | bytes 2359300
  37.0 14.7 %copy-start.14 = (s32[1,1,4]{2,1,0:T(1,128)S(1)}, s32[1,1,4]{2,1,0:T(1,128)}, u32[]{:S(2)}) copy-start(s32[1,1,4]{2,1,0:T(1,128)} %param.18) | copy-start | bytes 52
  37.0 12.0 %collective-permute-start.16 = (bf16[2,1,64,1536]{3,2,1,0:T(8,128)(2,1)}, bf16[2,1,64,1536]{3,2,1,0:T(8,128)(2,1)}, u32[]{:S(2)}, u32[]{:S(2)}) collective-permute-start(bf16[2,1,64,1536]{3,2,1,0:T(8,128)(2,1)} %get-tuple-element.16), channel_id=1, source_target_pairs={{4,0},{8,4},{12,8},{14,12},{10,14},{6,10},{2,6},{0,2},{5,1},{9,5},... | collective-permute-start | bytes 1179656 | tf_op jit(solution)/shard_map/ppermute | solution.py:70
  37.9 11.4 %collective-permute-start.6 = (bf16[2,1,64,1536]{3,2,0,1:T(8,128)(2,1)}, bf16[2,1,64,1536]{3,2,0,1:T(8,128)(2,1)S(1)}, u32[]{:S(2)}, u32[]{:S(2)}) collective-permute-start(bf16[2,1,64,1536]{3,2,0,1:T(8,128)(2,1)} %slice.50), channel_id=1, source_target_pairs={{12,14},{13,15},{28,30},{29,31}} | collective-permute-start | bytes 1179656 | tf_op jit(solution)/shard_map/ppermute | solution.py:234
  40.0 12.9 %copy-start.1 = (s32[7,2]{1,0:T(8,128)S(1)}, s32[7,2]{1,0:T(8,128)}, u32[]{:S(2)}) copy-start(s32[7,2]{1,0:T(8,128)} %constant.100.clone) | copy-start | bytes 172
  41.0 61.6 %collective-permute-start.3 = (bf16[2,2,64,1536]{3,2,0,1:T(8,128)(2,1)S(1)}, bf16[2,2,64,1536]{3,2,0,1:T(8,128)(2,1)S(1)}, u32[]{:S(2)}, u32[]{:S(2)}) collective-permute-start(bf16[2,2,64,1536]{3,2,0,1:T(8,128)(2,1)S(1)} %copy-done.5), channel_id=1, source_target_pairs={{0,2},{2,4},{4,6},{6,8},{8,10},{10,12},{12,14},{1,3},{3,5},{5,7},{... | collective-permute-start | bytes 2359304 | tf_op jit(solution)/shard_map/ppermute | solution.py:34
  45.0 60.4 %collective-permute-start.5 = (bf16[2,2,64,1536]{3,2,0,1:T(8,128)(2,1)}, bf16[2,2,64,1536]{3,2,0,1:T(8,128)(2,1)S(1)}, u32[]{:S(2)}, u32[]{:S(2)}) collective-permute-start(bf16[2,2,64,1536]{3,2,0,1:T(8,128)(2,1)} %slice.49), channel_id=1, source_target_pairs={{2,0},{4,2},{6,4},{8,6},{10,8},{12,10},{14,12},{3,1},{5,3},{7,5},{... | collective-permute-start | bytes 2359304 | tf_op jit(solution)/shard_map/ppermute | solution.py:34
  46.3 29.7 %collective-permute-start.10 = (bf16[2,1,64,1536]{3,2,1,0:T(8,128)(2,1)}, bf16[2,1,64,1536]{3,2,1,0:T(8,128)(2,1)}, u32[]{:S(2)}, u32[]{:S(2)}) collective-permute-start(bf16[2,1,64,1536]{3,2,1,0:T(8,128)(2,1)} %collective-permute-done.8.rest_6_), channel_id=1, source_target_pairs={{0,4},{4,8},{8,12},{12,14},{14,10},{10,6},{6,2},{2,0},{1,5},{5,9},... | collective-permute-start | bytes 1179656 | tf_op jit(solution)/shard_map/ppermute | solution.py:67
  49.0 40.0 %collective-permute-start.11 = (bf16[2,1,64,1536]{3,2,1,0:T(8,128)(2,1)}, bf16[2,1,64,1536]{3,2,1,0:T(8,128)(2,1)}, u32[]{:S(2)}, u32[]{:S(2)}) collective-permute-start(bf16[2,1,64,1536]{3,2,1,0:T(8,128)(2,1)} %collective-permute-done.9.rest_7_), channel_id=1, source_target_pairs={{4,0},{8,4},{12,8},{14,12},{10,14},{6,10},{2,6},{0,2},{5,1},{9,5},... | collective-permute-start | bytes 1179656 | tf_op jit(solution)/shard_map/ppermute | solution.py:70
  49.3 2.3 %copy-start.6 = (bf16[2,1,64,1536]{3,2,0,1:T(8,128)(2,1)}, bf16[2,1,64,1536]{3,2,0,1:T(8,128)(2,1)S(1)}, u32[]{:S(2)}) copy-start(bf16[2,1,64,1536]{3,2,0,1:T(8,128)(2,1)S(1)} %collective-permute-done.6) | copy-start | bytes 1179652
  49.3 48.1 %collective-permute-start.18 = (bf16[2,1,64,1536]{3,2,1,0:T(8,128)(2,1)}, bf16[2,1,64,1536]{3,2,1,0:T(8,128)(2,1)}, u32[]{:S(2)}, u32[]{:S(2)}) collective-permute-start(bf16[2,1,64,1536]{3,2,1,0:T(8,128)(2,1)} %collective-permute-done.16.rest_14_), channel_id=1, source_target_pairs={{4,0},{8,4},{12,8},{14,12},{10,14},{6,10},{2,6},{0,2},{5,1},{9,5},... | collective-permute-start | bytes 1179656 | tf_op jit(solution)/shard_map/ppermute | solution.py:70
  76.0 25.4 %collective-permute-start.17 = (bf16[2,1,64,1536]{3,2,1,0:T(8,128)(2,1)}, bf16[2,1,64,1536]{3,2,1,0:T(8,128)(2,1)}, u32[]{:S(2)}, u32[]{:S(2)}) collective-permute-start(bf16[2,1,64,1536]{3,2,1,0:T(8,128)(2,1)} %collective-permute-done.15.rest_13_), channel_id=1, source_target_pairs={{0,4},{4,8},{8,12},{12,14},{14,10},{10,6},{6,2},{2,0},{1,5},{5,9},... | collective-permute-start | bytes 1179656 | tf_op jit(solution)/shard_map/ppermute | solution.py:67
  89.0 16.4 %collective-permute-start.12 = (bf16[2,1,64,1536]{3,2,1,0:T(8,128)(2,1)}, bf16[2,1,64,1536]{3,2,1,0:T(8,128)(2,1)}, u32[]{:S(2)}, u32[]{:S(2)}) collective-permute-start(bf16[2,1,64,1536]{3,2,1,0:T(8,128)(2,1)} %collective-permute-done.10.rest_8_), channel_id=1, source_target_pairs={{0,4},{4,8},{8,12},{12,14},{14,10},{10,6},{6,2},{2,0},{1,5},{5,9},... | collective-permute-start | bytes 1179656 | tf_op jit(solution)/shard_map/ppermute | solution.py:67
  97.4 12.3 %collective-permute-start.20 = (bf16[2,1,64,1536]{3,2,1,0:T(8,128)(2,1)}, bf16[2,1,64,1536]{3,2,1,0:T(8,128)(2,1)}, u32[]{:S(2)}, u32[]{:S(2)}) collective-permute-start(bf16[2,1,64,1536]{3,2,1,0:T(8,128)(2,1)} %collective-permute-done.18.rest_16_), channel_id=1, source_target_pairs={{4,0},{8,4},{12,8},{14,12},{10,14},{6,10},{2,6},{0,2},{5,1},{9,5},... | collective-permute-start | bytes 1179656 | tf_op jit(solution)/shard_map/ppermute | solution.py:70
  101.3 27.1 %collective-permute-start.7 = (bf16[2,1,64,1536]{3,2,0,1:T(8,128)(2,1)}, bf16[2,1,64,1536]{3,2,0,1:T(8,128)(2,1)S(1)}, u32[]{:S(2)}, u32[]{:S(2)}) collective-permute-start(bf16[2,1,64,1536]{3,2,0,1:T(8,128)(2,1)} %slice.51), channel_id=1, source_target_pairs={{2,0},{3,1},{18,16},{19,17}} | collective-permute-start | bytes 1179656 | tf_op jit(solution)/shard_map/ppermute | solution.py:235
  102.6 25.8 %collective-permute-start.13 = (bf16[2,1,64,1536]{3,2,1,0:T(8,128)(2,1)}, bf16[2,1,64,1536]{3,2,1,0:T(8,128)(2,1)S(1)}, u32[]{:S(2)}, u32[]{:S(2)}) collective-permute-start(bf16[2,1,64,1536]{3,2,1,0:T(8,128)(2,1)} %collective-permute-done.11.rest_9_), channel_id=1, source_target_pairs={{4,0},{8,4},{12,8},{14,12},{10,14},{6,10},{2,6},{0,2},{5,1},{9,5},... | collective-permute-start | bytes 1179656 | tf_op jit(solution)/shard_map/ppermute | solution.py:70
  105.3 23.1 %collective-permute-start.19 = (bf16[2,1,64,1536]{3,2,1,0:T(8,128)(2,1)}, bf16[2,1,64,1536]{3,2,1,0:T(8,128)(2,1)S(1)}, u32[]{:S(2)}, u32[]{:S(2)}) collective-permute-start(bf16[2,1,64,1536]{3,2,1,0:T(8,128)(2,1)} %collective-permute-done.17.rest_15_), channel_id=1, source_target_pairs={{0,4},{4,8},{8,12},{12,14},{14,10},{10,6},{6,2},{2,0},{1,5},{5,9},... | collective-permute-start | bytes 1179656 | tf_op jit(solution)/shard_map/ppermute | solution.py:67
  105.3 26.7 %collective-permute-start.14 = (bf16[2,1,64,1536]{3,2,1,0:T(8,128)(2,1)}, bf16[2,1,64,1536]{3,2,1,0:T(8,128)(2,1)S(1)}, u32[]{:S(2)}, u32[]{:S(2)}) collective-permute-start(bf16[2,1,64,1536]{3,2,1,0:T(8,128)(2,1)} %collective-permute-done.12.rest_10_), channel_id=1, source_target_pairs={{0,4},{4,8},{8,12},{12,14},{14,10},{10,6},{6,2},{2,0},{1,5},{5,9},... | collective-permute-start | bytes 1179656 | tf_op jit(solution)/shard_map/ppermute | solution.py:62
  109.6 22.4 %collective-permute-start.21 = (bf16[2,1,64,1536]{3,2,1,0:T(8,128)(2,1)}, bf16[2,1,64,1536]{3,2,1,0:T(8,128)(2,1)S(1)}, u32[]{:S(2)}, u32[]{:S(2)}) collective-permute-start(bf16[2,1,64,1536]{3,2,1,0:T(8,128)(2,1)} %collective-permute-done.20.rest_18_), channel_id=1, source_target_pairs={{4,0},{8,4},{12,8},{14,12},{10,14},{6,10},{2,6},{0,2},{5,1},{9,5},... | collective-permute-start | bytes 1179656 | tf_op jit(solution)/shard_map/ppermute | solution.py:64
  128.4 3.6 %copy-start.7 = (bf16[2,1,64,1536]{3,2,0,1:T(8,128)(2,1)}, bf16[2,1,64,1536]{3,2,0,1:T(8,128)(2,1)S(1)}, u32[]{:S(2)}) copy-start(bf16[2,1,64,1536]{3,2,0,1:T(8,128)(2,1)S(1)} %collective-permute-done.7) | copy-start | bytes 1179652
  128.4 3.6 %copy-start.8 = (bf16[2,1,64,1536]{3,2,1,0:T(8,128)(2,1)}, bf16[2,1,64,1536]{3,2,1,0:T(8,128)(2,1)S(1)}, u32[]{:S(2)}) copy-start(bf16[2,1,64,1536]{3,2,1,0:T(8,128)(2,1)S(1)} %collective-permute-done.13.rest_11_) | copy-start | bytes 1179652
  128.4 3.6 %copy-start.9 = (bf16[2,1,64,1536]{3,2,1,0:T(8,128)(2,1)}, bf16[2,1,64,1536]{3,2,1,0:T(8,128)(2,1)S(1)}, u32[]{:S(2)}) copy-start(bf16[2,1,64,1536]{3,2,1,0:T(8,128)(2,1)S(1)} %collective-permute-done.19.rest_17_) | copy-start | bytes 1179652
  132.0 0.7 copy-start.10
  132.0 0.9 copy-start.11

commit v7 on v5

--- a/solution.py
+++ b/solution.py
@@ -112,8 +112,8 @@
 
     key_count = k_vmem.shape[0] * block_length
 
-    def head(h, carry):
-        lanes = pl.ds(pl.multiple_of(h * HEAD_DIM, HEAD_DIM), HEAD_DIM)
+    for h in range(heads):
+        lanes = pl.ds(h * HEAD_DIM, HEAD_DIM)
         q = q_vmem[:, lanes]
         k = k_vmem[:, :, lanes].reshape(key_count, HEAD_DIM)
         v = v_vmem[:, :, lanes].reshape(key_count, HEAD_DIM)
@@ -126,9 +126,6 @@
         rounded = weights.astype(jnp.bfloat16)
         blended = jnp.dot(rounded, v, preferred_element_type=jnp.float32)
         o_ref[:, lanes] = (blended / row_total).astype(o_ref.dtype)
-        return carry
-
-    lax.fori_loop(0, heads, head, 0)
 
 
 def gather_attend(query_rows, own, cycle_list_sources, far_list_sources, table):

time: 145 us -> 136 us (0.938)
  Pallas kernels: 24 us -> 14.2 us
    pallas_call x1, Pallas kernels: 24 us -> 14.2 us  [gather_attend(): pl.pallas_call(kernel, out_shape=jax.ShapeDtypeStruct((token_count, width...]
  transfers between devices with their start and end apart: 22 -> 22, of which waited for: 6 -> 6; matrix products, arithmetic and copies ran while one was open for 22% -> 23% of each run, Pallas kernels for 0% -> 0%
where the time goes in v7:
time: 136 us; the launch traced here: 135 us
  waiting for transfers between devices  50.6 us (37%)
  starting transfers between devices  37.9 us (28%)
  local copies, waits for them, and re-layouts  19.8 us (15%)
  Pallas kernels  14.2 us (10%)
  other arithmetic  12.1 us (9%)
    ppermute x6, waiting for transfers between devices, ring_gather(): behind = lax.ppermute(behind, 'col', backward)  42.3 us
    ppermute x6, starting transfers between devices, shift(): return lax.ppermute(x, axis, pairs)  17.9 us
    pallas_call x1, Pallas kernels, gather_attend(): pl.pallas_call(kernel, out_shape=jax.ShapeDtypeStruct((token_count, width...  14.2 us
    ppermute x6, starting transfers between devices, ring_gather(): behind = lax.ppermute(behind, 'col', backward)  10.8 us
    ppermute x1, waiting for transfers between devices, ring_gather(): arrays.append(lax.ppermute(behind, 'col', backward))  7.49 us
    ppermute x2, local copies, waits for them, and re-layouts, shift(): return lax.ppermute(x, axis, pairs)  4.15 us
    ppermute x6, starting transfers between devices, ring_gather(): ahead = lax.ppermute(ahead, 'col', forward)  3.96 us
    gather x1, local copies, waits for them, and re-layouts, per_device(): right_payload = jnp.take(stacked, to_right, axis=1)  3.56 us
  transfers between devices with their start and end apart: 22, of which 6 were waited for; matrix products, arithmetic and copies ran while one was open for 23% of the time, Pallas kernels for 0%

profile of v7, /device:TPU:0, one launch (start us, length us, event | category | flops | bytes accessed | tf_op | source)
XLA Modules:
  0.0 135.2 jit_solution(4218880298923434039)
XLA Ops:
  0.0 4.9 %collective-permute-start.4 = (s32[4]{0:T(128)}, s32[4]{0:T(128)S(1)}, u32[]{:S(2)}, u32[]{:S(2)}) collective-permute-start(s32[4]{0:T(128)} %bitcast.89), channel_id=1, source_target_pairs={{0,2},{2,4},{4,6},{6,8},{8,10},{10,12},{12,14},{1,3},{3,5},{5,7},{... | collective-permute-start | bytes 56 | tf_op jit(solution)/shard_map/ppermute | solution.py:34
  4.9 1.3 collective-permute-start.2
  6.2 1.0 exponential_bitcast_fusion.1
  7.1 1.0 exponential_bitcast_fusion
  8.1 1.8 %fusion = bf16[8,1,64,1536]{3,2,0,1:T(8,128)(2,1)S(1)} fusion(bf16[8,1,64,1536]{3,2,1,0:T(8,128)(2,1)} %param.15, f32[8,2,1536]{2,1,0:T(2,128)S(1)} %exponential_bitcast_fusion), kind=kLoop, calls=%fused_computation.7 | loop fusion | flops 2359296 | bytes 3244032 | tf_op jit(solution)/shard_map/convert_element_type | solution.py:24
  9.9 0.1 copy-done.4
  10.0 0.3 fusion.1
  10.3 0.3 maximum_bitcast_fusion.own_hbm
  10.6 0.1 slice.33
  10.7 0.8 fusion.17
  11.5 2.6 %collective-permute-start.16 = (bf16[2,1,64,1536]{3,2,1,0:T(8,128)(2,1)}, bf16[2,1,64,1536]{3,2,1,0:T(8,128)(2,1)S(1)}, u32[]{:S(2)}, u32[]{:S(2)}) collective-permute-start(bf16[2,1,64,1536]{3,2,1,0:T(8,128)(2,1)} %get-tuple-element.10), channel_id=1, source_target_pairs={{4,0},{8,4},{12,8},{14,12},{10,14},{6,10},{2,6},{0,2},{5,1},{9,5},... | collective-permute-start | bytes 1179656 | tf_op jit(solution)/shard_map/ppermute | solution.py:70
  14.2 1.0 collective-permute-start.15
  15.1 1.1 collective-permute-start.9
  16.2 1.0 fusion.16
  17.2 0.6 dynamic_slice.3
  17.8 0.6 gather_fusion
  18.5 1.0 collective-permute-start.8
  19.5 0.2 reduce-window.37
  19.7 0.1 select_reduce_fusion
  19.8 1.3 collective-permute-start.1
  21.1 0.2 reduce-window.36
  21.3 0.5 add_bitcast_fusion.3
  21.9 2.5 %gather_fusion.4 = bf16[3,2,64,1536]{3,2,1,0:T(8,128)(2,1)S(1)} fusion(bf16[2,8,64,1536]{3,2,1,0:T(8,128)(2,1)} %copy-done.2, s32[1024]{0:T(1024)S(1)} %pad_clamp_fusion), kind=kCustom, calls=%fused_computation.1.clone | custom fusion | bytes 2359308 | tf_op jit(solution)/shard_map/jit(_take)/gather | solution.py:186
  24.4 0.2 select_bitcast_fusion
  24.6 0.5 copy-done.10
  25.0 0.1 select_reduce_fusion.1
  25.2 0.8 slice.51
  25.9 0.9 slice.49
  26.9 3.6 %gather_fusion.3 = bf16[3,2,64,1536]{3,2,1,0:T(8,128)(2,1)} fusion(bf16[2,8,64,1536]{3,2,1,0:T(8,128)(2,1)} %copy-done.2, s32[1024]{0:T(1024)S(1)} %pad_clamp_fusion.1), kind=kCustom, calls=%fused_computation.clone | custom fusion | bytes 2359308 | tf_op jit(solution)/shard_map/jit(_take)/gather | solution.py:185
  30.5 3.1 %collective-permute-start = (bf16[2,1,64,1536]{3,2,1,0:T(8,128)(2,1)}, bf16[2,1,64,1536]{3,2,1,0:T(8,128)(2,1)S(1)}, u32[]{:S(2)}, u32[]{:S(2)}) collective-permute-start(bf16[2,1,64,1536]{3,2,1,0:T(8,128)(2,1)} %get-tuple-element.9), channel_id=1, source_target_pairs={{0,1},{2,3},{4,5},{6,7},{8,9},{10,11},{12,13},{14,15},{16,17},{18,... | collective-permute-start | bytes 1179656 | tf_op jit(solution)/shard_map/ppermute | solution.py:34
  33.6 1.3 collective-permute-start.7
  34.9 1.5 %select_bitcast_fusion.1 = bf16[2,3,64,1536]{3,2,0,1:T(8,128)(2,1)S(1)} fusion(bf16[3,2,64,1536]{3,2,1,0:T(8,128)(2,1)} %gather_fusion.3, pred[3]{0:T(512)(128)(4,1)S(1)} %compare_and_fusion.1), kind=kLoop, calls=%fused_computation.11 | loop fusion | flops 589824 | bytes 2359299 | tf_op jit(solution)/shard_map/jit(_take)/select_n | solution.py:185
  36.3 1.0 slice.48
  37.4 1.3 collective-permute-start.5
  38.7 6.1 %collective-permute-start.3 = (bf16[2,2,64,1536]{3,2,0,1:T(8,128)(2,1)}, bf16[2,2,64,1536]{3,2,0,1:T(8,128)(2,1)}, u32[]{:S(2)}, u32[]{:S(2)}) collective-permute-start(bf16[2,2,64,1536]{3,2,0,1:T(8,128)(2,1)} %slice.48), channel_id=1, source_target_pairs={{0,2},{2,4},{4,6},{6,8},{8,10},{10,12},{12,14},{1,3},{3,5},{5,7},{... | collective-permute-start | bytes 2359304 | tf_op jit(solution)/shard_map/ppermute | solution.py:34
  44.8 2.1 %collective-permute-start.18 = (bf16[2,1,64,1536]{3,2,1,0:T(8,128)(2,1)S(1)}, bf16[2,1,64,1536]{3,2,1,0:T(8,128)(2,1)S(1)}, u32[]{:S(2)}, u32[]{:S(2)}) collective-permute-start(bf16[2,1,64,1536]{3,2,1,0:T(8,128)(2,1)S(1)} %collective-permute-done.16.rest_14_), channel_id=1, source_target_pairs={{4,0},{8,4},{12,8},{14,12},{10,14},{6,10},{2,6},{0,2},{5,1},{9,5},... | collective-permute-start | bytes 1179656 | tf_op jit(solution)/shard_map/ppermute | solution.py:70
  46.9 0.9 collective-permute-done.7
  47.7 0.6 fusion.15
  48.4 0.6 gather_fusion.1
  49.0 0.5 fusion.6
  49.5 34.8 %collective-permute-done.18.rest_16_ = bf16[2,1,64,1536]{3,2,1,0:T(8,128)(2,1)S(1)} collective-permute-done((bf16[2,1,64,1536]{3,2,1,0:T(8,128)(2,1)S(1)}, bf16[2,1,64,1536]{3,2,1,0:T(8,128)(2,1)S(1)}, u32[]{:S(2)}, u32[]{:S(2)}) %collective-permute-start.18) | collective-permute-done | bytes 393248 | tf_op jit(solution)/shard_map/ppermute | solution.py:70
  84.4 2.5 %collective-permute-start.11 = (bf16[2,1,64,1536]{3,2,1,0:T(8,128)(2,1)S(1)}, bf16[2,1,64,1536]{3,2,1,0:T(8,128)(2,1)}, u32[]{:S(2)}, u32[]{:S(2)}) collective-permute-start(bf16[2,1,64,1536]{3,2,1,0:T(8,128)(2,1)S(1)} %collective-permute-done.9.rest_7_), channel_id=1, source_target_pairs={{4,0},{8,4},{12,8},{14,12},{10,14},{6,10},{2,6},{0,2},{5,1},{9,5},... | collective-permute-start | bytes 1179656 | tf_op jit(solution)/shard_map/ppermute | solution.py:70
  86.9 0.0 collective-permute-start.20
  86.9 2.0 %collective-permute-start.12 = (bf16[2,1,64,1536]{3,2,1,0:T(8,128)(2,1)}, bf16[2,1,64,1536]{3,2,1,0:T(8,128)(2,1)}, u32[]{:S(2)}, u32[]{:S(2)}) collective-permute-start(bf16[2,1,64,1536]{3,2,1,0:T(8,128)(2,1)} %collective-permute-done.10.rest_8_), channel_id=1, source_target_pairs={{0,4},{4,8},{8,12},{12,14},{14,10},{10,6},{6,2},{2,0},{1,5},{5,9},... | collective-permute-start | bytes 1179656 | tf_op jit(solution)/shard_map/ppermute | solution.py:67
  88.9 0.5 broadcast_add_fusion.2
  89.4 1.3 reduce-window.34
  90.6 0.7 reduce-window.35
  91.3 0.6 gather_fusion.2
  91.9 0.6 compare_select_fusion.13
  92.6 0.6 add_bitcast_fusion
  93.2 1.8 %slice.50 = bf16[2,1,64,1536]{3,2,0,1:T(8,128)(2,1)} slice(bf16[2,3,64,1536]{3,2,0,1:T(8,128)(2,1)} %copy-done.3), slice={[0:2], [2:3], [0:64], [0:1536]} | slice | bytes 786432 | tf_op jit(solution)/shard_map/slice | solution.py:192
  95.0 1.5 %collective-permute-done.11.rest_9_ = bf16[2,1,64,1536]{3,2,1,0:T(8,128)(2,1)} collective-permute-done((bf16[2,1,64,1536]{3,2,1,0:T(8,128)(2,1)S(1)}, bf16[2,1,64,1536]{3,2,1,0:T(8,128)(2,1)}, u32[]{:S(2)}, u32[]{:S(2)}) %collective-permute-start.11) | collective-permute-done | bytes 393248 | tf_op jit(solution)/shard_map/ppermute | solution.py:70
  96.4 1.4 %collective-permute-start.6 = (bf16[2,1,64,1536]{3,2,0,1:T(8,128)(2,1)}, bf16[2,1,64,1536]{3,2,0,1:T(8,128)(2,1)}, u32[]{:S(2)}, u32[]{:S(2)}) collective-permute-start(bf16[2,1,64,1536]{3,2,0,1:T(8,128)(2,1)} %slice.50), channel_id=1, source_target_pairs={{12,14},{13,15},{28,30},{29,31}} | collective-permute-start | bytes 1179656 | tf_op jit(solution)/shard_map/ppermute | solution.py:192
  97.9 2.5 %collective-permute-start.13 = (bf16[2,1,64,1536]{3,2,1,0:T(8,128)(2,1)}, bf16[2,1,64,1536]{3,2,1,0:T(8,128)(2,1)}, u32[]{:S(2)}, u32[]{:S(2)}) collective-permute-start(bf16[2,1,64,1536]{3,2,1,0:T(8,128)(2,1)} %collective-permute-done.11.rest_9_), channel_id=1, source_target_pairs={{4,0},{8,4},{12,8},{14,12},{10,14},{6,10},{2,6},{0,2},{5,1},{9,5},... | collective-permute-start | bytes 1179656 | tf_op jit(solution)/shard_map/ppermute | solution.py:70
  100.4 4.4 %collective-permute-done.20.rest_18_ = bf16[2,1,64,1536]{3,2,1,0:T(8,128)(2,1)} collective-permute-done((bf16[2,1,64,1536]{3,2,1,0:T(8,128)(2,1)S(1)}, bf16[2,1,64,1536]{3,2,1,0:T(8,128)(2,1)}, u32[]{:S(2)}, u32[]{:S(2)}) %collective-permute-start.20) | collective-permute-done | bytes 393248 | tf_op jit(solution)/shard_map/ppermute | solution.py:70
  104.9 2.5 %collective-permute-start.21 = (bf16[2,1,64,1536]{3,2,1,0:T(8,128)(2,1)}, bf16[2,1,64,1536]{3,2,1,0:T(8,128)(2,1)}, u32[]{:S(2)}, u32[]{:S(2)}) collective-permute-start(bf16[2,1,64,1536]{3,2,1,0:T(8,128)(2,1)} %collective-permute-done.20.rest_18_), channel_id=1, source_target_pairs={{4,0},{8,4},{12,8},{14,12},{10,14},{6,10},{2,6},{0,2},{5,1},{9,5},... | collective-permute-start | bytes 1179656 | tf_op jit(solution)/shard_map/ppermute | solution.py:64
  107.4 0.1 add_bitcast_fusion.1
  107.5 0.1 copy.27
  107.5 0.1 reshape.421.table_ref
  107.6 2.1 %copy.31.rest_3_ = bf16[2,2,64,1536]{3,2,1,0:T(8,128)(2,1)} copy(bf16[2,2,64,1536]{3,2,0,1:T(8,128)(2,1)} %collective-permute-done.5) | data formatting | bytes 1572864 | tf_op jit(solution)/shard_map/ppermute | solution.py:34
  109.7 2.1 %copy.30.rest_2_ = bf16[2,2,64,1536]{3,2,1,0:T(8,128)(2,1)} copy(bf16[2,2,64,1536]{3,2,0,1:T(8,128)(2,1)} %collective-permute-done.3) | data formatting | bytes 1572864 | tf_op jit(solution)/shard_map/ppermute | solution.py:34
  111.8 1.5 %collective-permute-done.13.rest_11_ = bf16[2,1,64,1536]{3,2,1,0:T(8,128)(2,1)} collective-permute-done((bf16[2,1,64,1536]{3,2,1,0:T(8,128)(2,1)}, bf16[2,1,64,1536]{3,2,1,0:T(8,128)(2,1)}, u32[]{:S(2)}, u32[]{:S(2)}) %collective-permute-start.13) | collective-permute-done | bytes 393248 | tf_op jit(solution)/shard_map/ppermute | solution.py:70
  113.3 7.5 %collective-permute-done.21.rest_19_ = bf16[2,1,64,1536]{3,2,1,0:T(8,128)(2,1)} collective-permute-done((bf16[2,1,64,1536]{3,2,1,0:T(8,128)(2,1)}, bf16[2,1,64,1536]{3,2,1,0:T(8,128)(2,1)}, u32[]{:S(2)}, u32[]{:S(2)}) %collective-permute-start.21) | collective-permute-done | bytes 393248 | tf_op jit(solution)/shard_map/ppermute | solution.py:64
  120.8 14.2 %shard_map.100 = bf16[512,1536]{1,0:T(8,128)(2,1)} custom-call(s32[16]{0:T(128)S(1)} %reshape.421.table_ref, bf16[512,1536]{1,0:T(8,128)(2,1)} %bitcast.88, bf16[2,8,64,1536]{3,2,1,0:T(8,128)(2,1)} %copy-done.2, bf16[2,1,64,1536]{3,2,1,0:T(8,128)(2,1)S(1)} %collective-permute-done.rest_0_, bf16[2,1,64,1536]{3,2,1,0:T(8,128)(2,1)S(1)} %collective-permute-done.1.rest_1_, ...), custom_call_target="tpu_custom_call" | custom-call | flops 3221225472 | bytes 9437184 | tf_op jit(solution)/shard_map/pallas_call | solution.py:142
  (56 shorter events, 0.2 us)
Async XLA Ops:
  0.0 18.5 %collective-permute-start.4 = (s32[4]{0:T(128)}, s32[4]{0:T(128)S(1)}, u32[]{:S(2)}, u32[]{:S(2)}) collective-permute-start(s32[4]{0:T(128)} %bitcast.89), channel_id=1, source_target_pairs={{0,2},{2,4},{4,6},{6,8},{8,10},{10,12},{12,14},{1,3},{3,5},{5,7},{... | collective-permute-start | bytes 56 | tf_op jit(solution)/shard_map/ppermute | solution.py:34
  4.9 14.9 %collective-permute-start.2 = (s32[4]{0:T(128)}, s32[4]{0:T(128)S(1)}, u32[]{:S(2)}, u32[]{:S(2)}) collective-permute-start(s32[4]{0:T(128)} %bitcast.90), channel_id=1, source_target_pairs={{2,0},{4,2},{6,4},{8,6},{10,8},{12,10},{14,12},{3,1},{5,3},{7,5},{... | collective-permute-start | bytes 56 | tf_op jit(solution)/shard_map/ppermute | solution.py:34
  8.1 1.9 %copy-start.4 = (bf16[8,1,64,1536]{3,2,1,0:T(8,128)(2,1)S(1)}, bf16[8,1,64,1536]{3,2,1,0:T(8,128)(2,1)}, u32[]{:S(2)}) copy-start(bf16[8,1,64,1536]{3,2,1,0:T(8,128)(2,1)} %param.13) | copy-start | bytes 4718596
  10.6 5.6 %copy-start.2 = (bf16[2,8,64,1536]{3,2,1,0:T(8,128)(2,1)}, bf16[2,8,64,1536]{3,2,1,0:T(8,128)(2,1)S(1)}, u32[]{:S(2)}) copy-start(bf16[2,8,64,1536]{3,2,1,0:T(8,128)(2,1)S(1)} %maximum_bitcast_fusion.own_hbm) | copy-start | bytes 9437188
  10.7 6.5 %copy-start.6 = (s32[1,1,4]{2,1,0:T(1,128)S(1)}, s32[1,1,4]{2,1,0:T(1,128)}, u32[]{:S(2)}) copy-start(s32[1,1,4]{2,1,0:T(1,128)} %param.18) | copy-start | bytes 52
  10.7 6.5 %copy-start = (s32[8]{0:T(128)S(1)}, s32[8]{0:T(128)}, u32[]{:S(2)}) copy-start(s32[8]{0:T(128)} %constant.99.clone) | copy-start | bytes 100
  11.5 18.9 %collective-permute-start.16 = (bf16[2,1,64,1536]{3,2,1,0:T(8,128)(2,1)}, bf16[2,1,64,1536]{3,2,1,0:T(8,128)(2,1)S(1)}, u32[]{:S(2)}, u32[]{:S(2)}) collective-permute-start(bf16[2,1,64,1536]{3,2,1,0:T(8,128)(2,1)} %get-tuple-element.10), channel_id=1, source_target_pairs={{4,0},{8,4},{12,8},{14,12},{10,14},{6,10},{2,6},{0,2},{5,1},{9,5},... | collective-permute-start | bytes 1179656 | tf_op jit(solution)/shard_map/ppermute | solution.py:70
  14.2 19.4 %collective-permute-start.15 = (bf16[2,1,64,1536]{3,2,1,0:T(8,128)(2,1)}, bf16[2,1,64,1536]{3,2,1,0:T(8,128)(2,1)S(1)}, u32[]{:S(2)}, u32[]{:S(2)}) collective-permute-start(bf16[2,1,64,1536]{3,2,1,0:T(8,128)(2,1)} %get-tuple-element.10), channel_id=1, source_target_pairs={{0,4},{4,8},{8,12},{12,14},{14,10},{10,6},{6,2},{2,0},{1,5},{5,9},... | collective-permute-start | bytes 1179656 | tf_op jit(solution)/shard_map/ppermute | solution.py:67
  15.1 22.2 %collective-permute-start.9 = (bf16[2,1,64,1536]{3,2,1,0:T(8,128)(2,1)S(1)}, bf16[2,1,64,1536]{3,2,1,0:T(8,128)(2,1)S(1)}, u32[]{:S(2)}, u32[]{:S(2)}) collective-permute-start(bf16[2,1,64,1536]{3,2,1,0:T(8,128)(2,1)S(1)} %get-tuple-element.11), channel_id=1, source_target_pairs={{4,0},{8,4},{12,8},{14,12},{10,14},{6,10},{2,6},{0,2},{5,1},{9,5},... | collective-permute-start | bytes 1179656 | tf_op jit(solution)/shard_map/ppermute | solution.py:70
  18.5 20.2 %collective-permute-start.8 = (bf16[2,1,64,1536]{3,2,1,0:T(8,128)(2,1)S(1)}, bf16[2,1,64,1536]{3,2,1,0:T(8,128)(2,1)S(1)}, u32[]{:S(2)}, u32[]{:S(2)}) collective-permute-start(bf16[2,1,64,1536]{3,2,1,0:T(8,128)(2,1)S(1)} %get-tuple-element.11), channel_id=1, source_target_pairs={{0,4},{4,8},{8,12},{12,14},{14,10},{10,6},{6,2},{2,0},{1,5},{5,9},... | collective-permute-start | bytes 1179656 | tf_op jit(solution)/shard_map/ppermute | solution.py:67
  19.8 1.5 %copy-start.9 = (s32[4]{0:T(128)}, s32[4]{0:T(128)S(1)}, u32[]{:S(2)}) copy-start(s32[4]{0:T(128)S(1)} %collective-permute-done.2) | copy-start | bytes 52
  19.8 24.9 %collective-permute-start.1 = (bf16[2,1,64,1536]{3,2,1,0:T(8,128)(2,1)}, bf16[2,1,64,1536]{3,2,1,0:T(8,128)(2,1)S(1)}, u32[]{:S(2)}, u32[]{:S(2)}) collective-permute-start(bf16[2,1,64,1536]{3,2,1,0:T(8,128)(2,1)} %get-tuple-element.8), channel_id=1, source_target_pairs={{1,0},{3,2},{5,4},{7,6},{9,8},{11,10},{13,12},{15,14},{17,16},{19,... | collective-permute-start | bytes 1179656 | tf_op jit(solution)/shard_map/ppermute | solution.py:34
  24.4 0.7 copy-start.10
  24.4 0.7 copy-start.8
  30.4 17.3 %copy-start.7 = (s32[1,1,4]{2,1,0:T(1,128)S(1)}, s32[1,1,4]{2,1,0:T(1,128)}, u32[]{:S(2)}) copy-start(s32[1,1,4]{2,1,0:T(1,128)} %param.18) | copy-start | bytes 52
  30.5 17.9 %copy-start.1 = (s32[7,2]{1,0:T(8,128)S(1)}, s32[7,2]{1,0:T(8,128)}, u32[]{:S(2)}) copy-start(s32[7,2]{1,0:T(8,128)} %constant.100.clone) | copy-start | bytes 172
  30.5 16.4 %collective-permute-start = (bf16[2,1,64,1536]{3,2,1,0:T(8,128)(2,1)}, bf16[2,1,64,1536]{3,2,1,0:T(8,128)(2,1)S(1)}, u32[]{:S(2)}, u32[]{:S(2)}) collective-permute-start(bf16[2,1,64,1536]{3,2,1,0:T(8,128)(2,1)} %get-tuple-element.9), channel_id=1, source_target_pairs={{0,1},{2,3},{4,5},{6,7},{8,9},{10,11},{12,13},{14,15},{16,17},{18,... | collective-permute-start | bytes 1179656 | tf_op jit(solution)/shard_map/ppermute | solution.py:34
  33.6 14.2 %collective-permute-start.7 = (bf16[2,1,64,1536]{3,2,0,1:T(8,128)(2,1)}, bf16[2,1,64,1536]{3,2,0,1:T(8,128)(2,1)S(1)}, u32[]{:S(2)}, u32[]{:S(2)}) collective-permute-start(bf16[2,1,64,1536]{3,2,0,1:T(8,128)(2,1)} %slice.51), channel_id=1, source_target_pairs={{2,0},{3,1},{18,16},{19,17}} | collective-permute-start | bytes 1179656 | tf_op jit(solution)/shard_map/ppermute | solution.py:193
  36.3 11.4 %copy-start.3 = (bf16[2,3,64,1536]{3,2,0,1:T(8,128)(2,1)}, bf16[2,3,64,1536]{3,2,0,1:T(8,128)(2,1)S(1)}, u32[]{:S(2)}) copy-start(bf16[2,3,64,1536]{3,2,0,1:T(8,128)(2,1)S(1)} %select_bitcast_fusion.1) | copy-start | bytes 3538948
  36.3 12.7 %copy-start.5 = (s32[1,1,4]{2,1,0:T(1,128)S(1)}, s32[1,1,4]{2,1,0:T(1,128)}, u32[]{:S(2)}) copy-start(s32[1,1,4]{2,1,0:T(1,128)} %param.17) | copy-start | bytes 52
  37.4 60.5 %collective-permute-start.5 = (bf16[2,2,64,1536]{3,2,0,1:T(8,128)(2,1)}, bf16[2,2,64,1536]{3,2,0,1:T(8,128)(2,1)}, u32[]{:S(2)}, u32[]{:S(2)}) collective-permute-start(bf16[2,2,64,1536]{3,2,0,1:T(8,128)(2,1)} %slice.49), channel_id=1, source_target_pairs={{2,0},{4,2},{6,4},{8,6},{10,8},{12,10},{14,12},{3,1},{5,3},{7,5},{... | collective-permute-start | bytes 2359304 | tf_op jit(solution)/shard_map/ppermute | solution.py:34
  38.7 59.2 %collective-permute-start.3 = (bf16[2,2,64,1536]{3,2,0,1:T(8,128)(2,1)}, bf16[2,2,64,1536]{3,2,0,1:T(8,128)(2,1)}, u32[]{:S(2)}, u32[]{:S(2)}) collective-permute-start(bf16[2,2,64,1536]{3,2,0,1:T(8,128)(2,1)} %slice.48), channel_id=1, source_target_pairs={{0,2},{2,4},{4,6},{6,8},{8,10},{10,12},{12,14},{1,3},{3,5},{5,7},{... | collective-permute-start | bytes 2359304 | tf_op jit(solution)/shard_map/ppermute | solution.py:34
  44.8 39.6 %collective-permute-start.18 = (bf16[2,1,64,1536]{3,2,1,0:T(8,128)(2,1)S(1)}, bf16[2,1,64,1536]{3,2,1,0:T(8,128)(2,1)S(1)}, u32[]{:S(2)}, u32[]{:S(2)}) collective-permute-start(bf16[2,1,64,1536]{3,2,1,0:T(8,128)(2,1)S(1)} %collective-permute-done.16.rest_14_), channel_id=1, source_target_pairs={{4,0},{8,4},{12,8},{14,12},{10,14},{6,10},{2,6},{0,2},{5,1},{9,5},... | collective-permute-start | bytes 1179656 | tf_op jit(solution)/shard_map/ppermute | solution.py:70
  46.9 40.0 %collective-permute-start.17 = (bf16[2,1,64,1536]{3,2,1,0:T(8,128)(2,1)S(1)}, bf16[2,1,64,1536]{3,2,1,0:T(8,128)(2,1)S(1)}, u32[]{:S(2)}, u32[]{:S(2)}) collective-permute-start(bf16[2,1,64,1536]{3,2,1,0:T(8,128)(2,1)S(1)} %collective-permute-done.15.rest_13_), channel_id=1, source_target_pairs={{0,4},{4,8},{8,12},{12,14},{14,10},{10,6},{6,2},{2,0},{1,5},{5,9},... | collective-permute-start | bytes 1179656 | tf_op jit(solution)/shard_map/ppermute | solution.py:67
  47.7 39.2 %collective-permute-start.10 = (bf16[2,1,64,1536]{3,2,1,0:T(8,128)(2,1)S(1)}, bf16[2,1,64,1536]{3,2,1,0:T(8,128)(2,1)}, u32[]{:S(2)}, u32[]{:S(2)}) collective-permute-start(bf16[2,1,64,1536]{3,2,1,0:T(8,128)(2,1)S(1)} %collective-permute-done.8.rest_6_), channel_id=1, source_target_pairs={{0,4},{4,8},{8,12},{12,14},{14,10},{10,6},{6,2},{2,0},{1,5},{5,9},... | collective-permute-start | bytes 1179656 | tf_op jit(solution)/shard_map/ppermute | solution.py:67
  84.4 12.1 %collective-permute-start.11 = (bf16[2,1,64,1536]{3,2,1,0:T(8,128)(2,1)S(1)}, bf16[2,1,64,1536]{3,2,1,0:T(8,128)(2,1)}, u32[]{:S(2)}, u32[]{:S(2)}) collective-permute-start(bf16[2,1,64,1536]{3,2,1,0:T(8,128)(2,1)S(1)} %collective-permute-done.9.rest_7_), channel_id=1, source_target_pairs={{4,0},{8,4},{12,8},{14,12},{10,14},{6,10},{2,6},{0,2},{5,1},{9,5},... | collective-permute-start | bytes 1179656 | tf_op jit(solution)/shard_map/ppermute | solution.py:70
  86.9 18.0 %collective-permute-start.20 = (bf16[2,1,64,1536]{3,2,1,0:T(8,128)(2,1)S(1)}, bf16[2,1,64,1536]{3,2,1,0:T(8,128)(2,1)}, u32[]{:S(2)}, u32[]{:S(2)}) collective-permute-start(bf16[2,1,64,1536]{3,2,1,0:T(8,128)(2,1)S(1)} %collective-permute-done.18.rest_16_), channel_id=1, source_target_pairs={{4,0},{8,4},{12,8},{14,12},{10,14},{6,10},{2,6},{0,2},{5,1},{9,5},... | collective-permute-start | bytes 1179656 | tf_op jit(solution)/shard_map/ppermute | solution.py:70
  86.9 20.5 %collective-permute-start.12 = (bf16[2,1,64,1536]{3,2,1,0:T(8,128)(2,1)}, bf16[2,1,64,1536]{3,2,1,0:T(8,128)(2,1)}, u32[]{:S(2)}, u32[]{:S(2)}) collective-permute-start(bf16[2,1,64,1536]{3,2,1,0:T(8,128)(2,1)} %collective-permute-done.10.rest_8_), channel_id=1, source_target_pairs={{0,4},{4,8},{8,12},{12,14},{14,10},{10,6},{6,2},{2,0},{1,5},{5,9},... | collective-permute-start | bytes 1179656 | tf_op jit(solution)/shard_map/ppermute | solution.py:67
  96.4 15.3 %collective-permute-start.6 = (bf16[2,1,64,1536]{3,2,0,1:T(8,128)(2,1)}, bf16[2,1,64,1536]{3,2,0,1:T(8,128)(2,1)}, u32[]{:S(2)}, u32[]{:S(2)}) collective-permute-start(bf16[2,1,64,1536]{3,2,0,1:T(8,128)(2,1)} %slice.50), channel_id=1, source_target_pairs={{12,14},{13,15},{28,30},{29,31}} | collective-permute-start | bytes 1179656 | tf_op jit(solution)/shard_map/ppermute | solution.py:192
  97.9 13.9 %collective-permute-start.19 = (bf16[2,1,64,1536]{3,2,1,0:T(8,128)(2,1)S(1)}, bf16[2,1,64,1536]{3,2,1,0:T(8,128)(2,1)}, u32[]{:S(2)}, u32[]{:S(2)}) collective-permute-start(bf16[2,1,64,1536]{3,2,1,0:T(8,128)(2,1)S(1)} %collective-permute-done.17.rest_15_), channel_id=1, source_target_pairs={{0,4},{4,8},{8,12},{12,14},{14,10},{10,6},{6,2},{2,0},{1,5},{5,9},... | collective-permute-start | bytes 1179656 | tf_op jit(solution)/shard_map/ppermute | solution.py:67
  97.9 15.4 %collective-permute-start.13 = (bf16[2,1,64,1536]{3,2,1,0:T(8,128)(2,1)}, bf16[2,1,64,1536]{3,2,1,0:T(8,128)(2,1)}, u32[]{:S(2)}, u32[]{:S(2)}) collective-permute-start(bf16[2,1,64,1536]{3,2,1,0:T(8,128)(2,1)} %collective-permute-done.11.rest_9_), channel_id=1, source_target_pairs={{4,0},{8,4},{12,8},{14,12},{10,14},{6,10},{2,6},{0,2},{5,1},{9,5},... | collective-permute-start | bytes 1179656 | tf_op jit(solution)/shard_map/ppermute | solution.py:70
  104.9 15.9 %collective-permute-start.21 = (bf16[2,1,64,1536]{3,2,1,0:T(8,128)(2,1)}, bf16[2,1,64,1536]{3,2,1,0:T(8,128)(2,1)}, u32[]{:S(2)}, u32[]{:S(2)}) collective-permute-start(bf16[2,1,64,1536]{3,2,1,0:T(8,128)(2,1)} %collective-permute-done.20.rest_18_), channel_id=1, source_target_pairs={{4,0},{8,4},{12,8},{14,12},{10,14},{6,10},{2,6},{0,2},{5,1},{9,5},... | collective-permute-start | bytes 1179656 | tf_op jit(solution)/shard_map/ppermute | solution.py:64
  107.4 13.4 %collective-permute-start.14 = (bf16[2,1,64,1536]{3,2,1,0:T(8,128)(2,1)}, bf16[2,1,64,1536]{3,2,1,0:T(8,128)(2,1)}, u32[]{:S(2)}, u32[]{:S(2)}) collective-permute-start(bf16[2,1,64,1536]{3,2,1,0:T(8,128)(2,1)} %collective-permute-done.12.rest_10_), channel_id=1, source_target_pairs={{0,4},{4,8},{8,12},{12,14},{14,10},{10,6},{6,2},{2,0},{1,5},{5,9},... | collective-permute-start | bytes 1179656 | tf_op jit(solution)/shard_map/ppermute | solution.py:62

commit v8 on v7

--- a/solution.py
+++ b/solution.py
@@ -85,47 +85,66 @@
     block_length = own_hbm.shape[2]
     extra = table_ref.shape[0] // 2
     heads = q_vmem.shape[1] // HEAD_DIM
-
-    copies = [pltpu.make_async_copy(q_hbm, q_vmem, sems.at[0, 0])]
-    copies.append(pltpu.make_async_copy(own_hbm.at[0], k_vmem.at[pl.ds(0, tile_blocks)], sems.at[0, 1]))
-    copies.append(pltpu.make_async_copy(own_hbm.at[1], v_vmem.at[pl.ds(0, tile_blocks)], sems.at[1, 1]))
-    for c in copies:
-        c.start()
-    for slot in range(extra):
-        src = table_ref[2 * slot]
-        index = table_ref[2 * slot + 1]
-        lo, hi = (0, cycle_sources) if slot < extra // 2 else (cycle_sources, cycle_sources + far_sources)
-        for cand in range(lo, hi):
-            @pl.when(src == cand)
-            def _():
-                for kv, dst in ((0, k_vmem), (1, v_vmem)):
-                    pltpu.make_async_copy(
-                        sources[cand].at[kv, index], dst.at[tile_blocks + slot], sems.at[kv, 2 + slot]
-                    ).start()
-    for c in copies:
-        c.wait()
-    for slot in range(extra):
-        for kv, dst in ((0, k_vmem), (1, v_vmem)):
-            pltpu.make_async_copy(
-                own_hbm.at[kv, 0], dst.at[tile_blocks + slot], sems.at[kv, 2 + slot]
-            ).wait()
+    chunks = sems.shape[0]
+    chunk_heads = heads // chunks
+    chunk_width = chunk_heads * HEAD_DIM
+
+    def chunk_copies(c):
+        lanes = pl.ds(c * chunk_width, chunk_width)
+        fixed = [
+            (q_hbm.at[:, lanes], q_vmem.at[:, lanes], sems.at[c, 0, 0]),
+            (own_hbm.at[0, :, :, lanes], k_vmem.at[pl.ds(0, tile_blocks), :, lanes], sems.at[c, 0, 1]),
+            (own_hbm.at[1, :, :, lanes], v_vmem.at[pl.ds(0, tile_blocks), :, lanes], sems.at[c, 1, 1]),
+        ]
+        return lanes, fixed
+
+    for c in range(chunks):
+        lanes, fixed = chunk_copies(c)
+        for src, dst, sem in fixed:
+            pltpu.make_async_copy(src, dst, sem).start()
+        for slot in range(extra):
+            src = table_ref[2 * slot]
+            index = table_ref[2 * slot + 1]
+            lo, hi = (0, cycle_sources) if slot < extra // 2 else (cycle_sources, cycle_sources + far_sources)
+            for cand in range(lo, hi):
+                @pl.when(src == cand)
+                def _():
+                    for kv, dst in ((0, k_vmem), (1, v_vmem)):
+                        pltpu.make_async_copy(
+                            sources[cand].at[kv, index, :, lanes],
+                            dst.at[tile_blocks + slot, :, lanes],
+                            sems.at[c, kv, 2 + slot],
+                        ).start()
 
     key_count = k_vmem.shape[0] * block_length
 
-    for h in range(heads):
-        lanes = pl.ds(h * HEAD_DIM, HEAD_DIM)
-        q = q_vmem[:, lanes]
-        k = k_vmem[:, :, lanes].reshape(key_count, HEAD_DIM)
-        v = v_vmem[:, :, lanes].reshape(key_count, HEAD_DIM)
-        scores = lax.dot_general(
-            q, k, (((1,), (1,)), ((), ())), preferred_element_type=jnp.float32
-        ) * HEAD_DIM ** (-0.5)
-        row_max = jnp.max(scores, axis=1, keepdims=True)
-        weights = jnp.exp(scores - row_max)
-        row_total = jnp.sum(weights, axis=1, keepdims=True)
-        rounded = weights.astype(jnp.bfloat16)
-        blended = jnp.dot(rounded, v, preferred_element_type=jnp.float32)
-        o_ref[:, lanes] = (blended / row_total).astype(o_ref.dtype)
+    for c in range(chunks):
+        lanes, fixed = chunk_copies(c)
+        for src, dst, sem in fixed:
+            pltpu.make_async_copy(src, dst, sem).wait()
+        for slot in range(extra):
+            for kv, dst in ((0, k_vmem), (1, v_vmem)):
+                pltpu.make_async_copy(
+                    own_hbm.at[kv, 0, :, lanes], dst.at[tile_blocks + slot, :, lanes], sems.at[c, kv, 2 + slot]
+                ).wait()
+        for h in range(c * chunk_heads, (c + 1) * chunk_heads):
+            lanes = pl.ds(h * HEAD_DIM, HEAD_DIM)
+            q = q_vmem[:, lanes]
+            k = k_vmem[:, :, lanes].reshape(key_count, HEAD_DIM)
+            v = v_vmem[:, :, lanes].reshape(key_count, HEAD_DIM)
+            scores = lax.dot_general(
+                q, k, (((1,), (1,)), ((), ())), preferred_element_type=jnp.float32
+            ) * HEAD_DIM ** (-0.5)
+            row_max = jnp.max(scores, axis=1, keepdims=True)
+            weights = jnp.exp(scores - row_max)
+            row_total = jnp.sum(weights, axis=1, keepdims=True)
+            rounded = weights.astype(jnp.bfloat16)
+            blended = jnp.dot(rounded, v, preferred_element_type=jnp.float32)
+            o_ref[:, lanes] = (blended / row_total).astype(o_ref.dtype)
+
+
+def lane_chunks(heads):
+    return 3 if heads % 3 == 0 else (2 if heads % 2 == 0 else 1)
 
 
 def gather_attend(query_rows, own, cycle_list_sources, far_list_sources, table):
@@ -149,7 +168,7 @@
             pltpu.VMEM((token_count, width), jnp.bfloat16),
             pltpu.VMEM((blocks, block_length, width), jnp.bfloat16),
             pltpu.VMEM((blocks, block_length, width), jnp.bfloat16),
-            pltpu.SemaphoreType.DMA((2, 2 + extra)),
+            pltpu.SemaphoreType.DMA((lane_chunks(heads), 2, 2 + extra)),
         ],
         compiler_params=pltpu.CompilerParams(vmem_limit_bytes=48 * 1024 * 1024),
         cost_estimate=pl.CostEstimate(

time: 136 us -> 136 us (level)
  no operation moved by 1% of the time
where the time goes in v8:
time: 136 us
  waiting for transfers between devices  50.6 us (37%)
  starting transfers between devices  37.9 us (28%)
  local copies, waits for them, and re-layouts  19.8 us (15%)
  Pallas kernels  14.6 us (11%)
  other arithmetic  12.1 us (9%)
    ppermute x6, waiting for transfers between devices, ring_gather(): behind = lax.ppermute(behind, 'col', backward)  42.3 us
    ppermute x6, starting transfers between devices, shift(): return lax.ppermute(x, axis, pairs)  17.9 us
    pallas_call x1, Pallas kernels, gather_attend(): pl.pallas_call(kernel, out_shape=jax.ShapeDtypeStruct((token_count, width...  14.6 us
    ppermute x6, starting transfers between devices, ring_gather(): behind = lax.ppermute(behind, 'col', backward)  10.8 us
    ppermute x1, waiting for transfers between devices, ring_gather(): arrays.append(lax.ppermute(behind, 'col', backward))  7.49 us
    ppermute x2, local copies, waits for them, and re-layouts, shift(): return lax.ppermute(x, axis, pairs)  4.15 us
    ppermute x6, starting transfers between devices, ring_gather(): ahead = lax.ppermute(ahead, 'col', forward)  3.96 us
    gather x1, local copies, waits for them, and re-layouts, per_device(): right_payload = jnp.take(stacked, to_right, axis=1)  3.56 us
  transfers between devices with their start and end apart: 22, of which 6 were waited for; matrix products, arithmetic and copies ran while one was open for 23% of the time, Pallas kernels for 0%

profile of v8, /device:TPU:0, one launch (start us, length us, event | category | flops | bytes accessed | tf_op | source)
XLA Modules:
  0.0 135.6 jit_solution(11460604068172831489)
XLA Ops:
  0.0 4.9 %collective-permute-start.4 = (s32[4]{0:T(128)}, s32[4]{0:T(128)S(1)}, u32[]{:S(2)}, u32[]{:S(2)}) collective-permute-start(s32[4]{0:T(128)} %bitcast.89), channel_id=1, source_target_pairs={{0,2},{2,4},{4,6},{6,8},{8,10},{10,12},{12,14},{1,3},{3,5},{5,7},{... | collective-permute-start | bytes 56 | tf_op jit(solution)/shard_map/ppermute | solution.py:34
  4.9 1.3 collective-permute-start.2
  6.2 1.0 exponential_bitcast_fusion.1
  7.1 1.0 exponential_bitcast_fusion
  8.1 1.8 %fusion = bf16[8,1,64,1536]{3,2,0,1:T(8,128)(2,1)S(1)} fusion(bf16[8,1,64,1536]{3,2,1,0:T(8,128)(2,1)} %param.15, f32[8,2,1536]{2,1,0:T(2,128)S(1)} %exponential_bitcast_fusion), kind=kLoop, calls=%fused_computation.7 | loop fusion | flops 2359296 | bytes 3244032 | tf_op jit(solution)/shard_map/convert_element_type | solution.py:24
  9.9 0.1 copy-done.4
  10.0 0.3 fusion.1
  10.3 0.3 maximum_bitcast_fusion.own_hbm
  10.6 0.1 slice.33
  10.7 0.8 fusion.17
  11.5 2.6 %collective-permute-start.16 = (bf16[2,1,64,1536]{3,2,1,0:T(8,128)(2,1)}, bf16[2,1,64,1536]{3,2,1,0:T(8,128)(2,1)S(1)}, u32[]{:S(2)}, u32[]{:S(2)}) collective-permute-start(bf16[2,1,64,1536]{3,2,1,0:T(8,128)(2,1)} %get-tuple-element.10), channel_id=1, source_target_pairs={{4,0},{8,4},{12,8},{14,12},{10,14},{6,10},{2,6},{0,2},{5,1},{9,5},... | collective-permute-start | bytes 1179656 | tf_op jit(solution)/shard_map/ppermute | solution.py:70
  14.2 1.0 collective-permute-start.15
  15.1 1.1 collective-permute-start.9
  16.2 1.0 fusion.16
  17.2 0.6 dynamic_slice.3
  17.8 0.6 gather_fusion
  18.5 1.0 collective-permute-start.8
  19.5 0.2 reduce-window.37
  19.7 0.1 select_reduce_fusion
  19.8 1.3 collective-permute-start.1
  21.1 0.2 reduce-window.36
  21.3 0.5 add_bitcast_fusion.3
  21.9 2.5 %gather_fusion.4 = bf16[3,2,64,1536]{3,2,1,0:T(8,128)(2,1)S(1)} fusion(bf16[2,8,64,1536]{3,2,1,0:T(8,128)(2,1)} %copy-done.2, s32[1024]{0:T(1024)S(1)} %pad_clamp_fusion), kind=kCustom, calls=%fused_computation.1.clone | custom fusion | bytes 2359308 | tf_op jit(solution)/shard_map/jit(_take)/gather | solution.py:205
  24.4 0.2 select_bitcast_fusion
  24.6 0.5 copy-done.10
  25.0 0.1 select_reduce_fusion.1
  25.2 0.8 slice.51
  25.9 0.9 slice.49
  26.9 3.6 %gather_fusion.3 = bf16[3,2,64,1536]{3,2,1,0:T(8,128)(2,1)} fusion(bf16[2,8,64,1536]{3,2,1,0:T(8,128)(2,1)} %copy-done.2, s32[1024]{0:T(1024)S(1)} %pad_clamp_fusion.1), kind=kCustom, calls=%fused_computation.clone | custom fusion | bytes 2359308 | tf_op jit(solution)/shard_map/jit(_take)/gather | solution.py:204
  30.5 3.1 %collective-permute-start = (bf16[2,1,64,1536]{3,2,1,0:T(8,128)(2,1)}, bf16[2,1,64,1536]{3,2,1,0:T(8,128)(2,1)S(1)}, u32[]{:S(2)}, u32[]{:S(2)}) collective-permute-start(bf16[2,1,64,1536]{3,2,1,0:T(8,128)(2,1)} %get-tuple-element.9), channel_id=1, source_target_pairs={{0,1},{2,3},{4,5},{6,7},{8,9},{10,11},{12,13},{14,15},{16,17},{18,... | collective-permute-start | bytes 1179656 | tf_op jit(solution)/shard_map/ppermute | solution.py:34
  33.6 1.3 collective-permute-start.7
  34.9 1.5 %select_bitcast_fusion.1 = bf16[2,3,64,1536]{3,2,0,1:T(8,128)(2,1)S(1)} fusion(bf16[3,2,64,1536]{3,2,1,0:T(8,128)(2,1)} %gather_fusion.3, pred[3]{0:T(512)(128)(4,1)S(1)} %compare_and_fusion.1), kind=kLoop, calls=%fused_computation.11 | loop fusion | flops 589824 | bytes 2359299 | tf_op jit(solution)/shard_map/jit(_take)/select_n | solution.py:204
  36.3 1.0 slice.48
  37.4 1.3 collective-permute-start.5
  38.7 6.1 %collective-permute-start.3 = (bf16[2,2,64,1536]{3,2,0,1:T(8,128)(2,1)}, bf16[2,2,64,1536]{3,2,0,1:T(8,128)(2,1)}, u32[]{:S(2)}, u32[]{:S(2)}) collective-permute-start(bf16[2,2,64,1536]{3,2,0,1:T(8,128)(2,1)} %slice.48), channel_id=1, source_target_pairs={{0,2},{2,4},{4,6},{6,8},{8,10},{10,12},{12,14},{1,3},{3,5},{5,7},{... | collective-permute-start | bytes 2359304 | tf_op jit(solution)/shard_map/ppermute | solution.py:34
  44.8 2.1 %collective-permute-start.18 = (bf16[2,1,64,1536]{3,2,1,0:T(8,128)(2,1)S(1)}, bf16[2,1,64,1536]{3,2,1,0:T(8,128)(2,1)S(1)}, u32[]{:S(2)}, u32[]{:S(2)}) collective-permute-start(bf16[2,1,64,1536]{3,2,1,0:T(8,128)(2,1)S(1)} %collective-permute-done.16.rest_14_), channel_id=1, source_target_pairs={{4,0},{8,4},{12,8},{14,12},{10,14},{6,10},{2,6},{0,2},{5,1},{9,5},... | collective-permute-start | bytes 1179656 | tf_op jit(solution)/shard_map/ppermute | solution.py:70
  46.9 0.9 collective-permute-done.7
  47.7 0.6 fusion.15
  48.4 0.6 gather_fusion.1
  49.0 0.5 fusion.6
  49.5 34.8 %collective-permute-done.18.rest_16_ = bf16[2,1,64,1536]{3,2,1,0:T(8,128)(2,1)S(1)} collective-permute-done((bf16[2,1,64,1536]{3,2,1,0:T(8,128)(2,1)S(1)}, bf16[2,1,64,1536]{3,2,1,0:T(8,128)(2,1)S(1)}, u32[]{:S(2)}, u32[]{:S(2)}) %collective-permute-start.18) | collective-permute-done | bytes 393248 | tf_op jit(solution)/shard_map/ppermute | solution.py:70
  84.4 2.5 %collective-permute-start.11 = (bf16[2,1,64,1536]{3,2,1,0:T(8,128)(2,1)S(1)}, bf16[2,1,64,1536]{3,2,1,0:T(8,128)(2,1)}, u32[]{:S(2)}, u32[]{:S(2)}) collective-permute-start(bf16[2,1,64,1536]{3,2,1,0:T(8,128)(2,1)S(1)} %collective-permute-done.9.rest_7_), channel_id=1, source_target_pairs={{4,0},{8,4},{12,8},{14,12},{10,14},{6,10},{2,6},{0,2},{5,1},{9,5},... | collective-permute-start | bytes 1179656 | tf_op jit(solution)/shard_map/ppermute | solution.py:70
  86.9 0.0 collective-permute-start.20
  86.9 2.0 %collective-permute-start.12 = (bf16[2,1,64,1536]{3,2,1,0:T(8,128)(2,1)}, bf16[2,1,64,1536]{3,2,1,0:T(8,128)(2,1)}, u32[]{:S(2)}, u32[]{:S(2)}) collective-permute-start(bf16[2,1,64,1536]{3,2,1,0:T(8,128)(2,1)} %collective-permute-done.10.rest_8_), channel_id=1, source_target_pairs={{0,4},{4,8},{8,12},{12,14},{14,10},{10,6},{6,2},{2,0},{1,5},{5,9},... | collective-permute-start | bytes 1179656 | tf_op jit(solution)/shard_map/ppermute | solution.py:67
  88.9 0.5 broadcast_add_fusion.2
  89.4 1.3 reduce-window.34
  90.6 0.7 reduce-window.35
  91.3 0.6 gather_fusion.2
  91.9 0.6 compare_select_fusion.13
  92.6 0.6 add_bitcast_fusion
  93.2 1.8 %slice.50 = bf16[2,1,64,1536]{3,2,0,1:T(8,128)(2,1)} slice(bf16[2,3,64,1536]{3,2,0,1:T(8,128)(2,1)} %copy-done.3), slice={[0:2], [2:3], [0:64], [0:1536]} | slice | bytes 786432 | tf_op jit(solution)/shard_map/slice | solution.py:211
  95.0 1.5 %collective-permute-done.11.rest_9_ = bf16[2,1,64,1536]{3,2,1,0:T(8,128)(2,1)} collective-permute-done((bf16[2,1,64,1536]{3,2,1,0:T(8,128)(2,1)S(1)}, bf16[2,1,64,1536]{3,2,1,0:T(8,128)(2,1)}, u32[]{:S(2)}, u32[]{:S(2)}) %collective-permute-start.11) | collective-permute-done | bytes 393248 | tf_op jit(solution)/shard_map/ppermute | solution.py:70
  96.4 1.4 %collective-permute-start.6 = (bf16[2,1,64,1536]{3,2,0,1:T(8,128)(2,1)}, bf16[2,1,64,1536]{3,2,0,1:T(8,128)(2,1)}, u32[]{:S(2)}, u32[]{:S(2)}) collective-permute-start(bf16[2,1,64,1536]{3,2,0,1:T(8,128)(2,1)} %slice.50), channel_id=1, source_target_pairs={{12,14},{13,15},{28,30},{29,31}} | collective-permute-start | bytes 1179656 | tf_op jit(solution)/shard_map/ppermute | solution.py:211
  97.9 2.5 %collective-permute-start.13 = (bf16[2,1,64,1536]{3,2,1,0:T(8,128)(2,1)}, bf16[2,1,64,1536]{3,2,1,0:T(8,128)(2,1)}, u32[]{:S(2)}, u32[]{:S(2)}) collective-permute-start(bf16[2,1,64,1536]{3,2,1,0:T(8,128)(2,1)} %collective-permute-done.11.rest_9_), channel_id=1, source_target_pairs={{4,0},{8,4},{12,8},{14,12},{10,14},{6,10},{2,6},{0,2},{5,1},{9,5},... | collective-permute-start | bytes 1179656 | tf_op jit(solution)/shard_map/ppermute | solution.py:70
  100.4 4.4 %collective-permute-done.20.rest_18_ = bf16[2,1,64,1536]{3,2,1,0:T(8,128)(2,1)} collective-permute-done((bf16[2,1,64,1536]{3,2,1,0:T(8,128)(2,1)S(1)}, bf16[2,1,64,1536]{3,2,1,0:T(8,128)(2,1)}, u32[]{:S(2)}, u32[]{:S(2)}) %collective-permute-start.20) | collective-permute-done | bytes 393248 | tf_op jit(solution)/shard_map/ppermute | solution.py:70
  104.9 2.5 %collective-permute-start.21 = (bf16[2,1,64,1536]{3,2,1,0:T(8,128)(2,1)}, bf16[2,1,64,1536]{3,2,1,0:T(8,128)(2,1)}, u32[]{:S(2)}, u32[]{:S(2)}) collective-permute-start(bf16[2,1,64,1536]{3,2,1,0:T(8,128)(2,1)} %collective-permute-done.20.rest_18_), channel_id=1, source_target_pairs={{4,0},{8,4},{12,8},{14,12},{10,14},{6,10},{2,6},{0,2},{5,1},{9,5},... | collective-permute-start | bytes 1179656 | tf_op jit(solution)/shard_map/ppermute | solution.py:64
  107.4 0.1 add_bitcast_fusion.1
  107.5 0.1 copy.27
  107.5 0.1 reshape.421.table_ref
  107.6 2.1 %copy.31.rest_3_ = bf16[2,2,64,1536]{3,2,1,0:T(8,128)(2,1)} copy(bf16[2,2,64,1536]{3,2,0,1:T(8,128)(2,1)} %collective-permute-done.5) | data formatting | bytes 1572864 | tf_op jit(solution)/shard_map/ppermute | solution.py:34
  109.7 2.1 %copy.30.rest_2_ = bf16[2,2,64,1536]{3,2,1,0:T(8,128)(2,1)} copy(bf16[2,2,64,1536]{3,2,0,1:T(8,128)(2,1)} %collective-permute-done.3) | data formatting | bytes 1572864 | tf_op jit(solution)/shard_map/ppermute | solution.py:34
  111.8 1.5 %collective-permute-done.13.rest_11_ = bf16[2,1,64,1536]{3,2,1,0:T(8,128)(2,1)} collective-permute-done((bf16[2,1,64,1536]{3,2,1,0:T(8,128)(2,1)}, bf16[2,1,64,1536]{3,2,1,0:T(8,128)(2,1)}, u32[]{:S(2)}, u32[]{:S(2)}) %collective-permute-start.13) | collective-permute-done | bytes 393248 | tf_op jit(solution)/shard_map/ppermute | solution.py:70
  113.3 7.5 %collective-permute-done.21.rest_19_ = bf16[2,1,64,1536]{3,2,1,0:T(8,128)(2,1)} collective-permute-done((bf16[2,1,64,1536]{3,2,1,0:T(8,128)(2,1)}, bf16[2,1,64,1536]{3,2,1,0:T(8,128)(2,1)}, u32[]{:S(2)}, u32[]{:S(2)}) %collective-permute-start.21) | collective-permute-done | bytes 393248 | tf_op jit(solution)/shard_map/ppermute | solution.py:64
  120.8 14.6 %shard_map.100 = bf16[512,1536]{1,0:T(8,128)(2,1)} custom-call(s32[16]{0:T(128)S(1)} %reshape.421.table_ref, bf16[512,1536]{1,0:T(8,128)(2,1)} %bitcast.88, bf16[2,8,64,1536]{3,2,1,0:T(8,128)(2,1)} %copy-done.2, bf16[2,1,64,1536]{3,2,1,0:T(8,128)(2,1)S(1)} %collective-permute-done.rest_0_, bf16[2,1,64,1536]{3,2,1,0:T(8,128)(2,1)S(1)} %collective-permute-done.1.rest_1_, ...), custom_call_target="tpu_custom_call" | custom-call | flops 3221225472 | bytes 9437184 | tf_op jit(solution)/shard_map/pallas_call | solution.py:161
  (56 shorter events, 0.2 us)
Async XLA Ops:
  0.0 18.5 %collective-permute-start.4 = (s32[4]{0:T(128)}, s32[4]{0:T(128)S(1)}, u32[]{:S(2)}, u32[]{:S(2)}) collective-permute-start(s32[4]{0:T(128)} %bitcast.89), channel_id=1, source_target_pairs={{0,2},{2,4},{4,6},{6,8},{8,10},{10,12},{12,14},{1,3},{3,5},{5,7},{... | collective-permute-start | bytes 56 | tf_op jit(solution)/shard_map/ppermute | solution.py:34
  4.9 14.9 %collective-permute-start.2 = (s32[4]{0:T(128)}, s32[4]{0:T(128)S(1)}, u32[]{:S(2)}, u32[]{:S(2)}) collective-permute-start(s32[4]{0:T(128)} %bitcast.90), channel_id=1, source_target_pairs={{2,0},{4,2},{6,4},{8,6},{10,8},{12,10},{14,12},{3,1},{5,3},{7,5},{... | collective-permute-start | bytes 56 | tf_op jit(solution)/shard_map/ppermute | solution.py:34
  8.1 1.9 %copy-start.4 = (bf16[8,1,64,1536]{3,2,1,0:T(8,128)(2,1)S(1)}, bf16[8,1,64,1536]{3,2,1,0:T(8,128)(2,1)}, u32[]{:S(2)}) copy-start(bf16[8,1,64,1536]{3,2,1,0:T(8,128)(2,1)} %param.13) | copy-start | bytes 4718596
  10.6 5.6 %copy-start.2 = (bf16[2,8,64,1536]{3,2,1,0:T(8,128)(2,1)}, bf16[2,8,64,1536]{3,2,1,0:T(8,128)(2,1)S(1)}, u32[]{:S(2)}) copy-start(bf16[2,8,64,1536]{3,2,1,0:T(8,128)(2,1)S(1)} %maximum_bitcast_fusion.own_hbm) | copy-start | bytes 9437188
  10.7 6.5 %copy-start.6 = (s32[1,1,4]{2,1,0:T(1,128)S(1)}, s32[1,1,4]{2,1,0:T(1,128)}, u32[]{:S(2)}) copy-start(s32[1,1,4]{2,1,0:T(1,128)} %param.18) | copy-start | bytes 52
  10.7 6.5 %copy-start = (s32[8]{0:T(128)S(1)}, s32[8]{0:T(128)}, u32[]{:S(2)}) copy-start(s32[8]{0:T(128)} %constant.99.clone) | copy-start | bytes 100
  11.5 18.9 %collective-permute-start.16 = (bf16[2,1,64,1536]{3,2,1,0:T(8,128)(2,1)}, bf16[2,1,64,1536]{3,2,1,0:T(8,128)(2,1)S(1)}, u32[]{:S(2)}, u32[]{:S(2)}) collective-permute-start(bf16[2,1,64,1536]{3,2,1,0:T(8,128)(2,1)} %get-tuple-element.10), channel_id=1, source_target_pairs={{4,0},{8,4},{12,8},{14,12},{10,14},{6,10},{2,6},{0,2},{5,1},{9,5},... | collective-permute-start | bytes 1179656 | tf_op jit(solution)/shard_map/ppermute | solution.py:70
  14.2 19.4 %collective-permute-start.15 = (bf16[2,1,64,1536]{3,2,1,0:T(8,128)(2,1)}, bf16[2,1,64,1536]{3,2,1,0:T(8,128)(2,1)S(1)}, u32[]{:S(2)}, u32[]{:S(2)}) collective-permute-start(bf16[2,1,64,1536]{3,2,1,0:T(8,128)(2,1)} %get-tuple-element.10), channel_id=1, source_target_pairs={{0,4},{4,8},{8,12},{12,14},{14,10},{10,6},{6,2},{2,0},{1,5},{5,9},... | collective-permute-start | bytes 1179656 | tf_op jit(solution)/shard_map/ppermute | solution.py:67
  15.1 22.2 %collective-permute-start.9 = (bf16[2,1,64,1536]{3,2,1,0:T(8,128)(2,1)S(1)}, bf16[2,1,64,1536]{3,2,1,0:T(8,128)(2,1)S(1)}, u32[]{:S(2)}, u32[]{:S(2)}) collective-permute-start(bf16[2,1,64,1536]{3,2,1,0:T(8,128)(2,1)S(1)} %get-tuple-element.11), channel_id=1, source_target_pairs={{4,0},{8,4},{12,8},{14,12},{10,14},{6,10},{2,6},{0,2},{5,1},{9,5},... | collective-permute-start | bytes 1179656 | tf_op jit(solution)/shard_map/ppermute | solution.py:70
  18.5 20.2 %collective-permute-start.8 = (bf16[2,1,64,1536]{3,2,1,0:T(8,128)(2,1)S(1)}, bf16[2,1,64,1536]{3,2,1,0:T(8,128)(2,1)S(1)}, u32[]{:S(2)}, u32[]{:S(2)}) collective-permute-start(bf16[2,1,64,1536]{3,2,1,0:T(8,128)(2,1)S(1)} %get-tuple-element.11), channel_id=1, source_target_pairs={{0,4},{4,8},{8,12},{12,14},{14,10},{10,6},{6,2},{2,0},{1,5},{5,9},... | collective-permute-start | bytes 1179656 | tf_op jit(solution)/shard_map/ppermute | solution.py:67
  19.8 1.5 %copy-start.9 = (s32[4]{0:T(128)}, s32[4]{0:T(128)S(1)}, u32[]{:S(2)}) copy-start(s32[4]{0:T(128)S(1)} %collective-permute-done.2) | copy-start | bytes 52
  19.8 24.9 %collective-permute-start.1 = (bf16[2,1,64,1536]{3,2,1,0:T(8,128)(2,1)}, bf16[2,1,64,1536]{3,2,1,0:T(8,128)(2,1)S(1)}, u32[]{:S(2)}, u32[]{:S(2)}) collective-permute-start(bf16[2,1,64,1536]{3,2,1,0:T(8,128)(2,1)} %get-tuple-element.8), channel_id=1, source_target_pairs={{1,0},{3,2},{5,4},{7,6},{9,8},{11,10},{13,12},{15,14},{17,16},{19,... | collective-permute-start | bytes 1179656 | tf_op jit(solution)/shard_map/ppermute | solution.py:34
  24.4 0.7 copy-start.10
  24.4 0.7 copy-start.8
  30.4 17.3 %copy-start.7 = (s32[1,1,4]{2,1,0:T(1,128)S(1)}, s32[1,1,4]{2,1,0:T(1,128)}, u32[]{:S(2)}) copy-start(s32[1,1,4]{2,1,0:T(1,128)} %param.18) | copy-start | bytes 52
  30.5 17.9 %copy-start.1 = (s32[7,2]{1,0:T(8,128)S(1)}, s32[7,2]{1,0:T(8,128)}, u32[]{:S(2)}) copy-start(s32[7,2]{1,0:T(8,128)} %constant.100.clone) | copy-start | bytes 172
  30.5 16.4 %collective-permute-start = (bf16[2,1,64,1536]{3,2,1,0:T(8,128)(2,1)}, bf16[2,1,64,1536]{3,2,1,0:T(8,128)(2,1)S(1)}, u32[]{:S(2)}, u32[]{:S(2)}) collective-permute-start(bf16[2,1,64,1536]{3,2,1,0:T(8,128)(2,1)} %get-tuple-element.9), channel_id=1, source_target_pairs={{0,1},{2,3},{4,5},{6,7},{8,9},{10,11},{12,13},{14,15},{16,17},{18,... | collective-permute-start | bytes 1179656 | tf_op jit(solution)/shard_map/ppermute | solution.py:34
  33.6 14.2 %collective-permute-start.7 = (bf16[2,1,64,1536]{3,2,0,1:T(8,128)(2,1)}, bf16[2,1,64,1536]{3,2,0,1:T(8,128)(2,1)S(1)}, u32[]{:S(2)}, u32[]{:S(2)}) collective-permute-start(bf16[2,1,64,1536]{3,2,0,1:T(8,128)(2,1)} %slice.51), channel_id=1, source_target_pairs={{2,0},{3,1},{18,16},{19,17}} | collective-permute-start | bytes 1179656 | tf_op jit(solution)/shard_map/ppermute | solution.py:212
  36.3 11.4 %copy-start.3 = (bf16[2,3,64,1536]{3,2,0,1:T(8,128)(2,1)}, bf16[2,3,64,1536]{3,2,0,1:T(8,128)(2,1)S(1)}, u32[]{:S(2)}) copy-start(bf16[2,3,64,1536]{3,2,0,1:T(8,128)(2,1)S(1)} %select_bitcast_fusion.1) | copy-start | bytes 3538948
  36.3 12.7 %copy-start.5 = (s32[1,1,4]{2,1,0:T(1,128)S(1)}, s32[1,1,4]{2,1,0:T(1,128)}, u32[]{:S(2)}) copy-start(s32[1,1,4]{2,1,0:T(1,128)} %param.17) | copy-start | bytes 52
  37.4 60.5 %collective-permute-start.5 = (bf16[2,2,64,1536]{3,2,0,1:T(8,128)(2,1)}, bf16[2,2,64,1536]{3,2,0,1:T(8,128)(2,1)}, u32[]{:S(2)}, u32[]{:S(2)}) collective-permute-start(bf16[2,2,64,1536]{3,2,0,1:T(8,128)(2,1)} %slice.49), channel_id=1, source_target_pairs={{2,0},{4,2},{6,4},{8,6},{10,8},{12,10},{14,12},{3,1},{5,3},{7,5},{... | collective-permute-start | bytes 2359304 | tf_op jit(solution)/shard_map/ppermute | solution.py:34
  38.7 59.2 %collective-permute-start.3 = (bf16[2,2,64,1536]{3,2,0,1:T(8,128)(2,1)}, bf16[2,2,64,1536]{3,2,0,1:T(8,128)(2,1)}, u32[]{:S(2)}, u32[]{:S(2)}) collective-permute-start(bf16[2,2,64,1536]{3,2,0,1:T(8,128)(2,1)} %slice.48), channel_id=1, source_target_pairs={{0,2},{2,4},{4,6},{6,8},{8,10},{10,12},{12,14},{1,3},{3,5},{5,7},{... | collective-permute-start | bytes 2359304 | tf_op jit(solution)/shard_map/ppermute | solution.py:34
  44.8 39.6 %collective-permute-start.18 = (bf16[2,1,64,1536]{3,2,1,0:T(8,128)(2,1)S(1)}, bf16[2,1,64,1536]{3,2,1,0:T(8,128)(2,1)S(1)}, u32[]{:S(2)}, u32[]{:S(2)}) collective-permute-start(bf16[2,1,64,1536]{3,2,1,0:T(8,128)(2,1)S(1)} %collective-permute-done.16.rest_14_), channel_id=1, source_target_pairs={{4,0},{8,4},{12,8},{14,12},{10,14},{6,10},{2,6},{0,2},{5,1},{9,5},... | collective-permute-start | bytes 1179656 | tf_op jit(solution)/shard_map/ppermute | solution.py:70
  46.9 40.0 %collective-permute-start.17 = (bf16[2,1,64,1536]{3,2,1,0:T(8,128)(2,1)S(1)}, bf16[2,1,64,1536]{3,2,1,0:T(8,128)(2,1)S(1)}, u32[]{:S(2)}, u32[]{:S(2)}) collective-permute-start(bf16[2,1,64,1536]{3,2,1,0:T(8,128)(2,1)S(1)} %collective-permute-done.15.rest_13_), channel_id=1, source_target_pairs={{0,4},{4,8},{8,12},{12,14},{14,10},{10,6},{6,2},{2,0},{1,5},{5,9},... | collective-permute-start | bytes 1179656 | tf_op jit(solution)/shard_map/ppermute | solution.py:67
  47.7 39.2 %collective-permute-start.10 = (bf16[2,1,64,1536]{3,2,1,0:T(8,128)(2,1)S(1)}, bf16[2,1,64,1536]{3,2,1,0:T(8,128)(2,1)}, u32[]{:S(2)}, u32[]{:S(2)}) collective-permute-start(bf16[2,1,64,1536]{3,2,1,0:T(8,128)(2,1)S(1)} %collective-permute-done.8.rest_6_), channel_id=1, source_target_pairs={{0,4},{4,8},{8,12},{12,14},{14,10},{10,6},{6,2},{2,0},{1,5},{5,9},... | collective-permute-start | bytes 1179656 | tf_op jit(solution)/shard_map/ppermute | solution.py:67
  84.4 12.1 %collective-permute-start.11 = (bf16[2,1,64,1536]{3,2,1,0:T(8,128)(2,1)S(1)}, bf16[2,1,64,1536]{3,2,1,0:T(8,128)(2,1)}, u32[]{:S(2)}, u32[]{:S(2)}) collective-permute-start(bf16[2,1,64,1536]{3,2,1,0:T(8,128)(2,1)S(1)} %collective-permute-done.9.rest_7_), channel_id=1, source_target_pairs={{4,0},{8,4},{12,8},{14,12},{10,14},{6,10},{2,6},{0,2},{5,1},{9,5},... | collective-permute-start | bytes 1179656 | tf_op jit(solution)/shard_map/ppermute | solution.py:70
  86.9 18.0 %collective-permute-start.20 = (bf16[2,1,64,1536]{3,2,1,0:T(8,128)(2,1)S(1)}, bf16[2,1,64,1536]{3,2,1,0:T(8,128)(2,1)}, u32[]{:S(2)}, u32[]{:S(2)}) collective-permute-start(bf16[2,1,64,1536]{3,2,1,0:T(8,128)(2,1)S(1)} %collective-permute-done.18.rest_16_), channel_id=1, source_target_pairs={{4,0},{8,4},{12,8},{14,12},{10,14},{6,10},{2,6},{0,2},{5,1},{9,5},... | collective-permute-start | bytes 1179656 | tf_op jit(solution)/shard_map/ppermute | solution.py:70
  86.9 20.5 %collective-permute-start.12 = (bf16[2,1,64,1536]{3,2,1,0:T(8,128)(2,1)}, bf16[2,1,64,1536]{3,2,1,0:T(8,128)(2,1)}, u32[]{:S(2)}, u32[]{:S(2)}) collective-permute-start(bf16[2,1,64,1536]{3,2,1,0:T(8,128)(2,1)} %collective-permute-done.10.rest_8_), channel_id=1, source_target_pairs={{0,4},{4,8},{8,12},{12,14},{14,10},{10,6},{6,2},{2,0},{1,5},{5,9},... | collective-permute-start | bytes 1179656 | tf_op jit(solution)/shard_map/ppermute | solution.py:67
  96.4 15.3 %collective-permute-start.6 = (bf16[2,1,64,1536]{3,2,0,1:T(8,128)(2,1)}, bf16[2,1,64,1536]{3,2,0,1:T(8,128)(2,1)}, u32[]{:S(2)}, u32[]{:S(2)}) collective-permute-start(bf16[2,1,64,1536]{3,2,0,1:T(8,128)(2,1)} %slice.50), channel_id=1, source_target_pairs={{12,14},{13,15},{28,30},{29,31}} | collective-permute-start | bytes 1179656 | tf_op jit(solution)/shard_map/ppermute | solution.py:211
  97.9 13.9 %collective-permute-start.19 = (bf16[2,1,64,1536]{3,2,1,0:T(8,128)(2,1)S(1)}, bf16[2,1,64,1536]{3,2,1,0:T(8,128)(2,1)}, u32[]{:S(2)}, u32[]{:S(2)}) collective-permute-start(bf16[2,1,64,1536]{3,2,1,0:T(8,128)(2,1)S(1)} %collective-permute-done.17.rest_15_), channel_id=1, source_target_pairs={{0,4},{4,8},{8,12},{12,14},{14,10},{10,6},{6,2},{2,0},{1,5},{5,9},... | collective-permute-start | bytes 1179656 | tf_op jit(solution)/shard_map/ppermute | solution.py:67
  97.9 15.4 %collective-permute-start.13 = (bf16[2,1,64,1536]{3,2,1,0:T(8,128)(2,1)}, bf16[2,1,64,1536]{3,2,1,0:T(8,128)(2,1)}, u32[]{:S(2)}, u32[]{:S(2)}) collective-permute-start(bf16[2,1,64,1536]{3,2,1,0:T(8,128)(2,1)} %collective-permute-done.11.rest_9_), channel_id=1, source_target_pairs={{4,0},{8,4},{12,8},{14,12},{10,14},{6,10},{2,6},{0,2},{5,1},{9,5},... | collective-permute-start | bytes 1179656 | tf_op jit(solution)/shard_map/ppermute | solution.py:70
  104.9 15.9 %collective-permute-start.21 = (bf16[2,1,64,1536]{3,2,1,0:T(8,128)(2,1)}, bf16[2,1,64,1536]{3,2,1,0:T(8,128)(2,1)}, u32[]{:S(2)}, u32[]{:S(2)}) collective-permute-start(bf16[2,1,64,1536]{3,2,1,0:T(8,128)(2,1)} %collective-permute-done.20.rest_18_), channel_id=1, source_target_pairs={{4,0},{8,4},{12,8},{14,12},{10,14},{6,10},{2,6},{0,2},{5,1},{9,5},... | collective-permute-start | bytes 1179656 | tf_op jit(solution)/shard_map/ppermute | solution.py:64
  107.4 13.4 %collective-permute-start.14 = (bf16[2,1,64,1536]{3,2,1,0:T(8,128)(2,1)}, bf16[2,1,64,1536]{3,2,1,0:T(8,128)(2,1)}, u32[]{:S(2)}, u32[]{:S(2)}) collective-permute-start(bf16[2,1,64,1536]{3,2,1,0:T(8,128)(2,1)} %collective-permute-done.12.rest_10_), channel_id=1, source_target_pairs={{0,4},{4,8},{8,12},{12,14},{14,10},{10,6},{6,2},{2,0},{1,5},{5,9},... | collective-permute-start | bytes 1179656 | tf_op jit(solution)/shard_map/ppermute | solution.py:62

commit v9 on v7

--- a/solution.py
+++ b/solution.py
@@ -175,34 +175,6 @@
     above = shift(stacked[:, tile_blocks - 1 :], "row", row_count, 1)
     below = shift(stacked[:, :1], "row", row_count, -1)
 
-    edge_cap = min(3 if row_count >= 2 else 4, tile_blocks)
-    main_cap = edge_cap - 1 if col_count >= 3 else edge_cap
-    entries = cycle_list[0, 0]
-    right_entries = shift(entries, "col", col_count, -1)
-    left_entries = shift(entries, "col", col_count, 1)
-    to_right, _, _ = side_slots(right_entries, 2, tile_blocks, edge_cap)
-    to_left, _, _ = side_slots(left_entries, 2 + tile_blocks, tile_blocks, edge_cap)
-    right_payload = jnp.take(stacked, to_right, axis=1)
-    left_payload = jnp.take(stacked, to_left, axis=1)
-    cycle_sources = [above, below]
-    cycle_sources.append(shift(right_payload[:, :main_cap], "col", col_count, 1))
-    cycle_sources.append(shift(left_payload[:, :main_cap], "col", col_count, -1))
-    if main_cap < edge_cap:
-        last = col_count - 1
-        cycle_sources.append(lax.ppermute(right_payload[:, main_cap:], "col", [(last - 1, last)]))
-        cycle_sources.append(lax.ppermute(left_payload[:, main_cap:], "col", [(1, 0)]))
-
-    _, is_left, left_rank = side_slots(entries, 2, tile_blocks, edge_cap)
-    _, is_right, right_rank = side_slots(entries, 2 + tile_blocks, tile_blocks, edge_cap)
-    side_rank = jnp.where(is_left, left_rank, right_rank)
-    overflow = side_rank >= main_cap
-    cycle_src = jnp.where(
-        entries == 0,
-        0,
-        jnp.where(entries == 1, 1, 2 + is_right.astype(jnp.int32) + 2 * overflow.astype(jnp.int32)),
-    )
-    cycle_idx = jnp.where(entries < 2, 0, jnp.where(overflow, side_rank - main_cap, side_rank))
-
     far_source = stacked[:, 0::4]
     dilated_entries = dilated_list[0, 0]
     hop_slot = dilated_entries // distant_rows
@@ -218,6 +190,34 @@
             route = [((i + distance) % col_count, i) for i in range(col_count)]
             far_sources.append(lax.ppermute(far_source, "col", route))
             lookup.append([(hop - 1, r) for r in range(distant_rows)])
+    entries, _ = lax.optimization_barrier((cycle_list[0, 0], far_sources[0]))
+    edge_cap = min(3 if row_count >= 2 else 4, tile_blocks)
+    main_cap = edge_cap - 1 if col_count >= 3 else edge_cap
+    right_entries = shift(entries, "col", col_count, -1)
+    left_entries = shift(entries, "col", col_count, 1)
+    to_right, _, _ = side_slots(right_entries, 2, tile_blocks, edge_cap)
+    to_left, _, _ = side_slots(left_entries, 2 + tile_blocks, tile_blocks, edge_cap)
+    right_payload = jnp.take(stacked, to_right, axis=1)
+    left_payload = jnp.take(stacked, to_left, axis=1)
+    cycle_sources = [above, below]
+    cycle_sources.append(shift(right_payload[:, :main_cap], "col", col_count, 1))
+    cycle_sources.append(shift(left_payload[:, :main_cap], "col", col_count, -1))
+    if main_cap < edge_cap:
+        last = col_count - 1
+        cycle_sources.append(lax.ppermute(right_payload[:, main_cap:], "col", [(last - 1, last)]))
+        cycle_sources.append(lax.ppermute(left_payload[:, main_cap:], "col", [(1, 0)]))
+
+    _, is_left, left_rank = side_slots(entries, 2, tile_blocks, edge_cap)
+    _, is_right, right_rank = side_slots(entries, 2 + tile_blocks, tile_blocks, edge_cap)
+    side_rank = jnp.where(is_left, left_rank, right_rank)
+    overflow = side_rank >= main_cap
+    cycle_src = jnp.where(
+        entries == 0,
+        0,
+        jnp.where(entries == 1, 1, 2 + is_right.astype(jnp.int32) + 2 * overflow.astype(jnp.int32)),
+    )
+    cycle_idx = jnp.where(entries < 2, 0, jnp.where(overflow, side_rank - main_cap, side_rank))
+
     lookup_src = jnp.array([[a for a, _ in row] for row in lookup], dtype=jnp.int32)
     lookup_idx = jnp.array([[b for _, b in row] for row in lookup], dtype=jnp.int32)
     far_src = len(cycle_sources) + lookup_src[hop_slot, far_row]

time: 136 us -> 139 us (1.022)
  starting transfers between devices: 37.9 us -> 33.5 us
  other arithmetic: 12.1 us -> 15 us
  waiting for transfers between devices: 50.6 us -> 52.9 us
  local copies, waits for them, and re-layouts: 19.8 us -> 21.8 us
    ppermute x6, waiting for transfers between devices: 0.02 us -> 22 us  [ring_gather(): ahead = lax.ppermute(ahead, 'col', forward)]
    ppermute x6, waiting for transfers between devices: 42.3 us -> 21 us  [ring_gather(): behind = lax.ppermute(behind, 'col', backward)]
    ppermute x6, waiting for transfers between devices: 0.02 us -> 5.65 us  [shift(): return lax.ppermute(x, axis, pairs)]
    ppermute x6, starting transfers between devices: 17.9 us -> 13.4 us  [shift(): return lax.ppermute(x, axis, pairs)]
    ppermute x1, waiting for transfers between devices: 7.49 us -> 3.54 us  [ring_gather(): arrays.append(lax.ppermute(behind, 'col', backward))]
    ppermute x6, starting transfers between devices: 10.8 us -> 14.4 us  [ring_gather(): behind = lax.ppermute(behind, 'col', backward)]
    ppermute x6, starting transfers between devices: 3.96 us -> 1.03 us  [ring_gather(): ahead = lax.ppermute(ahead, 'col', forward)]
    another operation x4 -> x5, other arithmetic: 2.31 us -> 3.02 us
  transfers between devices with their start and end apart: 22 -> 22, of which waited for: 6 -> 9; matrix products, arithmetic and copies ran while one was open for 23% -> 23% of each run, Pallas kernels for 0% -> 0%
where the time goes in v9:
time: 139 us; the launch traced here: 138 us
  waiting for transfers between devices  52.9 us (38%)
  starting transfers between devices  33.5 us (24%)
  local copies, waits for them, and re-layouts  21.8 us (16%)
  other arithmetic  15 us (11%)
  Pallas kernels  14.2 us (10%)
    ppermute x6, waiting for transfers between devices, ring_gather(): ahead = lax.ppermute(ahead, 'col', forward)  22 us
    ppermute x6, waiting for transfers between devices, ring_gather(): behind = lax.ppermute(behind, 'col', backward)  21 us
    ppermute x6, starting transfers between devices, ring_gather(): behind = lax.ppermute(behind, 'col', backward)  14.4 us
    pallas_call x1, Pallas kernels, gather_attend(): pl.pallas_call(kernel, out_shape=jax.ShapeDtypeStruct((token_count, width...  14.2 us
    ppermute x6, starting transfers between devices, shift(): return lax.ppermute(x, axis, pairs)  13.4 us
    ppermute x6, waiting for transfers between devices, shift(): return lax.ppermute(x, axis, pairs)  5.65 us
    ppermute x2, local copies, waits for them, and re-layouts, shift(): return lax.ppermute(x, axis, pairs)  4.19 us
    gather x1, local copies, waits for them, and re-layouts, per_device(): right_payload = jnp.take(stacked, to_right, axis=1)  3.56 us
  transfers between devices with their start and end apart: 22, of which 9 were waited for; matrix products, arithmetic and copies ran while one was open for 23% of the time, Pallas kernels for 0%

profile of v9, /device:TPU:0, one launch (start us, length us, event | category | flops | bytes accessed | tf_op | source)
XLA Modules:
  0.0 137.9 jit_solution(12602435178755262444)
XLA Ops:
  0.0 1.0 exponential_bitcast_fusion.1
  1.0 1.0 exponential_bitcast_fusion
  2.0 1.8 %fusion = bf16[8,1,64,1536]{3,2,0,1:T(8,128)(2,1)S(1)} fusion(bf16[8,1,64,1536]{3,2,1,0:T(8,128)(2,1)} %param.15, f32[8,2,1536]{2,1,0:T(2,128)S(1)} %exponential_bitcast_fusion), kind=kLoop, calls=%fused_computation.7 | loop fusion | flops 2359296 | bytes 3244032 | tf_op jit(solution)/shard_map/convert_element_type | solution.py:24
  3.8 0.3 fusion.1
  4.1 0.3 maximum_bitcast_fusion.own_hbm
  4.6 3.0 %collective-permute-start.16 = (bf16[2,1,64,1536]{3,2,1,0:T(8,128)(2,1)S(1)}, bf16[2,1,64,1536]{3,2,1,0:T(8,128)(2,1)S(1)}, u32[]{:S(2)}, u32[]{:S(2)}) collective-permute-start(bf16[2,1,64,1536]{3,2,1,0:T(8,128)(2,1)S(1)} %get-tuple-element.10), channel_id=1, source_target_pairs={{4,0},{8,4},{12,8},{14,12},{10,14},{6,10},{2,6},{0,2},{5,1},{9,5},... | collective-permute-start | bytes 1179656 | tf_op jit(solution)/shard_map/ppermute | solution.py:70
  7.6 0.1 collective-permute-start.15
  7.7 1.9 %collective-permute-start.9 = (bf16[2,1,64,1536]{3,2,1,0:T(8,128)(2,1)S(1)}, bf16[2,1,64,1536]{3,2,1,0:T(8,128)(2,1)S(1)}, u32[]{:S(2)}, u32[]{:S(2)}) collective-permute-start(bf16[2,1,64,1536]{3,2,1,0:T(8,128)(2,1)S(1)} %get-tuple-element.11), channel_id=1, source_target_pairs={{4,0},{8,4},{12,8},{14,12},{10,14},{6,10},{2,6},{0,2},{5,1},{9,5},... | collective-permute-start | bytes 1179656 | tf_op jit(solution)/shard_map/ppermute | solution.py:70
  9.6 0.1 collective-permute-start
  9.8 1.0 fusion.14
  10.7 1.3 collective-permute-start.2
  12.0 14.6 %collective-permute-done.rest_6_ = bf16[2,1,64,1536]{3,2,1,0:T(8,128)(2,1)S(1)} collective-permute-done((bf16[2,1,64,1536]{3,2,1,0:T(8,128)(2,1)S(1)}, bf16[2,1,64,1536]{3,2,1,0:T(8,128)(2,1)S(1)}, u32[]{:S(2)}, u32[]{:S(2)}) %collective-permute-start) | collective-permute-done | bytes 393248 | tf_op jit(solution)/shard_map/ppermute | solution.py:67
  26.6 3.5 %collective-permute-start.5 = (s32[4]{0:T(128)S(1)}, s32[4]{0:T(128)S(1)}, u32[]{:S(2)}, u32[]{:S(2)}) collective-permute-start(s32[4]{0:T(128)S(1)} %bitcast.92), channel_id=1, source_target_pairs={{0,2},{2,4},{4,6},{6,8},{8,10},{10,12},{12,14},{1,3},{3,5},{5,7},{... | collective-permute-start | bytes 56 | tf_op jit(solution)/shard_map/ppermute | solution.py:34
  30.1 1.3 collective-permute-done.5
  31.4 1.3 collective-permute-start.1
  32.7 0.2 reduce-window.37
  32.9 0.1 select_reduce_fusion
  33.0 1.3 collective-permute-start.3
  34.3 4.4 %collective-permute-done.3 = s32[4]{0:T(128)S(1)} collective-permute-done((s32[4]{0:T(128)S(1)}, s32[4]{0:T(128)S(1)}, u32[]{:S(2)}, u32[]{:S(2)}) %collective-permute-start.3) | collective-permute-done | bytes 48 | tf_op jit(solution)/shard_map/ppermute | solution.py:34
  38.7 3.0 %collective-permute-start.18 = (bf16[2,1,64,1536]{3,2,1,0:T(8,128)(2,1)S(1)}, bf16[2,1,64,1536]{3,2,1,0:T(8,128)(2,1)S(1)}, u32[]{:S(2)}, u32[]{:S(2)}) collective-permute-start(bf16[2,1,64,1536]{3,2,1,0:T(8,128)(2,1)S(1)} %collective-permute-done.16.rest_14_), channel_id=1, source_target_pairs={{4,0},{8,4},{12,8},{14,12},{10,14},{6,10},{2,6},{0,2},{5,1},{9,5},... | collective-permute-start | bytes 1179656 | tf_op jit(solution)/shard_map/ppermute | solution.py:70
  41.7 0.5 compare_and_fusion.3
  42.2 1.3 reduce-window.36
  43.5 0.6 add_bitcast_fusion.3
  44.1 0.1 select_reduce_fusion.1
  44.3 3.6 %gather_fusion.3 = bf16[3,2,64,1536]{3,2,1,0:T(8,128)(2,1)} fusion(bf16[2,8,64,1536]{3,2,1,0:T(8,128)(2,1)} %copy-done.2, s32[1024]{0:T(1024)S(1)} %pad_clamp_fusion.1), kind=kCustom, calls=%fused_computation.clone | custom fusion | bytes 2359308 | tf_op jit(solution)/shard_map/jit(_take)/gather | solution.py:200
  47.8 1.4 %select_bitcast_fusion.1 = bf16[2,3,64,1536]{3,2,0,1:T(8,128)(2,1)S(1)} fusion(bf16[3,2,64,1536]{3,2,1,0:T(8,128)(2,1)} %gather_fusion.3, pred[3]{0:T(512)(128)(4,1)S(1)} %compare_and_fusion.1), kind=kLoop, calls=%fused_computation.11 | loop fusion | flops 589824 | bytes 2359299 | tf_op jit(solution)/shard_map/jit(_take)/select_n | solution.py:200
  49.3 1.1 copy-done.4
  50.4 0.9 slice.49
  51.3 3.6 %gather_fusion.4 = bf16[3,2,64,1536]{3,2,1,0:T(8,128)(2,1)} fusion(bf16[2,8,64,1536]{3,2,1,0:T(8,128)(2,1)} %copy-done.2, s32[1024]{0:T(1024)S(1)} %pad_clamp_fusion), kind=kCustom, calls=%fused_computation.1.clone | custom fusion | bytes 2359308 | tf_op jit(solution)/shard_map/jit(_take)/gather | solution.py:201
  54.9 1.5 %select_bitcast_fusion = bf16[2,3,64,1536]{3,2,0,1:T(8,128)(2,1)S(1)} fusion(bf16[3,2,64,1536]{3,2,1,0:T(8,128)(2,1)} %gather_fusion.4, pred[3]{0:T(512)(128)(4,1)S(1)} %compare_and_fusion), kind=kLoop, calls=%fused_computation.10 | loop fusion | flops 589824 | bytes 2359299 | tf_op jit(solution)/shard_map/jit(_take)/select_n | solution.py:201
  56.4 1.1 slice.50
  57.4 0.8 collective-permute-start.17
  58.2 1.3 collective-permute-start.11
  59.5 4.8 %collective-permute-start.4 = (bf16[2,2,64,1536]{3,2,0,1:T(8,128)(2,1)}, bf16[2,2,64,1536]{3,2,0,1:T(8,128)(2,1)}, u32[]{:S(2)}, u32[]{:S(2)}) collective-permute-start(bf16[2,2,64,1536]{3,2,0,1:T(8,128)(2,1)} %slice.49), channel_id=1, source_target_pairs={{0,2},{2,4},{4,6},{6,8},{8,10},{10,12},{12,14},{1,3},{3,5},{5,7},{... | collective-permute-start | bytes 2359304 | tf_op jit(solution)/shard_map/ppermute | solution.py:34
  64.3 1.3 collective-permute-start.6
  65.6 0.6 dynamic_slice.3
  66.2 0.6 gather_fusion
  66.9 1.3 fusion.12
  68.2 0.6 gather_fusion.1
  68.8 0.6 gather_fusion.2
  69.4 1.8 %slice.51 = bf16[2,1,64,1536]{3,2,0,1:T(8,128)(2,1)} slice(bf16[2,3,64,1536]{3,2,0,1:T(8,128)(2,1)} %copy-done.4), slice={[0:2], [2:3], [0:64], [0:1536]} | slice | bytes 786432 | tf_op jit(solution)/shard_map/slice | solution.py:207
  71.3 6.6 %collective-permute-done.17.rest_15_ = bf16[2,1,64,1536]{3,2,1,0:T(8,128)(2,1)S(1)} collective-permute-done((bf16[2,1,64,1536]{3,2,1,0:T(8,128)(2,1)S(1)}, bf16[2,1,64,1536]{3,2,1,0:T(8,128)(2,1)S(1)}, u32[]{:S(2)}, u32[]{:S(2)}) %collective-permute-start.17) | collective-permute-done | bytes 393248 | tf_op jit(solution)/shard_map/ppermute | solution.py:67
  77.9 1.4 %collective-permute-start.7 = (bf16[2,1,64,1536]{3,2,0,1:T(8,128)(2,1)}, bf16[2,1,64,1536]{3,2,0,1:T(8,128)(2,1)}, u32[]{:S(2)}, u32[]{:S(2)}) collective-permute-start(bf16[2,1,64,1536]{3,2,0,1:T(8,128)(2,1)} %slice.51), channel_id=1, source_target_pairs={{12,14},{13,15},{28,30},{29,31}} | collective-permute-start | bytes 1179656 | tf_op jit(solution)/shard_map/ppermute | solution.py:207
  79.3 6.6 %collective-permute-done.11.rest_9_ = bf16[2,1,64,1536]{3,2,1,0:T(8,128)(2,1)} collective-permute-done((bf16[2,1,64,1536]{3,2,1,0:T(8,128)(2,1)S(1)}, bf16[2,1,64,1536]{3,2,1,0:T(8,128)(2,1)}, u32[]{:S(2)}, u32[]{:S(2)}) %collective-permute-start.11) | collective-permute-done | bytes 393248 | tf_op jit(solution)/shard_map/ppermute | solution.py:70
  85.9 2.6 %collective-permute-start.20 = (bf16[2,1,64,1536]{3,2,1,0:T(8,128)(2,1)S(1)}, bf16[2,1,64,1536]{3,2,1,0:T(8,128)(2,1)}, u32[]{:S(2)}, u32[]{:S(2)}) collective-permute-start(bf16[2,1,64,1536]{3,2,1,0:T(8,128)(2,1)S(1)} %collective-permute-done.18.rest_16_), channel_id=1, source_target_pairs={{4,0},{8,4},{12,8},{14,12},{10,14},{6,10},{2,6},{0,2},{5,1},{9,5},... | collective-permute-start | bytes 1179656 | tf_op jit(solution)/shard_map/ppermute | solution.py:70
  88.5 0.6 broadcast_add_fusion.2
  89.1 0.7 convert_bitcast_fusion.2
  89.8 0.2 reduce-window.34
  90.0 0.7 reduce-window.35
  90.7 1.8 %slice.52 = bf16[2,1,64,1536]{3,2,0,1:T(8,128)(2,1)} slice(bf16[2,3,64,1536]{3,2,0,1:T(8,128)(2,1)} %copy-done.3), slice={[0:2], [2:3], [0:64], [0:1536]} | slice | bytes 786432 | tf_op jit(solution)/shard_map/slice | solution.py:208
  92.4 1.3 collective-permute-start.8
  93.7 14.4 %collective-permute-done.20.rest_18_ = bf16[2,1,64,1536]{3,2,1,0:T(8,128)(2,1)} collective-permute-done((bf16[2,1,64,1536]{3,2,1,0:T(8,128)(2,1)S(1)}, bf16[2,1,64,1536]{3,2,1,0:T(8,128)(2,1)}, u32[]{:S(2)}, u32[]{:S(2)}) %collective-permute-start.20) | collective-permute-done | bytes 393248 | tf_op jit(solution)/shard_map/ppermute | solution.py:70
  108.1 2.6 %collective-permute-start.13 = (bf16[2,1,64,1536]{3,2,1,0:T(8,128)(2,1)}, bf16[2,1,64,1536]{3,2,1,0:T(8,128)(2,1)}, u32[]{:S(2)}, u32[]{:S(2)}) collective-permute-start(bf16[2,1,64,1536]{3,2,1,0:T(8,128)(2,1)} %collective-permute-done.11.rest_9_), channel_id=1, source_target_pairs={{4,0},{8,4},{12,8},{14,12},{10,14},{6,10},{2,6},{0,2},{5,1},{9,5},... | collective-permute-start | bytes 1179656 | tf_op jit(solution)/shard_map/ppermute | solution.py:70
  110.7 2.0 %collective-permute-start.21 = (bf16[2,1,64,1536]{3,2,1,0:T(8,128)(2,1)}, bf16[2,1,64,1536]{3,2,1,0:T(8,128)(2,1)}, u32[]{:S(2)}, u32[]{:S(2)}) collective-permute-start(bf16[2,1,64,1536]{3,2,1,0:T(8,128)(2,1)} %collective-permute-done.20.rest_18_), channel_id=1, source_target_pairs={{4,0},{8,4},{12,8},{14,12},{10,14},{6,10},{2,6},{0,2},{5,1},{9,5},... | collective-permute-start | bytes 1179656 | tf_op jit(solution)/shard_map/ppermute | solution.py:64
  112.8 0.7 compare_select_fusion.13
  113.4 0.8 add_bitcast_fusion
  114.2 0.1 copy.29
  114.3 0.1 reshape.372.table_ref
  114.4 2.1 %copy.30.rest_2_ = bf16[2,2,64,1536]{3,2,1,0:T(8,128)(2,1)} copy(bf16[2,2,64,1536]{3,2,0,1:T(8,128)(2,1)} %collective-permute-done.4) | data formatting | bytes 1572864 | tf_op jit(solution)/shard_map/ppermute | solution.py:34
  116.5 2.1 %copy.31.rest_3_ = bf16[2,2,64,1536]{3,2,1,0:T(8,128)(2,1)} copy(bf16[2,2,64,1536]{3,2,0,1:T(8,128)(2,1)} %collective-permute-done.6) | data formatting | bytes 1572864 | tf_op jit(solution)/shard_map/ppermute | solution.py:34
  118.5 0.8 collective-permute-done.19.rest_17_
  119.3 3.5 %collective-permute-done.21.rest_19_ = bf16[2,1,64,1536]{3,2,1,0:T(8,128)(2,1)} collective-permute-done((bf16[2,1,64,1536]{3,2,1,0:T(8,128)(2,1)}, bf16[2,1,64,1536]{3,2,1,0:T(8,128)(2,1)}, u32[]{:S(2)}, u32[]{:S(2)}) %collective-permute-start.21) | collective-permute-done | bytes 393248 | tf_op jit(solution)/shard_map/ppermute | solution.py:64
  122.8 0.7 collective-permute-done.14.rest_12_
  123.5 14.2 %shard_map.100 = bf16[512,1536]{1,0:T(8,128)(2,1)} custom-call(s32[16]{0:T(128)S(1)} %reshape.372.table_ref, bf16[512,1536]{1,0:T(8,128)(2,1)} %bitcast.89, bf16[2,8,64,1536]{3,2,1,0:T(8,128)(2,1)} %copy-done.2, bf16[2,1,64,1536]{3,2,1,0:T(8,128)(2,1)S(1)} %collective-permute-done.1.rest_0_, bf16[2,1,64,1536]{3,2,1,0:T(8,128)(2,1)S(1)} %collective-permute-done.2.rest_1_, ...), custom_call_target="tpu_custom_call" | custom-call | flops 3221225472 | bytes 9437184 | tf_op jit(solution)/shard_map/pallas_call | solution.py:142
  (48 shorter events, 0.4 us)
Async XLA Ops:
  1.9 1.9 %copy-start.5 = (bf16[8,1,64,1536]{3,2,1,0:T(8,128)(2,1)S(1)}, bf16[8,1,64,1536]{3,2,1,0:T(8,128)(2,1)}, u32[]{:S(2)}) copy-start(bf16[8,1,64,1536]{3,2,1,0:T(8,128)(2,1)} %param.13) | copy-start | bytes 4718596
  4.4 5.3 %copy-start.2 = (bf16[2,8,64,1536]{3,2,1,0:T(8,128)(2,1)}, bf16[2,8,64,1536]{3,2,1,0:T(8,128)(2,1)S(1)}, u32[]{:S(2)}) copy-start(bf16[2,8,64,1536]{3,2,1,0:T(8,128)(2,1)S(1)} %maximum_bitcast_fusion.own_hbm) | copy-start | bytes 9437188
  4.5 22.1 %copy-start.6 = (s32[1,1,4]{2,1,0:T(1,128)S(1)}, s32[1,1,4]{2,1,0:T(1,128)}, u32[]{:S(2)}) copy-start(s32[1,1,4]{2,1,0:T(1,128)} %param.17) | copy-start | bytes 52
  4.6 28.4 %collective-permute-start.16 = (bf16[2,1,64,1536]{3,2,1,0:T(8,128)(2,1)S(1)}, bf16[2,1,64,1536]{3,2,1,0:T(8,128)(2,1)S(1)}, u32[]{:S(2)}, u32[]{:S(2)}) collective-permute-start(bf16[2,1,64,1536]{3,2,1,0:T(8,128)(2,1)S(1)} %get-tuple-element.10), channel_id=1, source_target_pairs={{4,0},{8,4},{12,8},{14,12},{10,14},{6,10},{2,6},{0,2},{5,1},{9,5},... | collective-permute-start | bytes 1179656 | tf_op jit(solution)/shard_map/ppermute | solution.py:70
  7.6 49.8 %collective-permute-start.15 = (bf16[2,1,64,1536]{3,2,1,0:T(8,128)(2,1)S(1)}, bf16[2,1,64,1536]{3,2,1,0:T(8,128)(2,1)S(1)}, u32[]{:S(2)}, u32[]{:S(2)}) collective-permute-start(bf16[2,1,64,1536]{3,2,1,0:T(8,128)(2,1)S(1)} %get-tuple-element.10), channel_id=1, source_target_pairs={{0,4},{4,8},{8,12},{12,14},{14,10},{10,6},{6,2},{2,0},{1,5},{5,9},... | collective-permute-start | bytes 1179656 | tf_op jit(solution)/shard_map/ppermute | solution.py:67
  7.7 49.7 %collective-permute-start.9 = (bf16[2,1,64,1536]{3,2,1,0:T(8,128)(2,1)S(1)}, bf16[2,1,64,1536]{3,2,1,0:T(8,128)(2,1)S(1)}, u32[]{:S(2)}, u32[]{:S(2)}) collective-permute-start(bf16[2,1,64,1536]{3,2,1,0:T(8,128)(2,1)S(1)} %get-tuple-element.11), channel_id=1, source_target_pairs={{4,0},{8,4},{12,8},{14,12},{10,14},{6,10},{2,6},{0,2},{5,1},{9,5},... | collective-permute-start | bytes 1179656 | tf_op jit(solution)/shard_map/ppermute | solution.py:70
  9.6 17.0 %collective-permute-start = (bf16[2,1,64,1536]{3,2,1,0:T(8,128)(2,1)S(1)}, bf16[2,1,64,1536]{3,2,1,0:T(8,128)(2,1)S(1)}, u32[]{:S(2)}, u32[]{:S(2)}) collective-permute-start(bf16[2,1,64,1536]{3,2,1,0:T(8,128)(2,1)S(1)} %get-tuple-element.11), channel_id=1, source_target_pairs={{0,4},{4,8},{8,12},{12,14},{14,10},{10,6},{6,2},{2,0},{1,5},{5,9},... | collective-permute-start | bytes 1179656 | tf_op jit(solution)/shard_map/ppermute | solution.py:67
  10.7 47.5 %collective-permute-start.2 = (bf16[2,1,64,1536]{3,2,1,0:T(8,128)(2,1)}, bf16[2,1,64,1536]{3,2,1,0:T(8,128)(2,1)S(1)}, u32[]{:S(2)}, u32[]{:S(2)}) collective-permute-start(bf16[2,1,64,1536]{3,2,1,0:T(8,128)(2,1)} %get-tuple-element.8), channel_id=1, source_target_pairs={{1,0},{3,2},{5,4},{7,6},{9,8},{11,10},{13,12},{15,14},{17,16},{19,... | collective-permute-start | bytes 1179656 | tf_op jit(solution)/shard_map/ppermute | solution.py:34
  26.6 4.8 %collective-permute-start.5 = (s32[4]{0:T(128)S(1)}, s32[4]{0:T(128)S(1)}, u32[]{:S(2)}, u32[]{:S(2)}) collective-permute-start(s32[4]{0:T(128)S(1)} %bitcast.92), channel_id=1, source_target_pairs={{0,2},{2,4},{4,6},{6,8},{8,10},{10,12},{12,14},{1,3},{3,5},{5,7},{... | collective-permute-start | bytes 56 | tf_op jit(solution)/shard_map/ppermute | solution.py:34
  31.4 28.2 %collective-permute-start.1 = (bf16[2,1,64,1536]{3,2,1,0:T(8,128)(2,1)}, bf16[2,1,64,1536]{3,2,1,0:T(8,128)(2,1)S(1)}, u32[]{:S(2)}, u32[]{:S(2)}) collective-permute-start(bf16[2,1,64,1536]{3,2,1,0:T(8,128)(2,1)} %get-tuple-element.9), channel_id=1, source_target_pairs={{0,1},{2,3},{4,5},{6,7},{8,9},{10,11},{12,13},{14,15},{16,17},{18,... | collective-permute-start | bytes 1179656 | tf_op jit(solution)/shard_map/ppermute | solution.py:34
  33.0 5.7 %collective-permute-start.3 = (s32[4]{0:T(128)S(1)}, s32[4]{0:T(128)S(1)}, u32[]{:S(2)}, u32[]{:S(2)}) collective-permute-start(s32[4]{0:T(128)S(1)} %bitcast.93), channel_id=1, source_target_pairs={{2,0},{4,2},{6,4},{8,6},{10,8},{12,10},{14,12},{3,1},{5,3},{7,5},{... | collective-permute-start | bytes 56 | tf_op jit(solution)/shard_map/ppermute | solution.py:34
  38.7 25.6 %collective-permute-start.18 = (bf16[2,1,64,1536]{3,2,1,0:T(8,128)(2,1)S(1)}, bf16[2,1,64,1536]{3,2,1,0:T(8,128)(2,1)S(1)}, u32[]{:S(2)}, u32[]{:S(2)}) collective-permute-start(bf16[2,1,64,1536]{3,2,1,0:T(8,128)(2,1)S(1)} %collective-permute-done.16.rest_14_), channel_id=1, source_target_pairs={{4,0},{8,4},{12,8},{14,12},{10,14},{6,10},{2,6},{0,2},{5,1},{9,5},... | collective-permute-start | bytes 1179656 | tf_op jit(solution)/shard_map/ppermute | solution.py:70
  49.3 1.1 copy-start.4
  54.9 10.7 %copy-start.7 = (s32[1,1,4]{2,1,0:T(1,128)S(1)}, s32[1,1,4]{2,1,0:T(1,128)}, u32[]{:S(2)}) copy-start(s32[1,1,4]{2,1,0:T(1,128)} %param.18) | copy-start | bytes 52
  54.9 10.8 %copy-start = (s32[8]{0:T(128)S(1)}, s32[8]{0:T(128)}, u32[]{:S(2)}) copy-start(s32[8]{0:T(128)} %constant.99.clone) | copy-start | bytes 100
  56.3 8.0 %copy-start.3 = (bf16[2,3,64,1536]{3,2,0,1:T(8,128)(2,1)}, bf16[2,3,64,1536]{3,2,0,1:T(8,128)(2,1)S(1)}, u32[]{:S(2)}) copy-start(bf16[2,3,64,1536]{3,2,0,1:T(8,128)(2,1)S(1)} %select_bitcast_fusion) | copy-start | bytes 3538948
  56.4 11.8 %copy-start.1 = (s32[7,2]{1,0:T(8,128)S(1)}, s32[7,2]{1,0:T(8,128)}, u32[]{:S(2)}) copy-start(s32[7,2]{1,0:T(8,128)} %constant.100.clone) | copy-start | bytes 172
  57.4 31.1 %collective-permute-start.10 = (bf16[2,1,64,1536]{3,2,1,0:T(8,128)(2,1)S(1)}, bf16[2,1,64,1536]{3,2,1,0:T(8,128)(2,1)S(1)}, u32[]{:S(2)}, u32[]{:S(2)}) collective-permute-start(bf16[2,1,64,1536]{3,2,1,0:T(8,128)(2,1)S(1)} %collective-permute-done.rest_6_), channel_id=1, source_target_pairs={{0,4},{4,8},{8,12},{12,14},{14,10},{10,6},{6,2},{2,0},{1,5},{5,9},... | collective-permute-start | bytes 1179656 | tf_op jit(solution)/shard_map/ppermute | solution.py:67
  57.4 20.5 %collective-permute-start.17 = (bf16[2,1,64,1536]{3,2,1,0:T(8,128)(2,1)S(1)}, bf16[2,1,64,1536]{3,2,1,0:T(8,128)(2,1)S(1)}, u32[]{:S(2)}, u32[]{:S(2)}) collective-permute-start(bf16[2,1,64,1536]{3,2,1,0:T(8,128)(2,1)S(1)} %collective-permute-done.15.rest_13_), channel_id=1, source_target_pairs={{0,4},{4,8},{8,12},{12,14},{14,10},{10,6},{6,2},{2,0},{1,5},{5,9},... | collective-permute-start | bytes 1179656 | tf_op jit(solution)/shard_map/ppermute | solution.py:67
  58.2 27.7 %collective-permute-start.11 = (bf16[2,1,64,1536]{3,2,1,0:T(8,128)(2,1)S(1)}, bf16[2,1,64,1536]{3,2,1,0:T(8,128)(2,1)}, u32[]{:S(2)}, u32[]{:S(2)}) collective-permute-start(bf16[2,1,64,1536]{3,2,1,0:T(8,128)(2,1)S(1)} %collective-permute-done.9.rest_7_), channel_id=1, source_target_pairs={{4,0},{8,4},{12,8},{14,12},{10,14},{6,10},{2,6},{0,2},{5,1},{9,5},... | collective-permute-start | bytes 1179656 | tf_op jit(solution)/shard_map/ppermute | solution.py:70
  59.5 51.2 %collective-permute-start.4 = (bf16[2,2,64,1536]{3,2,0,1:T(8,128)(2,1)}, bf16[2,2,64,1536]{3,2,0,1:T(8,128)(2,1)}, u32[]{:S(2)}, u32[]{:S(2)}) collective-permute-start(bf16[2,2,64,1536]{3,2,0,1:T(8,128)(2,1)} %slice.49), channel_id=1, source_target_pairs={{0,2},{2,4},{4,6},{6,8},{8,10},{10,12},{12,14},{1,3},{3,5},{5,7},{... | collective-permute-start | bytes 2359304 | tf_op jit(solution)/shard_map/ppermute | solution.py:34
  64.3 48.5 %collective-permute-start.6 = (bf16[2,2,64,1536]{3,2,0,1:T(8,128)(2,1)}, bf16[2,2,64,1536]{3,2,0,1:T(8,128)(2,1)}, u32[]{:S(2)}, u32[]{:S(2)}) collective-permute-start(bf16[2,2,64,1536]{3,2,0,1:T(8,128)(2,1)} %slice.50), channel_id=1, source_target_pairs={{2,0},{4,2},{6,4},{8,6},{10,8},{12,10},{14,12},{3,1},{5,3},{7,5},{... | collective-permute-start | bytes 2359304 | tf_op jit(solution)/shard_map/ppermute | solution.py:34
  77.9 14.5 %collective-permute-start.7 = (bf16[2,1,64,1536]{3,2,0,1:T(8,128)(2,1)}, bf16[2,1,64,1536]{3,2,0,1:T(8,128)(2,1)}, u32[]{:S(2)}, u32[]{:S(2)}) collective-permute-start(bf16[2,1,64,1536]{3,2,0,1:T(8,128)(2,1)} %slice.51), channel_id=1, source_target_pairs={{12,14},{13,15},{28,30},{29,31}} | collective-permute-start | bytes 1179656 | tf_op jit(solution)/shard_map/ppermute | solution.py:207
  85.9 22.2 %collective-permute-start.20 = (bf16[2,1,64,1536]{3,2,1,0:T(8,128)(2,1)S(1)}, bf16[2,1,64,1536]{3,2,1,0:T(8,128)(2,1)}, u32[]{:S(2)}, u32[]{:S(2)}) collective-permute-start(bf16[2,1,64,1536]{3,2,1,0:T(8,128)(2,1)S(1)} %collective-permute-done.18.rest_16_), channel_id=1, source_target_pairs={{4,0},{8,4},{12,8},{14,12},{10,14},{6,10},{2,6},{0,2},{5,1},{9,5},... | collective-permute-start | bytes 1179656 | tf_op jit(solution)/shard_map/ppermute | solution.py:70
  88.5 19.6 %collective-permute-start.12 = (bf16[2,1,64,1536]{3,2,1,0:T(8,128)(2,1)S(1)}, bf16[2,1,64,1536]{3,2,1,0:T(8,128)(2,1)}, u32[]{:S(2)}, u32[]{:S(2)}) collective-permute-start(bf16[2,1,64,1536]{3,2,1,0:T(8,128)(2,1)S(1)} %collective-permute-done.10.rest_8_), channel_id=1, source_target_pairs={{0,4},{4,8},{8,12},{12,14},{14,10},{10,6},{6,2},{2,0},{1,5},{5,9},... | collective-permute-start | bytes 1179656 | tf_op jit(solution)/shard_map/ppermute | solution.py:67
  92.4 26.1 %collective-permute-start.8 = (bf16[2,1,64,1536]{3,2,0,1:T(8,128)(2,1)}, bf16[2,1,64,1536]{3,2,0,1:T(8,128)(2,1)}, u32[]{:S(2)}, u32[]{:S(2)}) collective-permute-start(bf16[2,1,64,1536]{3,2,0,1:T(8,128)(2,1)} %slice.52), channel_id=1, source_target_pairs={{2,0},{3,1},{18,16},{19,17}} | collective-permute-start | bytes 1179656 | tf_op jit(solution)/shard_map/ppermute | solution.py:208
  108.1 11.2 %collective-permute-start.19 = (bf16[2,1,64,1536]{3,2,1,0:T(8,128)(2,1)S(1)}, bf16[2,1,64,1536]{3,2,1,0:T(8,128)(2,1)}, u32[]{:S(2)}, u32[]{:S(2)}) collective-permute-start(bf16[2,1,64,1536]{3,2,1,0:T(8,128)(2,1)S(1)} %collective-permute-done.17.rest_15_), channel_id=1, source_target_pairs={{0,4},{4,8},{8,12},{12,14},{14,10},{10,6},{6,2},{2,0},{1,5},{5,9},... | collective-permute-start | bytes 1179656 | tf_op jit(solution)/shard_map/ppermute | solution.py:67
  108.1 11.2 %collective-permute-start.13 = (bf16[2,1,64,1536]{3,2,1,0:T(8,128)(2,1)}, bf16[2,1,64,1536]{3,2,1,0:T(8,128)(2,1)}, u32[]{:S(2)}, u32[]{:S(2)}) collective-permute-start(bf16[2,1,64,1536]{3,2,1,0:T(8,128)(2,1)} %collective-permute-done.11.rest_9_), channel_id=1, source_target_pairs={{4,0},{8,4},{12,8},{14,12},{10,14},{6,10},{2,6},{0,2},{5,1},{9,5},... | collective-permute-start | bytes 1179656 | tf_op jit(solution)/shard_map/ppermute | solution.py:70
  110.7 12.1 %collective-permute-start.21 = (bf16[2,1,64,1536]{3,2,1,0:T(8,128)(2,1)}, bf16[2,1,64,1536]{3,2,1,0:T(8,128)(2,1)}, u32[]{:S(2)}, u32[]{:S(2)}) collective-permute-start(bf16[2,1,64,1536]{3,2,1,0:T(8,128)(2,1)} %collective-permute-done.20.rest_18_), channel_id=1, source_target_pairs={{4,0},{8,4},{12,8},{14,12},{10,14},{6,10},{2,6},{0,2},{5,1},{9,5},... | collective-permute-start | bytes 1179656 | tf_op jit(solution)/shard_map/ppermute | solution.py:64
  112.8 10.8 %collective-permute-start.14 = (bf16[2,1,64,1536]{3,2,1,0:T(8,128)(2,1)}, bf16[2,1,64,1536]{3,2,1,0:T(8,128)(2,1)}, u32[]{:S(2)}, u32[]{:S(2)}) collective-permute-start(bf16[2,1,64,1536]{3,2,1,0:T(8,128)(2,1)} %collective-permute-done.12.rest_10_), channel_id=1, source_target_pairs={{0,4},{4,8},{8,12},{12,14},{14,10},{10,6},{6,2},{2,0},{1,5},{5,9},... | collective-permute-start | bytes 1179656 | tf_op jit(solution)/shard_map/ppermute | solution.py:62

commit v10 on v7

--- a/solution.py
+++ b/solution.py
@@ -177,9 +177,9 @@
 
     edge_cap = min(3 if row_count >= 2 else 4, tile_blocks)
     main_cap = edge_cap - 1 if col_count >= 3 else edge_cap
-    entries = cycle_list[0, 0]
-    right_entries = shift(entries, "col", col_count, -1)
-    left_entries = shift(entries, "col", col_count, 1)
+    entries = cycle_list[0, me_col]
+    right_entries = cycle_list[0, jnp.minimum(me_col + 1, col_count - 1)]
+    left_entries = cycle_list[0, jnp.maximum(me_col - 1, 0)]
     to_right, _, _ = side_slots(right_entries, 2, tile_blocks, edge_cap)
     to_left, _, _ = side_slots(left_entries, 2 + tile_blocks, tile_blocks, edge_cap)
     right_payload = jnp.take(stacked, to_right, axis=1)
@@ -240,7 +240,7 @@
         P(("groups", "row"), "col", None, None),
         P(("groups", "row"), "col", None, None),
         P(("groups", "row"), "col", None, None),
-        P(("groups", "row"), "col", None),
+        P(("groups", "row"), None, None),
         P(("groups", "row"), "col", None),
     )
     out_specs = P(("groups", "row"), "col", None, None)

time: 136 us -> 150 us (1.10)
  blocking collectives: 0 us -> 27.7 us
  starting transfers between devices: 37.9 us -> 29.3 us
  waiting for transfers between devices: 50.6 us -> 46 us
    unnamed x0 -> x1, blocking collectives: none -> 27.7 us
    ppermute x6 -> x4, starting transfers between devices: 17.9 us -> 9.97 us  [shift(): return lax.ppermute(x, axis, pairs)]
    ppermute x6, waiting for transfers between devices: 42.3 us -> 37.7 us  [ring_gather(): behind = lax.ppermute(behind, 'col', backward)]
    ppermute x6, starting transfers between devices: 3.96 us -> 2.12 us  [ring_gather(): ahead = lax.ppermute(ahead, 'col', forward)]
  transfers between devices with their start and end apart: 22 -> 20, of which waited for: 6 -> 6; matrix products, arithmetic and copies ran while one was open for 23% -> 18% of each run, Pallas kernels for 0% -> 0%
where the time goes in v10:
time: 150 us
  waiting for transfers between devices  46 us (31%)
  starting transfers between devices  29.3 us (20%)
  blocking collectives  27.7 us (18%)
  local copies, waits for them, and re-layouts  19.6 us (13%)
  Pallas kernels  14.5 us (10%)
  other arithmetic  12.4 us (8%)
    ppermute x6, waiting for transfers between devices, ring_gather(): behind = lax.ppermute(behind, 'col', backward)  37.7 us
    unnamed x1, blocking collectives  27.7 us
    pallas_call x1, Pallas kernels, gather_attend(): pl.pallas_call(kernel, out_shape=jax.ShapeDtypeStruct((token_count, width...  14.5 us
    ppermute x6, starting transfers between devices, ring_gather(): behind = lax.ppermute(behind, 'col', backward)  12.1 us
    ppermute x4, starting transfers between devices, shift(): return lax.ppermute(x, axis, pairs)  9.97 us
    ppermute x1, waiting for transfers between devices, ring_gather(): arrays.append(lax.ppermute(behind, 'col', backward))  7.49 us
    ppermute x2, local copies, waits for them, and re-layouts, shift(): return lax.ppermute(x, axis, pairs)  4.19 us
    gather x1, local copies, waits for them, and re-layouts, per_device(): right_payload = jnp.take(stacked, to_right, axis=1)  3.56 us
  transfers between devices with their start and end apart: 20, of which 6 were waited for; matrix products, arithmetic and copies ran while one was open for 18% of the time, Pallas kernels for 0%

profile of v10, /device:TPU:0, one launch (start us, length us, event | category | flops | bytes accessed | tf_op | source)
XLA Modules:
  0.0 149.9 jit_solution(10886988560922842476)
XLA Ops:
  0.0 1.0 exponential_bitcast_fusion.1
  1.0 1.0 exponential_bitcast_fusion
  2.0 1.8 %fusion = bf16[8,1,64,1536]{3,2,0,1:T(8,128)(2,1)S(1)} fusion(bf16[8,1,64,1536]{3,2,1,0:T(8,128)(2,1)} %param.15, f32[8,2,1536]{2,1,0:T(2,128)S(1)} %exponential_bitcast_fusion), kind=kLoop, calls=%fused_computation.7 | loop fusion | flops 2359296 | bytes 3244032 | tf_op jit(solution)/shard_map/convert_element_type | solution.py:24
  3.8 0.1 copy-done.3
  3.8 0.3 fusion.1
  4.1 0.3 maximum_bitcast_fusion.own_hbm
  4.5 0.1 slice.33
  4.5 0.0 copy-start.5
  4.5 1.0 fusion.15
  5.5 3.0 %collective-permute-start.14 = (bf16[2,1,64,1536]{3,2,1,0:T(8,128)(2,1)}, bf16[2,1,64,1536]{3,2,1,0:T(8,128)(2,1)S(1)}, u32[]{:S(2)}, u32[]{:S(2)}) collective-permute-start(bf16[2,1,64,1536]{3,2,1,0:T(8,128)(2,1)} %get-tuple-element.14), channel_id=1, source_target_pairs={{4,0},{8,4},{12,8},{14,12},{10,14},{6,10},{2,6},{0,2},{5,1},{9,5},... | collective-permute-start | bytes 1179656 | tf_op jit(solution)/shard_map/ppermute | solution.py:70
  8.5 0.1 collective-permute-start.13
  8.5 2.0 %collective-permute-start.7 = (bf16[2,1,64,1536]{3,2,1,0:T(8,128)(2,1)S(1)}, bf16[2,1,64,1536]{3,2,1,0:T(8,128)(2,1)S(1)}, u32[]{:S(2)}, u32[]{:S(2)}) collective-permute-start(bf16[2,1,64,1536]{3,2,1,0:T(8,128)(2,1)S(1)} %get-tuple-element.15), channel_id=1, source_target_pairs={{4,0},{8,4},{12,8},{14,12},{10,14},{6,10},{2,6},{0,2},{5,1},{9,5},... | collective-permute-start | bytes 1179656 | tf_op jit(solution)/shard_map/ppermute | solution.py:70
  10.5 0.1 collective-permute-start.6
  10.6 1.0 fusion.14
  11.5 1.3 collective-permute-start.1
  12.8 27.7 %all-gather = s32[1,8,4]{2,0,1:T(1,128)S(1)} all-gather(s32[1,1,4]{2,0,1:T(1,128)S(1)} %bitcast.115), channel_id=2, replica_groups=[4,8]<=[2,8,2]T(0,2,1), dimensions={1}, use_global_device_ids=true | all-gather | bytes 144 | tf_op args[5]
  40.6 0.5 convert_bitcast_fusion
  41.1 0.2 reduce-window.37
  41.3 0.2 reduce-window.36
  41.5 0.1 select_reduce_fusion
  41.6 0.1 select_reduce_fusion.1
  41.7 0.5 compare_select_fusion
  42.2 2.5 %gather_fusion.4 = bf16[3,2,64,1536]{3,2,1,0:T(8,128)(2,1)S(1)} fusion(bf16[2,8,64,1536]{3,2,1,0:T(8,128)(2,1)} %copy-done.2, s32[1024]{0:T(1024)S(1)} %pad_clamp_fusion), kind=kCustom, calls=%fused_computation.1.clone | custom fusion | bytes 2359308 | tf_op jit(solution)/shard_map/jit(_take)/gather | solution.py:186
  44.8 0.2 select_bitcast_fusion
  44.9 0.8 slice.51
  45.7 0.9 slice.49
  46.7 3.6 %gather_fusion.3 = bf16[3,2,64,1536]{3,2,1,0:T(8,128)(2,1)} fusion(bf16[2,8,64,1536]{3,2,1,0:T(8,128)(2,1)} %copy-done.2, s32[1024]{0:T(1024)S(1)} %pad_clamp_fusion.1), kind=kCustom, calls=%fused_computation.clone | custom fusion | bytes 2359308 | tf_op jit(solution)/shard_map/jit(_take)/gather | solution.py:185
  50.3 1.3 collective-permute-start
  51.6 1.3 collective-permute-start.5
  52.9 1.5 select_bitcast_fusion.1
  54.4 0.0 copy-start
  54.4 0.0 copy-start.1
  54.4 0.9 slice.48
  55.3 1.3 collective-permute-start.3
  56.6 6.1 %collective-permute-start.2 = (bf16[2,2,64,1536]{3,2,0,1:T(8,128)(2,1)}, bf16[2,2,64,1536]{3,2,0,1:T(8,128)(2,1)}, u32[]{:S(2)}, u32[]{:S(2)}) collective-permute-start(bf16[2,2,64,1536]{3,2,0,1:T(8,128)(2,1)} %slice.48), channel_id=1, source_target_pairs={{0,2},{2,4},{4,6},{6,8},{8,10},{10,12},{12,14},{1,3},{3,5},{5,7},{... | collective-permute-start | bytes 2359304 | tf_op jit(solution)/shard_map/ppermute | solution.py:34
  62.7 2.1 %collective-permute-start.16 = (bf16[2,1,64,1536]{3,2,1,0:T(8,128)(2,1)S(1)}, bf16[2,1,64,1536]{3,2,1,0:T(8,128)(2,1)S(1)}, u32[]{:S(2)}, u32[]{:S(2)}) collective-permute-start(bf16[2,1,64,1536]{3,2,1,0:T(8,128)(2,1)S(1)} %collective-permute-done.14.rest_14_), channel_id=1, source_target_pairs={{4,0},{8,4},{12,8},{14,12},{10,14},{6,10},{2,6},{0,2},{5,1},{9,5},... | collective-permute-start | bytes 1179656 | tf_op jit(solution)/shard_map/ppermute | solution.py:70
  64.8 0.8 collective-permute-done.5
  65.7 0.8 slice.50
  66.5 0.7 dynamic_slice.13
  67.1 1.2 gather_fusion
  68.3 1.3 reduce-window.34
  69.6 0.7 reduce-window.35
  70.3 28.6 %collective-permute-done.16.rest_16_ = bf16[2,1,64,1536]{3,2,1,0:T(8,128)(2,1)S(1)} collective-permute-done((bf16[2,1,64,1536]{3,2,1,0:T(8,128)(2,1)S(1)}, bf16[2,1,64,1536]{3,2,1,0:T(8,128)(2,1)S(1)}, u32[]{:S(2)}, u32[]{:S(2)}) %collective-permute-start.16) | collective-permute-done | bytes 393248 | tf_op jit(solution)/shard_map/ppermute | solution.py:70
  98.9 2.5 %collective-permute-start.9 = (bf16[2,1,64,1536]{3,2,1,0:T(8,128)(2,1)S(1)}, bf16[2,1,64,1536]{3,2,1,0:T(8,128)(2,1)}, u32[]{:S(2)}, u32[]{:S(2)}) collective-permute-start(bf16[2,1,64,1536]{3,2,1,0:T(8,128)(2,1)S(1)} %collective-permute-done.7.rest_7_), channel_id=1, source_target_pairs={{4,0},{8,4},{12,8},{14,12},{10,14},{6,10},{2,6},{0,2},{5,1},{9,5},... | collective-permute-start | bytes 1179656 | tf_op jit(solution)/shard_map/ppermute | solution.py:70
  101.4 0.0 collective-permute-start.18
  101.4 2.0 %collective-permute-start.10 = (bf16[2,1,64,1536]{3,2,1,0:T(8,128)(2,1)}, bf16[2,1,64,1536]{3,2,1,0:T(8,128)(2,1)}, u32[]{:S(2)}, u32[]{:S(2)}) collective-permute-start(bf16[2,1,64,1536]{3,2,1,0:T(8,128)(2,1)} %collective-permute-done.8.rest_8_), channel_id=1, source_target_pairs={{0,4},{4,8},{8,12},{12,14},{14,10},{10,6},{6,2},{2,0},{1,5},{5,9},... | collective-permute-start | bytes 1179656 | tf_op jit(solution)/shard_map/ppermute | solution.py:67
  103.4 1.4 fusion.12
  104.8 1.1 gather_fusion.1
  105.9 0.6 gather_fusion.2
  106.5 0.6 bitcast_select_fusion.3
  107.2 3.8 %collective-permute-done.9.rest_9_ = bf16[2,1,64,1536]{3,2,1,0:T(8,128)(2,1)} collective-permute-done((bf16[2,1,64,1536]{3,2,1,0:T(8,128)(2,1)S(1)}, bf16[2,1,64,1536]{3,2,1,0:T(8,128)(2,1)}, u32[]{:S(2)}, u32[]{:S(2)}) %collective-permute-start.9) | collective-permute-done | bytes 393248 | tf_op jit(solution)/shard_map/ppermute | solution.py:70
  111.0 1.4 collective-permute-start.4
  112.4 2.5 %collective-permute-start.11 = (bf16[2,1,64,1536]{3,2,1,0:T(8,128)(2,1)}, bf16[2,1,64,1536]{3,2,1,0:T(8,128)(2,1)}, u32[]{:S(2)}, u32[]{:S(2)}) collective-permute-start(bf16[2,1,64,1536]{3,2,1,0:T(8,128)(2,1)} %collective-permute-done.9.rest_9_), channel_id=1, source_target_pairs={{4,0},{8,4},{12,8},{14,12},{10,14},{6,10},{2,6},{0,2},{5,1},{9,5},... | collective-permute-start | bytes 1179656 | tf_op jit(solution)/shard_map/ppermute | solution.py:70
  114.9 4.5 %collective-permute-done.18.rest_18_ = bf16[2,1,64,1536]{3,2,1,0:T(8,128)(2,1)} collective-permute-done((bf16[2,1,64,1536]{3,2,1,0:T(8,128)(2,1)S(1)}, bf16[2,1,64,1536]{3,2,1,0:T(8,128)(2,1)}, u32[]{:S(2)}, u32[]{:S(2)}) %collective-permute-start.18) | collective-permute-done | bytes 393248 | tf_op jit(solution)/shard_map/ppermute | solution.py:70
  119.4 2.5 %collective-permute-start.19 = (bf16[2,1,64,1536]{3,2,1,0:T(8,128)(2,1)}, bf16[2,1,64,1536]{3,2,1,0:T(8,128)(2,1)}, u32[]{:S(2)}, u32[]{:S(2)}) collective-permute-start(bf16[2,1,64,1536]{3,2,1,0:T(8,128)(2,1)} %collective-permute-done.18.rest_18_), channel_id=1, source_target_pairs={{4,0},{8,4},{12,8},{14,12},{10,14},{6,10},{2,6},{0,2},{5,1},{9,5},... | collective-permute-start | bytes 1179656 | tf_op jit(solution)/shard_map/ppermute | solution.py:64
  121.9 0.6 broadcast_add_fusion
  122.5 0.1 add_bitcast_fusion
  122.6 0.1 copy.37
  122.7 0.1 reshape.543.table_ref
  122.8 2.1 %copy.41.rest_3_ = bf16[2,2,64,1536]{3,2,1,0:T(8,128)(2,1)} copy(bf16[2,2,64,1536]{3,2,0,1:T(8,128)(2,1)} %collective-permute-done.3) | data formatting | bytes 1572864 | tf_op jit(solution)/shard_map/ppermute | solution.py:34
  124.9 2.1 %copy.40.rest_2_ = bf16[2,2,64,1536]{3,2,1,0:T(8,128)(2,1)} copy(bf16[2,2,64,1536]{3,2,0,1:T(8,128)(2,1)} %collective-permute-done.2) | data formatting | bytes 1572864 | tf_op jit(solution)/shard_map/ppermute | solution.py:34
  127.0 0.9 collective-permute-done.11.rest_11_
  127.8 7.5 %collective-permute-done.19.rest_19_ = bf16[2,1,64,1536]{3,2,1,0:T(8,128)(2,1)} collective-permute-done((bf16[2,1,64,1536]{3,2,1,0:T(8,128)(2,1)}, bf16[2,1,64,1536]{3,2,1,0:T(8,128)(2,1)}, u32[]{:S(2)}, u32[]{:S(2)}) %collective-permute-start.19) | collective-permute-done | bytes 393248 | tf_op jit(solution)/shard_map/ppermute | solution.py:64
  135.3 14.5 %shard_map.100 = bf16[512,1536]{1,0:T(8,128)(2,1)} custom-call(s32[16]{0:T(128)S(1)} %reshape.543.table_ref, bf16[512,1536]{1,0:T(8,128)(2,1)} %bitcast.112, bf16[2,8,64,1536]{3,2,1,0:T(8,128)(2,1)} %copy-done.2, bf16[2,1,64,1536]{3,2,1,0:T(8,128)(2,1)S(1)} %collective-permute-done.rest_0_, bf16[2,1,64,1536]{3,2,1,0:T(8,128)(2,1)S(1)} %collective-permute-done.1.rest_1_, ...), custom_call_target="tpu_custom_call" | custom-call | flops 3221225472 | bytes 9437184 | tf_op jit(solution)/shard_map/pallas_call | solution.py:142
  (39 shorter events, 0.2 us)
Async XLA Ops:
  1.9 1.9 %copy-start.3 = (bf16[8,1,64,1536]{3,2,1,0:T(8,128)(2,1)S(1)}, bf16[8,1,64,1536]{3,2,1,0:T(8,128)(2,1)}, u32[]{:S(2)}) copy-start(bf16[8,1,64,1536]{3,2,1,0:T(8,128)(2,1)} %param.13) | copy-start | bytes 4718596
  4.4 6.1 %copy-start.2 = (bf16[2,8,64,1536]{3,2,1,0:T(8,128)(2,1)}, bf16[2,8,64,1536]{3,2,1,0:T(8,128)(2,1)S(1)}, u32[]{:S(2)}) copy-start(bf16[2,8,64,1536]{3,2,1,0:T(8,128)(2,1)S(1)} %maximum_bitcast_fusion.own_hbm) | copy-start | bytes 9437188
  4.5 8.3 %copy-start.5 = (s32[1,1,4]{2,1,0:T(1,128)S(1)}, s32[1,1,4]{2,1,0:T(1,128)}, u32[]{:S(2)}) copy-start(s32[1,1,4]{2,1,0:T(1,128)} %param.17) | copy-start | bytes 52
  5.5 44.8 %collective-permute-start.14 = (bf16[2,1,64,1536]{3,2,1,0:T(8,128)(2,1)}, bf16[2,1,64,1536]{3,2,1,0:T(8,128)(2,1)S(1)}, u32[]{:S(2)}, u32[]{:S(2)}) collective-permute-start(bf16[2,1,64,1536]{3,2,1,0:T(8,128)(2,1)} %get-tuple-element.14), channel_id=1, source_target_pairs={{4,0},{8,4},{12,8},{14,12},{10,14},{6,10},{2,6},{0,2},{5,1},{9,5},... | collective-permute-start | bytes 1179656 | tf_op jit(solution)/shard_map/ppermute | solution.py:70
  8.5 43.1 %collective-permute-start.13 = (bf16[2,1,64,1536]{3,2,1,0:T(8,128)(2,1)}, bf16[2,1,64,1536]{3,2,1,0:T(8,128)(2,1)S(1)}, u32[]{:S(2)}, u32[]{:S(2)}) collective-permute-start(bf16[2,1,64,1536]{3,2,1,0:T(8,128)(2,1)} %get-tuple-element.14), channel_id=1, source_target_pairs={{0,4},{4,8},{8,12},{12,14},{14,10},{10,6},{6,2},{2,0},{1,5},{5,9},... | collective-permute-start | bytes 1179656 | tf_op jit(solution)/shard_map/ppermute | solution.py:67
  8.5 46.8 %collective-permute-start.7 = (bf16[2,1,64,1536]{3,2,1,0:T(8,128)(2,1)S(1)}, bf16[2,1,64,1536]{3,2,1,0:T(8,128)(2,1)S(1)}, u32[]{:S(2)}, u32[]{:S(2)}) collective-permute-start(bf16[2,1,64,1536]{3,2,1,0:T(8,128)(2,1)S(1)} %get-tuple-element.15), channel_id=1, source_target_pairs={{4,0},{8,4},{12,8},{14,12},{10,14},{6,10},{2,6},{0,2},{5,1},{9,5},... | collective-permute-start | bytes 1179656 | tf_op jit(solution)/shard_map/ppermute | solution.py:70
  10.5 46.1 %collective-permute-start.6 = (bf16[2,1,64,1536]{3,2,1,0:T(8,128)(2,1)S(1)}, bf16[2,1,64,1536]{3,2,1,0:T(8,128)(2,1)S(1)}, u32[]{:S(2)}, u32[]{:S(2)}) collective-permute-start(bf16[2,1,64,1536]{3,2,1,0:T(8,128)(2,1)S(1)} %get-tuple-element.15), channel_id=1, source_target_pairs={{0,4},{4,8},{8,12},{12,14},{14,10},{10,6},{6,2},{2,0},{1,5},{5,9},... | collective-permute-start | bytes 1179656 | tf_op jit(solution)/shard_map/ppermute | solution.py:67
  11.5 51.2 %collective-permute-start.1 = (bf16[2,1,64,1536]{3,2,1,0:T(8,128)(2,1)}, bf16[2,1,64,1536]{3,2,1,0:T(8,128)(2,1)S(1)}, u32[]{:S(2)}, u32[]{:S(2)}) collective-permute-start(bf16[2,1,64,1536]{3,2,1,0:T(8,128)(2,1)} %get-tuple-element.12), channel_id=1, source_target_pairs={{1,0},{3,2},{5,4},{7,6},{9,8},{11,10},{13,12},{15,14},{17,16},{19,... | collective-permute-start | bytes 1179656 | tf_op jit(solution)/shard_map/ppermute | solution.py:34
  44.9 1.8 %copy-start.4 = (s32[3]{0:T(128)S(1)}, s32[3]{0:T(128)}, u32[]{:S(2)}) copy-start(s32[3]{0:T(128)} %get-tuple-element.25) | copy-start | bytes 40
  50.3 14.5 %collective-permute-start = (bf16[2,1,64,1536]{3,2,1,0:T(8,128)(2,1)}, bf16[2,1,64,1536]{3,2,1,0:T(8,128)(2,1)S(1)}, u32[]{:S(2)}, u32[]{:S(2)}) collective-permute-start(bf16[2,1,64,1536]{3,2,1,0:T(8,128)(2,1)} %get-tuple-element.13), channel_id=1, source_target_pairs={{0,1},{2,3},{4,5},{6,7},{8,9},{10,11},{12,13},{14,15},{16,17},{18,... | collective-permute-start | bytes 1179656 | tf_op jit(solution)/shard_map/ppermute | solution.py:34
  51.6 14.0 %collective-permute-start.5 = (bf16[2,1,64,1536]{3,2,0,1:T(8,128)(2,1)}, bf16[2,1,64,1536]{3,2,0,1:T(8,128)(2,1)S(1)}, u32[]{:S(2)}, u32[]{:S(2)}) collective-permute-start(bf16[2,1,64,1536]{3,2,0,1:T(8,128)(2,1)} %slice.51), channel_id=1, source_target_pairs={{2,0},{3,1},{18,16},{19,17}} | collective-permute-start | bytes 1179656 | tf_op jit(solution)/shard_map/ppermute | solution.py:193
  52.9 12.7 %copy-start.6 = (s32[1,1,4]{2,1,0:T(1,128)S(1)}, s32[1,1,4]{2,1,0:T(1,128)}, u32[]{:S(2)}) copy-start(s32[1,1,4]{2,1,0:T(1,128)} %param.18) | copy-start | bytes 52
  54.4 12.1 %copy-start = (s32[8]{0:T(128)S(1)}, s32[8]{0:T(128)}, u32[]{:S(2)}) copy-start(s32[8]{0:T(128)} %constant.102.clone) | copy-start | bytes 100
  54.4 50.4 %copy-start.1 = (s32[7,2]{1,0:T(8,128)S(1)}, s32[7,2]{1,0:T(8,128)}, u32[]{:S(2)}) copy-start(s32[7,2]{1,0:T(8,128)} %constant.103.clone) | copy-start | bytes 172
  55.3 57.0 %collective-permute-start.3 = (bf16[2,2,64,1536]{3,2,0,1:T(8,128)(2,1)}, bf16[2,2,64,1536]{3,2,0,1:T(8,128)(2,1)}, u32[]{:S(2)}, u32[]{:S(2)}) collective-permute-start(bf16[2,2,64,1536]{3,2,0,1:T(8,128)(2,1)} %slice.49), channel_id=1, source_target_pairs={{2,0},{4,2},{6,4},{8,6},{10,8},{12,10},{14,12},{3,1},{5,3},{7,5},{... | collective-permute-start | bytes 2359304 | tf_op jit(solution)/shard_map/ppermute | solution.py:34
  56.6 55.8 %collective-permute-start.2 = (bf16[2,2,64,1536]{3,2,0,1:T(8,128)(2,1)}, bf16[2,2,64,1536]{3,2,0,1:T(8,128)(2,1)}, u32[]{:S(2)}, u32[]{:S(2)}) collective-permute-start(bf16[2,2,64,1536]{3,2,0,1:T(8,128)(2,1)} %slice.48), channel_id=1, source_target_pairs={{0,2},{2,4},{4,6},{6,8},{8,10},{10,12},{12,14},{1,3},{3,5},{5,7},{... | collective-permute-start | bytes 2359304 | tf_op jit(solution)/shard_map/ppermute | solution.py:34
  62.7 36.2 %collective-permute-start.16 = (bf16[2,1,64,1536]{3,2,1,0:T(8,128)(2,1)S(1)}, bf16[2,1,64,1536]{3,2,1,0:T(8,128)(2,1)S(1)}, u32[]{:S(2)}, u32[]{:S(2)}) collective-permute-start(bf16[2,1,64,1536]{3,2,1,0:T(8,128)(2,1)S(1)} %collective-permute-done.14.rest_14_), channel_id=1, source_target_pairs={{4,0},{8,4},{12,8},{14,12},{10,14},{6,10},{2,6},{0,2},{5,1},{9,5},... | collective-permute-start | bytes 1179656 | tf_op jit(solution)/shard_map/ppermute | solution.py:70
  64.8 36.6 %collective-permute-start.15 = (bf16[2,1,64,1536]{3,2,1,0:T(8,128)(2,1)S(1)}, bf16[2,1,64,1536]{3,2,1,0:T(8,128)(2,1)S(1)}, u32[]{:S(2)}, u32[]{:S(2)}) collective-permute-start(bf16[2,1,64,1536]{3,2,1,0:T(8,128)(2,1)S(1)} %collective-permute-done.13.rest_13_), channel_id=1, source_target_pairs={{0,4},{4,8},{8,12},{12,14},{14,10},{10,6},{6,2},{2,0},{1,5},{5,9},... | collective-permute-start | bytes 1179656 | tf_op jit(solution)/shard_map/ppermute | solution.py:67
  65.6 35.8 %collective-permute-start.8 = (bf16[2,1,64,1536]{3,2,1,0:T(8,128)(2,1)S(1)}, bf16[2,1,64,1536]{3,2,1,0:T(8,128)(2,1)}, u32[]{:S(2)}, u32[]{:S(2)}) collective-permute-start(bf16[2,1,64,1536]{3,2,1,0:T(8,128)(2,1)S(1)} %collective-permute-done.6.rest_6_), channel_id=1, source_target_pairs={{0,4},{4,8},{8,12},{12,14},{14,10},{10,6},{6,2},{2,0},{1,5},{5,9},... | collective-permute-start | bytes 1179656 | tf_op jit(solution)/shard_map/ppermute | solution.py:67
  98.9 12.1 %collective-permute-start.9 = (bf16[2,1,64,1536]{3,2,1,0:T(8,128)(2,1)S(1)}, bf16[2,1,64,1536]{3,2,1,0:T(8,128)(2,1)}, u32[]{:S(2)}, u32[]{:S(2)}) collective-permute-start(bf16[2,1,64,1536]{3,2,1,0:T(8,128)(2,1)S(1)} %collective-permute-done.7.rest_7_), channel_id=1, source_target_pairs={{4,0},{8,4},{12,8},{14,12},{10,14},{6,10},{2,6},{0,2},{5,1},{9,5},... | collective-permute-start | bytes 1179656 | tf_op jit(solution)/shard_map/ppermute | solution.py:70
  101.4 18.0 %collective-permute-start.18 = (bf16[2,1,64,1536]{3,2,1,0:T(8,128)(2,1)S(1)}, bf16[2,1,64,1536]{3,2,1,0:T(8,128)(2,1)}, u32[]{:S(2)}, u32[]{:S(2)}) collective-permute-start(bf16[2,1,64,1536]{3,2,1,0:T(8,128)(2,1)S(1)} %collective-permute-done.16.rest_16_), channel_id=1, source_target_pairs={{4,0},{8,4},{12,8},{14,12},{10,14},{6,10},{2,6},{0,2},{5,1},{9,5},... | collective-permute-start | bytes 1179656 | tf_op jit(solution)/shard_map/ppermute | solution.py:70
  101.4 20.5 %collective-permute-start.10 = (bf16[2,1,64,1536]{3,2,1,0:T(8,128)(2,1)}, bf16[2,1,64,1536]{3,2,1,0:T(8,128)(2,1)}, u32[]{:S(2)}, u32[]{:S(2)}) collective-permute-start(bf16[2,1,64,1536]{3,2,1,0:T(8,128)(2,1)} %collective-permute-done.8.rest_8_), channel_id=1, source_target_pairs={{0,4},{4,8},{8,12},{12,14},{14,10},{10,6},{6,2},{2,0},{1,5},{5,9},... | collective-permute-start | bytes 1179656 | tf_op jit(solution)/shard_map/ppermute | solution.py:67
  111.0 16.0 %collective-permute-start.4 = (bf16[2,1,64,1536]{3,2,0,1:T(8,128)(2,1)}, bf16[2,1,64,1536]{3,2,0,1:T(8,128)(2,1)}, u32[]{:S(2)}, u32[]{:S(2)}) collective-permute-start(bf16[2,1,64,1536]{3,2,0,1:T(8,128)(2,1)} %slice.50), channel_id=1, source_target_pairs={{12,14},{13,15},{28,30},{29,31}} | collective-permute-start | bytes 1179656 | tf_op jit(solution)/shard_map/ppermute | solution.py:192
  112.4 14.6 %collective-permute-start.17 = (bf16[2,1,64,1536]{3,2,1,0:T(8,128)(2,1)S(1)}, bf16[2,1,64,1536]{3,2,1,0:T(8,128)(2,1)}, u32[]{:S(2)}, u32[]{:S(2)}) collective-permute-start(bf16[2,1,64,1536]{3,2,1,0:T(8,128)(2,1)S(1)} %collective-permute-done.15.rest_15_), channel_id=1, source_target_pairs={{0,4},{4,8},{8,12},{12,14},{14,10},{10,6},{6,2},{2,0},{1,5},{5,9},... | collective-permute-start | bytes 1179656 | tf_op jit(solution)/shard_map/ppermute | solution.py:67
  112.4 15.4 %collective-permute-start.11 = (bf16[2,1,64,1536]{3,2,1,0:T(8,128)(2,1)}, bf16[2,1,64,1536]{3,2,1,0:T(8,128)(2,1)}, u32[]{:S(2)}, u32[]{:S(2)}) collective-permute-start(bf16[2,1,64,1536]{3,2,1,0:T(8,128)(2,1)} %collective-permute-done.9.rest_9_), channel_id=1, source_target_pairs={{4,0},{8,4},{12,8},{14,12},{10,14},{6,10},{2,6},{0,2},{5,1},{9,5},... | collective-permute-start | bytes 1179656 | tf_op jit(solution)/shard_map/ppermute | solution.py:70
  119.4 15.9 %collective-permute-start.19 = (bf16[2,1,64,1536]{3,2,1,0:T(8,128)(2,1)}, bf16[2,1,64,1536]{3,2,1,0:T(8,128)(2,1)}, u32[]{:S(2)}, u32[]{:S(2)}) collective-permute-start(bf16[2,1,64,1536]{3,2,1,0:T(8,128)(2,1)} %collective-permute-done.18.rest_18_), channel_id=1, source_target_pairs={{4,0},{8,4},{12,8},{14,12},{10,14},{6,10},{2,6},{0,2},{5,1},{9,5},... | collective-permute-start | bytes 1179656 | tf_op jit(solution)/shard_map/ppermute | solution.py:64
  121.9 13.4 %collective-permute-start.12 = (bf16[2,1,64,1536]{3,2,1,0:T(8,128)(2,1)}, bf16[2,1,64,1536]{3,2,1,0:T(8,128)(2,1)}, u32[]{:S(2)}, u32[]{:S(2)}) collective-permute-start(bf16[2,1,64,1536]{3,2,1,0:T(8,128)(2,1)} %collective-permute-done.10.rest_10_), channel_id=1, source_target_pairs={{0,4},{4,8},{8,12},{12,14},{14,10},{10,6},{6,2},{2,0},{1,5},{5,9},... | collective-permute-start | bytes 1179656 | tf_op jit(solution)/shard_map/ppermute | solution.py:62

commit v11 on v9

--- a/solution.py
+++ b/solution.py
@@ -190,33 +190,37 @@
             route = [((i + distance) % col_count, i) for i in range(col_count)]
             far_sources.append(lax.ppermute(far_source, "col", route))
             lookup.append([(hop - 1, r) for r in range(distant_rows)])
-    entries, _ = lax.optimization_barrier((cycle_list[0, 0], far_sources[0]))
     edge_cap = min(3 if row_count >= 2 else 4, tile_blocks)
     main_cap = edge_cap - 1 if col_count >= 3 else edge_cap
+    entries = cycle_list[0, 0]
     right_entries = shift(entries, "col", col_count, -1)
     left_entries = shift(entries, "col", col_count, 1)
     to_right, _, _ = side_slots(right_entries, 2, tile_blocks, edge_cap)
     to_left, _, _ = side_slots(left_entries, 2 + tile_blocks, tile_blocks, edge_cap)
     right_payload = jnp.take(stacked, to_right, axis=1)
     left_payload = jnp.take(stacked, to_left, axis=1)
+    later = far_sources[min(2, len(far_sources) - 1)]
     cycle_sources = [above, below]
-    cycle_sources.append(shift(right_payload[:, :main_cap], "col", col_count, 1))
-    cycle_sources.append(shift(left_payload[:, :main_cap], "col", col_count, -1))
-    if main_cap < edge_cap:
-        last = col_count - 1
-        cycle_sources.append(lax.ppermute(right_payload[:, main_cap:], "col", [(last - 1, last)]))
-        cycle_sources.append(lax.ppermute(left_payload[:, main_cap:], "col", [(1, 0)]))
+    last = col_count - 1
+    for slot in range(edge_cap):
+        to_r = right_payload[:, slot : slot + 1]
+        to_l = left_payload[:, slot : slot + 1]
+        if slot > 0:
+            to_r, to_l, _ = lax.optimization_barrier((to_r, to_l, later))
+        if slot < main_cap:
+            cycle_sources.append(shift(to_r, "col", col_count, 1))
+            cycle_sources.append(shift(to_l, "col", col_count, -1))
+        else:
+            cycle_sources.append(lax.ppermute(to_r, "col", [(last - 1, last)]))
+            cycle_sources.append(lax.ppermute(to_l, "col", [(1, 0)]))
 
     _, is_left, left_rank = side_slots(entries, 2, tile_blocks, edge_cap)
     _, is_right, right_rank = side_slots(entries, 2 + tile_blocks, tile_blocks, edge_cap)
     side_rank = jnp.where(is_left, left_rank, right_rank)
-    overflow = side_rank >= main_cap
     cycle_src = jnp.where(
-        entries == 0,
-        0,
-        jnp.where(entries == 1, 1, 2 + is_right.astype(jnp.int32) + 2 * overflow.astype(jnp.int32)),
-    )
-    cycle_idx = jnp.where(entries < 2, 0, jnp.where(overflow, side_rank - main_cap, side_rank))
+        entries == 0, 0, jnp.where(entries == 1, 1, 2 + is_right.astype(jnp.int32) + 2 * side_rank)
+    )
+    cycle_idx = jnp.zeros_like(entries)
 
     lookup_src = jnp.array([[a for a, _ in row] for row in lookup], dtype=jnp.int32)
     lookup_idx = jnp.array([[b for _, b in row] for row in lookup], dtype=jnp.int32)

time: 139 us -> 133 us (0.957)
  the two profiles are of different devices: /device:TPU:0 before, /device:TPU:16 now
where the time goes in v11:
time: 133 us; the launch traced here: 131 us
  starting transfers between devices  50.3 us (38%)
  waiting for transfers between devices  42.9 us (32%)
  Pallas kernels  14.3 us (11%)
  local copies, waits for them, and re-layouts  13.5 us (10%)
  other arithmetic  10 us (8%)
    ppermute x6, starting transfers between devices, ring_gather(): ahead = lax.ppermute(ahead, 'col', forward)  23 us
    ppermute x6, waiting for transfers between devices, ring_gather(): behind = lax.ppermute(behind, 'col', backward)  22.4 us
    ppermute x8, starting transfers between devices, shift(): return lax.ppermute(x, axis, pairs)  20 us
    pallas_call x1, Pallas kernels, gather_attend(): pl.pallas_call(kernel, out_shape=jax.ShapeDtypeStruct((token_count, width...  14.3 us
    ppermute x8, waiting for transfers between devices, shift(): return lax.ppermute(x, axis, pairs)  13.1 us
    ppermute x1, waiting for transfers between devices, ring_gather(): arrays.append(lax.ppermute(behind, 'col', backward))  7.28 us
    gather x1, local copies, waits for them, and re-layouts, per_device(): right_payload = jnp.take(stacked, to_right, axis=1)  3.56 us
    another operation x4, other arithmetic  3.02 us
  transfers between devices with their start and end apart: 24, of which 9 were waited for; matrix products, arithmetic and copies ran while one was open for 17% of the time, Pallas kernels for 0%

profile of v11, /device:TPU:16, one launch (start us, length us, event | category | flops | bytes accessed | tf_op | source)
XLA Modules:
  0.0 131.5 jit_solution(13302880706336850507)
XLA Ops:
  0.0 3.4 %collective-permute-start.4 = (s32[4]{0:T(128)}, s32[4]{0:T(128)S(1)}, u32[]{:S(2)}, u32[]{:S(2)}) collective-permute-start(s32[4]{0:T(128)} %bitcast.94), channel_id=1, source_target_pairs={{0,2},{2,4},{4,6},{6,8},{8,10},{10,12},{12,14},{1,3},{3,5},{5,7},{... | collective-permute-start | bytes 56 | tf_op jit(solution)/shard_map/ppermute | solution.py:34
  3.4 3.3 %collective-permute-start.2 = (s32[4]{0:T(128)}, s32[4]{0:T(128)S(1)}, u32[]{:S(2)}, u32[]{:S(2)}) collective-permute-start(s32[4]{0:T(128)} %bitcast.95), channel_id=1, source_target_pairs={{2,0},{4,2},{6,4},{8,6},{10,8},{12,10},{14,12},{3,1},{5,3},{7,5},{... | collective-permute-start | bytes 56 | tf_op jit(solution)/shard_map/ppermute | solution.py:34
  6.8 1.0 exponential_bitcast_fusion.1
  7.7 1.0 exponential_bitcast_fusion
  8.7 1.8 %fusion.1 = bf16[8,1,64,1536]{3,2,0,1:T(8,128)(2,1)S(1)} fusion(bf16[8,1,64,1536]{3,2,1,0:T(8,128)(2,1)} %param.13, f32[8,2,1536]{2,1,0:T(2,128)S(1)} %exponential_bitcast_fusion.1), kind=kLoop, calls=%fused_computation.9 | loop fusion | flops 2359296 | bytes 3244032 | tf_op jit(solution)/shard_map/convert_element_type | solution.py:24
  10.5 0.1 copy-done.4
  10.6 0.3 fusion
  10.9 0.3 maximum_bitcast_fusion.own_hbm
  11.3 1.1 fusion.19
  12.4 1.6 %collective-permute-start.6 = (bf16[2,1,64,1536]{3,2,1,0:T(8,128)(2,1)}, bf16[2,1,64,1536]{3,2,1,0:T(8,128)(2,1)S(1)}, u32[]{:S(2)}, u32[]{:S(2)}) collective-permute-start(bf16[2,1,64,1536]{3,2,1,0:T(8,128)(2,1)} %get-tuple-element.23), channel_id=1, source_target_pairs={{0,4},{4,8},{8,12},{12,14},{14,10},{10,6},{6,2},{2,0},{1,5},{5,9},... | collective-permute-start | bytes 1179656 | tf_op jit(solution)/shard_map/ppermute | solution.py:67
  13.9 0.4 collective-permute-start.12
  14.4 0.4 collective-permute-start.18
  14.8 0.9 fusion.16
  15.8 1.6 %collective-permute-start.17 = (bf16[2,1,64,1536]{3,2,1,0:T(8,128)(2,1)}, bf16[2,1,64,1536]{3,2,1,0:T(8,128)(2,1)}, u32[]{:S(2)}, u32[]{:S(2)}) collective-permute-start(bf16[2,1,64,1536]{3,2,1,0:T(8,128)(2,1)} %get-tuple-element.22), channel_id=1, source_target_pairs={{0,4},{4,8},{8,12},{12,14},{14,10},{10,6},{6,2},{2,0},{1,5},{5,9},... | collective-permute-start | bytes 1179656 | tf_op jit(solution)/shard_map/ppermute | solution.py:67
  17.3 0.2 reduce-window.37
  17.5 0.1 select_reduce_fusion
  17.7 1.3 collective-permute-start
  19.0 0.2 reduce-window.36
  19.2 0.1 select_reduce_fusion.1
  19.4 2.5 %gather_fusion.4 = bf16[3,2,64,1536]{3,2,1,0:T(8,128)(2,1)S(1)} fusion(bf16[2,8,64,1536]{3,2,1,0:T(8,128)(2,1)} %copy-done.2, s32[1024]{0:T(1024)S(1)} %pad_clamp_fusion), kind=kCustom, calls=%fused_computation.1.clone | custom fusion | bytes 2359308 | tf_op jit(solution)/shard_map/jit(_take)/gather | solution.py:201
  21.9 3.6 %gather_fusion.3 = bf16[3,2,64,1536]{3,2,1,0:T(8,128)(2,1)} fusion(bf16[2,8,64,1536]{3,2,1,0:T(8,128)(2,1)} %copy-done.2, s32[1024]{0:T(1024)S(1)} %pad_clamp_fusion.1), kind=kCustom, calls=%fused_computation.clone | custom fusion | bytes 2359308 | tf_op jit(solution)/shard_map/jit(_take)/gather | solution.py:200
  25.5 0.2 select_bitcast_fusion
  25.6 1.1 copy-done.3
  26.7 0.2 select_bitcast_fusion.1
  27.0 1.4 %collective-permute-start.1 = (bf16[2,1,64,1536]{3,2,1,0:T(8,128)(2,1)}, bf16[2,1,64,1536]{3,2,1,0:T(8,128)(2,1)S(1)}, u32[]{:S(2)}, u32[]{:S(2)}) collective-permute-start(bf16[2,1,64,1536]{3,2,1,0:T(8,128)(2,1)} %get-tuple-element.14), channel_id=1, source_target_pairs={{1,0},{3,2},{5,4},{7,6},{9,8},{11,10},{13,12},{15,14},{17,16},{19,... | collective-permute-start | bytes 1179656 | tf_op jit(solution)/shard_map/ppermute | solution.py:34
  28.4 4.3 %collective-permute-done.18.rest_16_ = bf16[2,1,64,1536]{3,2,1,0:T(8,128)(2,1)} collective-permute-done((bf16[2,1,64,1536]{3,2,1,0:T(8,128)(2,1)}, bf16[2,1,64,1536]{3,2,1,0:T(8,128)(2,1)}, u32[]{:S(2)}, u32[]{:S(2)}) %collective-permute-start.18) | collective-permute-done | bytes 393248 | tf_op jit(solution)/shard_map/ppermute | solution.py:70
  32.7 0.6 collective-permute-start.7
  33.3 1.4 %fusion.17 = (bf16[2,1,64,1536]{3,2,0,1:T(8,128)(2,1)}, bf16[2,1,64,1536]{3,2,0,1:T(8,128)(2,1)}, bf16[2,1,64,1536]{3,2,0,1:T(8,128)(2,1)}, bf16[2,1,64,1536]{3,...) fusion(bf16[2,3,64,1536]{3,2,0,1:T(8,128)(2,1)S(1)} %select_bitcast_fusion, ...), kind=kLoop, calls=%fused_computation.73 | loop fusion | bytes 4718592 | tf_op jit(solution)/shard_map/slice | solution.py:207
  34.7 1.9 %collective-permute-start.3 = (bf16[2,1,64,1536]{3,2,0,1:T(8,128)(2,1)}, bf16[2,1,64,1536]{3,2,0,1:T(8,128)(2,1)S(1)}, u32[]{:S(2)}, u32[]{:S(2)}) collective-permute-start(bf16[2,1,64,1536]{3,2,0,1:T(8,128)(2,1)} %get-tuple-element.30), channel_id=1, source_target_pairs={{0,2},{2,4},{4,6},{6,8},{8,10},{10,12},{12,14},{1,3},{3,5},{5,7},{... | collective-permute-start | bytes 1179656 | tf_op jit(solution)/shard_map/ppermute | solution.py:34
  36.7 4.8 %collective-permute-start.5 = (bf16[2,1,64,1536]{3,2,0,1:T(8,128)(2,1)}, bf16[2,1,64,1536]{3,2,0,1:T(8,128)(2,1)S(1)}, u32[]{:S(2)}, u32[]{:S(2)}) collective-permute-start(bf16[2,1,64,1536]{3,2,0,1:T(8,128)(2,1)} %get-tuple-element.18), channel_id=1, source_target_pairs={{2,0},{4,2},{6,4},{8,6},{10,8},{12,10},{14,12},{3,1},{5,3},{7,5},{... | collective-permute-start | bytes 1179656 | tf_op jit(solution)/shard_map/ppermute | solution.py:34
  41.5 1.5 %collective-permute-start.20 = (bf16[2,1,64,1536]{3,2,1,0:T(8,128)(2,1)}, bf16[2,1,64,1536]{3,2,1,0:T(8,128)(2,1)}, u32[]{:S(2)}, u32[]{:S(2)}) collective-permute-start(bf16[2,1,64,1536]{3,2,1,0:T(8,128)(2,1)} %collective-permute-done.18.rest_16_), channel_id=1, source_target_pairs={{4,0},{8,4},{12,8},{14,12},{10,14},{6,10},{2,6},{0,2},{5,1},{9,5},... | collective-permute-start | bytes 1179656 | tf_op jit(solution)/shard_map/ppermute | solution.py:70
  43.0 0.1 collective-permute-start.13
  43.0 2.0 %collective-permute-start.19 = (bf16[2,1,64,1536]{3,2,1,0:T(8,128)(2,1)}, bf16[2,1,64,1536]{3,2,1,0:T(8,128)(2,1)}, u32[]{:S(2)}, u32[]{:S(2)}) collective-permute-start(bf16[2,1,64,1536]{3,2,1,0:T(8,128)(2,1)} %collective-permute-done.17.rest_15_), channel_id=1, source_target_pairs={{0,4},{4,8},{8,12},{12,14},{14,10},{10,6},{6,2},{2,0},{1,5},{5,9},... | collective-permute-start | bytes 1179656 | tf_op jit(solution)/shard_map/ppermute | solution.py:67
  45.0 0.6 dynamic_slice.3
  45.6 0.6 gather_fusion
  46.3 0.6 fusion.6
  46.9 5.1 %collective-permute-done.3 = bf16[2,1,64,1536]{3,2,0,1:T(8,128)(2,1)S(1)} collective-permute-done((bf16[2,1,64,1536]{3,2,0,1:T(8,128)(2,1)}, bf16[2,1,64,1536]{3,2,0,1:T(8,128)(2,1)S(1)}, u32[]{:S(2)}, u32[]{:S(2)}) %collective-permute-start.3) | collective-permute-done | bytes 393248 | tf_op jit(solution)/shard_map/ppermute | solution.py:34
  52.0 0.7 collective-permute-start.10
  52.7 2.3 %collective-permute-done.5 = bf16[2,1,64,1536]{3,2,0,1:T(8,128)(2,1)S(1)} collective-permute-done((bf16[2,1,64,1536]{3,2,0,1:T(8,128)(2,1)}, bf16[2,1,64,1536]{3,2,0,1:T(8,128)(2,1)S(1)}, u32[]{:S(2)}, u32[]{:S(2)}) %collective-permute-start.5) | collective-permute-done | bytes 393248 | tf_op jit(solution)/shard_map/ppermute | solution.py:34
  55.0 1.4 %collective-permute-start.11 = (bf16[2,1,64,1536]{3,2,0,1:T(8,128)(2,1)}, bf16[2,1,64,1536]{3,2,0,1:T(8,128)(2,1)}, u32[]{:S(2)}, u32[]{:S(2)}) collective-permute-start(bf16[2,1,64,1536]{3,2,0,1:T(8,128)(2,1)} %get-tuple-element.13), channel_id=1, source_target_pairs={{2,0},{3,1},{18,16},{19,17}} | collective-permute-start | bytes 1179656 | tf_op jit(solution)/shard_map/ppermute | solution.py:215
  56.4 4.3 %collective-permute-done.20.rest_18_ = bf16[2,1,64,1536]{3,2,1,0:T(8,128)(2,1)} collective-permute-done((bf16[2,1,64,1536]{3,2,1,0:T(8,128)(2,1)}, bf16[2,1,64,1536]{3,2,1,0:T(8,128)(2,1)}, u32[]{:S(2)}, u32[]{:S(2)}) %collective-permute-start.20) | collective-permute-done | bytes 393248 | tf_op jit(solution)/shard_map/ppermute | solution.py:70
  60.7 1.9 %collective-permute-start.8 = (bf16[2,1,64,1536]{3,2,0,1:T(8,128)(2,1)}, bf16[2,1,64,1536]{3,2,0,1:T(8,128)(2,1)}, u32[]{:S(2)}, u32[]{:S(2)}) collective-permute-start(bf16[2,1,64,1536]{3,2,0,1:T(8,128)(2,1)} %get-tuple-element.10), channel_id=1, source_target_pairs={{0,2},{2,4},{4,6},{6,8},{8,10},{10,12},{12,14},{1,3},{3,5},{5,7},{... | collective-permute-start | bytes 1179656 | tf_op jit(solution)/shard_map/ppermute | solution.py:34
  62.6 2.9 %collective-permute-done.13.rest_11_ = bf16[2,1,64,1536]{3,2,1,0:T(8,128)(2,1)S(1)} collective-permute-done((bf16[2,1,64,1536]{3,2,1,0:T(8,128)(2,1)S(1)}, bf16[2,1,64,1536]{3,2,1,0:T(8,128)(2,1)S(1)}, u32[]{:S(2)}, u32[]{:S(2)}) %collective-permute-start.13) | collective-permute-done | bytes 393248 | tf_op jit(solution)/shard_map/ppermute | solution.py:70
  65.5 15.2 %collective-permute-start.14 = (bf16[2,1,64,1536]{3,2,1,0:T(8,128)(2,1)S(1)}, bf16[2,1,64,1536]{3,2,1,0:T(8,128)(2,1)}, u32[]{:S(2)}, u32[]{:S(2)}) collective-permute-start(bf16[2,1,64,1536]{3,2,1,0:T(8,128)(2,1)S(1)} %collective-permute-done.7.rest_10_), channel_id=1, source_target_pairs={{0,4},{4,8},{8,12},{12,14},{14,10},{10,6},{6,2},{2,0},{1,5},{5,9},... | collective-permute-start | bytes 1179656 | tf_op jit(solution)/shard_map/ppermute | solution.py:67
  80.7 0.6 fusion.15
  81.3 1.3 reduce-window.34
  82.6 1.4 %reduce-window.35 = s32[4,1]{0,1:T(1,128)} reduce-window(s32[4,1]{0,1:T(1,128)} %get-tuple-element.29, s32[]{:T(128)} %constant.98.clone), window={size=4x1 pad=3_0x0_0}, to_apply=%region_1.2 | reduce-window | flops 12 | bytes 36 | tf_op jit(solution)/shard_map/reduce-window.15
  84.0 0.6 gather_fusion.1
  84.6 0.6 gather_fusion.2
  85.3 0.1 pad_bitcast_fusion
  85.3 0.7 compare_select_fusion.10
  86.0 1.9 %collective-permute-start.9 = (bf16[2,1,64,1536]{3,2,0,1:T(8,128)(2,1)}, bf16[2,1,64,1536]{3,2,0,1:T(8,128)(2,1)}, u32[]{:S(2)}, u32[]{:S(2)}) collective-permute-start(bf16[2,1,64,1536]{3,2,0,1:T(8,128)(2,1)} %get-tuple-element.11), channel_id=1, source_target_pairs={{2,0},{4,2},{6,4},{8,6},{10,8},{12,10},{14,12},{3,1},{5,3},{7,5},{... | collective-permute-start | bytes 1179656 | tf_op jit(solution)/shard_map/ppermute | solution.py:34
  87.9 0.1 collective-permute-start.15
  88.0 2.1 %collective-permute-start.21 = (bf16[2,1,64,1536]{3,2,1,0:T(8,128)(2,1)}, bf16[2,1,64,1536]{3,2,1,0:T(8,128)(2,1)}, u32[]{:S(2)}, u32[]{:S(2)}) collective-permute-start(bf16[2,1,64,1536]{3,2,1,0:T(8,128)(2,1)} %collective-permute-done.19.rest_17_), channel_id=1, source_target_pairs={{0,4},{4,8},{8,12},{12,14},{14,10},{10,6},{6,2},{2,0},{1,5},{5,9},... | collective-permute-start | bytes 1179656 | tf_op jit(solution)/shard_map/ppermute | solution.py:67
  90.1 2.7 %collective-permute-start.16 = (bf16[2,1,64,1536]{3,2,1,0:T(8,128)(2,1)}, bf16[2,1,64,1536]{3,2,1,0:T(8,128)(2,1)}, u32[]{:S(2)}, u32[]{:S(2)}) collective-permute-start(bf16[2,1,64,1536]{3,2,1,0:T(8,128)(2,1)} %collective-permute-done.14.rest_12_), channel_id=1, source_target_pairs={{0,4},{4,8},{8,12},{12,14},{14,10},{10,6},{6,2},{2,0},{1,5},{5,9},... | collective-permute-start | bytes 1179656 | tf_op jit(solution)/shard_map/ppermute | solution.py:62
  92.8 0.1 collective-permute-done.22.rest_20_
  92.9 0.1 collective-permute-start.23
  93.0 0.1 add_bitcast_fusion
  93.1 0.1 copy.31
  93.2 0.1 reshape.421.table_ref
  93.2 5.7 %collective-permute-done.9 = bf16[2,1,64,1536]{3,2,0,1:T(8,128)(2,1)} collective-permute-done((bf16[2,1,64,1536]{3,2,0,1:T(8,128)(2,1)}, bf16[2,1,64,1536]{3,2,0,1:T(8,128)(2,1)}, u32[]{:S(2)}, u32[]{:S(2)}) %collective-permute-start.9) | collective-permute-done | bytes 393248 | tf_op jit(solution)/shard_map/ppermute | solution.py:34
  99.0 10.8 %collective-permute-done.15.rest_13_ = bf16[2,1,64,1536]{3,2,1,0:T(8,128)(2,1)} collective-permute-done((bf16[2,1,64,1536]{3,2,1,0:T(8,128)(2,1)S(1)}, bf16[2,1,64,1536]{3,2,1,0:T(8,128)(2,1)}, u32[]{:S(2)}, u32[]{:S(2)}) %collective-permute-start.15) | collective-permute-done | bytes 393248 | tf_op jit(solution)/shard_map/ppermute | solution.py:70
  109.8 7.3 %collective-permute-done.23.rest_21_ = bf16[2,1,64,1536]{3,2,1,0:T(8,128)(2,1)} collective-permute-done((bf16[2,1,64,1536]{3,2,1,0:T(8,128)(2,1)}, bf16[2,1,64,1536]{3,2,1,0:T(8,128)(2,1)}, u32[]{:S(2)}, u32[]{:S(2)}) %collective-permute-start.23) | collective-permute-done | bytes 393248 | tf_op jit(solution)/shard_map/ppermute | solution.py:64
  117.0 14.3 %shard_map.100 = bf16[512,1536]{1,0:T(8,128)(2,1)} custom-call(s32[16]{0:T(128)S(1)} %reshape.421.table_ref, bf16[512,1536]{1,0:T(8,128)(2,1)} %bitcast.93, bf16[2,8,64,1536]{3,2,1,0:T(8,128)(2,1)} %copy-done.2, bf16[2,1,64,1536]{3,2,1,0:T(8,128)(2,1)S(1)} %collective-permute-done.rest_0_, bf16[2,1,64,1536]{3,2,1,0:T(8,128)(2,1)S(1)} %collective-permute-done.1.rest_1_, ...), custom_call_target="tpu_custom_call" | custom-call | flops 3221225472 | bytes 9437184 | tf_op jit(solution)/shard_map/pallas_call | solution.py:142
  (46 shorter events, 0.2 us)
Async XLA Ops:
  0.0 15.8 %collective-permute-start.4 = (s32[4]{0:T(128)}, s32[4]{0:T(128)S(1)}, u32[]{:S(2)}, u32[]{:S(2)}) collective-permute-start(s32[4]{0:T(128)} %bitcast.94), channel_id=1, source_target_pairs={{0,2},{2,4},{4,6},{6,8},{8,10},{10,12},{12,14},{1,3},{3,5},{5,7},{... | collective-permute-start | bytes 56 | tf_op jit(solution)/shard_map/ppermute | solution.py:34
  3.4 14.2 %collective-permute-start.2 = (s32[4]{0:T(128)}, s32[4]{0:T(128)S(1)}, u32[]{:S(2)}, u32[]{:S(2)}) collective-permute-start(s32[4]{0:T(128)} %bitcast.95), channel_id=1, source_target_pairs={{2,0},{4,2},{6,4},{8,6},{10,8},{12,10},{14,12},{3,1},{5,3},{7,5},{... | collective-permute-start | bytes 56 | tf_op jit(solution)/shard_map/ppermute | solution.py:34
  8.7 1.9 %copy-start.4 = (bf16[8,1,64,1536]{3,2,1,0:T(8,128)(2,1)S(1)}, bf16[8,1,64,1536]{3,2,1,0:T(8,128)(2,1)}, u32[]{:S(2)}) copy-start(bf16[8,1,64,1536]{3,2,1,0:T(8,128)(2,1)} %param.15) | copy-start | bytes 4718596
  11.2 3.6 %copy-start.2 = (bf16[2,8,64,1536]{3,2,1,0:T(8,128)(2,1)}, bf16[2,8,64,1536]{3,2,1,0:T(8,128)(2,1)S(1)}, u32[]{:S(2)}) copy-start(bf16[2,8,64,1536]{3,2,1,0:T(8,128)(2,1)S(1)} %maximum_bitcast_fusion.own_hbm) | copy-start | bytes 9437188
  12.4 14.5 %collective-permute-start.6 = (bf16[2,1,64,1536]{3,2,1,0:T(8,128)(2,1)}, bf16[2,1,64,1536]{3,2,1,0:T(8,128)(2,1)S(1)}, u32[]{:S(2)}, u32[]{:S(2)}) collective-permute-start(bf16[2,1,64,1536]{3,2,1,0:T(8,128)(2,1)} %get-tuple-element.23), channel_id=1, source_target_pairs={{0,4},{4,8},{8,12},{12,14},{14,10},{10,6},{6,2},{2,0},{1,5},{5,9},... | collective-permute-start | bytes 1179656 | tf_op jit(solution)/shard_map/ppermute | solution.py:67
  13.9 20.8 %collective-permute-start.12 = (bf16[2,1,64,1536]{3,2,1,0:T(8,128)(2,1)}, bf16[2,1,64,1536]{3,2,1,0:T(8,128)(2,1)S(1)}, u32[]{:S(2)}, u32[]{:S(2)}) collective-permute-start(bf16[2,1,64,1536]{3,2,1,0:T(8,128)(2,1)} %get-tuple-element.23), channel_id=1, source_target_pairs={{4,0},{8,4},{12,8},{14,12},{10,14},{6,10},{2,6},{0,2},{5,1},{9,5},... | collective-permute-start | bytes 1179656 | tf_op jit(solution)/shard_map/ppermute | solution.py:70
  14.4 18.3 %collective-permute-start.18 = (bf16[2,1,64,1536]{3,2,1,0:T(8,128)(2,1)}, bf16[2,1,64,1536]{3,2,1,0:T(8,128)(2,1)}, u32[]{:S(2)}, u32[]{:S(2)}) collective-permute-start(bf16[2,1,64,1536]{3,2,1,0:T(8,128)(2,1)} %get-tuple-element.22), channel_id=1, source_target_pairs={{4,0},{8,4},{12,8},{14,12},{10,14},{6,10},{2,6},{0,2},{5,1},{9,5},... | collective-permute-start | bytes 1179656 | tf_op jit(solution)/shard_map/ppermute | solution.py:70
  15.8 20.9 %collective-permute-start.17 = (bf16[2,1,64,1536]{3,2,1,0:T(8,128)(2,1)}, bf16[2,1,64,1536]{3,2,1,0:T(8,128)(2,1)}, u32[]{:S(2)}, u32[]{:S(2)}) collective-permute-start(bf16[2,1,64,1536]{3,2,1,0:T(8,128)(2,1)} %get-tuple-element.22), channel_id=1, source_target_pairs={{0,4},{4,8},{8,12},{12,14},{14,10},{10,6},{6,2},{2,0},{1,5},{5,9},... | collective-permute-start | bytes 1179656 | tf_op jit(solution)/shard_map/ppermute | solution.py:67
  17.7 23.8 %collective-permute-start = (bf16[2,1,64,1536]{3,2,1,0:T(8,128)(2,1)}, bf16[2,1,64,1536]{3,2,1,0:T(8,128)(2,1)S(1)}, u32[]{:S(2)}, u32[]{:S(2)}) collective-permute-start(bf16[2,1,64,1536]{3,2,1,0:T(8,128)(2,1)} %get-tuple-element.15), channel_id=1, source_target_pairs={{0,1},{2,3},{4,5},{6,7},{8,9},{10,11},{12,13},{14,15},{16,17},{18,... | collective-permute-start | bytes 1179656 | tf_op jit(solution)/shard_map/ppermute | solution.py:34
  25.4 1.3 copy-start.3
  26.9 18.1 %copy-start.5 = (s32[1,1,4]{2,1,0:T(1,128)S(1)}, s32[1,1,4]{2,1,0:T(1,128)}, u32[]{:S(2)}) copy-start(s32[1,1,4]{2,1,0:T(1,128)} %param.18) | copy-start | bytes 52
  26.9 18.1 %copy-start = (s32[8]{0:T(128)S(1)}, s32[8]{0:T(128)}, u32[]{:S(2)}) copy-start(s32[8]{0:T(128)} %constant.96.clone) | copy-start | bytes 100
  26.9 19.4 %copy-start.6 = (s32[1,1,4]{2,1,0:T(1,128)S(1)}, s32[1,1,4]{2,1,0:T(1,128)}, u32[]{:S(2)}) copy-start(s32[1,1,4]{2,1,0:T(1,128)} %param.17) | copy-start | bytes 52
  26.9 57.0 %copy-start.1 = (s32[7,2]{1,0:T(8,128)S(1)}, s32[7,2]{1,0:T(8,128)}, u32[]{:S(2)}) copy-start(s32[7,2]{1,0:T(8,128)} %constant.97.clone) | copy-start | bytes 172
  27.0 16.0 %collective-permute-start.1 = (bf16[2,1,64,1536]{3,2,1,0:T(8,128)(2,1)}, bf16[2,1,64,1536]{3,2,1,0:T(8,128)(2,1)S(1)}, u32[]{:S(2)}, u32[]{:S(2)}) collective-permute-start(bf16[2,1,64,1536]{3,2,1,0:T(8,128)(2,1)} %get-tuple-element.14), channel_id=1, source_target_pairs={{1,0},{3,2},{5,4},{7,6},{9,8},{11,10},{13,12},{15,14},{17,16},{19,... | collective-permute-start | bytes 1179656 | tf_op jit(solution)/shard_map/ppermute | solution.py:34
  32.7 10.3 %collective-permute-start.7 = (bf16[2,1,64,1536]{3,2,1,0:T(8,128)(2,1)S(1)}, bf16[2,1,64,1536]{3,2,1,0:T(8,128)(2,1)S(1)}, u32[]{:S(2)}, u32[]{:S(2)}) collective-permute-start(bf16[2,1,64,1536]{3,2,1,0:T(8,128)(2,1)S(1)} %collective-permute-done.6.rest_8_), channel_id=1, source_target_pairs={{0,4},{4,8},{8,12},{12,14},{14,10},{10,6},{6,2},{2,0},{1,5},{5,9},... | collective-permute-start | bytes 1179656 | tf_op jit(solution)/shard_map/ppermute | solution.py:67
  34.7 17.2 %collective-permute-start.3 = (bf16[2,1,64,1536]{3,2,0,1:T(8,128)(2,1)}, bf16[2,1,64,1536]{3,2,0,1:T(8,128)(2,1)S(1)}, u32[]{:S(2)}, u32[]{:S(2)}) collective-permute-start(bf16[2,1,64,1536]{3,2,0,1:T(8,128)(2,1)} %get-tuple-element.30), channel_id=1, source_target_pairs={{0,2},{2,4},{4,6},{6,8},{8,10},{10,12},{12,14},{1,3},{3,5},{5,7},{... | collective-permute-start | bytes 1179656 | tf_op jit(solution)/shard_map/ppermute | solution.py:34
  36.7 18.3 %collective-permute-start.5 = (bf16[2,1,64,1536]{3,2,0,1:T(8,128)(2,1)}, bf16[2,1,64,1536]{3,2,0,1:T(8,128)(2,1)S(1)}, u32[]{:S(2)}, u32[]{:S(2)}) collective-permute-start(bf16[2,1,64,1536]{3,2,0,1:T(8,128)(2,1)} %get-tuple-element.18), channel_id=1, source_target_pairs={{2,0},{4,2},{6,4},{8,6},{10,8},{12,10},{14,12},{3,1},{5,3},{7,5},{... | collective-permute-start | bytes 1179656 | tf_op jit(solution)/shard_map/ppermute | solution.py:34
  41.5 19.2 %collective-permute-start.20 = (bf16[2,1,64,1536]{3,2,1,0:T(8,128)(2,1)}, bf16[2,1,64,1536]{3,2,1,0:T(8,128)(2,1)}, u32[]{:S(2)}, u32[]{:S(2)}) collective-permute-start(bf16[2,1,64,1536]{3,2,1,0:T(8,128)(2,1)} %collective-permute-done.18.rest_16_), channel_id=1, source_target_pairs={{4,0},{8,4},{12,8},{14,12},{10,14},{6,10},{2,6},{0,2},{5,1},{9,5},... | collective-permute-start | bytes 1179656 | tf_op jit(solution)/shard_map/ppermute | solution.py:70
  43.0 22.6 %collective-permute-start.13 = (bf16[2,1,64,1536]{3,2,1,0:T(8,128)(2,1)S(1)}, bf16[2,1,64,1536]{3,2,1,0:T(8,128)(2,1)S(1)}, u32[]{:S(2)}, u32[]{:S(2)}) collective-permute-start(bf16[2,1,64,1536]{3,2,1,0:T(8,128)(2,1)S(1)} %collective-permute-done.12.rest_9_), channel_id=1, source_target_pairs={{4,0},{8,4},{12,8},{14,12},{10,14},{6,10},{2,6},{0,2},{5,1},{9,5},... | collective-permute-start | bytes 1179656 | tf_op jit(solution)/shard_map/ppermute | solution.py:70
  43.0 37.7 %collective-permute-start.19 = (bf16[2,1,64,1536]{3,2,1,0:T(8,128)(2,1)}, bf16[2,1,64,1536]{3,2,1,0:T(8,128)(2,1)}, u32[]{:S(2)}, u32[]{:S(2)}) collective-permute-start(bf16[2,1,64,1536]{3,2,1,0:T(8,128)(2,1)} %collective-permute-done.17.rest_15_), channel_id=1, source_target_pairs={{0,4},{4,8},{8,12},{12,14},{14,10},{10,6},{6,2},{2,0},{1,5},{5,9},... | collective-permute-start | bytes 1179656 | tf_op jit(solution)/shard_map/ppermute | solution.py:67
  52.0 34.0 %collective-permute-start.10 = (bf16[2,1,64,1536]{3,2,0,1:T(8,128)(2,1)}, bf16[2,1,64,1536]{3,2,0,1:T(8,128)(2,1)S(1)}, u32[]{:S(2)}, u32[]{:S(2)}) collective-permute-start(bf16[2,1,64,1536]{3,2,0,1:T(8,128)(2,1)} %get-tuple-element.12), channel_id=1, source_target_pairs={{12,14},{13,15},{28,30},{29,31}} | collective-permute-start | bytes 1179656 | tf_op jit(solution)/shard_map/ppermute | solution.py:214
  55.0 33.0 %collective-permute-start.11 = (bf16[2,1,64,1536]{3,2,0,1:T(8,128)(2,1)}, bf16[2,1,64,1536]{3,2,0,1:T(8,128)(2,1)}, u32[]{:S(2)}, u32[]{:S(2)}) collective-permute-start(bf16[2,1,64,1536]{3,2,0,1:T(8,128)(2,1)} %get-tuple-element.13), channel_id=1, source_target_pairs={{2,0},{3,1},{18,16},{19,17}} | collective-permute-start | bytes 1179656 | tf_op jit(solution)/shard_map/ppermute | solution.py:215
  60.7 27.3 %collective-permute-start.8 = (bf16[2,1,64,1536]{3,2,0,1:T(8,128)(2,1)}, bf16[2,1,64,1536]{3,2,0,1:T(8,128)(2,1)}, u32[]{:S(2)}, u32[]{:S(2)}) collective-permute-start(bf16[2,1,64,1536]{3,2,0,1:T(8,128)(2,1)} %get-tuple-element.10), channel_id=1, source_target_pairs={{0,2},{2,4},{4,6},{6,8},{8,10},{10,12},{12,14},{1,3},{3,5},{5,7},{... | collective-permute-start | bytes 1179656 | tf_op jit(solution)/shard_map/ppermute | solution.py:34
  65.5 24.6 %collective-permute-start.14 = (bf16[2,1,64,1536]{3,2,1,0:T(8,128)(2,1)S(1)}, bf16[2,1,64,1536]{3,2,1,0:T(8,128)(2,1)}, u32[]{:S(2)}, u32[]{:S(2)}) collective-permute-start(bf16[2,1,64,1536]{3,2,1,0:T(8,128)(2,1)S(1)} %collective-permute-done.7.rest_10_), channel_id=1, source_target_pairs={{0,4},{4,8},{8,12},{12,14},{14,10},{10,6},{6,2},{2,0},{1,5},{5,9},... | collective-permute-start | bytes 1179656 | tf_op jit(solution)/shard_map/ppermute | solution.py:67
  80.7 12.2 %collective-permute-start.22 = (bf16[2,1,64,1536]{3,2,1,0:T(8,128)(2,1)}, bf16[2,1,64,1536]{3,2,1,0:T(8,128)(2,1)}, u32[]{:S(2)}, u32[]{:S(2)}) collective-permute-start(bf16[2,1,64,1536]{3,2,1,0:T(8,128)(2,1)} %collective-permute-done.20.rest_18_), channel_id=1, source_target_pairs={{4,0},{8,4},{12,8},{14,12},{10,14},{6,10},{2,6},{0,2},{5,1},{9,5},... | collective-permute-start | bytes 1179656 | tf_op jit(solution)/shard_map/ppermute | solution.py:70
  86.0 13.0 %collective-permute-start.9 = (bf16[2,1,64,1536]{3,2,0,1:T(8,128)(2,1)}, bf16[2,1,64,1536]{3,2,0,1:T(8,128)(2,1)}, u32[]{:S(2)}, u32[]{:S(2)}) collective-permute-start(bf16[2,1,64,1536]{3,2,0,1:T(8,128)(2,1)} %get-tuple-element.11), channel_id=1, source_target_pairs={{2,0},{4,2},{6,4},{8,6},{10,8},{12,10},{14,12},{3,1},{5,3},{7,5},{... | collective-permute-start | bytes 1179656 | tf_op jit(solution)/shard_map/ppermute | solution.py:34
  87.9 21.8 %collective-permute-start.15 = (bf16[2,1,64,1536]{3,2,1,0:T(8,128)(2,1)S(1)}, bf16[2,1,64,1536]{3,2,1,0:T(8,128)(2,1)}, u32[]{:S(2)}, u32[]{:S(2)}) collective-permute-start(bf16[2,1,64,1536]{3,2,1,0:T(8,128)(2,1)S(1)} %collective-permute-done.13.rest_11_), channel_id=1, source_target_pairs={{4,0},{8,4},{12,8},{14,12},{10,14},{6,10},{2,6},{0,2},{5,1},{9,5},... | collective-permute-start | bytes 1179656 | tf_op jit(solution)/shard_map/ppermute | solution.py:70
  88.0 21.7 %collective-permute-start.21 = (bf16[2,1,64,1536]{3,2,1,0:T(8,128)(2,1)}, bf16[2,1,64,1536]{3,2,1,0:T(8,128)(2,1)}, u32[]{:S(2)}, u32[]{:S(2)}) collective-permute-start(bf16[2,1,64,1536]{3,2,1,0:T(8,128)(2,1)} %collective-permute-done.19.rest_17_), channel_id=1, source_target_pairs={{0,4},{4,8},{8,12},{12,14},{14,10},{10,6},{6,2},{2,0},{1,5},{5,9},... | collective-permute-start | bytes 1179656 | tf_op jit(solution)/shard_map/ppermute | solution.py:67
  90.1 19.7 %collective-permute-start.16 = (bf16[2,1,64,1536]{3,2,1,0:T(8,128)(2,1)}, bf16[2,1,64,1536]{3,2,1,0:T(8,128)(2,1)}, u32[]{:S(2)}, u32[]{:S(2)}) collective-permute-start(bf16[2,1,64,1536]{3,2,1,0:T(8,128)(2,1)} %collective-permute-done.14.rest_12_), channel_id=1, source_target_pairs={{0,4},{4,8},{8,12},{12,14},{14,10},{10,6},{6,2},{2,0},{1,5},{5,9},... | collective-permute-start | bytes 1179656 | tf_op jit(solution)/shard_map/ppermute | solution.py:62
  92.9 24.1 %collective-permute-start.23 = (bf16[2,1,64,1536]{3,2,1,0:T(8,128)(2,1)}, bf16[2,1,64,1536]{3,2,1,0:T(8,128)(2,1)}, u32[]{:S(2)}, u32[]{:S(2)}) collective-permute-start(bf16[2,1,64,1536]{3,2,1,0:T(8,128)(2,1)} %collective-permute-done.22.rest_20_), channel_id=1, source_target_pairs={{4,0},{8,4},{12,8},{14,12},{10,14},{6,10},{2,6},{0,2},{5,1},{9,5},... | collective-permute-start | bytes 1179656 | tf_op jit(solution)/shard_map/ppermute | solution.py:64

commit v12 on v11

--- a/solution.py
+++ b/solution.py
@@ -199,14 +199,13 @@
     to_left, _, _ = side_slots(left_entries, 2 + tile_blocks, tile_blocks, edge_cap)
     right_payload = jnp.take(stacked, to_right, axis=1)
     left_payload = jnp.take(stacked, to_left, axis=1)
-    later = far_sources[min(2, len(far_sources) - 1)]
     cycle_sources = [above, below]
     last = col_count - 1
     for slot in range(edge_cap):
         to_r = right_payload[:, slot : slot + 1]
         to_l = left_payload[:, slot : slot + 1]
-        if slot > 0:
-            to_r, to_l, _ = lax.optimization_barrier((to_r, to_l, later))
+        later = far_sources[min(2 * slot, len(far_sources) - 1)]
+        to_r, to_l, _ = lax.optimization_barrier((to_r, to_l, later))
         if slot < main_cap:
             cycle_sources.append(shift(to_r, "col", col_count, 1))
             cycle_sources.append(shift(to_l, "col", col_count, -1))

time: 133 us -> 131 us (0.985)
  the two profiles are of different devices: /device:TPU:16 before, /device:TPU:24 now
where the time goes in v12:
time: 131 us
  waiting for transfers between devices  51.3 us (39%)
  starting transfers between devices  39.8 us (30%)
  Pallas kernels  15.1 us (12%)
  local copies, waits for them, and re-layouts  13.4 us (10%)
  other arithmetic  10.9 us (8%)
    ppermute x6, waiting for transfers between devices, ring_gather(): behind = lax.ppermute(behind, 'col', backward)  35.5 us
    ppermute x8, starting transfers between devices, shift(): return lax.ppermute(x, axis, pairs)  20.9 us
    pallas_call x1, Pallas kernels, gather_attend(): pl.pallas_call(kernel, out_shape=jax.ShapeDtypeStruct((token_count, width...  15.1 us
    ppermute x6, starting transfers between devices, ring_gather(): ahead = lax.ppermute(ahead, 'col', forward)  7.93 us
    ppermute x1, waiting for transfers between devices, ring_gather(): arrays.append(lax.ppermute(ahead, 'col', forward))  6.95 us
    ppermute x6, starting transfers between devices, ring_gather(): behind = lax.ppermute(behind, 'col', backward)  4.9 us
    ppermute x8, waiting for transfers between devices, shift(): return lax.ppermute(x, axis, pairs)  4.77 us
    ppermute x1, starting transfers between devices, per_device(): cycle_sources.append(lax.ppermute(to_r, 'col', [(last - 1, last)]))  4.65 us
  transfers between devices with their start and end apart: 24, of which 10 were waited for; matrix products, arithmetic and copies ran while one was open for 18% of the time, Pallas kernels for 0%

profile of v12, /device:TPU:24, one launch (start us, length us, event | category | flops | bytes accessed | tf_op | source)
XLA Modules:
  0.0 130.9 jit_solution(8815860510094303737)
XLA Ops:
  0.0 3.4 %collective-permute-start.3 = (s32[4]{0:T(128)}, s32[4]{0:T(128)S(1)}, u32[]{:S(2)}, u32[]{:S(2)}) collective-permute-start(s32[4]{0:T(128)} %bitcast.93), channel_id=1, source_target_pairs={{0,2},{2,4},{4,6},{6,8},{8,10},{10,12},{12,14},{1,3},{3,5},{5,7},{... | collective-permute-start | bytes 56 | tf_op jit(solution)/shard_map/ppermute | solution.py:34
  3.4 3.3 %collective-permute-start.2 = (s32[4]{0:T(128)}, s32[4]{0:T(128)S(1)}, u32[]{:S(2)}, u32[]{:S(2)}) collective-permute-start(s32[4]{0:T(128)} %bitcast.94), channel_id=1, source_target_pairs={{2,0},{4,2},{6,4},{8,6},{10,8},{12,10},{14,12},{3,1},{5,3},{7,5},{... | collective-permute-start | bytes 56 | tf_op jit(solution)/shard_map/ppermute | solution.py:34
  6.8 1.0 exponential_bitcast_fusion.1
  7.7 1.0 exponential_bitcast_fusion
  8.7 1.8 %fusion.1 = bf16[8,1,64,1536]{3,2,0,1:T(8,128)(2,1)S(1)} fusion(bf16[8,1,64,1536]{3,2,1,0:T(8,128)(2,1)} %param.13, f32[8,2,1536]{2,1,0:T(2,128)S(1)} %exponential_bitcast_fusion.1), kind=kLoop, calls=%fused_computation.9 | loop fusion | flops 2359296 | bytes 3244032 | tf_op jit(solution)/shard_map/convert_element_type | solution.py:24
  10.5 0.1 copy-done.4
  10.6 0.3 fusion
  10.9 0.3 maximum_bitcast_fusion.own_hbm
  11.2 0.1 slice.37
  11.3 0.9 fusion.19
  12.2 0.6 collective-permute-start.4
  12.8 1.4 %collective-permute-start.13 = (bf16[2,1,64,1536]{3,2,1,0:T(8,128)(2,1)}, bf16[2,1,64,1536]{3,2,1,0:T(8,128)(2,1)S(1)}, u32[]{:S(2)}, u32[]{:S(2)}) collective-permute-start(bf16[2,1,64,1536]{3,2,1,0:T(8,128)(2,1)} %get-tuple-element.27), channel_id=1, source_target_pairs={{4,0},{8,4},{12,8},{14,12},{10,14},{6,10},{2,6},{0,2},{5,1},{9,5},... | collective-permute-start | bytes 1179656 | tf_op jit(solution)/shard_map/ppermute | solution.py:70
  14.2 0.4 collective-permute-start.18
  14.7 1.0 fusion.16
  15.6 1.6 %collective-permute-start.17 = (bf16[2,1,64,1536]{3,2,1,0:T(8,128)(2,1)S(1)}, bf16[2,1,64,1536]{3,2,1,0:T(8,128)(2,1)}, u32[]{:S(2)}, u32[]{:S(2)}) collective-permute-start(bf16[2,1,64,1536]{3,2,1,0:T(8,128)(2,1)S(1)} %get-tuple-element.26), channel_id=1, source_target_pairs={{0,4},{4,8},{8,12},{12,14},{14,10},{10,6},{6,2},{2,0},{1,5},{5,9},... | collective-permute-start | bytes 1179656 | tf_op jit(solution)/shard_map/ppermute | solution.py:67
  17.2 0.2 reduce-window.37
  17.4 0.1 select_reduce_fusion
  17.6 1.3 %collective-permute-start = (bf16[2,1,64,1536]{3,2,1,0:T(8,128)(2,1)}, bf16[2,1,64,1536]{3,2,1,0:T(8,128)(2,1)S(1)}, u32[]{:S(2)}, u32[]{:S(2)}) collective-permute-start(bf16[2,1,64,1536]{3,2,1,0:T(8,128)(2,1)} %get-tuple-element.19), channel_id=1, source_target_pairs={{0,1},{2,3},{4,5},{6,7},{8,9},{10,11},{12,13},{14,15},{16,17},{18,... | collective-permute-start | bytes 1179656 | tf_op jit(solution)/shard_map/ppermute | solution.py:34
  18.9 0.2 reduce-window.36
  19.1 0.1 select_reduce_fusion.1
  19.2 2.5 %gather_fusion.4 = bf16[3,2,64,1536]{3,2,1,0:T(8,128)(2,1)S(1)} fusion(bf16[2,8,64,1536]{3,2,1,0:T(8,128)(2,1)} %copy-done.2, s32[1024]{0:T(1024)S(1)} %pad_clamp_fusion), kind=kCustom, calls=%fused_computation.1.clone | custom fusion | bytes 2359308 | tf_op jit(solution)/shard_map/jit(_take)/gather | solution.py:201
  21.8 3.6 %gather_fusion.3 = bf16[3,2,64,1536]{3,2,1,0:T(8,128)(2,1)} fusion(bf16[2,8,64,1536]{3,2,1,0:T(8,128)(2,1)} %copy-done.2, s32[1024]{0:T(1024)S(1)} %pad_clamp_fusion.1), kind=kCustom, calls=%fused_computation.clone | custom fusion | bytes 2359308 | tf_op jit(solution)/shard_map/jit(_take)/gather | solution.py:200
  25.3 0.2 select_bitcast_fusion
  25.5 1.1 copy-done.3
  26.6 0.2 select_bitcast_fusion.1
  26.8 0.0 copy-start
  26.8 1.4 %collective-permute-start.1 = (bf16[2,1,64,1536]{3,2,1,0:T(8,128)(2,1)}, bf16[2,1,64,1536]{3,2,1,0:T(8,128)(2,1)S(1)}, u32[]{:S(2)}, u32[]{:S(2)}) collective-permute-start(bf16[2,1,64,1536]{3,2,1,0:T(8,128)(2,1)} %get-tuple-element.18), channel_id=1, source_target_pairs={{1,0},{3,2},{5,4},{7,6},{9,8},{11,10},{13,12},{15,14},{17,16},{19,... | collective-permute-start | bytes 1179656 | tf_op jit(solution)/shard_map/ppermute | solution.py:34
  28.3 3.3 %collective-permute-done.18.rest_16_ = bf16[2,1,64,1536]{3,2,1,0:T(8,128)(2,1)} collective-permute-done((bf16[2,1,64,1536]{3,2,1,0:T(8,128)(2,1)S(1)}, bf16[2,1,64,1536]{3,2,1,0:T(8,128)(2,1)}, u32[]{:S(2)}, u32[]{:S(2)}) %collective-permute-start.18) | collective-permute-done | bytes 393248 | tf_op jit(solution)/shard_map/ppermute | solution.py:70
  31.6 0.5 collective-permute-start.7
  32.0 1.4 %fusion.17 = (bf16[2,1,64,1536]{3,2,0,1:T(8,128)(2,1)}, bf16[2,1,64,1536]{3,2,0,1:T(8,128)(2,1)}, bf16[2,1,64,1536]{3,2,0,1:T(8,128)(2,1)}, bf16[2,1,64,1536]{3,...) fusion(bf16[2,3,64,1536]{3,2,0,1:T(8,128)(2,1)S(1)} %select_bitcast_fusion, ...), kind=kLoop, calls=%fused_computation.73 | loop fusion | bytes 4718592 | tf_op jit(solution)/shard_map/slice | solution.py:206
  33.5 2.3 %collective-permute-start.5 = (bf16[2,1,64,1536]{3,2,0,1:T(8,128)(2,1)}, bf16[2,1,64,1536]{3,2,0,1:T(8,128)(2,1)S(1)}, u32[]{:S(2)}, u32[]{:S(2)}) collective-permute-start(bf16[2,1,64,1536]{3,2,0,1:T(8,128)(2,1)} %get-tuple-element.12), channel_id=1, source_target_pairs={{0,2},{2,4},{4,6},{6,8},{8,10},{10,12},{12,14},{1,3},{3,5},{5,7},{... | collective-permute-start | bytes 1179656 | tf_op jit(solution)/shard_map/ppermute | solution.py:34
  35.8 4.4 %collective-permute-start.6 = (bf16[2,1,64,1536]{3,2,0,1:T(8,128)(2,1)}, bf16[2,1,64,1536]{3,2,0,1:T(8,128)(2,1)S(1)}, u32[]{:S(2)}, u32[]{:S(2)}) collective-permute-start(bf16[2,1,64,1536]{3,2,0,1:T(8,128)(2,1)} %get-tuple-element.13), channel_id=1, source_target_pairs={{2,0},{4,2},{6,4},{8,6},{10,8},{12,10},{14,12},{3,1},{5,3},{7,5},{... | collective-permute-start | bytes 1179656 | tf_op jit(solution)/shard_map/ppermute | solution.py:34
  40.2 1.6 %collective-permute-start.20 = (bf16[2,1,64,1536]{3,2,1,0:T(8,128)(2,1)}, bf16[2,1,64,1536]{3,2,1,0:T(8,128)(2,1)}, u32[]{:S(2)}, u32[]{:S(2)}) collective-permute-start(bf16[2,1,64,1536]{3,2,1,0:T(8,128)(2,1)} %collective-permute-done.18.rest_16_), channel_id=1, source_target_pairs={{4,0},{8,4},{12,8},{14,12},{10,14},{6,10},{2,6},{0,2},{5,1},{9,5},... | collective-permute-start | bytes 1179656 | tf_op jit(solution)/shard_map/ppermute | solution.py:70
  41.8 1.4 %collective-permute-start.14 = (bf16[2,1,64,1536]{3,2,1,0:T(8,128)(2,1)S(1)}, bf16[2,1,64,1536]{3,2,1,0:T(8,128)(2,1)S(1)}, u32[]{:S(2)}, u32[]{:S(2)}) collective-permute-start(bf16[2,1,64,1536]{3,2,1,0:T(8,128)(2,1)S(1)} %collective-permute-done.13.rest_9_), channel_id=1, source_target_pairs={{4,0},{8,4},{12,8},{14,12},{10,14},{6,10},{2,6},{0,2},{5,1},{9,5},... | collective-permute-start | bytes 1179656 | tf_op jit(solution)/shard_map/ppermute | solution.py:70
  43.3 0.8 collective-permute-start.10
  44.1 0.7 dynamic_slice.3
  44.8 0.6 gather_fusion
  45.4 1.2 fusion.6
  46.6 3.5 %collective-permute-done.5 = bf16[2,1,64,1536]{3,2,0,1:T(8,128)(2,1)S(1)} collective-permute-done((bf16[2,1,64,1536]{3,2,0,1:T(8,128)(2,1)}, bf16[2,1,64,1536]{3,2,0,1:T(8,128)(2,1)S(1)}, u32[]{:S(2)}, u32[]{:S(2)}) %collective-permute-start.5) | collective-permute-done | bytes 393248 | tf_op jit(solution)/shard_map/ppermute | solution.py:34
  50.1 2.4 %collective-permute-start.19 = (bf16[2,1,64,1536]{3,2,1,0:T(8,128)(2,1)}, bf16[2,1,64,1536]{3,2,1,0:T(8,128)(2,1)}, u32[]{:S(2)}, u32[]{:S(2)}) collective-permute-start(bf16[2,1,64,1536]{3,2,1,0:T(8,128)(2,1)} %collective-permute-done.17.rest_15_), channel_id=1, source_target_pairs={{0,4},{4,8},{8,12},{12,14},{14,10},{10,6},{6,2},{2,0},{1,5},{5,9},... | collective-permute-start | bytes 1179656 | tf_op jit(solution)/shard_map/ppermute | solution.py:67
  52.5 1.3 collective-permute-done.6
  53.8 2.8 %collective-permute-start.8 = (bf16[2,1,64,1536]{3,2,0,1:T(8,128)(2,1)}, bf16[2,1,64,1536]{3,2,0,1:T(8,128)(2,1)}, u32[]{:S(2)}, u32[]{:S(2)}) collective-permute-start(bf16[2,1,64,1536]{3,2,0,1:T(8,128)(2,1)} %get-tuple-element.14), channel_id=1, source_target_pairs={{0,2},{2,4},{4,6},{6,8},{8,10},{10,12},{12,14},{1,3},{3,5},{5,7},{... | collective-permute-start | bytes 1179656 | tf_op jit(solution)/shard_map/ppermute | solution.py:34
  56.6 8.6 %collective-permute-done.20.rest_18_ = bf16[2,1,64,1536]{3,2,1,0:T(8,128)(2,1)} collective-permute-done((bf16[2,1,64,1536]{3,2,1,0:T(8,128)(2,1)}, bf16[2,1,64,1536]{3,2,1,0:T(8,128)(2,1)}, u32[]{:S(2)}, u32[]{:S(2)}) %collective-permute-start.20) | collective-permute-done | bytes 393248 | tf_op jit(solution)/shard_map/ppermute | solution.py:70
  65.1 1.9 %collective-permute-start.9 = (bf16[2,1,64,1536]{3,2,0,1:T(8,128)(2,1)}, bf16[2,1,64,1536]{3,2,0,1:T(8,128)(2,1)}, u32[]{:S(2)}, u32[]{:S(2)}) collective-permute-start(bf16[2,1,64,1536]{3,2,0,1:T(8,128)(2,1)} %get-tuple-element.15), channel_id=1, source_target_pairs={{2,0},{4,2},{6,4},{8,6},{10,8},{12,10},{14,12},{3,1},{5,3},{7,5},{... | collective-permute-start | bytes 1179656 | tf_op jit(solution)/shard_map/ppermute | solution.py:34
  67.0 12.0 %collective-permute-done.14.rest_11_ = bf16[2,1,64,1536]{3,2,1,0:T(8,128)(2,1)S(1)} collective-permute-done((bf16[2,1,64,1536]{3,2,1,0:T(8,128)(2,1)S(1)}, bf16[2,1,64,1536]{3,2,1,0:T(8,128)(2,1)S(1)}, u32[]{:S(2)}, u32[]{:S(2)}) %collective-permute-start.14) | collective-permute-done | bytes 393248 | tf_op jit(solution)/shard_map/ppermute | solution.py:70
  79.1 1.3 %fusion.15 = s32[4]{0:T(128)S(1)} fusion(s32[4]{0:T(128)S(1)} %gather_fusion, s32[]{:T(128)} %bitcast.5, s32[1,1,4]{2,1,0:T(1,128)} %param.18), kind=kLoop, calls=%fused_computation.68 | loop fusion | flops 140 | bytes 52 | tf_op jit(solution)/shard_map/concatenate | solution.py:226
  80.4 1.4 %reduce-window.34 = s32[4,1]{0,1:T(1,128)} reduce-window(s32[4,1]{0,1:T(1,128)} %get-tuple-element.32, s32[]{:T(128)} %constant.98.clone), window={size=4x1 pad=3_0x0_0}, to_apply=%region_0.1 | reduce-window | flops 12 | bytes 36 | tf_op jit(solution)/shard_map/reduce-window.14
  81.8 0.7 reduce-window.35
  82.6 0.6 gather_fusion.1
  83.2 0.6 gather_fusion.2
  83.8 0.1 pad_bitcast_fusion
  83.9 0.7 compare_select_fusion.10
  84.6 2.1 %collective-permute-start.21 = (bf16[2,1,64,1536]{3,2,1,0:T(8,128)(2,1)}, bf16[2,1,64,1536]{3,2,1,0:T(8,128)(2,1)}, u32[]{:S(2)}, u32[]{:S(2)}) collective-permute-start(bf16[2,1,64,1536]{3,2,1,0:T(8,128)(2,1)} %collective-permute-done.19.rest_17_), channel_id=1, source_target_pairs={{0,4},{4,8},{8,12},{12,14},{14,10},{10,6},{6,2},{2,0},{1,5},{5,9},... | collective-permute-start | bytes 1179656 | tf_op jit(solution)/shard_map/ppermute | solution.py:67
  86.7 4.7 %collective-permute-start.11 = (bf16[2,1,64,1536]{3,2,0,1:T(8,128)(2,1)}, bf16[2,1,64,1536]{3,2,0,1:T(8,128)(2,1)}, u32[]{:S(2)}, u32[]{:S(2)}) collective-permute-start(bf16[2,1,64,1536]{3,2,0,1:T(8,128)(2,1)} %get-tuple-element.16), channel_id=1, source_target_pairs={{12,14},{13,15},{28,30},{29,31}} | collective-permute-start | bytes 1179656 | tf_op jit(solution)/shard_map/ppermute | solution.py:213
  91.4 1.4 %collective-permute-start.12 = (bf16[2,1,64,1536]{3,2,0,1:T(8,128)(2,1)}, bf16[2,1,64,1536]{3,2,0,1:T(8,128)(2,1)}, u32[]{:S(2)}, u32[]{:S(2)}) collective-permute-start(bf16[2,1,64,1536]{3,2,0,1:T(8,128)(2,1)} %get-tuple-element.17), channel_id=1, source_target_pairs={{2,0},{3,1},{18,16},{19,17}} | collective-permute-start | bytes 1179656 | tf_op jit(solution)/shard_map/ppermute | solution.py:214
  92.8 3.2 %collective-permute-done.22.rest_20_ = bf16[2,1,64,1536]{3,2,1,0:T(8,128)(2,1)} collective-permute-done((bf16[2,1,64,1536]{3,2,1,0:T(8,128)(2,1)}, bf16[2,1,64,1536]{3,2,1,0:T(8,128)(2,1)}, u32[]{:S(2)}, u32[]{:S(2)}) %collective-permute-start.22) | collective-permute-done | bytes 393248 | tf_op jit(solution)/shard_map/ppermute | solution.py:70
  96.0 8.3 %collective-permute-done.15.rest_13_ = bf16[2,1,64,1536]{3,2,1,0:T(8,128)(2,1)} collective-permute-done((bf16[2,1,64,1536]{3,2,1,0:T(8,128)(2,1)S(1)}, bf16[2,1,64,1536]{3,2,1,0:T(8,128)(2,1)}, u32[]{:S(2)}, u32[]{:S(2)}) %collective-permute-start.15) | collective-permute-done | bytes 393248 | tf_op jit(solution)/shard_map/ppermute | solution.py:70
  104.4 0.1 add_bitcast_fusion
  104.4 0.1 copy.31
  104.5 0.1 reshape.421.table_ref
  104.6 0.4 collective-permute-done.11
  105.0 7.0 %collective-permute-done.16.rest_14_ = bf16[2,1,64,1536]{3,2,1,0:T(8,128)(2,1)} collective-permute-done((bf16[2,1,64,1536]{3,2,1,0:T(8,128)(2,1)S(1)}, bf16[2,1,64,1536]{3,2,1,0:T(8,128)(2,1)}, u32[]{:S(2)}, u32[]{:S(2)}) %collective-permute-start.16) | collective-permute-done | bytes 393248 | tf_op jit(solution)/shard_map/ppermute | solution.py:62
  111.9 3.8 %collective-permute-done.23.rest_21_ = bf16[2,1,64,1536]{3,2,1,0:T(8,128)(2,1)} collective-permute-done((bf16[2,1,64,1536]{3,2,1,0:T(8,128)(2,1)}, bf16[2,1,64,1536]{3,2,1,0:T(8,128)(2,1)}, u32[]{:S(2)}, u32[]{:S(2)}) %collective-permute-start.23) | collective-permute-done | bytes 393248 | tf_op jit(solution)/shard_map/ppermute | solution.py:64
  115.7 15.1 %shard_map.100 = bf16[512,1536]{1,0:T(8,128)(2,1)} custom-call(s32[16]{0:T(128)S(1)} %reshape.421.table_ref, bf16[512,1536]{1,0:T(8,128)(2,1)} %bitcast.92, bf16[2,8,64,1536]{3,2,1,0:T(8,128)(2,1)} %copy-done.2, bf16[2,1,64,1536]{3,2,1,0:T(8,128)(2,1)S(1)} %collective-permute-done.rest_0_, bf16[2,1,64,1536]{3,2,1,0:T(8,128)(2,1)S(1)} %collective-permute-done.1.rest_1_, ...), custom_call_target="tpu_custom_call" | custom-call | flops 3221225472 | bytes 9437184 | tf_op jit(solution)/shard_map/pallas_call | solution.py:142
  (44 shorter events, 0.2 us)
Async XLA Ops:
  0.0 15.6 %collective-permute-start.3 = (s32[4]{0:T(128)}, s32[4]{0:T(128)S(1)}, u32[]{:S(2)}, u32[]{:S(2)}) collective-permute-start(s32[4]{0:T(128)} %bitcast.93), channel_id=1, source_target_pairs={{0,2},{2,4},{4,6},{6,8},{8,10},{10,12},{12,14},{1,3},{3,5},{5,7},{... | collective-permute-start | bytes 56 | tf_op jit(solution)/shard_map/ppermute | solution.py:34
  3.4 14.1 %collective-permute-start.2 = (s32[4]{0:T(128)}, s32[4]{0:T(128)S(1)}, u32[]{:S(2)}, u32[]{:S(2)}) collective-permute-start(s32[4]{0:T(128)} %bitcast.94), channel_id=1, source_target_pairs={{2,0},{4,2},{6,4},{8,6},{10,8},{12,10},{14,12},{3,1},{5,3},{7,5},{... | collective-permute-start | bytes 56 | tf_op jit(solution)/shard_map/ppermute | solution.py:34
  8.7 1.9 %copy-start.4 = (bf16[8,1,64,1536]{3,2,1,0:T(8,128)(2,1)S(1)}, bf16[8,1,64,1536]{3,2,1,0:T(8,128)(2,1)}, u32[]{:S(2)}) copy-start(bf16[8,1,64,1536]{3,2,1,0:T(8,128)(2,1)} %param.15) | copy-start | bytes 4718596
  11.2 3.5 %copy-start.2 = (bf16[2,8,64,1536]{3,2,1,0:T(8,128)(2,1)}, bf16[2,8,64,1536]{3,2,1,0:T(8,128)(2,1)S(1)}, u32[]{:S(2)}) copy-start(bf16[2,8,64,1536]{3,2,1,0:T(8,128)(2,1)S(1)} %maximum_bitcast_fusion.own_hbm) | copy-start | bytes 9437188
  12.2 14.6 %collective-permute-start.4 = (bf16[2,1,64,1536]{3,2,1,0:T(8,128)(2,1)}, bf16[2,1,64,1536]{3,2,1,0:T(8,128)(2,1)S(1)}, u32[]{:S(2)}, u32[]{:S(2)}) collective-permute-start(bf16[2,1,64,1536]{3,2,1,0:T(8,128)(2,1)} %get-tuple-element.27), channel_id=1, source_target_pairs={{0,4},{4,8},{8,12},{12,14},{14,10},{10,6},{6,2},{2,0},{1,5},{5,9},... | collective-permute-start | bytes 1179656 | tf_op jit(solution)/shard_map/ppermute | solution.py:67
  12.8 20.6 %collective-permute-start.13 = (bf16[2,1,64,1536]{3,2,1,0:T(8,128)(2,1)}, bf16[2,1,64,1536]{3,2,1,0:T(8,128)(2,1)S(1)}, u32[]{:S(2)}, u32[]{:S(2)}) collective-permute-start(bf16[2,1,64,1536]{3,2,1,0:T(8,128)(2,1)} %get-tuple-element.27), channel_id=1, source_target_pairs={{4,0},{8,4},{12,8},{14,12},{10,14},{6,10},{2,6},{0,2},{5,1},{9,5},... | collective-permute-start | bytes 1179656 | tf_op jit(solution)/shard_map/ppermute | solution.py:70
  14.2 17.3 %collective-permute-start.18 = (bf16[2,1,64,1536]{3,2,1,0:T(8,128)(2,1)S(1)}, bf16[2,1,64,1536]{3,2,1,0:T(8,128)(2,1)}, u32[]{:S(2)}, u32[]{:S(2)}) collective-permute-start(bf16[2,1,64,1536]{3,2,1,0:T(8,128)(2,1)S(1)} %get-tuple-element.26), channel_id=1, source_target_pairs={{4,0},{8,4},{12,8},{14,12},{10,14},{6,10},{2,6},{0,2},{5,1},{9,5},... | collective-permute-start | bytes 1179656 | tf_op jit(solution)/shard_map/ppermute | solution.py:70
  15.6 20.2 %collective-permute-start.17 = (bf16[2,1,64,1536]{3,2,1,0:T(8,128)(2,1)S(1)}, bf16[2,1,64,1536]{3,2,1,0:T(8,128)(2,1)}, u32[]{:S(2)}, u32[]{:S(2)}) collective-permute-start(bf16[2,1,64,1536]{3,2,1,0:T(8,128)(2,1)S(1)} %get-tuple-element.26), channel_id=1, source_target_pairs={{0,4},{4,8},{8,12},{12,14},{14,10},{10,6},{6,2},{2,0},{1,5},{5,9},... | collective-permute-start | bytes 1179656 | tf_op jit(solution)/shard_map/ppermute | solution.py:67
  17.6 22.7 %collective-permute-start = (bf16[2,1,64,1536]{3,2,1,0:T(8,128)(2,1)}, bf16[2,1,64,1536]{3,2,1,0:T(8,128)(2,1)S(1)}, u32[]{:S(2)}, u32[]{:S(2)}) collective-permute-start(bf16[2,1,64,1536]{3,2,1,0:T(8,128)(2,1)} %get-tuple-element.19), channel_id=1, source_target_pairs={{0,1},{2,3},{4,5},{6,7},{8,9},{10,11},{12,13},{14,15},{16,17},{18,... | collective-permute-start | bytes 1179656 | tf_op jit(solution)/shard_map/ppermute | solution.py:34
  25.3 1.3 copy-start.3
  26.8 17.3 %copy-start.5 = (s32[1,1,4]{2,1,0:T(1,128)S(1)}, s32[1,1,4]{2,1,0:T(1,128)}, u32[]{:S(2)}) copy-start(s32[1,1,4]{2,1,0:T(1,128)} %param.18) | copy-start | bytes 52
  26.8 17.3 %copy-start = (s32[8]{0:T(128)S(1)}, s32[8]{0:T(128)}, u32[]{:S(2)}) copy-start(s32[8]{0:T(128)} %constant.96.clone) | copy-start | bytes 100
  26.8 55.8 %copy-start.1 = (s32[7,2]{1,0:T(8,128)S(1)}, s32[7,2]{1,0:T(8,128)}, u32[]{:S(2)}) copy-start(s32[7,2]{1,0:T(8,128)} %constant.97.clone) | copy-start | bytes 172
  26.8 15.0 %collective-permute-start.1 = (bf16[2,1,64,1536]{3,2,1,0:T(8,128)(2,1)}, bf16[2,1,64,1536]{3,2,1,0:T(8,128)(2,1)S(1)}, u32[]{:S(2)}, u32[]{:S(2)}) collective-permute-start(bf16[2,1,64,1536]{3,2,1,0:T(8,128)(2,1)} %get-tuple-element.18), channel_id=1, source_target_pairs={{1,0},{3,2},{5,4},{7,6},{9,8},{11,10},{13,12},{15,14},{17,16},{19,... | collective-permute-start | bytes 1179656 | tf_op jit(solution)/shard_map/ppermute | solution.py:34
  31.6 11.7 %collective-permute-start.7 = (bf16[2,1,64,1536]{3,2,1,0:T(8,128)(2,1)S(1)}, bf16[2,1,64,1536]{3,2,1,0:T(8,128)(2,1)S(1)}, u32[]{:S(2)}, u32[]{:S(2)}) collective-permute-start(bf16[2,1,64,1536]{3,2,1,0:T(8,128)(2,1)S(1)} %collective-permute-done.4.rest_8_), channel_id=1, source_target_pairs={{0,4},{4,8},{8,12},{12,14},{14,10},{10,6},{6,2},{2,0},{1,5},{5,9},... | collective-permute-start | bytes 1179656 | tf_op jit(solution)/shard_map/ppermute | solution.py:67
  33.5 16.7 %collective-permute-start.5 = (bf16[2,1,64,1536]{3,2,0,1:T(8,128)(2,1)}, bf16[2,1,64,1536]{3,2,0,1:T(8,128)(2,1)S(1)}, u32[]{:S(2)}, u32[]{:S(2)}) collective-permute-start(bf16[2,1,64,1536]{3,2,0,1:T(8,128)(2,1)} %get-tuple-element.12), channel_id=1, source_target_pairs={{0,2},{2,4},{4,6},{6,8},{8,10},{10,12},{12,14},{1,3},{3,5},{5,7},{... | collective-permute-start | bytes 1179656 | tf_op jit(solution)/shard_map/ppermute | solution.py:34
  35.8 18.0 %collective-permute-start.6 = (bf16[2,1,64,1536]{3,2,0,1:T(8,128)(2,1)}, bf16[2,1,64,1536]{3,2,0,1:T(8,128)(2,1)S(1)}, u32[]{:S(2)}, u32[]{:S(2)}) collective-permute-start(bf16[2,1,64,1536]{3,2,0,1:T(8,128)(2,1)} %get-tuple-element.13), channel_id=1, source_target_pairs={{2,0},{4,2},{6,4},{8,6},{10,8},{12,10},{14,12},{3,1},{5,3},{7,5},{... | collective-permute-start | bytes 1179656 | tf_op jit(solution)/shard_map/ppermute | solution.py:34
  40.2 24.9 %collective-permute-start.20 = (bf16[2,1,64,1536]{3,2,1,0:T(8,128)(2,1)}, bf16[2,1,64,1536]{3,2,1,0:T(8,128)(2,1)}, u32[]{:S(2)}, u32[]{:S(2)}) collective-permute-start(bf16[2,1,64,1536]{3,2,1,0:T(8,128)(2,1)} %collective-permute-done.18.rest_16_), channel_id=1, source_target_pairs={{4,0},{8,4},{12,8},{14,12},{10,14},{6,10},{2,6},{0,2},{5,1},{9,5},... | collective-permute-start | bytes 1179656 | tf_op jit(solution)/shard_map/ppermute | solution.py:70
  41.8 37.2 %collective-permute-start.14 = (bf16[2,1,64,1536]{3,2,1,0:T(8,128)(2,1)S(1)}, bf16[2,1,64,1536]{3,2,1,0:T(8,128)(2,1)S(1)}, u32[]{:S(2)}, u32[]{:S(2)}) collective-permute-start(bf16[2,1,64,1536]{3,2,1,0:T(8,128)(2,1)S(1)} %collective-permute-done.13.rest_9_), channel_id=1, source_target_pairs={{4,0},{8,4},{12,8},{14,12},{10,14},{6,10},{2,6},{0,2},{5,1},{9,5},... | collective-permute-start | bytes 1179656 | tf_op jit(solution)/shard_map/ppermute | solution.py:70
  43.3 35.8 %collective-permute-start.10 = (bf16[2,1,64,1536]{3,2,1,0:T(8,128)(2,1)S(1)}, bf16[2,1,64,1536]{3,2,1,0:T(8,128)(2,1)S(1)}, u32[]{:S(2)}, u32[]{:S(2)}) collective-permute-start(bf16[2,1,64,1536]{3,2,1,0:T(8,128)(2,1)S(1)} %collective-permute-done.7.rest_10_), channel_id=1, source_target_pairs={{0,4},{4,8},{8,12},{12,14},{14,10},{10,6},{6,2},{2,0},{1,5},{5,9},... | collective-permute-start | bytes 1179656 | tf_op jit(solution)/shard_map/ppermute | solution.py:67
  50.1 34.5 %collective-permute-start.19 = (bf16[2,1,64,1536]{3,2,1,0:T(8,128)(2,1)}, bf16[2,1,64,1536]{3,2,1,0:T(8,128)(2,1)}, u32[]{:S(2)}, u32[]{:S(2)}) collective-permute-start(bf16[2,1,64,1536]{3,2,1,0:T(8,128)(2,1)} %collective-permute-done.17.rest_15_), channel_id=1, source_target_pairs={{0,4},{4,8},{8,12},{12,14},{14,10},{10,6},{6,2},{2,0},{1,5},{5,9},... | collective-permute-start | bytes 1179656 | tf_op jit(solution)/shard_map/ppermute | solution.py:67
  53.8 32.9 %collective-permute-start.8 = (bf16[2,1,64,1536]{3,2,0,1:T(8,128)(2,1)}, bf16[2,1,64,1536]{3,2,0,1:T(8,128)(2,1)}, u32[]{:S(2)}, u32[]{:S(2)}) collective-permute-start(bf16[2,1,64,1536]{3,2,0,1:T(8,128)(2,1)} %get-tuple-element.14), channel_id=1, source_target_pairs={{0,2},{2,4},{4,6},{6,8},{8,10},{10,12},{12,14},{1,3},{3,5},{5,7},{... | collective-permute-start | bytes 1179656 | tf_op jit(solution)/shard_map/ppermute | solution.py:34
  65.1 26.2 %collective-permute-start.9 = (bf16[2,1,64,1536]{3,2,0,1:T(8,128)(2,1)}, bf16[2,1,64,1536]{3,2,0,1:T(8,128)(2,1)}, u32[]{:S(2)}, u32[]{:S(2)}) collective-permute-start(bf16[2,1,64,1536]{3,2,0,1:T(8,128)(2,1)} %get-tuple-element.15), channel_id=1, source_target_pairs={{2,0},{4,2},{6,4},{8,6},{10,8},{12,10},{14,12},{3,1},{5,3},{7,5},{... | collective-permute-start | bytes 1179656 | tf_op jit(solution)/shard_map/ppermute | solution.py:34
  79.1 17.0 %collective-permute-start.22 = (bf16[2,1,64,1536]{3,2,1,0:T(8,128)(2,1)}, bf16[2,1,64,1536]{3,2,1,0:T(8,128)(2,1)}, u32[]{:S(2)}, u32[]{:S(2)}) collective-permute-start(bf16[2,1,64,1536]{3,2,1,0:T(8,128)(2,1)} %collective-permute-done.20.rest_18_), channel_id=1, source_target_pairs={{4,0},{8,4},{12,8},{14,12},{10,14},{6,10},{2,6},{0,2},{5,1},{9,5},... | collective-permute-start | bytes 1179656 | tf_op jit(solution)/shard_map/ppermute | solution.py:70
  79.1 25.3 %collective-permute-start.15 = (bf16[2,1,64,1536]{3,2,1,0:T(8,128)(2,1)S(1)}, bf16[2,1,64,1536]{3,2,1,0:T(8,128)(2,1)}, u32[]{:S(2)}, u32[]{:S(2)}) collective-permute-start(bf16[2,1,64,1536]{3,2,1,0:T(8,128)(2,1)S(1)} %collective-permute-done.14.rest_11_), channel_id=1, source_target_pairs={{4,0},{8,4},{12,8},{14,12},{10,14},{6,10},{2,6},{0,2},{5,1},{9,5},... | collective-permute-start | bytes 1179656 | tf_op jit(solution)/shard_map/ppermute | solution.py:70
  84.6 20.0 %collective-permute-start.21 = (bf16[2,1,64,1536]{3,2,1,0:T(8,128)(2,1)}, bf16[2,1,64,1536]{3,2,1,0:T(8,128)(2,1)}, u32[]{:S(2)}, u32[]{:S(2)}) collective-permute-start(bf16[2,1,64,1536]{3,2,1,0:T(8,128)(2,1)} %collective-permute-done.19.rest_17_), channel_id=1, source_target_pairs={{0,4},{4,8},{8,12},{12,14},{14,10},{10,6},{6,2},{2,0},{1,5},{5,9},... | collective-permute-start | bytes 1179656 | tf_op jit(solution)/shard_map/ppermute | solution.py:67
  86.7 18.3 %collective-permute-start.11 = (bf16[2,1,64,1536]{3,2,0,1:T(8,128)(2,1)}, bf16[2,1,64,1536]{3,2,0,1:T(8,128)(2,1)}, u32[]{:S(2)}, u32[]{:S(2)}) collective-permute-start(bf16[2,1,64,1536]{3,2,0,1:T(8,128)(2,1)} %get-tuple-element.16), channel_id=1, source_target_pairs={{12,14},{13,15},{28,30},{29,31}} | collective-permute-start | bytes 1179656 | tf_op jit(solution)/shard_map/ppermute | solution.py:213
  91.4 13.6 %collective-permute-start.12 = (bf16[2,1,64,1536]{3,2,0,1:T(8,128)(2,1)}, bf16[2,1,64,1536]{3,2,0,1:T(8,128)(2,1)}, u32[]{:S(2)}, u32[]{:S(2)}) collective-permute-start(bf16[2,1,64,1536]{3,2,0,1:T(8,128)(2,1)} %get-tuple-element.17), channel_id=1, source_target_pairs={{2,0},{3,1},{18,16},{19,17}} | collective-permute-start | bytes 1179656 | tf_op jit(solution)/shard_map/ppermute | solution.py:214
  96.0 15.9 %collective-permute-start.16 = (bf16[2,1,64,1536]{3,2,1,0:T(8,128)(2,1)S(1)}, bf16[2,1,64,1536]{3,2,1,0:T(8,128)(2,1)}, u32[]{:S(2)}, u32[]{:S(2)}) collective-permute-start(bf16[2,1,64,1536]{3,2,1,0:T(8,128)(2,1)S(1)} %collective-permute-done.10.rest_12_), channel_id=1, source_target_pairs={{0,4},{4,8},{8,12},{12,14},{14,10},{10,6},{6,2},{2,0},{1,5},{5,9},... | collective-permute-start | bytes 1179656 | tf_op jit(solution)/shard_map/ppermute | solution.py:62
  104.3 11.4 %collective-permute-start.23 = (bf16[2,1,64,1536]{3,2,1,0:T(8,128)(2,1)}, bf16[2,1,64,1536]{3,2,1,0:T(8,128)(2,1)}, u32[]{:S(2)}, u32[]{:S(2)}) collective-permute-start(bf16[2,1,64,1536]{3,2,1,0:T(8,128)(2,1)} %collective-permute-done.22.rest_20_), channel_id=1, source_target_pairs={{4,0},{8,4},{12,8},{14,12},{10,14},{6,10},{2,6},{0,2},{5,1},{9,5},... | collective-permute-start | bytes 1179656 | tf_op jit(solution)/shard_map/ppermute | solution.py:64

commit v13 on v12

--- a/solution.py
+++ b/solution.py
@@ -175,7 +175,9 @@
     above = shift(stacked[:, tile_blocks - 1 :], "row", row_count, 1)
     below = shift(stacked[:, :1], "row", row_count, -1)
 
-    far_source = stacked[:, 0::4]
+    far_source = jnp.stack(
+        [dequant(key_mant[0::4], key_exp[0::4]), dequant(value_mant[0::4], value_exp[0::4])]
+    )[:, :, 0]
     dilated_entries = dilated_list[0, 0]
     hop_slot = dilated_entries // distant_rows
     far_row = dilated_entries % distant_rows

time: 131 us -> 136 us (1.038)
  the two profiles are of different devices: /device:TPU:24 before, /device:TPU:26 now
where the time goes in v13:
time: 136 us; the launch traced here: 135 us
  waiting for transfers between devices  53.2 us (39%)
  starting transfers between devices  38.2 us (28%)
  local copies, waits for them, and re-layouts  14.7 us (11%)
  Pallas kernels  14.4 us (11%)
  other arithmetic  13.7 us (10%)
    ppermute x6, waiting for transfers between devices, ring_gather(): behind = lax.ppermute(behind, 'col', backward)  32.8 us
    ppermute x8, starting transfers between devices, shift(): return lax.ppermute(x, axis, pairs)  20.4 us
    pallas_call x1, Pallas kernels, gather_attend(): pl.pallas_call(kernel, out_shape=jax.ShapeDtypeStruct((token_count, width...  14.4 us
    ppermute x8, waiting for transfers between devices, shift(): return lax.ppermute(x, axis, pairs)  8.1 us
    ppermute x6, starting transfers between devices, ring_gather(): ahead = lax.ppermute(ahead, 'col', forward)  7.95 us
    ppermute x1, waiting for transfers between devices, ring_gather(): arrays.append(lax.ppermute(ahead, 'col', forward))  7.1 us
    ppermute x1, starting transfers between devices, per_device(): cycle_sources.append(lax.ppermute(to_r, 'col', [(last - 1, last)]))  4.66 us
    ppermute x1, waiting for transfers between devices, ring_gather(): arrays.append(lax.ppermute(behind, 'col', backward))  3.91 us
  transfers between devices with their start and end apart: 24, of which 10 were waited for; matrix products, arithmetic and copies ran while one was open for 18% of the time, Pallas kernels for 0%

profile of v13, /device:TPU:26, one launch (start us, length us, event | category | flops | bytes accessed | tf_op | source)
XLA Modules:
  0.0 134.6 jit_solution(7561164291660880195)
XLA Ops:
  0.0 3.4 %collective-permute-start.3 = (s32[4]{0:T(128)}, s32[4]{0:T(128)S(1)}, u32[]{:S(2)}, u32[]{:S(2)}) collective-permute-start(s32[4]{0:T(128)} %bitcast.105), channel_id=1, source_target_pairs={{0,2},{2,4},{4,6},{6,8},{8,10},{10,12},{12,14},{1,3},{3,5},{5,7},{... | collective-permute-start | bytes 56 | tf_op jit(solution)/shard_map/ppermute | solution.py:34
  3.4 3.3 %collective-permute-start.2 = (s32[4]{0:T(128)}, s32[4]{0:T(128)S(1)}, u32[]{:S(2)}, u32[]{:S(2)}) collective-permute-start(s32[4]{0:T(128)} %bitcast.106), channel_id=1, source_target_pairs={{2,0},{4,2},{6,4},{8,6},{10,8},{12,10},{14,12},{3,1},{5,3},{7,5},{... | collective-permute-start | bytes 56 | tf_op jit(solution)/shard_map/ppermute | solution.py:34
  6.8 0.8 exponential_bitcast_fusion.3
  7.5 0.8 exponential_bitcast_fusion.2
  8.3 1.1 fusion.5
  9.4 1.1 fusion.4
  10.5 0.9 fusion.23
  11.5 0.6 collective-permute-start.4
  12.1 1.4 %collective-permute-start.13 = (bf16[2,1,64,1536]{3,2,1,0:T(8,128)(2,1)}, bf16[2,1,64,1536]{3,2,1,0:T(8,128)(2,1)S(1)}, u32[]{:S(2)}, u32[]{:S(2)}) collective-permute-start(bf16[2,1,64,1536]{3,2,1,0:T(8,128)(2,1)} %get-tuple-element.27), channel_id=1, source_target_pairs={{4,0},{8,4},{12,8},{14,12},{10,14},{6,10},{2,6},{0,2},{5,1},{9,5},... | collective-permute-start | bytes 1179656 | tf_op jit(solution)/shard_map/ppermute | solution.py:70
  13.5 0.4 collective-permute-start.18
  14.2 0.3 fusion.1
  14.5 1.1 copy-done.4
  15.6 1.4 %fusion = bf16[8,1,64,1536]{3,2,0,1:T(8,128)(2,1)} fusion(f32[8,2,1536]{2,1,0:T(2,128)S(1)} %exponential_bitcast_fusion, bf16[8,1,64,1536]{3,2,1,0:T(8,128)(2,1)S(1)} %copy-done.4), kind=kLoop, calls=%fused_computation.7 | loop fusion | flops 2359296 | bytes 3244032 | tf_op jit(solution)/shard_map/convert_element_type | solution.py:24
  17.0 1.7 %maximum_bitcast_fusion.own_hbm = bf16[2,8,64,1536]{3,2,1,0:T(8,128)(2,1)S(1)} fusion(bf16[1,8,1,64,1536]{4,3,1,0,2:T(8,128)(2,1)} %bitcast.99, bf16[1,8,1,64,1536]{4,3,1,0,2:T(8,128)(2,1)S(1)} %bitcast.98), kind=kLoop, calls=%fused_computation.5 | loop fusion | flops 1572864 | bytes 6291456 | tf_op jit(solution)/shard_map/squeeze | solution.py:173
  18.7 1.6 %copy-done.2 = bf16[2,8,64,1536]{3,2,1,0:T(8,128)(2,1)} copy-done((bf16[2,8,64,1536]{3,2,1,0:T(8,128)(2,1)}, bf16[2,8,64,1536]{3,2,1,0:T(8,128)(2,1)S(1)}, u32[]{:S(2)}) %copy-start.2) | copy-done | bytes 3145752
  20.3 0.9 fusion.20
  21.3 1.6 %collective-permute-start.17 = (bf16[2,1,64,1536]{3,2,1,0:T(8,128)(2,1)}, bf16[2,1,64,1536]{3,2,1,0:T(8,128)(2,1)}, u32[]{:S(2)}, u32[]{:S(2)}) collective-permute-start(bf16[2,1,64,1536]{3,2,1,0:T(8,128)(2,1)} %get-tuple-element.26), channel_id=1, source_target_pairs={{0,4},{4,8},{8,12},{12,14},{14,10},{10,6},{6,2},{2,0},{1,5},{5,9},... | collective-permute-start | bytes 1179656 | tf_op jit(solution)/shard_map/ppermute | solution.py:67
  22.9 0.2 reduce-window.37
  23.1 0.1 select_reduce_fusion
  23.2 1.3 collective-permute-start
  24.5 0.2 reduce-window.36
  24.7 0.1 select_reduce_fusion.1
  24.9 2.5 %gather_fusion.4 = bf16[3,2,64,1536]{3,2,1,0:T(8,128)(2,1)S(1)} fusion(bf16[2,8,64,1536]{3,2,1,0:T(8,128)(2,1)} %copy-done.2, s32[1024]{0:T(1024)S(1)} %pad_clamp_fusion), kind=kCustom, calls=%fused_computation.1.clone | custom fusion | bytes 2359308 | tf_op jit(solution)/shard_map/jit(_take)/gather | solution.py:203
  27.4 2.5 %gather_fusion.3 = bf16[3,2,64,1536]{3,2,1,0:T(8,128)(2,1)S(1)} fusion(bf16[2,8,64,1536]{3,2,1,0:T(8,128)(2,1)} %copy-done.2, s32[1024]{0:T(1024)S(1)} %pad_clamp_fusion.1), kind=kCustom, calls=%fused_computation.clone | custom fusion | bytes 2359308 | tf_op jit(solution)/shard_map/jit(_take)/gather | solution.py:202
  29.9 0.2 fusion.2
  30.1 0.2 fusion.3
  30.3 0.8 copy-done.5
  31.1 1.4 %collective-permute-start.1 = (bf16[2,1,64,1536]{3,2,1,0:T(8,128)(2,1)S(1)}, bf16[2,1,64,1536]{3,2,1,0:T(8,128)(2,1)S(1)}, u32[]{:S(2)}, u32[]{:S(2)}) collective-permute-start(bf16[2,1,64,1536]{3,2,1,0:T(8,128)(2,1)S(1)} %copy-done.5), channel_id=1, source_target_pairs={{1,0},{3,2},{5,4},{7,6},{9,8},{11,10},{13,12},{15,14},{17,16},{19,... | collective-permute-start | bytes 1179656 | tf_op jit(solution)/shard_map/ppermute | solution.py:34
  32.6 0.7 collective-permute-start.7
  33.2 1.4 %fusion.21 = (bf16[2,1,64,1536]{3,2,1,0:T(8,128)(2,1)}, bf16[2,1,64,1536]{3,2,1,0:T(8,128)(2,1)}, bf16[2,1,64,1536]{3,2,1,0:T(8,128)(2,1)}, bf16[2,1,64,1536]{3,...) fusion(bf16[2,3,64,1536]{3,2,1,0:T(8,128)(2,1)S(1)} %fusion.2, ...), kind=kLoop, calls=%fused_computation.82 | loop fusion | bytes 4718592 | tf_op jit(solution)/shard_map/slice | solution.py:208
  34.7 2.4 %collective-permute-start.5 = (bf16[2,1,64,1536]{3,2,1,0:T(8,128)(2,1)}, bf16[2,1,64,1536]{3,2,1,0:T(8,128)(2,1)S(1)}, u32[]{:S(2)}, u32[]{:S(2)}) collective-permute-start(bf16[2,1,64,1536]{3,2,1,0:T(8,128)(2,1)} %get-tuple-element.12), channel_id=1, source_target_pairs={{0,2},{2,4},{4,6},{6,8},{8,10},{10,12},{12,14},{1,3},{3,5},{5,7},{... | collective-permute-start | bytes 1179656 | tf_op jit(solution)/shard_map/ppermute | solution.py:34
  37.0 4.4 %collective-permute-start.6 = (bf16[2,1,64,1536]{3,2,1,0:T(8,128)(2,1)}, bf16[2,1,64,1536]{3,2,1,0:T(8,128)(2,1)S(1)}, u32[]{:S(2)}, u32[]{:S(2)}) collective-permute-start(bf16[2,1,64,1536]{3,2,1,0:T(8,128)(2,1)} %get-tuple-element.13), channel_id=1, source_target_pairs={{2,0},{4,2},{6,4},{8,6},{10,8},{12,10},{14,12},{3,1},{5,3},{7,5},{... | collective-permute-start | bytes 1179656 | tf_op jit(solution)/shard_map/ppermute | solution.py:34
  41.4 1.5 %collective-permute-start.20 = (bf16[2,1,64,1536]{3,2,1,0:T(8,128)(2,1)}, bf16[2,1,64,1536]{3,2,1,0:T(8,128)(2,1)}, u32[]{:S(2)}, u32[]{:S(2)}) collective-permute-start(bf16[2,1,64,1536]{3,2,1,0:T(8,128)(2,1)} %collective-permute-done.18.rest_16_), channel_id=1, source_target_pairs={{4,0},{8,4},{12,8},{14,12},{10,14},{6,10},{2,6},{0,2},{5,1},{9,5},... | collective-permute-start | bytes 1179656 | tf_op jit(solution)/shard_map/ppermute | solution.py:70
  42.9 0.5 collective-permute-start.14
  43.4 1.1 collective-permute-done.7.rest_10_
  44.4 0.6 collective-permute-start.10
  45.1 0.6 dynamic_slice.3
  45.7 0.6 gather_fusion
  46.3 1.2 fusion.10
  47.5 3.6 %collective-permute-done.5.rest_2_ = bf16[2,1,64,1536]{3,2,1,0:T(8,128)(2,1)S(1)} collective-permute-done((bf16[2,1,64,1536]{3,2,1,0:T(8,128)(2,1)}, bf16[2,1,64,1536]{3,2,1,0:T(8,128)(2,1)S(1)}, u32[]{:S(2)}, u32[]{:S(2)}) %collective-permute-start.5) | collective-permute-done | bytes 393248 | tf_op jit(solution)/shard_map/ppermute | solution.py:34
  51.1 2.4 %collective-permute-start.19 = (bf16[2,1,64,1536]{3,2,1,0:T(8,128)(2,1)}, bf16[2,1,64,1536]{3,2,1,0:T(8,128)(2,1)}, u32[]{:S(2)}, u32[]{:S(2)}) collective-permute-start(bf16[2,1,64,1536]{3,2,1,0:T(8,128)(2,1)} %collective-permute-done.17.rest_15_), channel_id=1, source_target_pairs={{0,4},{4,8},{8,12},{12,14},{14,10},{10,6},{6,2},{2,0},{1,5},{5,9},... | collective-permute-start | bytes 1179656 | tf_op jit(solution)/shard_map/ppermute | solution.py:67
  53.5 4.5 %collective-permute-done.6.rest_3_ = bf16[2,1,64,1536]{3,2,1,0:T(8,128)(2,1)S(1)} collective-permute-done((bf16[2,1,64,1536]{3,2,1,0:T(8,128)(2,1)}, bf16[2,1,64,1536]{3,2,1,0:T(8,128)(2,1)S(1)}, u32[]{:S(2)}, u32[]{:S(2)}) %collective-permute-start.6) | collective-permute-done | bytes 393248 | tf_op jit(solution)/shard_map/ppermute | solution.py:34
  58.0 2.3 %collective-permute-start.8 = (bf16[2,1,64,1536]{3,2,1,0:T(8,128)(2,1)}, bf16[2,1,64,1536]{3,2,1,0:T(8,128)(2,1)}, u32[]{:S(2)}, u32[]{:S(2)}) collective-permute-start(bf16[2,1,64,1536]{3,2,1,0:T(8,128)(2,1)} %get-tuple-element.14), channel_id=1, source_target_pairs={{0,2},{2,4},{4,6},{6,8},{8,10},{10,12},{12,14},{1,3},{3,5},{5,7},{... | collective-permute-start | bytes 1179656 | tf_op jit(solution)/shard_map/ppermute | solution.py:34
  60.3 6.3 %collective-permute-done.20.rest_18_ = bf16[2,1,64,1536]{3,2,1,0:T(8,128)(2,1)} collective-permute-done((bf16[2,1,64,1536]{3,2,1,0:T(8,128)(2,1)}, bf16[2,1,64,1536]{3,2,1,0:T(8,128)(2,1)}, u32[]{:S(2)}, u32[]{:S(2)}) %collective-permute-start.20) | collective-permute-done | bytes 393248 | tf_op jit(solution)/shard_map/ppermute | solution.py:70
  66.6 1.9 %collective-permute-start.9 = (bf16[2,1,64,1536]{3,2,1,0:T(8,128)(2,1)}, bf16[2,1,64,1536]{3,2,1,0:T(8,128)(2,1)}, u32[]{:S(2)}, u32[]{:S(2)}) collective-permute-start(bf16[2,1,64,1536]{3,2,1,0:T(8,128)(2,1)} %get-tuple-element.15), channel_id=1, source_target_pairs={{2,0},{4,2},{6,4},{8,6},{10,8},{12,10},{14,12},{3,1},{5,3},{7,5},{... | collective-permute-start | bytes 1179656 | tf_op jit(solution)/shard_map/ppermute | solution.py:34
  68.5 14.7 %collective-permute-done.14.rest_11_ = bf16[2,1,64,1536]{3,2,1,0:T(8,128)(2,1)S(1)} collective-permute-done((bf16[2,1,64,1536]{3,2,1,0:T(8,128)(2,1)S(1)}, bf16[2,1,64,1536]{3,2,1,0:T(8,128)(2,1)S(1)}, u32[]{:S(2)}, u32[]{:S(2)}) %collective-permute-start.14) | collective-permute-done | bytes 393248 | tf_op jit(solution)/shard_map/ppermute | solution.py:70
  83.3 1.3 fusion.19
  84.6 1.3 reduce-window.34
  85.9 0.7 reduce-window.35
  86.6 0.6 gather_fusion.1
  87.3 0.6 gather_fusion.2
  88.0 0.7 compare_select_fusion.10
  88.7 2.1 %collective-permute-start.21 = (bf16[2,1,64,1536]{3,2,1,0:T(8,128)(2,1)}, bf16[2,1,64,1536]{3,2,1,0:T(8,128)(2,1)}, u32[]{:S(2)}, u32[]{:S(2)}) collective-permute-start(bf16[2,1,64,1536]{3,2,1,0:T(8,128)(2,1)} %collective-permute-done.19.rest_17_), channel_id=1, source_target_pairs={{0,4},{4,8},{8,12},{12,14},{14,10},{10,6},{6,2},{2,0},{1,5},{5,9},... | collective-permute-start | bytes 1179656 | tf_op jit(solution)/shard_map/ppermute | solution.py:67
  90.8 4.7 %collective-permute-start.11 = (bf16[2,1,64,1536]{3,2,1,0:T(8,128)(2,1)}, bf16[2,1,64,1536]{3,2,1,0:T(8,128)(2,1)}, u32[]{:S(2)}, u32[]{:S(2)}) collective-permute-start(bf16[2,1,64,1536]{3,2,1,0:T(8,128)(2,1)} %get-tuple-element.16), channel_id=1, source_target_pairs={{12,14},{13,15},{28,30},{29,31}} | collective-permute-start | bytes 1179656 | tf_op jit(solution)/shard_map/ppermute | solution.py:215
  95.4 1.4 %collective-permute-start.12 = (bf16[2,1,64,1536]{3,2,1,0:T(8,128)(2,1)}, bf16[2,1,64,1536]{3,2,1,0:T(8,128)(2,1)}, u32[]{:S(2)}, u32[]{:S(2)}) collective-permute-start(bf16[2,1,64,1536]{3,2,1,0:T(8,128)(2,1)} %get-tuple-element.17), channel_id=1, source_target_pairs={{2,0},{3,1},{18,16},{19,17}} | collective-permute-start | bytes 1179656 | tf_op jit(solution)/shard_map/ppermute | solution.py:216
  96.8 3.4 %collective-permute-done.22.rest_20_ = bf16[2,1,64,1536]{3,2,1,0:T(8,128)(2,1)} collective-permute-done((bf16[2,1,64,1536]{3,2,1,0:T(8,128)(2,1)}, bf16[2,1,64,1536]{3,2,1,0:T(8,128)(2,1)}, u32[]{:S(2)}, u32[]{:S(2)}) %collective-permute-start.22) | collective-permute-done | bytes 393248 | tf_op jit(solution)/shard_map/ppermute | solution.py:70
  100.2 8.4 %collective-permute-done.15.rest_13_ = bf16[2,1,64,1536]{3,2,1,0:T(8,128)(2,1)} collective-permute-done((bf16[2,1,64,1536]{3,2,1,0:T(8,128)(2,1)S(1)}, bf16[2,1,64,1536]{3,2,1,0:T(8,128)(2,1)}, u32[]{:S(2)}, u32[]{:S(2)}) %collective-permute-start.15) | collective-permute-done | bytes 393248 | tf_op jit(solution)/shard_map/ppermute | solution.py:70
  108.6 0.1 add_bitcast_fusion
  108.7 0.1 copy.25
  108.8 0.1 reshape.449.table_ref
  108.9 0.1 collective-permute-done.11.rest_6_
  109.0 7.1 %collective-permute-done.16.rest_14_ = bf16[2,1,64,1536]{3,2,1,0:T(8,128)(2,1)} collective-permute-done((bf16[2,1,64,1536]{3,2,1,0:T(8,128)(2,1)S(1)}, bf16[2,1,64,1536]{3,2,1,0:T(8,128)(2,1)}, u32[]{:S(2)}, u32[]{:S(2)}) %collective-permute-start.16) | collective-permute-done | bytes 393248 | tf_op jit(solution)/shard_map/ppermute | solution.py:62
  116.1 3.9 %collective-permute-done.23.rest_21_ = bf16[2,1,64,1536]{3,2,1,0:T(8,128)(2,1)} collective-permute-done((bf16[2,1,64,1536]{3,2,1,0:T(8,128)(2,1)}, bf16[2,1,64,1536]{3,2,1,0:T(8,128)(2,1)}, u32[]{:S(2)}, u32[]{:S(2)}) %collective-permute-start.23) | collective-permute-done | bytes 393248 | tf_op jit(solution)/shard_map/ppermute | solution.py:64
  120.0 14.4 %shard_map.100 = bf16[512,1536]{1,0:T(8,128)(2,1)} custom-call(s32[16]{0:T(128)S(1)} %reshape.449.table_ref, bf16[512,1536]{1,0:T(8,128)(2,1)} %bitcast.102, bf16[2,8,64,1536]{3,2,1,0:T(8,128)(2,1)} %copy-done.2, bf16[2,1,64,1536]{3,2,1,0:T(8,128)(2,1)S(1)} %collective-permute-done.rest_0_, bf16[2,1,64,1536]{3,2,1,0:T(8,128)(2,1)S(1)} %collective-permute-done.1.rest_1_, ...), custom_call_target="tpu_custom_call" | custom-call | flops 3221225472 | bytes 9437184 | tf_op jit(solution)/shard_map/pallas_call | solution.py:142
  (54 shorter events, 0.5 us)
Async XLA Ops:
  0.0 21.3 %collective-permute-start.3 = (s32[4]{0:T(128)}, s32[4]{0:T(128)S(1)}, u32[]{:S(2)}, u32[]{:S(2)}) collective-permute-start(s32[4]{0:T(128)} %bitcast.105), channel_id=1, source_target_pairs={{0,2},{2,4},{4,6},{6,8},{8,10},{10,12},{12,14},{1,3},{3,5},{5,7},{... | collective-permute-start | bytes 56 | tf_op jit(solution)/shard_map/ppermute | solution.py:34
  3.4 19.8 %collective-permute-start.2 = (s32[4]{0:T(128)}, s32[4]{0:T(128)S(1)}, u32[]{:S(2)}, u32[]{:S(2)}) collective-permute-start(s32[4]{0:T(128)} %bitcast.106), channel_id=1, source_target_pairs={{2,0},{4,2},{6,4},{8,6},{10,8},{12,10},{14,12},{3,1},{5,3},{7,5},{... | collective-permute-start | bytes 56 | tf_op jit(solution)/shard_map/ppermute | solution.py:34
  10.4 3.5 %copy-start.6 = (s32[8,1,2,1536]{3,2,1,0:T(2,128)S(1)}, s32[8,1,2,1536]{3,2,1,0:T(2,128)}, u32[]{:S(2)}) copy-start(s32[8,1,2,1536]{3,2,1,0:T(2,128)} %param.14) | copy-start | bytes 294916
  10.4 3.6 %copy-start.7 = (s32[8,1,2,1536]{3,2,1,0:T(2,128)S(1)}, s32[8,1,2,1536]{3,2,1,0:T(2,128)}, u32[]{:S(2)}) copy-start(s32[8,1,2,1536]{3,2,1,0:T(2,128)} %param.16) | copy-start | bytes 294916
  10.5 3.7 %copy-start.3 = (bf16[8,1,64,1536]{3,2,1,0:T(8,128)(2,1)S(1)}, bf16[8,1,64,1536]{3,2,1,0:T(8,128)(2,1)}, u32[]{:S(2)}) copy-start(bf16[8,1,64,1536]{3,2,1,0:T(8,128)(2,1)} %param.13) | copy-start | bytes 4718596
  11.5 18.8 %collective-permute-start.4 = (bf16[2,1,64,1536]{3,2,1,0:T(8,128)(2,1)}, bf16[2,1,64,1536]{3,2,1,0:T(8,128)(2,1)S(1)}, u32[]{:S(2)}, u32[]{:S(2)}) collective-permute-start(bf16[2,1,64,1536]{3,2,1,0:T(8,128)(2,1)} %get-tuple-element.27), channel_id=1, source_target_pairs={{0,4},{4,8},{8,12},{12,14},{14,10},{10,6},{6,2},{2,0},{1,5},{5,9},... | collective-permute-start | bytes 1179656 | tf_op jit(solution)/shard_map/ppermute | solution.py:67
  12.1 29.3 %collective-permute-start.13 = (bf16[2,1,64,1536]{3,2,1,0:T(8,128)(2,1)}, bf16[2,1,64,1536]{3,2,1,0:T(8,128)(2,1)S(1)}, u32[]{:S(2)}, u32[]{:S(2)}) collective-permute-start(bf16[2,1,64,1536]{3,2,1,0:T(8,128)(2,1)} %get-tuple-element.27), channel_id=1, source_target_pairs={{4,0},{8,4},{12,8},{14,12},{10,14},{6,10},{2,6},{0,2},{5,1},{9,5},... | collective-permute-start | bytes 1179656 | tf_op jit(solution)/shard_map/ppermute | solution.py:70
  13.5 19.0 %collective-permute-start.18 = (bf16[2,1,64,1536]{3,2,1,0:T(8,128)(2,1)}, bf16[2,1,64,1536]{3,2,1,0:T(8,128)(2,1)}, u32[]{:S(2)}, u32[]{:S(2)}) collective-permute-start(bf16[2,1,64,1536]{3,2,1,0:T(8,128)(2,1)} %get-tuple-element.26), channel_id=1, source_target_pairs={{4,0},{8,4},{12,8},{14,12},{10,14},{6,10},{2,6},{0,2},{5,1},{9,5},... | collective-permute-start | bytes 1179656 | tf_op jit(solution)/shard_map/ppermute | solution.py:70
  14.1 1.4 %copy-start.4 = (bf16[8,1,64,1536]{3,2,1,0:T(8,128)(2,1)S(1)}, bf16[8,1,64,1536]{3,2,1,0:T(8,128)(2,1)}, u32[]{:S(2)}) copy-start(bf16[8,1,64,1536]{3,2,1,0:T(8,128)(2,1)} %param.15) | copy-start | bytes 4718596
  18.7 1.7 %copy-start.2 = (bf16[2,8,64,1536]{3,2,1,0:T(8,128)(2,1)}, bf16[2,8,64,1536]{3,2,1,0:T(8,128)(2,1)S(1)}, u32[]{:S(2)}) copy-start(bf16[2,8,64,1536]{3,2,1,0:T(8,128)(2,1)S(1)} %maximum_bitcast_fusion.own_hbm) | copy-start | bytes 9437188
  21.3 21.6 %collective-permute-start.17 = (bf16[2,1,64,1536]{3,2,1,0:T(8,128)(2,1)}, bf16[2,1,64,1536]{3,2,1,0:T(8,128)(2,1)}, u32[]{:S(2)}, u32[]{:S(2)}) collective-permute-start(bf16[2,1,64,1536]{3,2,1,0:T(8,128)(2,1)} %get-tuple-element.26), channel_id=1, source_target_pairs={{0,4},{4,8},{8,12},{12,14},{14,10},{10,6},{6,2},{2,0},{1,5},{5,9},... | collective-permute-start | bytes 1179656 | tf_op jit(solution)/shard_map/ppermute | solution.py:67
  23.2 11.4 %collective-permute-start = (bf16[2,1,64,1536]{3,2,1,0:T(8,128)(2,1)}, bf16[2,1,64,1536]{3,2,1,0:T(8,128)(2,1)S(1)}, u32[]{:S(2)}, u32[]{:S(2)}) collective-permute-start(bf16[2,1,64,1536]{3,2,1,0:T(8,128)(2,1)} %get-tuple-element.19), channel_id=1, source_target_pairs={{0,1},{2,3},{4,5},{6,7},{8,9},{10,11},{12,13},{14,15},{16,17},{18,... | collective-permute-start | bytes 1179656 | tf_op jit(solution)/shard_map/ppermute | solution.py:34
  30.1 1.0 copy-start.5
  31.1 13.9 %copy-start.8 = (s32[1,1,4]{2,1,0:T(1,128)S(1)}, s32[1,1,4]{2,1,0:T(1,128)}, u32[]{:S(2)}) copy-start(s32[1,1,4]{2,1,0:T(1,128)} %param.18) | copy-start | bytes 52
  31.1 13.9 %copy-start = (s32[8]{0:T(128)S(1)}, s32[8]{0:T(128)}, u32[]{:S(2)}) copy-start(s32[8]{0:T(128)} %constant.97.clone) | copy-start | bytes 100
  31.1 55.5 %copy-start.1 = (s32[7,2]{1,0:T(8,128)S(1)}, s32[7,2]{1,0:T(8,128)}, u32[]{:S(2)}) copy-start(s32[7,2]{1,0:T(8,128)} %constant.98.clone) | copy-start | bytes 172
  31.1 5.9 %collective-permute-start.1 = (bf16[2,1,64,1536]{3,2,1,0:T(8,128)(2,1)S(1)}, bf16[2,1,64,1536]{3,2,1,0:T(8,128)(2,1)S(1)}, u32[]{:S(2)}, u32[]{:S(2)}) collective-permute-start(bf16[2,1,64,1536]{3,2,1,0:T(8,128)(2,1)S(1)} %copy-done.5), channel_id=1, source_target_pairs={{1,0},{3,2},{5,4},{7,6},{9,8},{11,10},{13,12},{15,14},{17,16},{19,... | collective-permute-start | bytes 1179656 | tf_op jit(solution)/shard_map/ppermute | solution.py:34
  32.6 11.9 %collective-permute-start.7 = (bf16[2,1,64,1536]{3,2,1,0:T(8,128)(2,1)S(1)}, bf16[2,1,64,1536]{3,2,1,0:T(8,128)(2,1)S(1)}, u32[]{:S(2)}, u32[]{:S(2)}) collective-permute-start(bf16[2,1,64,1536]{3,2,1,0:T(8,128)(2,1)S(1)} %collective-permute-done.4.rest_8_), channel_id=1, source_target_pairs={{0,4},{4,8},{8,12},{12,14},{14,10},{10,6},{6,2},{2,0},{1,5},{5,9},... | collective-permute-start | bytes 1179656 | tf_op jit(solution)/shard_map/ppermute | solution.py:67
  34.7 16.4 %collective-permute-start.5 = (bf16[2,1,64,1536]{3,2,1,0:T(8,128)(2,1)}, bf16[2,1,64,1536]{3,2,1,0:T(8,128)(2,1)S(1)}, u32[]{:S(2)}, u32[]{:S(2)}) collective-permute-start(bf16[2,1,64,1536]{3,2,1,0:T(8,128)(2,1)} %get-tuple-element.12), channel_id=1, source_target_pairs={{0,2},{2,4},{4,6},{6,8},{8,10},{10,12},{12,14},{1,3},{3,5},{5,7},{... | collective-permute-start | bytes 1179656 | tf_op jit(solution)/shard_map/ppermute | solution.py:34
  37.0 21.0 %collective-permute-start.6 = (bf16[2,1,64,1536]{3,2,1,0:T(8,128)(2,1)}, bf16[2,1,64,1536]{3,2,1,0:T(8,128)(2,1)S(1)}, u32[]{:S(2)}, u32[]{:S(2)}) collective-permute-start(bf16[2,1,64,1536]{3,2,1,0:T(8,128)(2,1)} %get-tuple-element.13), channel_id=1, source_target_pairs={{2,0},{4,2},{6,4},{8,6},{10,8},{12,10},{14,12},{3,1},{5,3},{7,5},{... | collective-permute-start | bytes 1179656 | tf_op jit(solution)/shard_map/ppermute | solution.py:34
  41.4 25.2 %collective-permute-start.20 = (bf16[2,1,64,1536]{3,2,1,0:T(8,128)(2,1)}, bf16[2,1,64,1536]{3,2,1,0:T(8,128)(2,1)}, u32[]{:S(2)}, u32[]{:S(2)}) collective-permute-start(bf16[2,1,64,1536]{3,2,1,0:T(8,128)(2,1)} %collective-permute-done.18.rest_16_), channel_id=1, source_target_pairs={{4,0},{8,4},{12,8},{14,12},{10,14},{6,10},{2,6},{0,2},{5,1},{9,5},... | collective-permute-start | bytes 1179656 | tf_op jit(solution)/shard_map/ppermute | solution.py:70
  42.9 40.4 %collective-permute-start.14 = (bf16[2,1,64,1536]{3,2,1,0:T(8,128)(2,1)S(1)}, bf16[2,1,64,1536]{3,2,1,0:T(8,128)(2,1)S(1)}, u32[]{:S(2)}, u32[]{:S(2)}) collective-permute-start(bf16[2,1,64,1536]{3,2,1,0:T(8,128)(2,1)S(1)} %collective-permute-done.13.rest_9_), channel_id=1, source_target_pairs={{4,0},{8,4},{12,8},{14,12},{10,14},{6,10},{2,6},{0,2},{5,1},{9,5},... | collective-permute-start | bytes 1179656 | tf_op jit(solution)/shard_map/ppermute | solution.py:70
  44.4 38.9 %collective-permute-start.10 = (bf16[2,1,64,1536]{3,2,1,0:T(8,128)(2,1)S(1)}, bf16[2,1,64,1536]{3,2,1,0:T(8,128)(2,1)S(1)}, u32[]{:S(2)}, u32[]{:S(2)}) collective-permute-start(bf16[2,1,64,1536]{3,2,1,0:T(8,128)(2,1)S(1)} %collective-permute-done.7.rest_10_), channel_id=1, source_target_pairs={{0,4},{4,8},{8,12},{12,14},{14,10},{10,6},{6,2},{2,0},{1,5},{5,9},... | collective-permute-start | bytes 1179656 | tf_op jit(solution)/shard_map/ppermute | solution.py:67
  51.1 37.6 %collective-permute-start.19 = (bf16[2,1,64,1536]{3,2,1,0:T(8,128)(2,1)}, bf16[2,1,64,1536]{3,2,1,0:T(8,128)(2,1)}, u32[]{:S(2)}, u32[]{:S(2)}) collective-permute-start(bf16[2,1,64,1536]{3,2,1,0:T(8,128)(2,1)} %collective-permute-done.17.rest_15_), channel_id=1, source_target_pairs={{0,4},{4,8},{8,12},{12,14},{14,10},{10,6},{6,2},{2,0},{1,5},{5,9},... | collective-permute-start | bytes 1179656 | tf_op jit(solution)/shard_map/ppermute | solution.py:67
  58.0 32.8 %collective-permute-start.8 = (bf16[2,1,64,1536]{3,2,1,0:T(8,128)(2,1)}, bf16[2,1,64,1536]{3,2,1,0:T(8,128)(2,1)}, u32[]{:S(2)}, u32[]{:S(2)}) collective-permute-start(bf16[2,1,64,1536]{3,2,1,0:T(8,128)(2,1)} %get-tuple-element.14), channel_id=1, source_target_pairs={{0,2},{2,4},{4,6},{6,8},{8,10},{10,12},{12,14},{1,3},{3,5},{5,7},{... | collective-permute-start | bytes 1179656 | tf_op jit(solution)/shard_map/ppermute | solution.py:34
  66.6 28.8 %collective-permute-start.9 = (bf16[2,1,64,1536]{3,2,1,0:T(8,128)(2,1)}, bf16[2,1,64,1536]{3,2,1,0:T(8,128)(2,1)}, u32[]{:S(2)}, u32[]{:S(2)}) collective-permute-start(bf16[2,1,64,1536]{3,2,1,0:T(8,128)(2,1)} %get-tuple-element.15), channel_id=1, source_target_pairs={{2,0},{4,2},{6,4},{8,6},{10,8},{12,10},{14,12},{3,1},{5,3},{7,5},{... | collective-permute-start | bytes 1179656 | tf_op jit(solution)/shard_map/ppermute | solution.py:34
  83.3 17.0 %collective-permute-start.22 = (bf16[2,1,64,1536]{3,2,1,0:T(8,128)(2,1)}, bf16[2,1,64,1536]{3,2,1,0:T(8,128)(2,1)}, u32[]{:S(2)}, u32[]{:S(2)}) collective-permute-start(bf16[2,1,64,1536]{3,2,1,0:T(8,128)(2,1)} %collective-permute-done.20.rest_18_), channel_id=1, source_target_pairs={{4,0},{8,4},{12,8},{14,12},{10,14},{6,10},{2,6},{0,2},{5,1},{9,5},... | collective-permute-start | bytes 1179656 | tf_op jit(solution)/shard_map/ppermute | solution.py:70
  83.3 25.4 %collective-permute-start.15 = (bf16[2,1,64,1536]{3,2,1,0:T(8,128)(2,1)S(1)}, bf16[2,1,64,1536]{3,2,1,0:T(8,128)(2,1)}, u32[]{:S(2)}, u32[]{:S(2)}) collective-permute-start(bf16[2,1,64,1536]{3,2,1,0:T(8,128)(2,1)S(1)} %collective-permute-done.14.rest_11_), channel_id=1, source_target_pairs={{4,0},{8,4},{12,8},{14,12},{10,14},{6,10},{2,6},{0,2},{5,1},{9,5},... | collective-permute-start | bytes 1179656 | tf_op jit(solution)/shard_map/ppermute | solution.py:70
  88.7 20.2 %collective-permute-start.21 = (bf16[2,1,64,1536]{3,2,1,0:T(8,128)(2,1)}, bf16[2,1,64,1536]{3,2,1,0:T(8,128)(2,1)}, u32[]{:S(2)}, u32[]{:S(2)}) collective-permute-start(bf16[2,1,64,1536]{3,2,1,0:T(8,128)(2,1)} %collective-permute-done.19.rest_17_), channel_id=1, source_target_pairs={{0,4},{4,8},{8,12},{12,14},{14,10},{10,6},{6,2},{2,0},{1,5},{5,9},... | collective-permute-start | bytes 1179656 | tf_op jit(solution)/shard_map/ppermute | solution.py:67
  90.8 18.3 %collective-permute-start.11 = (bf16[2,1,64,1536]{3,2,1,0:T(8,128)(2,1)}, bf16[2,1,64,1536]{3,2,1,0:T(8,128)(2,1)}, u32[]{:S(2)}, u32[]{:S(2)}) collective-permute-start(bf16[2,1,64,1536]{3,2,1,0:T(8,128)(2,1)} %get-tuple-element.16), channel_id=1, source_target_pairs={{12,14},{13,15},{28,30},{29,31}} | collective-permute-start | bytes 1179656 | tf_op jit(solution)/shard_map/ppermute | solution.py:215
  95.4 13.6 %collective-permute-start.12 = (bf16[2,1,64,1536]{3,2,1,0:T(8,128)(2,1)}, bf16[2,1,64,1536]{3,2,1,0:T(8,128)(2,1)}, u32[]{:S(2)}, u32[]{:S(2)}) collective-permute-start(bf16[2,1,64,1536]{3,2,1,0:T(8,128)(2,1)} %get-tuple-element.17), channel_id=1, source_target_pairs={{2,0},{3,1},{18,16},{19,17}} | collective-permute-start | bytes 1179656 | tf_op jit(solution)/shard_map/ppermute | solution.py:216
  100.2 15.9 %collective-permute-start.16 = (bf16[2,1,64,1536]{3,2,1,0:T(8,128)(2,1)S(1)}, bf16[2,1,64,1536]{3,2,1,0:T(8,128)(2,1)}, u32[]{:S(2)}, u32[]{:S(2)}) collective-permute-start(bf16[2,1,64,1536]{3,2,1,0:T(8,128)(2,1)S(1)} %collective-permute-done.10.rest_12_), channel_id=1, source_target_pairs={{0,4},{4,8},{8,12},{12,14},{14,10},{10,6},{6,2},{2,0},{1,5},{5,9},... | collective-permute-start | bytes 1179656 | tf_op jit(solution)/shard_map/ppermute | solution.py:62
  108.6 11.4 %collective-permute-start.23 = (bf16[2,1,64,1536]{3,2,1,0:T(8,128)(2,1)}, bf16[2,1,64,1536]{3,2,1,0:T(8,128)(2,1)}, u32[]{:S(2)}, u32[]{:S(2)}) collective-permute-start(bf16[2,1,64,1536]{3,2,1,0:T(8,128)(2,1)} %collective-permute-done.22.rest_20_), channel_id=1, source_target_pairs={{4,0},{8,4},{12,8},{14,12},{10,14},{6,10},{2,6},{0,2},{5,1},{9,5},... | collective-permute-start | bytes 1179656 | tf_op jit(solution)/shard_map/ppermute | solution.py:64

commit v14 on v12

--- a/solution.py
+++ b/solution.py
@@ -54,8 +54,13 @@
     split = (rows + 1) // 2
     arrays = []
     lookup = [[None] * rows for _ in range(count - 1)]
+    first_hop = None
     for r in range(rows):
         ahead = behind = item[:, r : r + 1]
+        if first_hop is not None:
+            ahead, _ = lax.optimization_barrier((ahead, arrays[first_hop]))
+            behind = ahead
+        first_hop = len(arrays)
         for distance in range(1, half + 1):
             if distance == half and count % 2 == 0:
                 if r < split:

time: 131 us -> 139 us (1.061)
  the two profiles are of different devices: /device:TPU:24 before, /device:TPU:0 now
where the time goes in v14:
time: 139 us; the launch traced here: 138 us
  waiting for transfers between devices  59.6 us (43%)
  starting transfers between devices  39.4 us (28%)
  Pallas kernels  14.6 us (11%)
  local copies, waits for them, and re-layouts  13.4 us (10%)
  other arithmetic  10.9 us (8%)
    ppermute x6, waiting for transfers between devices, ring_gather(): behind = lax.ppermute(behind, 'col', backward)  39.3 us
    ppermute x6, waiting for transfers between devices, ring_gather(): ahead = lax.ppermute(ahead, 'col', forward)  19.8 us
    ppermute x8, starting transfers between devices, shift(): return lax.ppermute(x, axis, pairs)  16.9 us
    pallas_call x1, Pallas kernels, gather_attend(): pl.pallas_call(kernel, out_shape=jax.ShapeDtypeStruct((token_count, width...  14.6 us
    ppermute x6, starting transfers between devices, ring_gather(): ahead = lax.ppermute(ahead, 'col', forward)  8.72 us
    ppermute x6, starting transfers between devices, ring_gather(): behind = lax.ppermute(behind, 'col', backward)  8.47 us
    gather x1, local copies, waits for them, and re-layouts, per_device(): right_payload = jnp.take(stacked, to_right, axis=1)  3.56 us
  transfers between devices with their start and end apart: 24, of which 7 were waited for; matrix products, arithmetic and copies ran while one was open for 17% of the time, Pallas kernels for 0%

profile of v14, /device:TPU:0, one launch (start us, length us, event | category | flops | bytes accessed | tf_op | source)
XLA Modules:
  0.0 138.4 jit_solution(16862134461641185355)
XLA Ops:
  0.0 4.9 %collective-permute-start.3 = (s32[4]{0:T(128)}, s32[4]{0:T(128)S(1)}, u32[]{:S(2)}, u32[]{:S(2)}) collective-permute-start(s32[4]{0:T(128)} %bitcast.93), channel_id=1, source_target_pairs={{0,2},{2,4},{4,6},{6,8},{8,10},{10,12},{12,14},{1,3},{3,5},{5,7},{... | collective-permute-start | bytes 56 | tf_op jit(solution)/shard_map/ppermute | solution.py:34
  4.9 1.3 collective-permute-start.2
  6.2 1.0 exponential_bitcast_fusion.1
  7.1 1.0 exponential_bitcast_fusion
  8.1 0.0 copy-start.4
  8.1 1.8 %fusion.1 = bf16[8,1,64,1536]{3,2,0,1:T(8,128)(2,1)S(1)} fusion(bf16[8,1,64,1536]{3,2,1,0:T(8,128)(2,1)} %param.13, f32[8,2,1536]{2,1,0:T(2,128)S(1)} %exponential_bitcast_fusion.1), kind=kLoop, calls=%fused_computation.9 | loop fusion | flops 2359296 | bytes 3244032 | tf_op jit(solution)/shard_map/convert_element_type | solution.py:24
  9.9 0.1 copy-done.4
  10.0 0.3 fusion
  10.3 0.3 maximum_bitcast_fusion.own_hbm
  10.6 0.1 slice.37
  10.7 1.1 fusion.19
  11.8 3.6 %collective-permute-start.4 = (bf16[2,1,64,1536]{3,2,1,0:T(8,128)(2,1)}, bf16[2,1,64,1536]{3,2,1,0:T(8,128)(2,1)S(1)}, u32[]{:S(2)}, u32[]{:S(2)}) collective-permute-start(bf16[2,1,64,1536]{3,2,1,0:T(8,128)(2,1)} %get-tuple-element.29), channel_id=1, source_target_pairs={{0,4},{4,8},{8,12},{12,14},{14,10},{10,6},{6,2},{2,0},{1,5},{5,9},... | collective-permute-start | bytes 1179656 | tf_op jit(solution)/shard_map/ppermute | solution.py:72
  15.4 0.9 fusion.16
  16.3 1.3 collective-permute-start
  17.6 1.3 collective-permute-start.1
  18.9 0.2 reduce-window.37
  19.1 0.1 select_reduce_fusion
  19.3 0.2 reduce-window.36
  19.5 0.1 select_reduce_fusion.1
  19.6 2.5 %gather_fusion.4 = bf16[3,2,64,1536]{3,2,1,0:T(8,128)(2,1)S(1)} fusion(bf16[2,8,64,1536]{3,2,1,0:T(8,128)(2,1)} %copy-done.2, s32[1024]{0:T(1024)S(1)} %pad_clamp_fusion), kind=kCustom, calls=%fused_computation.1.clone | custom fusion | bytes 2359308 | tf_op jit(solution)/shard_map/jit(_take)/gather | solution.py:206
  22.2 3.6 %gather_fusion.3 = bf16[3,2,64,1536]{3,2,1,0:T(8,128)(2,1)} fusion(bf16[2,8,64,1536]{3,2,1,0:T(8,128)(2,1)} %copy-done.2, s32[1024]{0:T(1024)S(1)} %pad_clamp_fusion.1), kind=kCustom, calls=%fused_computation.clone | custom fusion | bytes 2359308 | tf_op jit(solution)/shard_map/jit(_take)/gather | solution.py:205
  25.7 0.2 select_bitcast_fusion
  25.9 1.1 copy-done.3
  27.0 0.2 select_bitcast_fusion.1
  27.2 0.0 copy-start
  27.2 0.0 copy-start.1
  27.2 1.3 fusion.17
  28.5 3.0 %collective-permute-start.5 = (bf16[2,1,64,1536]{3,2,0,1:T(8,128)(2,1)S(1)}, bf16[2,1,64,1536]{3,2,0,1:T(8,128)(2,1)S(1)}, u32[]{:S(2)}, u32[]{:S(2)}) collective-permute-start(bf16[2,1,64,1536]{3,2,0,1:T(8,128)(2,1)S(1)} %get-tuple-element.13), channel_id=1, source_target_pairs={{0,2},{2,4},{4,6},{6,8},{8,10},{10,12},{12,14},{1,3},{3,5},{5,7},{... | collective-permute-start | bytes 1179656 | tf_op jit(solution)/shard_map/ppermute | solution.py:34
  31.5 1.6 %collective-permute-start.7 = (bf16[2,1,64,1536]{3,2,1,0:T(8,128)(2,1)S(1)}, bf16[2,1,64,1536]{3,2,1,0:T(8,128)(2,1)S(1)}, u32[]{:S(2)}, u32[]{:S(2)}) collective-permute-start(bf16[2,1,64,1536]{3,2,1,0:T(8,128)(2,1)S(1)} %collective-permute-done.4.rest_8_), channel_id=1, source_target_pairs={{0,4},{4,8},{8,12},{12,14},{14,10},{10,6},{6,2},{2,0},{1,5},{5,9},... | collective-permute-start | bytes 1179656 | tf_op jit(solution)/shard_map/ppermute | solution.py:72
  33.1 0.9 collective-permute-start.18
  34.1 1.1 collective-permute-start.17
  35.2 1.3 collective-permute-start.6
  36.5 7.3 %collective-permute-done.7.rest_10_ = bf16[2,1,64,1536]{3,2,1,0:T(8,128)(2,1)S(1)} collective-permute-done((bf16[2,1,64,1536]{3,2,1,0:T(8,128)(2,1)S(1)}, bf16[2,1,64,1536]{3,2,1,0:T(8,128)(2,1)S(1)}, u32[]{:S(2)}, u32[]{:S(2)}) %collective-permute-start.7) | collective-permute-done | bytes 393248 | tf_op jit(solution)/shard_map/ppermute | solution.py:72
  43.8 2.2 %collective-permute-start.14 = (bf16[2,1,64,1536]{3,2,1,0:T(8,128)(2,1)S(1)}, bf16[2,1,64,1536]{3,2,1,0:T(8,128)(2,1)S(1)}, u32[]{:S(2)}, u32[]{:S(2)}) collective-permute-start(bf16[2,1,64,1536]{3,2,1,0:T(8,128)(2,1)S(1)} %collective-permute-done.13.rest_9_), channel_id=1, source_target_pairs={{4,0},{8,4},{12,8},{14,12},{10,14},{6,10},{2,6},{0,2},{5,1},{9,5},... | collective-permute-start | bytes 1179656 | tf_op jit(solution)/shard_map/ppermute | solution.py:75
  46.0 11.8 %collective-permute-done.18.rest_16_ = bf16[2,1,64,1536]{3,2,1,0:T(8,128)(2,1)} collective-permute-done((bf16[2,1,64,1536]{3,2,1,0:T(8,128)(2,1)}, bf16[2,1,64,1536]{3,2,1,0:T(8,128)(2,1)}, u32[]{:S(2)}, u32[]{:S(2)}) %collective-permute-start.18) | collective-permute-done | bytes 393248 | tf_op jit(solution)/shard_map/ppermute | solution.py:75
  57.8 2.5 %collective-permute-start.20 = (bf16[2,1,64,1536]{3,2,1,0:T(8,128)(2,1)}, bf16[2,1,64,1536]{3,2,1,0:T(8,128)(2,1)}, u32[]{:S(2)}, u32[]{:S(2)}) collective-permute-start(bf16[2,1,64,1536]{3,2,1,0:T(8,128)(2,1)} %collective-permute-done.18.rest_16_), channel_id=1, source_target_pairs={{4,0},{8,4},{12,8},{14,12},{10,14},{6,10},{2,6},{0,2},{5,1},{9,5},... | collective-permute-start | bytes 1179656 | tf_op jit(solution)/shard_map/ppermute | solution.py:75
  60.3 0.7 dynamic_slice.3
  61.0 0.6 gather_fusion
  61.6 1.2 fusion.6
  62.8 2.7 %collective-permute-start.8 = (bf16[2,1,64,1536]{3,2,0,1:T(8,128)(2,1)}, bf16[2,1,64,1536]{3,2,0,1:T(8,128)(2,1)}, u32[]{:S(2)}, u32[]{:S(2)}) collective-permute-start(bf16[2,1,64,1536]{3,2,0,1:T(8,128)(2,1)} %get-tuple-element.15), channel_id=1, source_target_pairs={{0,2},{2,4},{4,6},{6,8},{8,10},{10,12},{12,14},{1,3},{3,5},{5,7},{... | collective-permute-start | bytes 1179656 | tf_op jit(solution)/shard_map/ppermute | solution.py:34
  65.5 1.3 collective-permute-start.9
  66.8 2.4 %collective-permute-start.19 = (bf16[2,1,64,1536]{3,2,1,0:T(8,128)(2,1)}, bf16[2,1,64,1536]{3,2,1,0:T(8,128)(2,1)}, u32[]{:S(2)}, u32[]{:S(2)}) collective-permute-start(bf16[2,1,64,1536]{3,2,1,0:T(8,128)(2,1)} %collective-permute-done.17.rest_15_), channel_id=1, source_target_pairs={{0,4},{4,8},{8,12},{12,14},{14,10},{10,6},{6,2},{2,0},{1,5},{5,9},... | collective-permute-start | bytes 1179656 | tf_op jit(solution)/shard_map/ppermute | solution.py:72
  69.2 0.4 collective-permute-start.15
  69.6 13.5 %collective-permute-done.20.rest_18_ = bf16[2,1,64,1536]{3,2,1,0:T(8,128)(2,1)} collective-permute-done((bf16[2,1,64,1536]{3,2,1,0:T(8,128)(2,1)}, bf16[2,1,64,1536]{3,2,1,0:T(8,128)(2,1)}, u32[]{:S(2)}, u32[]{:S(2)}) %collective-permute-start.20) | collective-permute-done | bytes 393248 | tf_op jit(solution)/shard_map/ppermute | solution.py:75
  83.0 2.5 %collective-permute-start.22 = (bf16[2,1,64,1536]{3,2,1,0:T(8,128)(2,1)}, bf16[2,1,64,1536]{3,2,1,0:T(8,128)(2,1)}, u32[]{:S(2)}, u32[]{:S(2)}) collective-permute-start(bf16[2,1,64,1536]{3,2,1,0:T(8,128)(2,1)} %collective-permute-done.20.rest_18_), channel_id=1, source_target_pairs={{4,0},{8,4},{12,8},{14,12},{10,14},{6,10},{2,6},{0,2},{5,1},{9,5},... | collective-permute-start | bytes 1179656 | tf_op jit(solution)/shard_map/ppermute | solution.py:75
  85.5 1.3 fusion.15
  86.9 1.4 %reduce-window.34 = s32[4,1]{0,1:T(1,128)} reduce-window(s32[4,1]{0,1:T(1,128)} %get-tuple-element.34, s32[]{:T(128)} %constant.98.clone), window={size=4x1 pad=3_0x0_0}, to_apply=%region_0.1 | reduce-window | flops 12 | bytes 36 | tf_op jit(solution)/shard_map/reduce-window.14
  88.3 0.7 reduce-window.35
  89.0 0.6 gather_fusion.1
  89.7 0.6 gather_fusion.2
  90.3 0.1 pad_bitcast_fusion
  90.4 0.7 compare_select_fusion.10
  91.1 0.4 collective-permute-done.8
  91.5 1.4 %collective-permute-start.11 = (bf16[2,1,64,1536]{3,2,0,1:T(8,128)(2,1)}, bf16[2,1,64,1536]{3,2,0,1:T(8,128)(2,1)}, u32[]{:S(2)}, u32[]{:S(2)}) collective-permute-start(bf16[2,1,64,1536]{3,2,0,1:T(8,128)(2,1)} %get-tuple-element.17), channel_id=1, source_target_pairs={{12,14},{13,15},{28,30},{29,31}} | collective-permute-start | bytes 1179656 | tf_op jit(solution)/shard_map/ppermute | solution.py:218
  92.9 1.3 collective-permute-start.12
  94.2 0.1 collective-permute-start.16
  94.3 5.5 %collective-permute-done.15.rest_13_ = bf16[2,1,64,1536]{3,2,1,0:T(8,128)(2,1)} collective-permute-done((bf16[2,1,64,1536]{3,2,1,0:T(8,128)(2,1)S(1)}, bf16[2,1,64,1536]{3,2,1,0:T(8,128)(2,1)}, u32[]{:S(2)}, u32[]{:S(2)}) %collective-permute-start.15) | collective-permute-done | bytes 393248 | tf_op jit(solution)/shard_map/ppermute | solution.py:75
  99.8 8.5 %collective-permute-done.22.rest_20_ = bf16[2,1,64,1536]{3,2,1,0:T(8,128)(2,1)} collective-permute-done((bf16[2,1,64,1536]{3,2,1,0:T(8,128)(2,1)}, bf16[2,1,64,1536]{3,2,1,0:T(8,128)(2,1)}, u32[]{:S(2)}, u32[]{:S(2)}) %collective-permute-start.22) | collective-permute-done | bytes 393248 | tf_op jit(solution)/shard_map/ppermute | solution.py:75
  108.3 2.5 %collective-permute-start.23 = (bf16[2,1,64,1536]{3,2,1,0:T(8,128)(2,1)}, bf16[2,1,64,1536]{3,2,1,0:T(8,128)(2,1)}, u32[]{:S(2)}, u32[]{:S(2)}) collective-permute-start(bf16[2,1,64,1536]{3,2,1,0:T(8,128)(2,1)} %collective-permute-done.22.rest_20_), channel_id=1, source_target_pairs={{4,0},{8,4},{12,8},{14,12},{10,14},{6,10},{2,6},{0,2},{5,1},{9,5},... | collective-permute-start | bytes 1179656 | tf_op jit(solution)/shard_map/ppermute | solution.py:69
  110.8 0.1 add_bitcast_fusion
  110.9 0.1 copy.31
  111.0 0.1 reshape.421.table_ref
  111.1 12.5 %collective-permute-done.21.rest_19_ = bf16[2,1,64,1536]{3,2,1,0:T(8,128)(2,1)} collective-permute-done((bf16[2,1,64,1536]{3,2,1,0:T(8,128)(2,1)}, bf16[2,1,64,1536]{3,2,1,0:T(8,128)(2,1)}, u32[]{:S(2)}, u32[]{:S(2)}) %collective-permute-start.21) | collective-permute-done | bytes 393248 | tf_op jit(solution)/shard_map/ppermute | solution.py:72
  123.6 14.6 %shard_map.100 = bf16[512,1536]{1,0:T(8,128)(2,1)} custom-call(s32[16]{0:T(128)S(1)} %reshape.421.table_ref, bf16[512,1536]{1,0:T(8,128)(2,1)} %bitcast.92, bf16[2,8,64,1536]{3,2,1,0:T(8,128)(2,1)} %copy-done.2, bf16[2,1,64,1536]{3,2,1,0:T(8,128)(2,1)S(1)} %collective-permute-done.rest_0_, bf16[2,1,64,1536]{3,2,1,0:T(8,128)(2,1)S(1)} %collective-permute-done.1.rest_1_, ...), custom_call_target="tpu_custom_call" | custom-call | flops 3221225472 | bytes 9437184 | tf_op jit(solution)/shard_map/pallas_call | solution.py:147
  (44 shorter events, 0.2 us)
Async XLA Ops:
  0.0 17.6 %collective-permute-start.3 = (s32[4]{0:T(128)}, s32[4]{0:T(128)S(1)}, u32[]{:S(2)}, u32[]{:S(2)}) collective-permute-start(s32[4]{0:T(128)} %bitcast.93), channel_id=1, source_target_pairs={{0,2},{2,4},{4,6},{6,8},{8,10},{10,12},{12,14},{1,3},{3,5},{5,7},{... | collective-permute-start | bytes 56 | tf_op jit(solution)/shard_map/ppermute | solution.py:34
  4.9 14.4 %collective-permute-start.2 = (s32[4]{0:T(128)}, s32[4]{0:T(128)S(1)}, u32[]{:S(2)}, u32[]{:S(2)}) collective-permute-start(s32[4]{0:T(128)} %bitcast.94), channel_id=1, source_target_pairs={{2,0},{4,2},{6,4},{8,6},{10,8},{12,10},{14,12},{3,1},{5,3},{7,5},{... | collective-permute-start | bytes 56 | tf_op jit(solution)/shard_map/ppermute | solution.py:34
  8.1 1.9 %copy-start.4 = (bf16[8,1,64,1536]{3,2,1,0:T(8,128)(2,1)S(1)}, bf16[8,1,64,1536]{3,2,1,0:T(8,128)(2,1)}, u32[]{:S(2)}) copy-start(bf16[8,1,64,1536]{3,2,1,0:T(8,128)(2,1)} %param.15) | copy-start | bytes 4718596
  10.6 4.7 %copy-start.2 = (bf16[2,8,64,1536]{3,2,1,0:T(8,128)(2,1)}, bf16[2,8,64,1536]{3,2,1,0:T(8,128)(2,1)S(1)}, u32[]{:S(2)}) copy-start(bf16[2,8,64,1536]{3,2,1,0:T(8,128)(2,1)S(1)} %maximum_bitcast_fusion.own_hbm) | copy-start | bytes 9437188
  11.8 16.8 %collective-permute-start.4 = (bf16[2,1,64,1536]{3,2,1,0:T(8,128)(2,1)}, bf16[2,1,64,1536]{3,2,1,0:T(8,128)(2,1)S(1)}, u32[]{:S(2)}, u32[]{:S(2)}) collective-permute-start(bf16[2,1,64,1536]{3,2,1,0:T(8,128)(2,1)} %get-tuple-element.29), channel_id=1, source_target_pairs={{0,4},{4,8},{8,12},{12,14},{14,10},{10,6},{6,2},{2,0},{1,5},{5,9},... | collective-permute-start | bytes 1179656 | tf_op jit(solution)/shard_map/ppermute | solution.py:72
  15.4 17.8 %collective-permute-start.13 = (bf16[2,1,64,1536]{3,2,1,0:T(8,128)(2,1)}, bf16[2,1,64,1536]{3,2,1,0:T(8,128)(2,1)S(1)}, u32[]{:S(2)}, u32[]{:S(2)}) collective-permute-start(bf16[2,1,64,1536]{3,2,1,0:T(8,128)(2,1)} %get-tuple-element.29), channel_id=1, source_target_pairs={{4,0},{8,4},{12,8},{14,12},{10,14},{6,10},{2,6},{0,2},{5,1},{9,5},... | collective-permute-start | bytes 1179656 | tf_op jit(solution)/shard_map/ppermute | solution.py:75
  16.3 17.8 %collective-permute-start = (bf16[2,1,64,1536]{3,2,1,0:T(8,128)(2,1)}, bf16[2,1,64,1536]{3,2,1,0:T(8,128)(2,1)S(1)}, u32[]{:S(2)}, u32[]{:S(2)}) collective-permute-start(bf16[2,1,64,1536]{3,2,1,0:T(8,128)(2,1)} %get-tuple-element.21), channel_id=1, source_target_pairs={{0,1},{2,3},{4,5},{6,7},{8,9},{10,11},{12,13},{14,15},{16,17},{18,... | collective-permute-start | bytes 1179656 | tf_op jit(solution)/shard_map/ppermute | solution.py:34
  17.6 17.6 %collective-permute-start.1 = (bf16[2,1,64,1536]{3,2,1,0:T(8,128)(2,1)}, bf16[2,1,64,1536]{3,2,1,0:T(8,128)(2,1)S(1)}, u32[]{:S(2)}, u32[]{:S(2)}) collective-permute-start(bf16[2,1,64,1536]{3,2,1,0:T(8,128)(2,1)} %get-tuple-element.20), channel_id=1, source_target_pairs={{1,0},{3,2},{5,4},{7,6},{9,8},{11,10},{13,12},{15,14},{17,16},{19,... | collective-permute-start | bytes 1179656 | tf_op jit(solution)/shard_map/ppermute | solution.py:34
  25.7 1.3 copy-start.3
  27.2 33.1 %copy-start.5 = (s32[1,1,4]{2,1,0:T(1,128)S(1)}, s32[1,1,4]{2,1,0:T(1,128)}, u32[]{:S(2)}) copy-start(s32[1,1,4]{2,1,0:T(1,128)} %param.18) | copy-start | bytes 52
  27.2 33.1 %copy-start = (s32[8]{0:T(128)S(1)}, s32[8]{0:T(128)}, u32[]{:S(2)}) copy-start(s32[8]{0:T(128)} %constant.96.clone) | copy-start | bytes 100
  27.2 61.8 %copy-start.1 = (s32[7,2]{1,0:T(8,128)S(1)}, s32[7,2]{1,0:T(8,128)}, u32[]{:S(2)}) copy-start(s32[7,2]{1,0:T(8,128)} %constant.97.clone) | copy-start | bytes 172
  28.5 17.4 %collective-permute-start.5 = (bf16[2,1,64,1536]{3,2,0,1:T(8,128)(2,1)S(1)}, bf16[2,1,64,1536]{3,2,0,1:T(8,128)(2,1)S(1)}, u32[]{:S(2)}, u32[]{:S(2)}) collective-permute-start(bf16[2,1,64,1536]{3,2,0,1:T(8,128)(2,1)S(1)} %get-tuple-element.13), channel_id=1, source_target_pairs={{0,2},{2,4},{4,6},{6,8},{8,10},{10,12},{12,14},{1,3},{3,5},{5,7},{... | collective-permute-start | bytes 1179656 | tf_op jit(solution)/shard_map/ppermute | solution.py:34
  31.5 12.2 %collective-permute-start.7 = (bf16[2,1,64,1536]{3,2,1,0:T(8,128)(2,1)S(1)}, bf16[2,1,64,1536]{3,2,1,0:T(8,128)(2,1)S(1)}, u32[]{:S(2)}, u32[]{:S(2)}) collective-permute-start(bf16[2,1,64,1536]{3,2,1,0:T(8,128)(2,1)S(1)} %collective-permute-done.4.rest_8_), channel_id=1, source_target_pairs={{0,4},{4,8},{8,12},{12,14},{14,10},{10,6},{6,2},{2,0},{1,5},{5,9},... | collective-permute-start | bytes 1179656 | tf_op jit(solution)/shard_map/ppermute | solution.py:72
  33.1 24.6 %collective-permute-start.18 = (bf16[2,1,64,1536]{3,2,1,0:T(8,128)(2,1)}, bf16[2,1,64,1536]{3,2,1,0:T(8,128)(2,1)}, u32[]{:S(2)}, u32[]{:S(2)}) collective-permute-start(bf16[2,1,64,1536]{3,2,1,0:T(8,128)(2,1)} %get-tuple-element.19), channel_id=1, source_target_pairs={{4,0},{8,4},{12,8},{14,12},{10,14},{6,10},{2,6},{0,2},{5,1},{9,5},... | collective-permute-start | bytes 1179656 | tf_op jit(solution)/shard_map/ppermute | solution.py:75
  34.1 31.4 %collective-permute-start.17 = (bf16[2,1,64,1536]{3,2,1,0:T(8,128)(2,1)}, bf16[2,1,64,1536]{3,2,1,0:T(8,128)(2,1)}, u32[]{:S(2)}, u32[]{:S(2)}) collective-permute-start(bf16[2,1,64,1536]{3,2,1,0:T(8,128)(2,1)} %get-tuple-element.19), channel_id=1, source_target_pairs={{0,4},{4,8},{8,12},{12,14},{14,10},{10,6},{6,2},{2,0},{1,5},{5,9},... | collective-permute-start | bytes 1179656 | tf_op jit(solution)/shard_map/ppermute | solution.py:72
  35.2 27.7 %collective-permute-start.6 = (bf16[2,1,64,1536]{3,2,0,1:T(8,128)(2,1)}, bf16[2,1,64,1536]{3,2,0,1:T(8,128)(2,1)S(1)}, u32[]{:S(2)}, u32[]{:S(2)}) collective-permute-start(bf16[2,1,64,1536]{3,2,0,1:T(8,128)(2,1)} %get-tuple-element.14), channel_id=1, source_target_pairs={{2,0},{4,2},{6,4},{8,6},{10,8},{12,10},{14,12},{3,1},{5,3},{7,5},{... | collective-permute-start | bytes 1179656 | tf_op jit(solution)/shard_map/ppermute | solution.py:34
  43.8 23.0 %collective-permute-start.14 = (bf16[2,1,64,1536]{3,2,1,0:T(8,128)(2,1)S(1)}, bf16[2,1,64,1536]{3,2,1,0:T(8,128)(2,1)S(1)}, u32[]{:S(2)}, u32[]{:S(2)}) collective-permute-start(bf16[2,1,64,1536]{3,2,1,0:T(8,128)(2,1)S(1)} %collective-permute-done.13.rest_9_), channel_id=1, source_target_pairs={{4,0},{8,4},{12,8},{14,12},{10,14},{6,10},{2,6},{0,2},{5,1},{9,5},... | collective-permute-start | bytes 1179656 | tf_op jit(solution)/shard_map/ppermute | solution.py:75
  46.0 23.2 %collective-permute-start.10 = (bf16[2,1,64,1536]{3,2,1,0:T(8,128)(2,1)S(1)}, bf16[2,1,64,1536]{3,2,1,0:T(8,128)(2,1)S(1)}, u32[]{:S(2)}, u32[]{:S(2)}) collective-permute-start(bf16[2,1,64,1536]{3,2,1,0:T(8,128)(2,1)S(1)} %collective-permute-done.7.rest_10_), channel_id=1, source_target_pairs={{0,4},{4,8},{8,12},{12,14},{14,10},{10,6},{6,2},{2,0},{1,5},{5,9},... | collective-permute-start | bytes 1179656 | tf_op jit(solution)/shard_map/ppermute | solution.py:72
  57.8 25.3 %collective-permute-start.20 = (bf16[2,1,64,1536]{3,2,1,0:T(8,128)(2,1)}, bf16[2,1,64,1536]{3,2,1,0:T(8,128)(2,1)}, u32[]{:S(2)}, u32[]{:S(2)}) collective-permute-start(bf16[2,1,64,1536]{3,2,1,0:T(8,128)(2,1)} %collective-permute-done.18.rest_16_), channel_id=1, source_target_pairs={{4,0},{8,4},{12,8},{14,12},{10,14},{6,10},{2,6},{0,2},{5,1},{9,5},... | collective-permute-start | bytes 1179656 | tf_op jit(solution)/shard_map/ppermute | solution.py:75
  62.8 28.6 %collective-permute-start.8 = (bf16[2,1,64,1536]{3,2,0,1:T(8,128)(2,1)}, bf16[2,1,64,1536]{3,2,0,1:T(8,128)(2,1)}, u32[]{:S(2)}, u32[]{:S(2)}) collective-permute-start(bf16[2,1,64,1536]{3,2,0,1:T(8,128)(2,1)} %get-tuple-element.15), channel_id=1, source_target_pairs={{0,2},{2,4},{4,6},{6,8},{8,10},{10,12},{12,14},{1,3},{3,5},{5,7},{... | collective-permute-start | bytes 1179656 | tf_op jit(solution)/shard_map/ppermute | solution.py:34
  65.5 27.4 %collective-permute-start.9 = (bf16[2,1,64,1536]{3,2,0,1:T(8,128)(2,1)}, bf16[2,1,64,1536]{3,2,0,1:T(8,128)(2,1)}, u32[]{:S(2)}, u32[]{:S(2)}) collective-permute-start(bf16[2,1,64,1536]{3,2,0,1:T(8,128)(2,1)} %get-tuple-element.16), channel_id=1, source_target_pairs={{2,0},{4,2},{6,4},{8,6},{10,8},{12,10},{14,12},{3,1},{5,3},{7,5},{... | collective-permute-start | bytes 1179656 | tf_op jit(solution)/shard_map/ppermute | solution.py:34
  66.8 27.4 %collective-permute-start.19 = (bf16[2,1,64,1536]{3,2,1,0:T(8,128)(2,1)}, bf16[2,1,64,1536]{3,2,1,0:T(8,128)(2,1)}, u32[]{:S(2)}, u32[]{:S(2)}) collective-permute-start(bf16[2,1,64,1536]{3,2,1,0:T(8,128)(2,1)} %collective-permute-done.17.rest_15_), channel_id=1, source_target_pairs={{0,4},{4,8},{8,12},{12,14},{14,10},{10,6},{6,2},{2,0},{1,5},{5,9},... | collective-permute-start | bytes 1179656 | tf_op jit(solution)/shard_map/ppermute | solution.py:72
  69.2 30.6 %collective-permute-start.15 = (bf16[2,1,64,1536]{3,2,1,0:T(8,128)(2,1)S(1)}, bf16[2,1,64,1536]{3,2,1,0:T(8,128)(2,1)}, u32[]{:S(2)}, u32[]{:S(2)}) collective-permute-start(bf16[2,1,64,1536]{3,2,1,0:T(8,128)(2,1)S(1)} %collective-permute-done.14.rest_11_), channel_id=1, source_target_pairs={{4,0},{8,4},{12,8},{14,12},{10,14},{6,10},{2,6},{0,2},{5,1},{9,5},... | collective-permute-start | bytes 1179656 | tf_op jit(solution)/shard_map/ppermute | solution.py:75
  83.0 25.3 %collective-permute-start.22 = (bf16[2,1,64,1536]{3,2,1,0:T(8,128)(2,1)}, bf16[2,1,64,1536]{3,2,1,0:T(8,128)(2,1)}, u32[]{:S(2)}, u32[]{:S(2)}) collective-permute-start(bf16[2,1,64,1536]{3,2,1,0:T(8,128)(2,1)} %collective-permute-done.20.rest_18_), channel_id=1, source_target_pairs={{4,0},{8,4},{12,8},{14,12},{10,14},{6,10},{2,6},{0,2},{5,1},{9,5},... | collective-permute-start | bytes 1179656 | tf_op jit(solution)/shard_map/ppermute | solution.py:75
  91.5 19.6 %collective-permute-start.11 = (bf16[2,1,64,1536]{3,2,0,1:T(8,128)(2,1)}, bf16[2,1,64,1536]{3,2,0,1:T(8,128)(2,1)}, u32[]{:S(2)}, u32[]{:S(2)}) collective-permute-start(bf16[2,1,64,1536]{3,2,0,1:T(8,128)(2,1)} %get-tuple-element.17), channel_id=1, source_target_pairs={{12,14},{13,15},{28,30},{29,31}} | collective-permute-start | bytes 1179656 | tf_op jit(solution)/shard_map/ppermute | solution.py:218
  92.9 18.2 %collective-permute-start.12 = (bf16[2,1,64,1536]{3,2,0,1:T(8,128)(2,1)}, bf16[2,1,64,1536]{3,2,0,1:T(8,128)(2,1)}, u32[]{:S(2)}, u32[]{:S(2)}) collective-permute-start(bf16[2,1,64,1536]{3,2,0,1:T(8,128)(2,1)} %get-tuple-element.18), channel_id=1, source_target_pairs={{2,0},{3,1},{18,16},{19,17}} | collective-permute-start | bytes 1179656 | tf_op jit(solution)/shard_map/ppermute | solution.py:219
  94.2 29.4 %collective-permute-start.16 = (bf16[2,1,64,1536]{3,2,1,0:T(8,128)(2,1)S(1)}, bf16[2,1,64,1536]{3,2,1,0:T(8,128)(2,1)}, u32[]{:S(2)}, u32[]{:S(2)}) collective-permute-start(bf16[2,1,64,1536]{3,2,1,0:T(8,128)(2,1)S(1)} %collective-permute-done.10.rest_12_), channel_id=1, source_target_pairs={{0,4},{4,8},{8,12},{12,14},{14,10},{10,6},{6,2},{2,0},{1,5},{5,9},... | collective-permute-start | bytes 1179656 | tf_op jit(solution)/shard_map/ppermute | solution.py:67
  99.8 23.8 %collective-permute-start.21 = (bf16[2,1,64,1536]{3,2,1,0:T(8,128)(2,1)}, bf16[2,1,64,1536]{3,2,1,0:T(8,128)(2,1)}, u32[]{:S(2)}, u32[]{:S(2)}) collective-permute-start(bf16[2,1,64,1536]{3,2,1,0:T(8,128)(2,1)} %collective-permute-done.19.rest_17_), channel_id=1, source_target_pairs={{0,4},{4,8},{8,12},{12,14},{14,10},{10,6},{6,2},{2,0},{1,5},{5,9},... | collective-permute-start | bytes 1179656 | tf_op jit(solution)/shard_map/ppermute | solution.py:72
  108.3 15.3 %collective-permute-start.23 = (bf16[2,1,64,1536]{3,2,1,0:T(8,128)(2,1)}, bf16[2,1,64,1536]{3,2,1,0:T(8,128)(2,1)}, u32[]{:S(2)}, u32[]{:S(2)}) collective-permute-start(bf16[2,1,64,1536]{3,2,1,0:T(8,128)(2,1)} %collective-permute-done.22.rest_20_), channel_id=1, source_target_pairs={{4,0},{8,4},{12,8},{14,12},{10,14},{6,10},{2,6},{0,2},{5,1},{9,5},... | collective-permute-start | bytes 1179656 | tf_op jit(solution)/shard_map/ppermute | solution.py:69

commit v15 on v12

--- a/solution.py
+++ b/solution.py
@@ -118,14 +118,16 @@
         k = k_vmem[:, :, lanes].reshape(key_count, HEAD_DIM)
         v = v_vmem[:, :, lanes].reshape(key_count, HEAD_DIM)
         scores = lax.dot_general(
-            q, k, (((1,), (1,)), ((), ())), preferred_element_type=jnp.float32
+            k, q, (((1,), (1,)), ((), ())), preferred_element_type=jnp.float32
         ) * HEAD_DIM ** (-0.5)
-        row_max = jnp.max(scores, axis=1, keepdims=True)
-        weights = jnp.exp(scores - row_max)
-        row_total = jnp.sum(weights, axis=1, keepdims=True)
+        col_max = jnp.max(scores, axis=0, keepdims=True)
+        weights = jnp.exp(scores - col_max)
+        col_total = jnp.sum(weights, axis=0, keepdims=True)
         rounded = weights.astype(jnp.bfloat16)
-        blended = jnp.dot(rounded, v, preferred_element_type=jnp.float32)
-        o_ref[:, lanes] = (blended / row_total).astype(o_ref.dtype)
+        blended = lax.dot_general(
+            v, rounded, (((0,), (0,)), ((), ())), preferred_element_type=jnp.float32
+        )
+        o_ref[:, lanes] = (blended / col_total).T.astype(o_ref.dtype)
 
 
 def gather_attend(query_rows, own, cycle_list_sources, far_list_sources, table):

time: 131 us -> 134 us (1.023)
  the two profiles are of different devices: /device:TPU:24 before, /device:TPU:16 now
where the time goes in v15:
time: 134 us
  starting transfers between devices  54 us (40%)
  waiting for transfers between devices  37 us (28%)
  Pallas kernels  18.1 us (14%)
  local copies, waits for them, and re-layouts  13.4 us (10%)
  other arithmetic  10.9 us (8%)
    ppermute x8, starting transfers between devices, shift(): return lax.ppermute(x, axis, pairs)  21.1 us
    pallas_call x1, Pallas kernels, gather_attend(): pl.pallas_call(kernel, out_shape=jax.ShapeDtypeStruct((token_count, width...  18.1 us
    ppermute x6, starting transfers between devices, ring_gather(): behind = lax.ppermute(behind, 'col', backward)  17.5 us
    ppermute x6, waiting for transfers between devices, ring_gather(): behind = lax.ppermute(behind, 'col', backward)  12.9 us
    ppermute x1, waiting for transfers between devices, ring_gather(): arrays.append(lax.ppermute(behind, 'col', backward))  9.48 us
    ppermute x8, waiting for transfers between devices, shift(): return lax.ppermute(x, axis, pairs)  7.41 us
    ppermute x1, starting transfers between devices, ring_gather(): arrays.append(lax.ppermute(ahead, 'col', forward))  6.71 us
    ppermute x6, starting transfers between devices, ring_gather(): ahead = lax.ppermute(ahead, 'col', forward)  5.78 us
  transfers between devices with their start and end apart: 24, of which 10 were waited for; matrix products, arithmetic and copies ran while one was open for 17% of the time, Pallas kernels for 0%

profile of v15, /device:TPU:16, one launch (start us, length us, event | category | flops | bytes accessed | tf_op | source)
XLA Modules:
  0.0 133.8 jit_solution(4700176571131622158)
XLA Ops:
  0.0 3.4 %collective-permute-start.3 = (s32[4]{0:T(128)}, s32[4]{0:T(128)S(1)}, u32[]{:S(2)}, u32[]{:S(2)}) collective-permute-start(s32[4]{0:T(128)} %bitcast.93), channel_id=1, source_target_pairs={{0,2},{2,4},{4,6},{6,8},{8,10},{10,12},{12,14},{1,3},{3,5},{5,7},{... | collective-permute-start | bytes 56 | tf_op jit(solution)/shard_map/ppermute | solution.py:34
  3.4 3.3 %collective-permute-start.2 = (s32[4]{0:T(128)}, s32[4]{0:T(128)S(1)}, u32[]{:S(2)}, u32[]{:S(2)}) collective-permute-start(s32[4]{0:T(128)} %bitcast.94), channel_id=1, source_target_pairs={{2,0},{4,2},{6,4},{8,6},{10,8},{12,10},{14,12},{3,1},{5,3},{7,5},{... | collective-permute-start | bytes 56 | tf_op jit(solution)/shard_map/ppermute | solution.py:34
  6.8 1.0 exponential_bitcast_fusion.1
  7.7 1.0 exponential_bitcast_fusion
  8.7 1.8 %fusion.1 = bf16[8,1,64,1536]{3,2,0,1:T(8,128)(2,1)S(1)} fusion(bf16[8,1,64,1536]{3,2,1,0:T(8,128)(2,1)} %param.13, f32[8,2,1536]{2,1,0:T(2,128)S(1)} %exponential_bitcast_fusion.1), kind=kLoop, calls=%fused_computation.9 | loop fusion | flops 2359296 | bytes 3244032 | tf_op jit(solution)/shard_map/convert_element_type | solution.py:24
  10.5 0.1 copy-done.4
  10.6 0.3 fusion
  10.9 0.3 maximum_bitcast_fusion.own_hbm
  11.3 0.9 fusion.19
  12.2 1.6 %collective-permute-start.4 = (bf16[2,1,64,1536]{3,2,1,0:T(8,128)(2,1)}, bf16[2,1,64,1536]{3,2,1,0:T(8,128)(2,1)S(1)}, u32[]{:S(2)}, u32[]{:S(2)}) collective-permute-start(bf16[2,1,64,1536]{3,2,1,0:T(8,128)(2,1)} %get-tuple-element.27), channel_id=1, source_target_pairs={{0,4},{4,8},{8,12},{12,14},{14,10},{10,6},{6,2},{2,0},{1,5},{5,9},... | collective-permute-start | bytes 1179656 | tf_op jit(solution)/shard_map/ppermute | solution.py:67
  13.8 0.4 collective-permute-start.13
  14.2 0.4 collective-permute-start.18
  14.7 1.0 fusion.16
  15.6 1.6 %collective-permute-start.17 = (bf16[2,1,64,1536]{3,2,1,0:T(8,128)(2,1)S(1)}, bf16[2,1,64,1536]{3,2,1,0:T(8,128)(2,1)}, u32[]{:S(2)}, u32[]{:S(2)}) collective-permute-start(bf16[2,1,64,1536]{3,2,1,0:T(8,128)(2,1)S(1)} %get-tuple-element.26), channel_id=1, source_target_pairs={{0,4},{4,8},{8,12},{12,14},{14,10},{10,6},{6,2},{2,0},{1,5},{5,9},... | collective-permute-start | bytes 1179656 | tf_op jit(solution)/shard_map/ppermute | solution.py:67
  17.2 0.2 reduce-window.37
  17.4 0.1 select_reduce_fusion
  17.6 1.3 collective-permute-start
  18.9 0.2 reduce-window.36
  19.1 0.1 select_reduce_fusion.1
  19.2 2.5 %gather_fusion.4 = bf16[3,2,64,1536]{3,2,1,0:T(8,128)(2,1)S(1)} fusion(bf16[2,8,64,1536]{3,2,1,0:T(8,128)(2,1)} %copy-done.2, s32[1024]{0:T(1024)S(1)} %pad_clamp_fusion), kind=kCustom, calls=%fused_computation.1.clone | custom fusion | bytes 2359308 | tf_op jit(solution)/shard_map/jit(_take)/gather | solution.py:203
  21.8 3.6 %gather_fusion.3 = bf16[3,2,64,1536]{3,2,1,0:T(8,128)(2,1)} fusion(bf16[2,8,64,1536]{3,2,1,0:T(8,128)(2,1)} %copy-done.2, s32[1024]{0:T(1024)S(1)} %pad_clamp_fusion.1), kind=kCustom, calls=%fused_computation.clone | custom fusion | bytes 2359308 | tf_op jit(solution)/shard_map/jit(_take)/gather | solution.py:202
  25.3 0.2 select_bitcast_fusion
  25.5 1.1 copy-done.3
  26.6 0.2 select_bitcast_fusion.1
  26.8 1.4 %collective-permute-start.1 = (bf16[2,1,64,1536]{3,2,1,0:T(8,128)(2,1)}, bf16[2,1,64,1536]{3,2,1,0:T(8,128)(2,1)S(1)}, u32[]{:S(2)}, u32[]{:S(2)}) collective-permute-start(bf16[2,1,64,1536]{3,2,1,0:T(8,128)(2,1)} %get-tuple-element.18), channel_id=1, source_target_pairs={{1,0},{3,2},{5,4},{7,6},{9,8},{11,10},{13,12},{15,14},{17,16},{19,... | collective-permute-start | bytes 1179656 | tf_op jit(solution)/shard_map/ppermute | solution.py:34
  28.3 4.3 %collective-permute-done.18.rest_16_ = bf16[2,1,64,1536]{3,2,1,0:T(8,128)(2,1)} collective-permute-done((bf16[2,1,64,1536]{3,2,1,0:T(8,128)(2,1)S(1)}, bf16[2,1,64,1536]{3,2,1,0:T(8,128)(2,1)}, u32[]{:S(2)}, u32[]{:S(2)}) %collective-permute-start.18) | collective-permute-done | bytes 393248 | tf_op jit(solution)/shard_map/ppermute | solution.py:70
  32.5 0.6 collective-permute-start.7
  33.1 1.4 %fusion.17 = (bf16[2,1,64,1536]{3,2,0,1:T(8,128)(2,1)}, bf16[2,1,64,1536]{3,2,0,1:T(8,128)(2,1)}, bf16[2,1,64,1536]{3,2,0,1:T(8,128)(2,1)}, bf16[2,1,64,1536]{3,...) fusion(bf16[2,3,64,1536]{3,2,0,1:T(8,128)(2,1)S(1)} %select_bitcast_fusion, ...), kind=kLoop, calls=%fused_computation.73 | loop fusion | bytes 4718592 | tf_op jit(solution)/shard_map/slice | solution.py:208
  34.6 1.9 %collective-permute-start.5 = (bf16[2,1,64,1536]{3,2,0,1:T(8,128)(2,1)}, bf16[2,1,64,1536]{3,2,0,1:T(8,128)(2,1)S(1)}, u32[]{:S(2)}, u32[]{:S(2)}) collective-permute-start(bf16[2,1,64,1536]{3,2,0,1:T(8,128)(2,1)} %get-tuple-element.12), channel_id=1, source_target_pairs={{0,2},{2,4},{4,6},{6,8},{8,10},{10,12},{12,14},{1,3},{3,5},{5,7},{... | collective-permute-start | bytes 1179656 | tf_op jit(solution)/shard_map/ppermute | solution.py:34
  36.5 4.8 %collective-permute-start.6 = (bf16[2,1,64,1536]{3,2,0,1:T(8,128)(2,1)}, bf16[2,1,64,1536]{3,2,0,1:T(8,128)(2,1)S(1)}, u32[]{:S(2)}, u32[]{:S(2)}) collective-permute-start(bf16[2,1,64,1536]{3,2,0,1:T(8,128)(2,1)} %get-tuple-element.13), channel_id=1, source_target_pairs={{2,0},{4,2},{6,4},{8,6},{10,8},{12,10},{14,12},{3,1},{5,3},{7,5},{... | collective-permute-start | bytes 1179656 | tf_op jit(solution)/shard_map/ppermute | solution.py:34
  41.3 1.5 %collective-permute-start.20 = (bf16[2,1,64,1536]{3,2,1,0:T(8,128)(2,1)}, bf16[2,1,64,1536]{3,2,1,0:T(8,128)(2,1)}, u32[]{:S(2)}, u32[]{:S(2)}) collective-permute-start(bf16[2,1,64,1536]{3,2,1,0:T(8,128)(2,1)} %collective-permute-done.18.rest_16_), channel_id=1, source_target_pairs={{4,0},{8,4},{12,8},{14,12},{10,14},{6,10},{2,6},{0,2},{5,1},{9,5},... | collective-permute-start | bytes 1179656 | tf_op jit(solution)/shard_map/ppermute | solution.py:70
  42.8 0.1 collective-permute-start.14
  42.9 2.0 %collective-permute-start.10 = (bf16[2,1,64,1536]{3,2,1,0:T(8,128)(2,1)S(1)}, bf16[2,1,64,1536]{3,2,1,0:T(8,128)(2,1)S(1)}, u32[]{:S(2)}, u32[]{:S(2)}) collective-permute-start(bf16[2,1,64,1536]{3,2,1,0:T(8,128)(2,1)S(1)} %collective-permute-done.7.rest_10_), channel_id=1, source_target_pairs={{0,4},{4,8},{8,12},{12,14},{14,10},{10,6},{6,2},{2,0},{1,5},{5,9},... | collective-permute-start | bytes 1179656 | tf_op jit(solution)/shard_map/ppermute | solution.py:67
  44.9 0.7 dynamic_slice.3
  45.5 0.6 gather_fusion
  46.2 1.2 fusion.6
  47.4 4.4 %collective-permute-done.5 = bf16[2,1,64,1536]{3,2,0,1:T(8,128)(2,1)S(1)} collective-permute-done((bf16[2,1,64,1536]{3,2,0,1:T(8,128)(2,1)}, bf16[2,1,64,1536]{3,2,0,1:T(8,128)(2,1)S(1)}, u32[]{:S(2)}, u32[]{:S(2)}) %collective-permute-start.5) | collective-permute-done | bytes 393248 | tf_op jit(solution)/shard_map/ppermute | solution.py:34
  51.8 3.0 %collective-permute-done.6 = bf16[2,1,64,1536]{3,2,0,1:T(8,128)(2,1)S(1)} collective-permute-done((bf16[2,1,64,1536]{3,2,0,1:T(8,128)(2,1)}, bf16[2,1,64,1536]{3,2,0,1:T(8,128)(2,1)S(1)}, u32[]{:S(2)}, u32[]{:S(2)}) %collective-permute-start.6) | collective-permute-done | bytes 393248 | tf_op jit(solution)/shard_map/ppermute | solution.py:34
  54.8 2.7 %collective-permute-start.8 = (bf16[2,1,64,1536]{3,2,0,1:T(8,128)(2,1)}, bf16[2,1,64,1536]{3,2,0,1:T(8,128)(2,1)}, u32[]{:S(2)}, u32[]{:S(2)}) collective-permute-start(bf16[2,1,64,1536]{3,2,0,1:T(8,128)(2,1)} %get-tuple-element.14), channel_id=1, source_target_pairs={{0,2},{2,4},{4,6},{6,8},{8,10},{10,12},{12,14},{1,3},{3,5},{5,7},{... | collective-permute-start | bytes 1179656 | tf_op jit(solution)/shard_map/ppermute | solution.py:34
  57.5 3.0 %collective-permute-done.20.rest_18_ = bf16[2,1,64,1536]{3,2,1,0:T(8,128)(2,1)} collective-permute-done((bf16[2,1,64,1536]{3,2,1,0:T(8,128)(2,1)}, bf16[2,1,64,1536]{3,2,1,0:T(8,128)(2,1)}, u32[]{:S(2)}, u32[]{:S(2)}) %collective-permute-start.20) | collective-permute-done | bytes 393248 | tf_op jit(solution)/shard_map/ppermute | solution.py:70
  60.5 2.2 %collective-permute-start.9 = (bf16[2,1,64,1536]{3,2,0,1:T(8,128)(2,1)}, bf16[2,1,64,1536]{3,2,0,1:T(8,128)(2,1)}, u32[]{:S(2)}, u32[]{:S(2)}) collective-permute-start(bf16[2,1,64,1536]{3,2,0,1:T(8,128)(2,1)} %get-tuple-element.15), channel_id=1, source_target_pairs={{2,0},{4,2},{6,4},{8,6},{10,8},{12,10},{14,12},{3,1},{5,3},{7,5},{... | collective-permute-start | bytes 1179656 | tf_op jit(solution)/shard_map/ppermute | solution.py:34
  62.7 4.4 %collective-permute-done.14.rest_11_ = bf16[2,1,64,1536]{3,2,1,0:T(8,128)(2,1)S(1)} collective-permute-done((bf16[2,1,64,1536]{3,2,1,0:T(8,128)(2,1)S(1)}, bf16[2,1,64,1536]{3,2,1,0:T(8,128)(2,1)S(1)}, u32[]{:S(2)}, u32[]{:S(2)}) %collective-permute-start.14) | collective-permute-done | bytes 393248 | tf_op jit(solution)/shard_map/ppermute | solution.py:70
  67.2 2.8 %collective-permute-start.22 = (bf16[2,1,64,1536]{3,2,1,0:T(8,128)(2,1)}, bf16[2,1,64,1536]{3,2,1,0:T(8,128)(2,1)}, u32[]{:S(2)}, u32[]{:S(2)}) collective-permute-start(bf16[2,1,64,1536]{3,2,1,0:T(8,128)(2,1)} %collective-permute-done.20.rest_18_), channel_id=1, source_target_pairs={{4,0},{8,4},{12,8},{14,12},{10,14},{6,10},{2,6},{0,2},{5,1},{9,5},... | collective-permute-start | bytes 1179656 | tf_op jit(solution)/shard_map/ppermute | solution.py:70
  70.0 12.2 %collective-permute-start.15 = (bf16[2,1,64,1536]{3,2,1,0:T(8,128)(2,1)S(1)}, bf16[2,1,64,1536]{3,2,1,0:T(8,128)(2,1)}, u32[]{:S(2)}, u32[]{:S(2)}) collective-permute-start(bf16[2,1,64,1536]{3,2,1,0:T(8,128)(2,1)S(1)} %collective-permute-done.14.rest_11_), channel_id=1, source_target_pairs={{4,0},{8,4},{12,8},{14,12},{10,14},{6,10},{2,6},{0,2},{5,1},{9,5},... | collective-permute-start | bytes 1179656 | tf_op jit(solution)/shard_map/ppermute | solution.py:70
  82.3 1.3 %fusion.15 = s32[4]{0:T(128)S(1)} fusion(s32[4]{0:T(128)S(1)} %gather_fusion, s32[]{:T(128)} %bitcast.5, s32[1,1,4]{2,1,0:T(1,128)} %param.18), kind=kLoop, calls=%fused_computation.68 | loop fusion | flops 140 | bytes 52 | tf_op jit(solution)/shard_map/concatenate | solution.py:228
  83.6 1.4 %reduce-window.34 = s32[4,1]{0,1:T(1,128)} reduce-window(s32[4,1]{0,1:T(1,128)} %get-tuple-element.32, s32[]{:T(128)} %constant.98.clone), window={size=4x1 pad=3_0x0_0}, to_apply=%region_0.1 | reduce-window | flops 12 | bytes 36 | tf_op jit(solution)/shard_map/reduce-window.14
  85.0 0.7 reduce-window.35
  85.8 0.6 gather_fusion.1
  86.4 0.6 gather_fusion.2
  87.0 0.1 pad_bitcast_fusion
  87.1 0.7 compare_select_fusion.10
  87.8 0.1 collective-permute-start.21
  87.9 1.4 %collective-permute-start.11 = (bf16[2,1,64,1536]{3,2,0,1:T(8,128)(2,1)}, bf16[2,1,64,1536]{3,2,0,1:T(8,128)(2,1)}, u32[]{:S(2)}, u32[]{:S(2)}) collective-permute-start(bf16[2,1,64,1536]{3,2,0,1:T(8,128)(2,1)} %get-tuple-element.16), channel_id=1, source_target_pairs={{12,14},{13,15},{28,30},{29,31}} | collective-permute-start | bytes 1179656 | tf_op jit(solution)/shard_map/ppermute | solution.py:215
  89.3 1.4 %collective-permute-start.12 = (bf16[2,1,64,1536]{3,2,0,1:T(8,128)(2,1)}, bf16[2,1,64,1536]{3,2,0,1:T(8,128)(2,1)}, u32[]{:S(2)}, u32[]{:S(2)}) collective-permute-start(bf16[2,1,64,1536]{3,2,0,1:T(8,128)(2,1)} %get-tuple-element.17), channel_id=1, source_target_pairs={{2,0},{3,1},{18,16},{19,17}} | collective-permute-start | bytes 1179656 | tf_op jit(solution)/shard_map/ppermute | solution.py:216
  90.7 0.2 collective-permute-done.22.rest_20_
  90.9 6.7 %collective-permute-start.16 = (bf16[2,1,64,1536]{3,2,1,0:T(8,128)(2,1)S(1)}, bf16[2,1,64,1536]{3,2,1,0:T(8,128)(2,1)}, u32[]{:S(2)}, u32[]{:S(2)}) collective-permute-start(bf16[2,1,64,1536]{3,2,1,0:T(8,128)(2,1)S(1)} %collective-permute-done.10.rest_12_), channel_id=1, source_target_pairs={{0,4},{4,8},{8,12},{12,14},{14,10},{10,6},{6,2},{2,0},{1,5},{5,9},... | collective-permute-start | bytes 1179656 | tf_op jit(solution)/shard_map/ppermute | solution.py:62
  97.6 1.0 collective-permute-done.15.rest_13_
  98.6 0.1 add_bitcast_fusion
  98.7 0.1 copy.31
  98.8 0.1 reshape.421.table_ref
  98.8 1.7 %collective-permute-done.21.rest_19_ = bf16[2,1,64,1536]{3,2,1,0:T(8,128)(2,1)} collective-permute-done((bf16[2,1,64,1536]{3,2,1,0:T(8,128)(2,1)}, bf16[2,1,64,1536]{3,2,1,0:T(8,128)(2,1)}, u32[]{:S(2)}, u32[]{:S(2)}) %collective-permute-start.21) | collective-permute-done | bytes 393248 | tf_op jit(solution)/shard_map/ppermute | solution.py:67
  100.6 5.5 %collective-permute-done.16.rest_14_ = bf16[2,1,64,1536]{3,2,1,0:T(8,128)(2,1)} collective-permute-done((bf16[2,1,64,1536]{3,2,1,0:T(8,128)(2,1)S(1)}, bf16[2,1,64,1536]{3,2,1,0:T(8,128)(2,1)}, u32[]{:S(2)}, u32[]{:S(2)}) %collective-permute-start.16) | collective-permute-done | bytes 393248 | tf_op jit(solution)/shard_map/ppermute | solution.py:62
  106.1 9.5 %collective-permute-done.23.rest_21_ = bf16[2,1,64,1536]{3,2,1,0:T(8,128)(2,1)} collective-permute-done((bf16[2,1,64,1536]{3,2,1,0:T(8,128)(2,1)}, bf16[2,1,64,1536]{3,2,1,0:T(8,128)(2,1)}, u32[]{:S(2)}, u32[]{:S(2)}) %collective-permute-start.23) | collective-permute-done | bytes 393248 | tf_op jit(solution)/shard_map/ppermute | solution.py:64
  115.5 18.1 %shard_map.100 = bf16[512,1536]{1,0:T(8,128)(2,1)} custom-call(s32[16]{0:T(128)S(1)} %reshape.421.table_ref, bf16[512,1536]{1,0:T(8,128)(2,1)} %bitcast.92, bf16[2,8,64,1536]{3,2,1,0:T(8,128)(2,1)} %copy-done.2, bf16[2,1,64,1536]{3,2,1,0:T(8,128)(2,1)S(1)} %collective-permute-done.rest_0_, bf16[2,1,64,1536]{3,2,1,0:T(8,128)(2,1)S(1)} %collective-permute-done.1.rest_1_, ...), custom_call_target="tpu_custom_call" | custom-call | flops 3221225472 | bytes 9437184 | tf_op jit(solution)/shard_map/pallas_call | solution.py:144
  (44 shorter events, 0.2 us)
Async XLA Ops:
  0.0 15.6 %collective-permute-start.3 = (s32[4]{0:T(128)}, s32[4]{0:T(128)S(1)}, u32[]{:S(2)}, u32[]{:S(2)}) collective-permute-start(s32[4]{0:T(128)} %bitcast.93), channel_id=1, source_target_pairs={{0,2},{2,4},{4,6},{6,8},{8,10},{10,12},{12,14},{1,3},{3,5},{5,7},{... | collective-permute-start | bytes 56 | tf_op jit(solution)/shard_map/ppermute | solution.py:34
  3.4 14.1 %collective-permute-start.2 = (s32[4]{0:T(128)}, s32[4]{0:T(128)S(1)}, u32[]{:S(2)}, u32[]{:S(2)}) collective-permute-start(s32[4]{0:T(128)} %bitcast.94), channel_id=1, source_target_pairs={{2,0},{4,2},{6,4},{8,6},{10,8},{12,10},{14,12},{3,1},{5,3},{7,5},{... | collective-permute-start | bytes 56 | tf_op jit(solution)/shard_map/ppermute | solution.py:34
  8.7 1.9 %copy-start.4 = (bf16[8,1,64,1536]{3,2,1,0:T(8,128)(2,1)S(1)}, bf16[8,1,64,1536]{3,2,1,0:T(8,128)(2,1)}, u32[]{:S(2)}) copy-start(bf16[8,1,64,1536]{3,2,1,0:T(8,128)(2,1)} %param.15) | copy-start | bytes 4718596
  11.2 3.5 %copy-start.2 = (bf16[2,8,64,1536]{3,2,1,0:T(8,128)(2,1)}, bf16[2,8,64,1536]{3,2,1,0:T(8,128)(2,1)S(1)}, u32[]{:S(2)}) copy-start(bf16[2,8,64,1536]{3,2,1,0:T(8,128)(2,1)S(1)} %maximum_bitcast_fusion.own_hbm) | copy-start | bytes 9437188
  12.2 14.6 %collective-permute-start.4 = (bf16[2,1,64,1536]{3,2,1,0:T(8,128)(2,1)}, bf16[2,1,64,1536]{3,2,1,0:T(8,128)(2,1)S(1)}, u32[]{:S(2)}, u32[]{:S(2)}) collective-permute-start(bf16[2,1,64,1536]{3,2,1,0:T(8,128)(2,1)} %get-tuple-element.27), channel_id=1, source_target_pairs={{0,4},{4,8},{8,12},{12,14},{14,10},{10,6},{6,2},{2,0},{1,5},{5,9},... | collective-permute-start | bytes 1179656 | tf_op jit(solution)/shard_map/ppermute | solution.py:67
  13.8 20.8 %collective-permute-start.13 = (bf16[2,1,64,1536]{3,2,1,0:T(8,128)(2,1)}, bf16[2,1,64,1536]{3,2,1,0:T(8,128)(2,1)S(1)}, u32[]{:S(2)}, u32[]{:S(2)}) collective-permute-start(bf16[2,1,64,1536]{3,2,1,0:T(8,128)(2,1)} %get-tuple-element.27), channel_id=1, source_target_pairs={{4,0},{8,4},{12,8},{14,12},{10,14},{6,10},{2,6},{0,2},{5,1},{9,5},... | collective-permute-start | bytes 1179656 | tf_op jit(solution)/shard_map/ppermute | solution.py:70
  14.2 18.3 %collective-permute-start.18 = (bf16[2,1,64,1536]{3,2,1,0:T(8,128)(2,1)S(1)}, bf16[2,1,64,1536]{3,2,1,0:T(8,128)(2,1)}, u32[]{:S(2)}, u32[]{:S(2)}) collective-permute-start(bf16[2,1,64,1536]{3,2,1,0:T(8,128)(2,1)S(1)} %get-tuple-element.26), channel_id=1, source_target_pairs={{4,0},{8,4},{12,8},{14,12},{10,14},{6,10},{2,6},{0,2},{5,1},{9,5},... | collective-permute-start | bytes 1179656 | tf_op jit(solution)/shard_map/ppermute | solution.py:70
  15.6 20.9 %collective-permute-start.17 = (bf16[2,1,64,1536]{3,2,1,0:T(8,128)(2,1)S(1)}, bf16[2,1,64,1536]{3,2,1,0:T(8,128)(2,1)}, u32[]{:S(2)}, u32[]{:S(2)}) collective-permute-start(bf16[2,1,64,1536]{3,2,1,0:T(8,128)(2,1)S(1)} %get-tuple-element.26), channel_id=1, source_target_pairs={{0,4},{4,8},{8,12},{12,14},{14,10},{10,6},{6,2},{2,0},{1,5},{5,9},... | collective-permute-start | bytes 1179656 | tf_op jit(solution)/shard_map/ppermute | solution.py:67
  17.6 23.8 %collective-permute-start = (bf16[2,1,64,1536]{3,2,1,0:T(8,128)(2,1)}, bf16[2,1,64,1536]{3,2,1,0:T(8,128)(2,1)S(1)}, u32[]{:S(2)}, u32[]{:S(2)}) collective-permute-start(bf16[2,1,64,1536]{3,2,1,0:T(8,128)(2,1)} %get-tuple-element.19), channel_id=1, source_target_pairs={{0,1},{2,3},{4,5},{6,7},{8,9},{10,11},{12,13},{14,15},{16,17},{18,... | collective-permute-start | bytes 1179656 | tf_op jit(solution)/shard_map/ppermute | solution.py:34
  25.3 1.3 copy-start.3
  26.8 18.0 %copy-start.5 = (s32[1,1,4]{2,1,0:T(1,128)S(1)}, s32[1,1,4]{2,1,0:T(1,128)}, u32[]{:S(2)}) copy-start(s32[1,1,4]{2,1,0:T(1,128)} %param.18) | copy-start | bytes 52
  26.8 18.1 %copy-start = (s32[8]{0:T(128)S(1)}, s32[8]{0:T(128)}, u32[]{:S(2)}) copy-start(s32[8]{0:T(128)} %constant.96.clone) | copy-start | bytes 100
  26.8 58.9 %copy-start.1 = (s32[7,2]{1,0:T(8,128)S(1)}, s32[7,2]{1,0:T(8,128)}, u32[]{:S(2)}) copy-start(s32[7,2]{1,0:T(8,128)} %constant.97.clone) | copy-start | bytes 172
  26.8 16.0 %collective-permute-start.1 = (bf16[2,1,64,1536]{3,2,1,0:T(8,128)(2,1)}, bf16[2,1,64,1536]{3,2,1,0:T(8,128)(2,1)S(1)}, u32[]{:S(2)}, u32[]{:S(2)}) collective-permute-start(bf16[2,1,64,1536]{3,2,1,0:T(8,128)(2,1)} %get-tuple-element.18), channel_id=1, source_target_pairs={{1,0},{3,2},{5,4},{7,6},{9,8},{11,10},{13,12},{15,14},{17,16},{19,... | collective-permute-start | bytes 1179656 | tf_op jit(solution)/shard_map/ppermute | solution.py:34
  32.5 10.4 %collective-permute-start.7 = (bf16[2,1,64,1536]{3,2,1,0:T(8,128)(2,1)S(1)}, bf16[2,1,64,1536]{3,2,1,0:T(8,128)(2,1)S(1)}, u32[]{:S(2)}, u32[]{:S(2)}) collective-permute-start(bf16[2,1,64,1536]{3,2,1,0:T(8,128)(2,1)S(1)} %collective-permute-done.4.rest_8_), channel_id=1, source_target_pairs={{0,4},{4,8},{8,12},{12,14},{14,10},{10,6},{6,2},{2,0},{1,5},{5,9},... | collective-permute-start | bytes 1179656 | tf_op jit(solution)/shard_map/ppermute | solution.py:67
  34.6 17.2 %collective-permute-start.5 = (bf16[2,1,64,1536]{3,2,0,1:T(8,128)(2,1)}, bf16[2,1,64,1536]{3,2,0,1:T(8,128)(2,1)S(1)}, u32[]{:S(2)}, u32[]{:S(2)}) collective-permute-start(bf16[2,1,64,1536]{3,2,0,1:T(8,128)(2,1)} %get-tuple-element.12), channel_id=1, source_target_pairs={{0,2},{2,4},{4,6},{6,8},{8,10},{10,12},{12,14},{1,3},{3,5},{5,7},{... | collective-permute-start | bytes 1179656 | tf_op jit(solution)/shard_map/ppermute | solution.py:34
  36.5 18.3 %collective-permute-start.6 = (bf16[2,1,64,1536]{3,2,0,1:T(8,128)(2,1)}, bf16[2,1,64,1536]{3,2,0,1:T(8,128)(2,1)S(1)}, u32[]{:S(2)}, u32[]{:S(2)}) collective-permute-start(bf16[2,1,64,1536]{3,2,0,1:T(8,128)(2,1)} %get-tuple-element.13), channel_id=1, source_target_pairs={{2,0},{4,2},{6,4},{8,6},{10,8},{12,10},{14,12},{3,1},{5,3},{7,5},{... | collective-permute-start | bytes 1179656 | tf_op jit(solution)/shard_map/ppermute | solution.py:34
  41.3 19.2 %collective-permute-start.20 = (bf16[2,1,64,1536]{3,2,1,0:T(8,128)(2,1)}, bf16[2,1,64,1536]{3,2,1,0:T(8,128)(2,1)}, u32[]{:S(2)}, u32[]{:S(2)}) collective-permute-start(bf16[2,1,64,1536]{3,2,1,0:T(8,128)(2,1)} %collective-permute-done.18.rest_16_), channel_id=1, source_target_pairs={{4,0},{8,4},{12,8},{14,12},{10,14},{6,10},{2,6},{0,2},{5,1},{9,5},... | collective-permute-start | bytes 1179656 | tf_op jit(solution)/shard_map/ppermute | solution.py:70
  42.8 24.4 %collective-permute-start.14 = (bf16[2,1,64,1536]{3,2,1,0:T(8,128)(2,1)S(1)}, bf16[2,1,64,1536]{3,2,1,0:T(8,128)(2,1)S(1)}, u32[]{:S(2)}, u32[]{:S(2)}) collective-permute-start(bf16[2,1,64,1536]{3,2,1,0:T(8,128)(2,1)S(1)} %collective-permute-done.13.rest_9_), channel_id=1, source_target_pairs={{4,0},{8,4},{12,8},{14,12},{10,14},{6,10},{2,6},{0,2},{5,1},{9,5},... | collective-permute-start | bytes 1179656 | tf_op jit(solution)/shard_map/ppermute | solution.py:70
  42.9 27.1 %collective-permute-start.10 = (bf16[2,1,64,1536]{3,2,1,0:T(8,128)(2,1)S(1)}, bf16[2,1,64,1536]{3,2,1,0:T(8,128)(2,1)S(1)}, u32[]{:S(2)}, u32[]{:S(2)}) collective-permute-start(bf16[2,1,64,1536]{3,2,1,0:T(8,128)(2,1)S(1)} %collective-permute-done.7.rest_10_), channel_id=1, source_target_pairs={{0,4},{4,8},{8,12},{12,14},{14,10},{10,6},{6,2},{2,0},{1,5},{5,9},... | collective-permute-start | bytes 1179656 | tf_op jit(solution)/shard_map/ppermute | solution.py:67
  51.8 36.0 %collective-permute-start.19 = (bf16[2,1,64,1536]{3,2,1,0:T(8,128)(2,1)}, bf16[2,1,64,1536]{3,2,1,0:T(8,128)(2,1)}, u32[]{:S(2)}, u32[]{:S(2)}) collective-permute-start(bf16[2,1,64,1536]{3,2,1,0:T(8,128)(2,1)} %collective-permute-done.17.rest_15_), channel_id=1, source_target_pairs={{0,4},{4,8},{8,12},{12,14},{14,10},{10,6},{6,2},{2,0},{1,5},{5,9},... | collective-permute-start | bytes 1179656 | tf_op jit(solution)/shard_map/ppermute | solution.py:67
  54.8 33.1 %collective-permute-start.8 = (bf16[2,1,64,1536]{3,2,0,1:T(8,128)(2,1)}, bf16[2,1,64,1536]{3,2,0,1:T(8,128)(2,1)}, u32[]{:S(2)}, u32[]{:S(2)}) collective-permute-start(bf16[2,1,64,1536]{3,2,0,1:T(8,128)(2,1)} %get-tuple-element.14), channel_id=1, source_target_pairs={{0,2},{2,4},{4,6},{6,8},{8,10},{10,12},{12,14},{1,3},{3,5},{5,7},{... | collective-permute-start | bytes 1179656 | tf_op jit(solution)/shard_map/ppermute | solution.py:34
  60.5 28.8 %collective-permute-start.9 = (bf16[2,1,64,1536]{3,2,0,1:T(8,128)(2,1)}, bf16[2,1,64,1536]{3,2,0,1:T(8,128)(2,1)}, u32[]{:S(2)}, u32[]{:S(2)}) collective-permute-start(bf16[2,1,64,1536]{3,2,0,1:T(8,128)(2,1)} %get-tuple-element.15), channel_id=1, source_target_pairs={{2,0},{4,2},{6,4},{8,6},{10,8},{12,10},{14,12},{3,1},{5,3},{7,5},{... | collective-permute-start | bytes 1179656 | tf_op jit(solution)/shard_map/ppermute | solution.py:34
  67.2 23.7 %collective-permute-start.22 = (bf16[2,1,64,1536]{3,2,1,0:T(8,128)(2,1)}, bf16[2,1,64,1536]{3,2,1,0:T(8,128)(2,1)}, u32[]{:S(2)}, u32[]{:S(2)}) collective-permute-start(bf16[2,1,64,1536]{3,2,1,0:T(8,128)(2,1)} %collective-permute-done.20.rest_18_), channel_id=1, source_target_pairs={{4,0},{8,4},{12,8},{14,12},{10,14},{6,10},{2,6},{0,2},{5,1},{9,5},... | collective-permute-start | bytes 1179656 | tf_op jit(solution)/shard_map/ppermute | solution.py:70
  70.0 28.6 %collective-permute-start.15 = (bf16[2,1,64,1536]{3,2,1,0:T(8,128)(2,1)S(1)}, bf16[2,1,64,1536]{3,2,1,0:T(8,128)(2,1)}, u32[]{:S(2)}, u32[]{:S(2)}) collective-permute-start(bf16[2,1,64,1536]{3,2,1,0:T(8,128)(2,1)S(1)} %collective-permute-done.14.rest_11_), channel_id=1, source_target_pairs={{4,0},{8,4},{12,8},{14,12},{10,14},{6,10},{2,6},{0,2},{5,1},{9,5},... | collective-permute-start | bytes 1179656 | tf_op jit(solution)/shard_map/ppermute | solution.py:70
  87.8 12.8 %collective-permute-start.21 = (bf16[2,1,64,1536]{3,2,1,0:T(8,128)(2,1)}, bf16[2,1,64,1536]{3,2,1,0:T(8,128)(2,1)}, u32[]{:S(2)}, u32[]{:S(2)}) collective-permute-start(bf16[2,1,64,1536]{3,2,1,0:T(8,128)(2,1)} %collective-permute-done.19.rest_17_), channel_id=1, source_target_pairs={{0,4},{4,8},{8,12},{12,14},{14,10},{10,6},{6,2},{2,0},{1,5},{5,9},... | collective-permute-start | bytes 1179656 | tf_op jit(solution)/shard_map/ppermute | solution.py:67
  87.9 12.7 %collective-permute-start.11 = (bf16[2,1,64,1536]{3,2,0,1:T(8,128)(2,1)}, bf16[2,1,64,1536]{3,2,0,1:T(8,128)(2,1)}, u32[]{:S(2)}, u32[]{:S(2)}) collective-permute-start(bf16[2,1,64,1536]{3,2,0,1:T(8,128)(2,1)} %get-tuple-element.16), channel_id=1, source_target_pairs={{12,14},{13,15},{28,30},{29,31}} | collective-permute-start | bytes 1179656 | tf_op jit(solution)/shard_map/ppermute | solution.py:215
  89.3 11.3 %collective-permute-start.12 = (bf16[2,1,64,1536]{3,2,0,1:T(8,128)(2,1)}, bf16[2,1,64,1536]{3,2,0,1:T(8,128)(2,1)}, u32[]{:S(2)}, u32[]{:S(2)}) collective-permute-start(bf16[2,1,64,1536]{3,2,0,1:T(8,128)(2,1)} %get-tuple-element.17), channel_id=1, source_target_pairs={{2,0},{3,1},{18,16},{19,17}} | collective-permute-start | bytes 1179656 | tf_op jit(solution)/shard_map/ppermute | solution.py:216
  90.9 15.2 %collective-permute-start.16 = (bf16[2,1,64,1536]{3,2,1,0:T(8,128)(2,1)S(1)}, bf16[2,1,64,1536]{3,2,1,0:T(8,128)(2,1)}, u32[]{:S(2)}, u32[]{:S(2)}) collective-permute-start(bf16[2,1,64,1536]{3,2,1,0:T(8,128)(2,1)S(1)} %collective-permute-done.10.rest_12_), channel_id=1, source_target_pairs={{0,4},{4,8},{8,12},{12,14},{14,10},{10,6},{6,2},{2,0},{1,5},{5,9},... | collective-permute-start | bytes 1179656 | tf_op jit(solution)/shard_map/ppermute | solution.py:62
  98.6 17.0 %collective-permute-start.23 = (bf16[2,1,64,1536]{3,2,1,0:T(8,128)(2,1)}, bf16[2,1,64,1536]{3,2,1,0:T(8,128)(2,1)}, u32[]{:S(2)}, u32[]{:S(2)}) collective-permute-start(bf16[2,1,64,1536]{3,2,1,0:T(8,128)(2,1)} %collective-permute-done.22.rest_20_), channel_id=1, source_target_pairs={{4,0},{8,4},{12,8},{14,12},{10,14},{6,10},{2,6},{0,2},{5,1},{9,5},... | collective-permute-start | bytes 1179656 | tf_op jit(solution)/shard_map/ppermute | solution.py:64

commit v16 on v12

--- a/solution.py
+++ b/solution.py
@@ -112,11 +112,15 @@
 
     key_count = k_vmem.shape[0] * block_length
 
+    token_count = q_vmem.shape[0]
+    part = token_count // 2 if token_count % 32 == 0 else token_count
     for h in range(heads):
-        lanes = pl.ds(h * HEAD_DIM, HEAD_DIM)
-        q = q_vmem[:, lanes]
-        k = k_vmem[:, :, lanes].reshape(key_count, HEAD_DIM)
-        v = v_vmem[:, :, lanes].reshape(key_count, HEAD_DIM)
+      lanes = pl.ds(h * HEAD_DIM, HEAD_DIM)
+      k = k_vmem[:, :, lanes].reshape(key_count, HEAD_DIM)
+      v = v_vmem[:, :, lanes].reshape(key_count, HEAD_DIM)
+      for first in range(0, token_count, part):
+        rows = pl.ds(first, part)
+        q = q_vmem[rows, lanes]
         scores = lax.dot_general(
             q, k, (((1,), (1,)), ((), ())), preferred_element_type=jnp.float32
         ) * HEAD_DIM ** (-0.5)
@@ -125,7 +129,7 @@
         row_total = jnp.sum(weights, axis=1, keepdims=True)
         rounded = weights.astype(jnp.bfloat16)
         blended = jnp.dot(rounded, v, preferred_element_type=jnp.float32)
-        o_ref[:, lanes] = (blended / row_total).astype(o_ref.dtype)
+        o_ref[rows, lanes] = (blended / row_total).astype(o_ref.dtype)
 
 
 def gather_attend(query_rows, own, cycle_list_sources, far_list_sources, table):

time: 131 us -> 134 us (1.023)
  the two profiles are of different devices: /device:TPU:24 before, /device:TPU:26 now
where the time goes in v16:
time: 134 us
  waiting for transfers between devices  51.3 us (38%)
  starting transfers between devices  39.8 us (30%)
  Pallas kernels  18 us (13%)
  local copies, waits for them, and re-layouts  13.4 us (10%)
  other arithmetic  10.9 us (8%)
    ppermute x6, waiting for transfers between devices, ring_gather(): behind = lax.ppermute(behind, 'col', backward)  35.5 us
    ppermute x8, starting transfers between devices, shift(): return lax.ppermute(x, axis, pairs)  20.9 us
    pallas_call x1, Pallas kernels, gather_attend(): pl.pallas_call(kernel, out_shape=jax.ShapeDtypeStruct((token_count, width...  18 us
    ppermute x6, starting transfers between devices, ring_gather(): ahead = lax.ppermute(ahead, 'col', forward)  7.93 us
    ppermute x1, waiting for transfers between devices, ring_gather(): arrays.append(lax.ppermute(ahead, 'col', forward))  6.95 us
    ppermute x6, starting transfers between devices, ring_gather(): behind = lax.ppermute(behind, 'col', backward)  4.9 us
    ppermute x8, waiting for transfers between devices, shift(): return lax.ppermute(x, axis, pairs)  4.77 us
    ppermute x1, starting transfers between devices, per_device(): cycle_sources.append(lax.ppermute(to_r, 'col', [(last - 1, last)]))  4.65 us
  transfers between devices with their start and end apart: 24, of which 10 were waited for; matrix products, arithmetic and copies ran while one was open for 17% of the time, Pallas kernels for 0%

profile of v16, /device:TPU:26, one launch (start us, length us, event | category | flops | bytes accessed | tf_op | source)
XLA Modules:
  0.0 133.9 jit_solution(408367829625856593)
XLA Ops:
  0.0 3.4 %collective-permute-start.3 = (s32[4]{0:T(128)}, s32[4]{0:T(128)S(1)}, u32[]{:S(2)}, u32[]{:S(2)}) collective-permute-start(s32[4]{0:T(128)} %bitcast.93), channel_id=1, source_target_pairs={{0,2},{2,4},{4,6},{6,8},{8,10},{10,12},{12,14},{1,3},{3,5},{5,7},{... | collective-permute-start | bytes 56 | tf_op jit(solution)/shard_map/ppermute | solution.py:34
  3.4 3.3 %collective-permute-start.2 = (s32[4]{0:T(128)}, s32[4]{0:T(128)S(1)}, u32[]{:S(2)}, u32[]{:S(2)}) collective-permute-start(s32[4]{0:T(128)} %bitcast.94), channel_id=1, source_target_pairs={{2,0},{4,2},{6,4},{8,6},{10,8},{12,10},{14,12},{3,1},{5,3},{7,5},{... | collective-permute-start | bytes 56 | tf_op jit(solution)/shard_map/ppermute | solution.py:34
  6.8 1.0 exponential_bitcast_fusion.1
  7.7 1.0 exponential_bitcast_fusion
  8.7 1.8 %fusion.1 = bf16[8,1,64,1536]{3,2,0,1:T(8,128)(2,1)S(1)} fusion(bf16[8,1,64,1536]{3,2,1,0:T(8,128)(2,1)} %param.13, f32[8,2,1536]{2,1,0:T(2,128)S(1)} %exponential_bitcast_fusion.1), kind=kLoop, calls=%fused_computation.9 | loop fusion | flops 2359296 | bytes 3244032 | tf_op jit(solution)/shard_map/convert_element_type | solution.py:24
  10.5 0.1 copy-done.4
  10.6 0.3 fusion
  10.9 0.3 maximum_bitcast_fusion.own_hbm
  11.2 0.1 slice.37
  11.3 0.9 fusion.19
  12.2 0.6 collective-permute-start.4
  12.8 1.4 %collective-permute-start.13 = (bf16[2,1,64,1536]{3,2,1,0:T(8,128)(2,1)}, bf16[2,1,64,1536]{3,2,1,0:T(8,128)(2,1)S(1)}, u32[]{:S(2)}, u32[]{:S(2)}) collective-permute-start(bf16[2,1,64,1536]{3,2,1,0:T(8,128)(2,1)} %get-tuple-element.27), channel_id=1, source_target_pairs={{4,0},{8,4},{12,8},{14,12},{10,14},{6,10},{2,6},{0,2},{5,1},{9,5},... | collective-permute-start | bytes 1179656 | tf_op jit(solution)/shard_map/ppermute | solution.py:70
  14.2 0.4 collective-permute-start.18
  14.7 1.0 fusion.16
  15.6 1.6 %collective-permute-start.17 = (bf16[2,1,64,1536]{3,2,1,0:T(8,128)(2,1)S(1)}, bf16[2,1,64,1536]{3,2,1,0:T(8,128)(2,1)}, u32[]{:S(2)}, u32[]{:S(2)}) collective-permute-start(bf16[2,1,64,1536]{3,2,1,0:T(8,128)(2,1)S(1)} %get-tuple-element.26), channel_id=1, source_target_pairs={{0,4},{4,8},{8,12},{12,14},{14,10},{10,6},{6,2},{2,0},{1,5},{5,9},... | collective-permute-start | bytes 1179656 | tf_op jit(solution)/shard_map/ppermute | solution.py:67
  17.2 0.2 reduce-window.37
  17.4 0.1 select_reduce_fusion
  17.6 1.3 collective-permute-start
  18.9 0.2 reduce-window.36
  19.1 0.1 select_reduce_fusion.1
  19.2 2.5 %gather_fusion.4 = bf16[3,2,64,1536]{3,2,1,0:T(8,128)(2,1)S(1)} fusion(bf16[2,8,64,1536]{3,2,1,0:T(8,128)(2,1)} %copy-done.2, s32[1024]{0:T(1024)S(1)} %pad_clamp_fusion), kind=kCustom, calls=%fused_computation.1.clone | custom fusion | bytes 2359308 | tf_op jit(solution)/shard_map/jit(_take)/gather | solution.py:205
  21.8 3.6 %gather_fusion.3 = bf16[3,2,64,1536]{3,2,1,0:T(8,128)(2,1)} fusion(bf16[2,8,64,1536]{3,2,1,0:T(8,128)(2,1)} %copy-done.2, s32[1024]{0:T(1024)S(1)} %pad_clamp_fusion.1), kind=kCustom, calls=%fused_computation.clone | custom fusion | bytes 2359308 | tf_op jit(solution)/shard_map/jit(_take)/gather | solution.py:204
  25.3 0.2 select_bitcast_fusion
  25.5 1.1 copy-done.3
  26.6 0.2 select_bitcast_fusion.1
  26.8 0.0 copy-start
  26.8 1.4 %collective-permute-start.1 = (bf16[2,1,64,1536]{3,2,1,0:T(8,128)(2,1)}, bf16[2,1,64,1536]{3,2,1,0:T(8,128)(2,1)S(1)}, u32[]{:S(2)}, u32[]{:S(2)}) collective-permute-start(bf16[2,1,64,1536]{3,2,1,0:T(8,128)(2,1)} %get-tuple-element.18), channel_id=1, source_target_pairs={{1,0},{3,2},{5,4},{7,6},{9,8},{11,10},{13,12},{15,14},{17,16},{19,... | collective-permute-start | bytes 1179656 | tf_op jit(solution)/shard_map/ppermute | solution.py:34
  28.3 3.3 %collective-permute-done.18.rest_16_ = bf16[2,1,64,1536]{3,2,1,0:T(8,128)(2,1)} collective-permute-done((bf16[2,1,64,1536]{3,2,1,0:T(8,128)(2,1)S(1)}, bf16[2,1,64,1536]{3,2,1,0:T(8,128)(2,1)}, u32[]{:S(2)}, u32[]{:S(2)}) %collective-permute-start.18) | collective-permute-done | bytes 393248 | tf_op jit(solution)/shard_map/ppermute | solution.py:70
  31.6 0.5 collective-permute-start.7
  32.0 1.4 %fusion.17 = (bf16[2,1,64,1536]{3,2,0,1:T(8,128)(2,1)}, bf16[2,1,64,1536]{3,2,0,1:T(8,128)(2,1)}, bf16[2,1,64,1536]{3,2,0,1:T(8,128)(2,1)}, bf16[2,1,64,1536]{3,...) fusion(bf16[2,3,64,1536]{3,2,0,1:T(8,128)(2,1)S(1)} %select_bitcast_fusion, ...), kind=kLoop, calls=%fused_computation.73 | loop fusion | bytes 4718592 | tf_op jit(solution)/shard_map/slice | solution.py:210
  33.5 2.3 %collective-permute-start.5 = (bf16[2,1,64,1536]{3,2,0,1:T(8,128)(2,1)}, bf16[2,1,64,1536]{3,2,0,1:T(8,128)(2,1)S(1)}, u32[]{:S(2)}, u32[]{:S(2)}) collective-permute-start(bf16[2,1,64,1536]{3,2,0,1:T(8,128)(2,1)} %get-tuple-element.12), channel_id=1, source_target_pairs={{0,2},{2,4},{4,6},{6,8},{8,10},{10,12},{12,14},{1,3},{3,5},{5,7},{... | collective-permute-start | bytes 1179656 | tf_op jit(solution)/shard_map/ppermute | solution.py:34
  35.8 4.4 %collective-permute-start.6 = (bf16[2,1,64,1536]{3,2,0,1:T(8,128)(2,1)}, bf16[2,1,64,1536]{3,2,0,1:T(8,128)(2,1)S(1)}, u32[]{:S(2)}, u32[]{:S(2)}) collective-permute-start(bf16[2,1,64,1536]{3,2,0,1:T(8,128)(2,1)} %get-tuple-element.13), channel_id=1, source_target_pairs={{2,0},{4,2},{6,4},{8,6},{10,8},{12,10},{14,12},{3,1},{5,3},{7,5},{... | collective-permute-start | bytes 1179656 | tf_op jit(solution)/shard_map/ppermute | solution.py:34
  40.2 1.6 %collective-permute-start.20 = (bf16[2,1,64,1536]{3,2,1,0:T(8,128)(2,1)}, bf16[2,1,64,1536]{3,2,1,0:T(8,128)(2,1)}, u32[]{:S(2)}, u32[]{:S(2)}) collective-permute-start(bf16[2,1,64,1536]{3,2,1,0:T(8,128)(2,1)} %collective-permute-done.18.rest_16_), channel_id=1, source_target_pairs={{4,0},{8,4},{12,8},{14,12},{10,14},{6,10},{2,6},{0,2},{5,1},{9,5},... | collective-permute-start | bytes 1179656 | tf_op jit(solution)/shard_map/ppermute | solution.py:70
  41.8 1.4 %collective-permute-start.14 = (bf16[2,1,64,1536]{3,2,1,0:T(8,128)(2,1)S(1)}, bf16[2,1,64,1536]{3,2,1,0:T(8,128)(2,1)S(1)}, u32[]{:S(2)}, u32[]{:S(2)}) collective-permute-start(bf16[2,1,64,1536]{3,2,1,0:T(8,128)(2,1)S(1)} %collective-permute-done.13.rest_9_), channel_id=1, source_target_pairs={{4,0},{8,4},{12,8},{14,12},{10,14},{6,10},{2,6},{0,2},{5,1},{9,5},... | collective-permute-start | bytes 1179656 | tf_op jit(solution)/shard_map/ppermute | solution.py:70
  43.3 0.8 collective-permute-start.10
  44.1 0.7 dynamic_slice.3
  44.8 0.6 gather_fusion
  45.4 1.2 fusion.6
  46.6 3.5 %collective-permute-done.5 = bf16[2,1,64,1536]{3,2,0,1:T(8,128)(2,1)S(1)} collective-permute-done((bf16[2,1,64,1536]{3,2,0,1:T(8,128)(2,1)}, bf16[2,1,64,1536]{3,2,0,1:T(8,128)(2,1)S(1)}, u32[]{:S(2)}, u32[]{:S(2)}) %collective-permute-start.5) | collective-permute-done | bytes 393248 | tf_op jit(solution)/shard_map/ppermute | solution.py:34
  50.1 2.4 %collective-permute-start.19 = (bf16[2,1,64,1536]{3,2,1,0:T(8,128)(2,1)}, bf16[2,1,64,1536]{3,2,1,0:T(8,128)(2,1)}, u32[]{:S(2)}, u32[]{:S(2)}) collective-permute-start(bf16[2,1,64,1536]{3,2,1,0:T(8,128)(2,1)} %collective-permute-done.17.rest_15_), channel_id=1, source_target_pairs={{0,4},{4,8},{8,12},{12,14},{14,10},{10,6},{6,2},{2,0},{1,5},{5,9},... | collective-permute-start | bytes 1179656 | tf_op jit(solution)/shard_map/ppermute | solution.py:67
  52.5 1.3 collective-permute-done.6
  53.8 2.8 %collective-permute-start.8 = (bf16[2,1,64,1536]{3,2,0,1:T(8,128)(2,1)}, bf16[2,1,64,1536]{3,2,0,1:T(8,128)(2,1)}, u32[]{:S(2)}, u32[]{:S(2)}) collective-permute-start(bf16[2,1,64,1536]{3,2,0,1:T(8,128)(2,1)} %get-tuple-element.14), channel_id=1, source_target_pairs={{0,2},{2,4},{4,6},{6,8},{8,10},{10,12},{12,14},{1,3},{3,5},{5,7},{... | collective-permute-start | bytes 1179656 | tf_op jit(solution)/shard_map/ppermute | solution.py:34
  56.6 8.6 %collective-permute-done.20.rest_18_ = bf16[2,1,64,1536]{3,2,1,0:T(8,128)(2,1)} collective-permute-done((bf16[2,1,64,1536]{3,2,1,0:T(8,128)(2,1)}, bf16[2,1,64,1536]{3,2,1,0:T(8,128)(2,1)}, u32[]{:S(2)}, u32[]{:S(2)}) %collective-permute-start.20) | collective-permute-done | bytes 393248 | tf_op jit(solution)/shard_map/ppermute | solution.py:70
  65.1 1.9 %collective-permute-start.9 = (bf16[2,1,64,1536]{3,2,0,1:T(8,128)(2,1)}, bf16[2,1,64,1536]{3,2,0,1:T(8,128)(2,1)}, u32[]{:S(2)}, u32[]{:S(2)}) collective-permute-start(bf16[2,1,64,1536]{3,2,0,1:T(8,128)(2,1)} %get-tuple-element.15), channel_id=1, source_target_pairs={{2,0},{4,2},{6,4},{8,6},{10,8},{12,10},{14,12},{3,1},{5,3},{7,5},{... | collective-permute-start | bytes 1179656 | tf_op jit(solution)/shard_map/ppermute | solution.py:34
  67.0 12.0 %collective-permute-done.14.rest_11_ = bf16[2,1,64,1536]{3,2,1,0:T(8,128)(2,1)S(1)} collective-permute-done((bf16[2,1,64,1536]{3,2,1,0:T(8,128)(2,1)S(1)}, bf16[2,1,64,1536]{3,2,1,0:T(8,128)(2,1)S(1)}, u32[]{:S(2)}, u32[]{:S(2)}) %collective-permute-start.14) | collective-permute-done | bytes 393248 | tf_op jit(solution)/shard_map/ppermute | solution.py:70
  79.1 1.3 %fusion.15 = s32[4]{0:T(128)S(1)} fusion(s32[4]{0:T(128)S(1)} %gather_fusion, s32[]{:T(128)} %bitcast.5, s32[1,1,4]{2,1,0:T(1,128)} %param.18), kind=kLoop, calls=%fused_computation.68 | loop fusion | flops 140 | bytes 52 | tf_op jit(solution)/shard_map/concatenate | solution.py:230
  80.4 1.4 %reduce-window.34 = s32[4,1]{0,1:T(1,128)} reduce-window(s32[4,1]{0,1:T(1,128)} %get-tuple-element.32, s32[]{:T(128)} %constant.98.clone), window={size=4x1 pad=3_0x0_0}, to_apply=%region_0.1 | reduce-window | flops 12 | bytes 36 | tf_op jit(solution)/shard_map/reduce-window.14
  81.8 0.7 reduce-window.35
  82.6 0.6 gather_fusion.1
  83.2 0.6 gather_fusion.2
  83.8 0.1 pad_bitcast_fusion
  83.9 0.7 compare_select_fusion.10
  84.6 2.1 %collective-permute-start.21 = (bf16[2,1,64,1536]{3,2,1,0:T(8,128)(2,1)}, bf16[2,1,64,1536]{3,2,1,0:T(8,128)(2,1)}, u32[]{:S(2)}, u32[]{:S(2)}) collective-permute-start(bf16[2,1,64,1536]{3,2,1,0:T(8,128)(2,1)} %collective-permute-done.19.rest_17_), channel_id=1, source_target_pairs={{0,4},{4,8},{8,12},{12,14},{14,10},{10,6},{6,2},{2,0},{1,5},{5,9},... | collective-permute-start | bytes 1179656 | tf_op jit(solution)/shard_map/ppermute | solution.py:67
  86.7 4.7 %collective-permute-start.11 = (bf16[2,1,64,1536]{3,2,0,1:T(8,128)(2,1)}, bf16[2,1,64,1536]{3,2,0,1:T(8,128)(2,1)}, u32[]{:S(2)}, u32[]{:S(2)}) collective-permute-start(bf16[2,1,64,1536]{3,2,0,1:T(8,128)(2,1)} %get-tuple-element.16), channel_id=1, source_target_pairs={{12,14},{13,15},{28,30},{29,31}} | collective-permute-start | bytes 1179656 | tf_op jit(solution)/shard_map/ppermute | solution.py:217
  91.4 1.4 %collective-permute-start.12 = (bf16[2,1,64,1536]{3,2,0,1:T(8,128)(2,1)}, bf16[2,1,64,1536]{3,2,0,1:T(8,128)(2,1)}, u32[]{:S(2)}, u32[]{:S(2)}) collective-permute-start(bf16[2,1,64,1536]{3,2,0,1:T(8,128)(2,1)} %get-tuple-element.17), channel_id=1, source_target_pairs={{2,0},{3,1},{18,16},{19,17}} | collective-permute-start | bytes 1179656 | tf_op jit(solution)/shard_map/ppermute | solution.py:218
  92.8 3.2 %collective-permute-done.22.rest_20_ = bf16[2,1,64,1536]{3,2,1,0:T(8,128)(2,1)} collective-permute-done((bf16[2,1,64,1536]{3,2,1,0:T(8,128)(2,1)}, bf16[2,1,64,1536]{3,2,1,0:T(8,128)(2,1)}, u32[]{:S(2)}, u32[]{:S(2)}) %collective-permute-start.22) | collective-permute-done | bytes 393248 | tf_op jit(solution)/shard_map/ppermute | solution.py:70
  96.0 8.3 %collective-permute-done.15.rest_13_ = bf16[2,1,64,1536]{3,2,1,0:T(8,128)(2,1)} collective-permute-done((bf16[2,1,64,1536]{3,2,1,0:T(8,128)(2,1)S(1)}, bf16[2,1,64,1536]{3,2,1,0:T(8,128)(2,1)}, u32[]{:S(2)}, u32[]{:S(2)}) %collective-permute-start.15) | collective-permute-done | bytes 393248 | tf_op jit(solution)/shard_map/ppermute | solution.py:70
  104.4 0.1 add_bitcast_fusion
  104.4 0.1 copy.31
  104.5 0.1 reshape.421.table_ref
  104.6 0.4 collective-permute-done.11
  105.0 7.0 %collective-permute-done.16.rest_14_ = bf16[2,1,64,1536]{3,2,1,0:T(8,128)(2,1)} collective-permute-done((bf16[2,1,64,1536]{3,2,1,0:T(8,128)(2,1)S(1)}, bf16[2,1,64,1536]{3,2,1,0:T(8,128)(2,1)}, u32[]{:S(2)}, u32[]{:S(2)}) %collective-permute-start.16) | collective-permute-done | bytes 393248 | tf_op jit(solution)/shard_map/ppermute | solution.py:62
  111.9 3.8 %collective-permute-done.23.rest_21_ = bf16[2,1,64,1536]{3,2,1,0:T(8,128)(2,1)} collective-permute-done((bf16[2,1,64,1536]{3,2,1,0:T(8,128)(2,1)}, bf16[2,1,64,1536]{3,2,1,0:T(8,128)(2,1)}, u32[]{:S(2)}, u32[]{:S(2)}) %collective-permute-start.23) | collective-permute-done | bytes 393248 | tf_op jit(solution)/shard_map/ppermute | solution.py:64
  115.7 18.0 %shard_map.100 = bf16[512,1536]{1,0:T(8,128)(2,1)} custom-call(s32[16]{0:T(128)S(1)} %reshape.421.table_ref, bf16[512,1536]{1,0:T(8,128)(2,1)} %bitcast.92, bf16[2,8,64,1536]{3,2,1,0:T(8,128)(2,1)} %copy-done.2, bf16[2,1,64,1536]{3,2,1,0:T(8,128)(2,1)S(1)} %collective-permute-done.rest_0_, bf16[2,1,64,1536]{3,2,1,0:T(8,128)(2,1)S(1)} %collective-permute-done.1.rest_1_, ...), custom_call_target="tpu_custom_call" | custom-call | flops 3221225472 | bytes 9437184 | tf_op jit(solution)/shard_map/pallas_call | solution.py:146
  (44 shorter events, 0.2 us)
Async XLA Ops:
  0.0 15.6 %collective-permute-start.3 = (s32[4]{0:T(128)}, s32[4]{0:T(128)S(1)}, u32[]{:S(2)}, u32[]{:S(2)}) collective-permute-start(s32[4]{0:T(128)} %bitcast.93), channel_id=1, source_target_pairs={{0,2},{2,4},{4,6},{6,8},{8,10},{10,12},{12,14},{1,3},{3,5},{5,7},{... | collective-permute-start | bytes 56 | tf_op jit(solution)/shard_map/ppermute | solution.py:34
  3.4 14.1 %collective-permute-start.2 = (s32[4]{0:T(128)}, s32[4]{0:T(128)S(1)}, u32[]{:S(2)}, u32[]{:S(2)}) collective-permute-start(s32[4]{0:T(128)} %bitcast.94), channel_id=1, source_target_pairs={{2,0},{4,2},{6,4},{8,6},{10,8},{12,10},{14,12},{3,1},{5,3},{7,5},{... | collective-permute-start | bytes 56 | tf_op jit(solution)/shard_map/ppermute | solution.py:34
  8.7 1.9 %copy-start.4 = (bf16[8,1,64,1536]{3,2,1,0:T(8,128)(2,1)S(1)}, bf16[8,1,64,1536]{3,2,1,0:T(8,128)(2,1)}, u32[]{:S(2)}) copy-start(bf16[8,1,64,1536]{3,2,1,0:T(8,128)(2,1)} %param.15) | copy-start | bytes 4718596
  11.2 3.5 %copy-start.2 = (bf16[2,8,64,1536]{3,2,1,0:T(8,128)(2,1)}, bf16[2,8,64,1536]{3,2,1,0:T(8,128)(2,1)S(1)}, u32[]{:S(2)}) copy-start(bf16[2,8,64,1536]{3,2,1,0:T(8,128)(2,1)S(1)} %maximum_bitcast_fusion.own_hbm) | copy-start | bytes 9437188
  12.2 14.6 %collective-permute-start.4 = (bf16[2,1,64,1536]{3,2,1,0:T(8,128)(2,1)}, bf16[2,1,64,1536]{3,2,1,0:T(8,128)(2,1)S(1)}, u32[]{:S(2)}, u32[]{:S(2)}) collective-permute-start(bf16[2,1,64,1536]{3,2,1,0:T(8,128)(2,1)} %get-tuple-element.27), channel_id=1, source_target_pairs={{0,4},{4,8},{8,12},{12,14},{14,10},{10,6},{6,2},{2,0},{1,5},{5,9},... | collective-permute-start | bytes 1179656 | tf_op jit(solution)/shard_map/ppermute | solution.py:67
  12.8 20.6 %collective-permute-start.13 = (bf16[2,1,64,1536]{3,2,1,0:T(8,128)(2,1)}, bf16[2,1,64,1536]{3,2,1,0:T(8,128)(2,1)S(1)}, u32[]{:S(2)}, u32[]{:S(2)}) collective-permute-start(bf16[2,1,64,1536]{3,2,1,0:T(8,128)(2,1)} %get-tuple-element.27), channel_id=1, source_target_pairs={{4,0},{8,4},{12,8},{14,12},{10,14},{6,10},{2,6},{0,2},{5,1},{9,5},... | collective-permute-start | bytes 1179656 | tf_op jit(solution)/shard_map/ppermute | solution.py:70
  14.2 17.3 %collective-permute-start.18 = (bf16[2,1,64,1536]{3,2,1,0:T(8,128)(2,1)S(1)}, bf16[2,1,64,1536]{3,2,1,0:T(8,128)(2,1)}, u32[]{:S(2)}, u32[]{:S(2)}) collective-permute-start(bf16[2,1,64,1536]{3,2,1,0:T(8,128)(2,1)S(1)} %get-tuple-element.26), channel_id=1, source_target_pairs={{4,0},{8,4},{12,8},{14,12},{10,14},{6,10},{2,6},{0,2},{5,1},{9,5},... | collective-permute-start | bytes 1179656 | tf_op jit(solution)/shard_map/ppermute | solution.py:70
  15.6 20.2 %collective-permute-start.17 = (bf16[2,1,64,1536]{3,2,1,0:T(8,128)(2,1)S(1)}, bf16[2,1,64,1536]{3,2,1,0:T(8,128)(2,1)}, u32[]{:S(2)}, u32[]{:S(2)}) collective-permute-start(bf16[2,1,64,1536]{3,2,1,0:T(8,128)(2,1)S(1)} %get-tuple-element.26), channel_id=1, source_target_pairs={{0,4},{4,8},{8,12},{12,14},{14,10},{10,6},{6,2},{2,0},{1,5},{5,9},... | collective-permute-start | bytes 1179656 | tf_op jit(solution)/shard_map/ppermute | solution.py:67
  17.6 22.7 %collective-permute-start = (bf16[2,1,64,1536]{3,2,1,0:T(8,128)(2,1)}, bf16[2,1,64,1536]{3,2,1,0:T(8,128)(2,1)S(1)}, u32[]{:S(2)}, u32[]{:S(2)}) collective-permute-start(bf16[2,1,64,1536]{3,2,1,0:T(8,128)(2,1)} %get-tuple-element.19), channel_id=1, source_target_pairs={{0,1},{2,3},{4,5},{6,7},{8,9},{10,11},{12,13},{14,15},{16,17},{18,... | collective-permute-start | bytes 1179656 | tf_op jit(solution)/shard_map/ppermute | solution.py:34
  25.3 1.3 copy-start.3
  26.8 17.3 %copy-start.5 = (s32[1,1,4]{2,1,0:T(1,128)S(1)}, s32[1,1,4]{2,1,0:T(1,128)}, u32[]{:S(2)}) copy-start(s32[1,1,4]{2,1,0:T(1,128)} %param.18) | copy-start | bytes 52
  26.8 17.3 %copy-start = (s32[8]{0:T(128)S(1)}, s32[8]{0:T(128)}, u32[]{:S(2)}) copy-start(s32[8]{0:T(128)} %constant.96.clone) | copy-start | bytes 100
  26.8 55.8 %copy-start.1 = (s32[7,2]{1,0:T(8,128)S(1)}, s32[7,2]{1,0:T(8,128)}, u32[]{:S(2)}) copy-start(s32[7,2]{1,0:T(8,128)} %constant.97.clone) | copy-start | bytes 172
  26.8 15.0 %collective-permute-start.1 = (bf16[2,1,64,1536]{3,2,1,0:T(8,128)(2,1)}, bf16[2,1,64,1536]{3,2,1,0:T(8,128)(2,1)S(1)}, u32[]{:S(2)}, u32[]{:S(2)}) collective-permute-start(bf16[2,1,64,1536]{3,2,1,0:T(8,128)(2,1)} %get-tuple-element.18), channel_id=1, source_target_pairs={{1,0},{3,2},{5,4},{7,6},{9,8},{11,10},{13,12},{15,14},{17,16},{19,... | collective-permute-start | bytes 1179656 | tf_op jit(solution)/shard_map/ppermute | solution.py:34
  31.6 11.7 %collective-permute-start.7 = (bf16[2,1,64,1536]{3,2,1,0:T(8,128)(2,1)S(1)}, bf16[2,1,64,1536]{3,2,1,0:T(8,128)(2,1)S(1)}, u32[]{:S(2)}, u32[]{:S(2)}) collective-permute-start(bf16[2,1,64,1536]{3,2,1,0:T(8,128)(2,1)S(1)} %collective-permute-done.4.rest_8_), channel_id=1, source_target_pairs={{0,4},{4,8},{8,12},{12,14},{14,10},{10,6},{6,2},{2,0},{1,5},{5,9},... | collective-permute-start | bytes 1179656 | tf_op jit(solution)/shard_map/ppermute | solution.py:67
  33.5 16.7 %collective-permute-start.5 = (bf16[2,1,64,1536]{3,2,0,1:T(8,128)(2,1)}, bf16[2,1,64,1536]{3,2,0,1:T(8,128)(2,1)S(1)}, u32[]{:S(2)}, u32[]{:S(2)}) collective-permute-start(bf16[2,1,64,1536]{3,2,0,1:T(8,128)(2,1)} %get-tuple-element.12), channel_id=1, source_target_pairs={{0,2},{2,4},{4,6},{6,8},{8,10},{10,12},{12,14},{1,3},{3,5},{5,7},{... | collective-permute-start | bytes 1179656 | tf_op jit(solution)/shard_map/ppermute | solution.py:34
  35.8 18.0 %collective-permute-start.6 = (bf16[2,1,64,1536]{3,2,0,1:T(8,128)(2,1)}, bf16[2,1,64,1536]{3,2,0,1:T(8,128)(2,1)S(1)}, u32[]{:S(2)}, u32[]{:S(2)}) collective-permute-start(bf16[2,1,64,1536]{3,2,0,1:T(8,128)(2,1)} %get-tuple-element.13), channel_id=1, source_target_pairs={{2,0},{4,2},{6,4},{8,6},{10,8},{12,10},{14,12},{3,1},{5,3},{7,5},{... | collective-permute-start | bytes 1179656 | tf_op jit(solution)/shard_map/ppermute | solution.py:34
  40.2 24.9 %collective-permute-start.20 = (bf16[2,1,64,1536]{3,2,1,0:T(8,128)(2,1)}, bf16[2,1,64,1536]{3,2,1,0:T(8,128)(2,1)}, u32[]{:S(2)}, u32[]{:S(2)}) collective-permute-start(bf16[2,1,64,1536]{3,2,1,0:T(8,128)(2,1)} %collective-permute-done.18.rest_16_), channel_id=1, source_target_pairs={{4,0},{8,4},{12,8},{14,12},{10,14},{6,10},{2,6},{0,2},{5,1},{9,5},... | collective-permute-start | bytes 1179656 | tf_op jit(solution)/shard_map/ppermute | solution.py:70
  41.8 37.2 %collective-permute-start.14 = (bf16[2,1,64,1536]{3,2,1,0:T(8,128)(2,1)S(1)}, bf16[2,1,64,1536]{3,2,1,0:T(8,128)(2,1)S(1)}, u32[]{:S(2)}, u32[]{:S(2)}) collective-permute-start(bf16[2,1,64,1536]{3,2,1,0:T(8,128)(2,1)S(1)} %collective-permute-done.13.rest_9_), channel_id=1, source_target_pairs={{4,0},{8,4},{12,8},{14,12},{10,14},{6,10},{2,6},{0,2},{5,1},{9,5},... | collective-permute-start | bytes 1179656 | tf_op jit(solution)/shard_map/ppermute | solution.py:70
  43.3 35.8 %collective-permute-start.10 = (bf16[2,1,64,1536]{3,2,1,0:T(8,128)(2,1)S(1)}, bf16[2,1,64,1536]{3,2,1,0:T(8,128)(2,1)S(1)}, u32[]{:S(2)}, u32[]{:S(2)}) collective-permute-start(bf16[2,1,64,1536]{3,2,1,0:T(8,128)(2,1)S(1)} %collective-permute-done.7.rest_10_), channel_id=1, source_target_pairs={{0,4},{4,8},{8,12},{12,14},{14,10},{10,6},{6,2},{2,0},{1,5},{5,9},... | collective-permute-start | bytes 1179656 | tf_op jit(solution)/shard_map/ppermute | solution.py:67
  50.1 34.5 %collective-permute-start.19 = (bf16[2,1,64,1536]{3,2,1,0:T(8,128)(2,1)}, bf16[2,1,64,1536]{3,2,1,0:T(8,128)(2,1)}, u32[]{:S(2)}, u32[]{:S(2)}) collective-permute-start(bf16[2,1,64,1536]{3,2,1,0:T(8,128)(2,1)} %collective-permute-done.17.rest_15_), channel_id=1, source_target_pairs={{0,4},{4,8},{8,12},{12,14},{14,10},{10,6},{6,2},{2,0},{1,5},{5,9},... | collective-permute-start | bytes 1179656 | tf_op jit(solution)/shard_map/ppermute | solution.py:67
  53.8 32.9 %collective-permute-start.8 = (bf16[2,1,64,1536]{3,2,0,1:T(8,128)(2,1)}, bf16[2,1,64,1536]{3,2,0,1:T(8,128)(2,1)}, u32[]{:S(2)}, u32[]{:S(2)}) collective-permute-start(bf16[2,1,64,1536]{3,2,0,1:T(8,128)(2,1)} %get-tuple-element.14), channel_id=1, source_target_pairs={{0,2},{2,4},{4,6},{6,8},{8,10},{10,12},{12,14},{1,3},{3,5},{5,7},{... | collective-permute-start | bytes 1179656 | tf_op jit(solution)/shard_map/ppermute | solution.py:34
  65.1 26.2 %collective-permute-start.9 = (bf16[2,1,64,1536]{3,2,0,1:T(8,128)(2,1)}, bf16[2,1,64,1536]{3,2,0,1:T(8,128)(2,1)}, u32[]{:S(2)}, u32[]{:S(2)}) collective-permute-start(bf16[2,1,64,1536]{3,2,0,1:T(8,128)(2,1)} %get-tuple-element.15), channel_id=1, source_target_pairs={{2,0},{4,2},{6,4},{8,6},{10,8},{12,10},{14,12},{3,1},{5,3},{7,5},{... | collective-permute-start | bytes 1179656 | tf_op jit(solution)/shard_map/ppermute | solution.py:34
  79.1 17.0 %collective-permute-start.22 = (bf16[2,1,64,1536]{3,2,1,0:T(8,128)(2,1)}, bf16[2,1,64,1536]{3,2,1,0:T(8,128)(2,1)}, u32[]{:S(2)}, u32[]{:S(2)}) collective-permute-start(bf16[2,1,64,1536]{3,2,1,0:T(8,128)(2,1)} %collective-permute-done.20.rest_18_), channel_id=1, source_target_pairs={{4,0},{8,4},{12,8},{14,12},{10,14},{6,10},{2,6},{0,2},{5,1},{9,5},... | collective-permute-start | bytes 1179656 | tf_op jit(solution)/shard_map/ppermute | solution.py:70
  79.1 25.3 %collective-permute-start.15 = (bf16[2,1,64,1536]{3,2,1,0:T(8,128)(2,1)S(1)}, bf16[2,1,64,1536]{3,2,1,0:T(8,128)(2,1)}, u32[]{:S(2)}, u32[]{:S(2)}) collective-permute-start(bf16[2,1,64,1536]{3,2,1,0:T(8,128)(2,1)S(1)} %collective-permute-done.14.rest_11_), channel_id=1, source_target_pairs={{4,0},{8,4},{12,8},{14,12},{10,14},{6,10},{2,6},{0,2},{5,1},{9,5},... | collective-permute-start | bytes 1179656 | tf_op jit(solution)/shard_map/ppermute | solution.py:70
  84.6 20.0 %collective-permute-start.21 = (bf16[2,1,64,1536]{3,2,1,0:T(8,128)(2,1)}, bf16[2,1,64,1536]{3,2,1,0:T(8,128)(2,1)}, u32[]{:S(2)}, u32[]{:S(2)}) collective-permute-start(bf16[2,1,64,1536]{3,2,1,0:T(8,128)(2,1)} %collective-permute-done.19.rest_17_), channel_id=1, source_target_pairs={{0,4},{4,8},{8,12},{12,14},{14,10},{10,6},{6,2},{2,0},{1,5},{5,9},... | collective-permute-start | bytes 1179656 | tf_op jit(solution)/shard_map/ppermute | solution.py:67
  86.7 18.3 %collective-permute-start.11 = (bf16[2,1,64,1536]{3,2,0,1:T(8,128)(2,1)}, bf16[2,1,64,1536]{3,2,0,1:T(8,128)(2,1)}, u32[]{:S(2)}, u32[]{:S(2)}) collective-permute-start(bf16[2,1,64,1536]{3,2,0,1:T(8,128)(2,1)} %get-tuple-element.16), channel_id=1, source_target_pairs={{12,14},{13,15},{28,30},{29,31}} | collective-permute-start | bytes 1179656 | tf_op jit(solution)/shard_map/ppermute | solution.py:217
  91.4 13.6 %collective-permute-start.12 = (bf16[2,1,64,1536]{3,2,0,1:T(8,128)(2,1)}, bf16[2,1,64,1536]{3,2,0,1:T(8,128)(2,1)}, u32[]{:S(2)}, u32[]{:S(2)}) collective-permute-start(bf16[2,1,64,1536]{3,2,0,1:T(8,128)(2,1)} %get-tuple-element.17), channel_id=1, source_target_pairs={{2,0},{3,1},{18,16},{19,17}} | collective-permute-start | bytes 1179656 | tf_op jit(solution)/shard_map/ppermute | solution.py:218
  96.0 15.9 %collective-permute-start.16 = (bf16[2,1,64,1536]{3,2,1,0:T(8,128)(2,1)S(1)}, bf16[2,1,64,1536]{3,2,1,0:T(8,128)(2,1)}, u32[]{:S(2)}, u32[]{:S(2)}) collective-permute-start(bf16[2,1,64,1536]{3,2,1,0:T(8,128)(2,1)S(1)} %collective-permute-done.10.rest_12_), channel_id=1, source_target_pairs={{0,4},{4,8},{8,12},{12,14},{14,10},{10,6},{6,2},{2,0},{1,5},{5,9},... | collective-permute-start | bytes 1179656 | tf_op jit(solution)/shard_map/ppermute | solution.py:62
  104.3 11.4 %collective-permute-start.23 = (bf16[2,1,64,1536]{3,2,1,0:T(8,128)(2,1)}, bf16[2,1,64,1536]{3,2,1,0:T(8,128)(2,1)}, u32[]{:S(2)}, u32[]{:S(2)}) collective-permute-start(bf16[2,1,64,1536]{3,2,1,0:T(8,128)(2,1)} %collective-permute-done.22.rest_20_), channel_id=1, source_target_pairs={{4,0},{8,4},{12,8},{14,12},{10,14},{6,10},{2,6},{0,2},{5,1},{9,5},... | collective-permute-start | bytes 1179656 | tf_op jit(solution)/shard_map/ppermute | solution.py:64

commit v17 on v12

--- a/solution.py
+++ b/solution.py
@@ -80,7 +80,7 @@
 
 def gather_attention_kernel(cycle_sources, far_sources, table_ref, q_hbm, own_hbm, *rest):
     sources = rest[: cycle_sources + far_sources]
-    o_ref, q_vmem, k_vmem, v_vmem, sems = rest[cycle_sources + far_sources :]
+    o_hbm, o_vmem, q_vmem, k_vmem, v_vmem, sems, out_sems = rest[cycle_sources + far_sources :]
     tile_blocks = own_hbm.shape[1]
     block_length = own_hbm.shape[2]
     extra = table_ref.shape[0] // 2
@@ -112,6 +112,9 @@
 
     key_count = k_vmem.shape[0] * block_length
 
+    groups = out_sems.shape[0]
+    group_heads = heads // groups
+    writes = []
     for h in range(heads):
         lanes = pl.ds(h * HEAD_DIM, HEAD_DIM)
         q = q_vmem[:, lanes]
@@ -125,7 +128,16 @@
         row_total = jnp.sum(weights, axis=1, keepdims=True)
         rounded = weights.astype(jnp.bfloat16)
         blended = jnp.dot(rounded, v, preferred_element_type=jnp.float32)
-        o_ref[:, lanes] = (blended / row_total).astype(o_ref.dtype)
+        o_vmem[:, lanes] = (blended / row_total).astype(o_vmem.dtype)
+        if (h + 1) % group_heads == 0:
+            group = h // group_heads
+            span = pl.ds(group * group_heads * HEAD_DIM, group_heads * HEAD_DIM)
+            writes.append(
+                pltpu.make_async_copy(o_vmem.at[:, span], o_hbm.at[:, span], out_sems.at[group])
+            )
+            writes[-1].start()
+    for w in writes:
+        w.wait()
 
 
 def gather_attend(query_rows, own, cycle_list_sources, far_list_sources, table):
@@ -144,12 +156,14 @@
         out_shape=jax.ShapeDtypeStruct((token_count, width), jnp.bfloat16),
         in_specs=[pl.BlockSpec(memory_space=pltpu.SMEM)]
         + [pl.BlockSpec(memory_space=pl.ANY)] * (2 + n_sources),
-        out_specs=pl.BlockSpec(memory_space=pltpu.VMEM),
+        out_specs=pl.BlockSpec(memory_space=pl.ANY),
         scratch_shapes=[
+            pltpu.VMEM((token_count, width), jnp.bfloat16),
             pltpu.VMEM((token_count, width), jnp.bfloat16),
             pltpu.VMEM((blocks, block_length, width), jnp.bfloat16),
             pltpu.VMEM((blocks, block_length, width), jnp.bfloat16),
             pltpu.SemaphoreType.DMA((2, 2 + extra)),
+            pltpu.SemaphoreType.DMA((3 if heads % 3 == 0 else 1,)),
         ],
         compiler_params=pltpu.CompilerParams(vmem_limit_bytes=48 * 1024 * 1024),
         cost_estimate=pl.CostEstimate(

time: 131 us -> 131 us (level)
  the two profiles are of different devices: /device:TPU:24 before, /device:TPU:19 now
where the time goes in v17:
time: 131 us; the launch traced here: 130 us
  starting transfers between devices  59 us (45%)
  waiting for transfers between devices  31.6 us (24%)
  Pallas kernels  14.8 us (11%)
  local copies, waits for them, and re-layouts  13.4 us (10%)
  other arithmetic  10.9 us (8%)
    ppermute x8, starting transfers between devices, shift(): return lax.ppermute(x, axis, pairs)  24.2 us
    ppermute x6, starting transfers between devices, ring_gather(): ahead = lax.ppermute(ahead, 'col', forward)  15.7 us
    pallas_call x1, Pallas kernels, gather_attend(): pl.pallas_call(kernel, out_shape=jax.ShapeDtypeStruct((token_count, width...  14.8 us
    ppermute x8, waiting for transfers between devices, shift(): return lax.ppermute(x, axis, pairs)  11.1 us
    ppermute x1, waiting for transfers between devices, ring_gather(): arrays.append(lax.ppermute(behind, 'col', backward))  9.91 us
    ppermute x6, starting transfers between devices, ring_gather(): behind = lax.ppermute(behind, 'col', backward)  8.54 us
    ppermute x1, starting transfers between devices, ring_gather(): arrays.append(lax.ppermute(ahead, 'col', forward))  7.7 us
    ppermute x1, waiting for transfers between devices, ring_gather(): arrays.append(lax.ppermute(ahead, 'col', forward))  6.87 us
  transfers between devices with their start and end apart: 24, of which 8 were waited for; matrix products, arithmetic and copies ran while one was open for 18% of the time, Pallas kernels for 0%

profile of v17, /device:TPU:19, one launch (start us, length us, event | category | flops | bytes accessed | tf_op | source)
XLA Modules:
  0.0 130.1 jit_solution(1868745462243597662)
XLA Ops:
  0.0 3.1 %collective-permute-start.3 = (s32[4]{0:T(128)}, s32[4]{0:T(128)S(1)}, u32[]{:S(2)}, u32[]{:S(2)}) collective-permute-start(s32[4]{0:T(128)} %bitcast.93), channel_id=1, source_target_pairs={{0,2},{2,4},{4,6},{6,8},{8,10},{10,12},{12,14},{1,3},{3,5},{5,7},{... | collective-permute-start | bytes 56 | tf_op jit(solution)/shard_map/ppermute | solution.py:34
  3.1 3.0 %collective-permute-start.2 = (s32[4]{0:T(128)}, s32[4]{0:T(128)S(1)}, u32[]{:S(2)}, u32[]{:S(2)}) collective-permute-start(s32[4]{0:T(128)} %bitcast.94), channel_id=1, source_target_pairs={{2,0},{4,2},{6,4},{8,6},{10,8},{12,10},{14,12},{3,1},{5,3},{7,5},{... | collective-permute-start | bytes 56 | tf_op jit(solution)/shard_map/ppermute | solution.py:34
  6.2 1.0 exponential_bitcast_fusion.1
  7.2 1.0 exponential_bitcast_fusion
  8.1 1.8 %fusion.1 = bf16[8,1,64,1536]{3,2,0,1:T(8,128)(2,1)S(1)} fusion(bf16[8,1,64,1536]{3,2,1,0:T(8,128)(2,1)} %param.13, f32[8,2,1536]{2,1,0:T(2,128)S(1)} %exponential_bitcast_fusion.1), kind=kLoop, calls=%fused_computation.9 | loop fusion | flops 2359296 | bytes 3244032 | tf_op jit(solution)/shard_map/convert_element_type | solution.py:24
  10.0 0.1 copy-done.4
  10.0 0.3 fusion
  10.3 0.3 maximum_bitcast_fusion.own_hbm
  10.6 0.1 slice.37
  10.7 0.9 fusion.19
  11.6 1.3 collective-permute-start.4
  12.9 0.2 collective-permute-start.13
  13.1 0.2 collective-permute-start.18
  13.3 1.0 fusion.16
  14.2 1.3 collective-permute-start.17
  15.5 0.2 reduce-window.37
  15.7 0.1 select_reduce_fusion
  15.9 1.3 collective-permute-start
  17.2 0.2 reduce-window.36
  17.4 0.1 select_reduce_fusion.1
  17.5 2.5 %gather_fusion.4 = bf16[3,2,64,1536]{3,2,1,0:T(8,128)(2,1)S(1)} fusion(bf16[2,8,64,1536]{3,2,1,0:T(8,128)(2,1)} %copy-done.2, s32[1024]{0:T(1024)S(1)} %pad_clamp_fusion), kind=kCustom, calls=%fused_computation.1.clone | custom fusion | bytes 2359308 | tf_op jit(solution)/shard_map/jit(_take)/gather | solution.py:215
  20.1 3.6 %gather_fusion.3 = bf16[3,2,64,1536]{3,2,1,0:T(8,128)(2,1)} fusion(bf16[2,8,64,1536]{3,2,1,0:T(8,128)(2,1)} %copy-done.2, s32[1024]{0:T(1024)S(1)} %pad_clamp_fusion.1), kind=kCustom, calls=%fused_computation.clone | custom fusion | bytes 2359308 | tf_op jit(solution)/shard_map/jit(_take)/gather | solution.py:214
  23.6 0.2 select_bitcast_fusion
  23.8 1.1 copy-done.3
  24.9 0.2 select_bitcast_fusion.1
  25.1 0.0 copy-start
  25.1 4.4 %collective-permute-start.1 = (bf16[2,1,64,1536]{3,2,1,0:T(8,128)(2,1)}, bf16[2,1,64,1536]{3,2,1,0:T(8,128)(2,1)S(1)}, u32[]{:S(2)}, u32[]{:S(2)}) collective-permute-start(bf16[2,1,64,1536]{3,2,1,0:T(8,128)(2,1)} %get-tuple-element.18), channel_id=1, source_target_pairs={{1,0},{3,2},{5,4},{7,6},{9,8},{11,10},{13,12},{15,14},{17,16},{19,... | collective-permute-start | bytes 1179656 | tf_op jit(solution)/shard_map/ppermute | solution.py:34
  29.6 1.2 collective-permute-done.18.rest_16_
  30.8 0.3 collective-permute-start.7
  31.1 1.4 %fusion.17 = (bf16[2,1,64,1536]{3,2,0,1:T(8,128)(2,1)}, bf16[2,1,64,1536]{3,2,0,1:T(8,128)(2,1)}, bf16[2,1,64,1536]{3,2,0,1:T(8,128)(2,1)}, bf16[2,1,64,1536]{3,...) fusion(bf16[2,3,64,1536]{3,2,0,1:T(8,128)(2,1)S(1)} %select_bitcast_fusion, ...), kind=kLoop, calls=%fused_computation.73 | loop fusion | bytes 4718592 | tf_op jit(solution)/shard_map/slice | solution.py:220
  32.5 1.9 %collective-permute-start.5 = (bf16[2,1,64,1536]{3,2,0,1:T(8,128)(2,1)}, bf16[2,1,64,1536]{3,2,0,1:T(8,128)(2,1)S(1)}, u32[]{:S(2)}, u32[]{:S(2)}) collective-permute-start(bf16[2,1,64,1536]{3,2,0,1:T(8,128)(2,1)} %get-tuple-element.12), channel_id=1, source_target_pairs={{0,2},{2,4},{4,6},{6,8},{8,10},{10,12},{12,14},{1,3},{3,5},{5,7},{... | collective-permute-start | bytes 1179656 | tf_op jit(solution)/shard_map/ppermute | solution.py:34
  34.5 4.3 %collective-permute-start.6 = (bf16[2,1,64,1536]{3,2,0,1:T(8,128)(2,1)}, bf16[2,1,64,1536]{3,2,0,1:T(8,128)(2,1)S(1)}, u32[]{:S(2)}, u32[]{:S(2)}) collective-permute-start(bf16[2,1,64,1536]{3,2,0,1:T(8,128)(2,1)} %get-tuple-element.13), channel_id=1, source_target_pairs={{2,0},{4,2},{6,4},{8,6},{10,8},{12,10},{14,12},{3,1},{5,3},{7,5},{... | collective-permute-start | bytes 1179656 | tf_op jit(solution)/shard_map/ppermute | solution.py:34
  38.7 1.2 collective-permute-start.20
  39.9 0.1 collective-permute-start.14
  40.0 1.4 %collective-permute-start.10 = (bf16[2,1,64,1536]{3,2,1,0:T(8,128)(2,1)S(1)}, bf16[2,1,64,1536]{3,2,1,0:T(8,128)(2,1)S(1)}, u32[]{:S(2)}, u32[]{:S(2)}) collective-permute-start(bf16[2,1,64,1536]{3,2,1,0:T(8,128)(2,1)S(1)} %collective-permute-done.7.rest_10_), channel_id=1, source_target_pairs={{0,4},{4,8},{8,12},{12,14},{14,10},{10,6},{6,2},{2,0},{1,5},{5,9},... | collective-permute-start | bytes 1179656 | tf_op jit(solution)/shard_map/ppermute | solution.py:67
  41.4 0.7 dynamic_slice.3
  42.1 0.6 gather_fusion
  42.7 1.2 fusion.6
  44.0 2.4 %collective-permute-done.5 = bf16[2,1,64,1536]{3,2,0,1:T(8,128)(2,1)S(1)} collective-permute-done((bf16[2,1,64,1536]{3,2,0,1:T(8,128)(2,1)}, bf16[2,1,64,1536]{3,2,0,1:T(8,128)(2,1)S(1)}, u32[]{:S(2)}, u32[]{:S(2)}) %collective-permute-start.5) | collective-permute-done | bytes 393248 | tf_op jit(solution)/shard_map/ppermute | solution.py:34
  46.4 8.7 %collective-permute-done.6 = bf16[2,1,64,1536]{3,2,0,1:T(8,128)(2,1)S(1)} collective-permute-done((bf16[2,1,64,1536]{3,2,0,1:T(8,128)(2,1)}, bf16[2,1,64,1536]{3,2,0,1:T(8,128)(2,1)S(1)}, u32[]{:S(2)}, u32[]{:S(2)}) %collective-permute-start.6) | collective-permute-done | bytes 393248 | tf_op jit(solution)/shard_map/ppermute | solution.py:34
  55.1 1.9 %collective-permute-start.8 = (bf16[2,1,64,1536]{3,2,0,1:T(8,128)(2,1)}, bf16[2,1,64,1536]{3,2,0,1:T(8,128)(2,1)}, u32[]{:S(2)}, u32[]{:S(2)}) collective-permute-start(bf16[2,1,64,1536]{3,2,0,1:T(8,128)(2,1)} %get-tuple-element.14), channel_id=1, source_target_pairs={{0,2},{2,4},{4,6},{6,8},{8,10},{10,12},{12,14},{1,3},{3,5},{5,7},{... | collective-permute-start | bytes 1179656 | tf_op jit(solution)/shard_map/ppermute | solution.py:34
  57.0 4.3 %collective-permute-start.9 = (bf16[2,1,64,1536]{3,2,0,1:T(8,128)(2,1)}, bf16[2,1,64,1536]{3,2,0,1:T(8,128)(2,1)}, u32[]{:S(2)}, u32[]{:S(2)}) collective-permute-start(bf16[2,1,64,1536]{3,2,0,1:T(8,128)(2,1)} %get-tuple-element.15), channel_id=1, source_target_pairs={{2,0},{4,2},{6,4},{8,6},{10,8},{12,10},{14,12},{3,1},{5,3},{7,5},{... | collective-permute-start | bytes 1179656 | tf_op jit(solution)/shard_map/ppermute | solution.py:34
  61.3 0.9 collective-permute-done.14.rest_11_
  62.2 1.3 collective-permute-start.22
  63.5 5.7 %collective-permute-start.15 = (bf16[2,1,64,1536]{3,2,1,0:T(8,128)(2,1)S(1)}, bf16[2,1,64,1536]{3,2,1,0:T(8,128)(2,1)}, u32[]{:S(2)}, u32[]{:S(2)}) collective-permute-start(bf16[2,1,64,1536]{3,2,1,0:T(8,128)(2,1)S(1)} %collective-permute-done.14.rest_11_), channel_id=1, source_target_pairs={{4,0},{8,4},{12,8},{14,12},{10,14},{6,10},{2,6},{0,2},{5,1},{9,5},... | collective-permute-start | bytes 1179656 | tf_op jit(solution)/shard_map/ppermute | solution.py:70
  69.1 1.3 %fusion.15 = s32[4]{0:T(128)S(1)} fusion(s32[4]{0:T(128)S(1)} %gather_fusion, s32[]{:T(128)} %bitcast.5, s32[1,1,4]{2,1,0:T(1,128)} %param.18), kind=kLoop, calls=%fused_computation.68 | loop fusion | flops 140 | bytes 52 | tf_op jit(solution)/shard_map/concatenate | solution.py:240
  70.5 1.4 %reduce-window.34 = s32[4,1]{0,1:T(1,128)} reduce-window(s32[4,1]{0,1:T(1,128)} %get-tuple-element.32, s32[]{:T(128)} %constant.98.clone), window={size=4x1 pad=3_0x0_0}, to_apply=%region_0.1 | reduce-window | flops 12 | bytes 36 | tf_op jit(solution)/shard_map/reduce-window.14
  71.9 0.7 reduce-window.35
  72.6 0.6 gather_fusion.1
  73.3 0.6 gather_fusion.2
  73.9 0.1 pad_bitcast_fusion
  74.0 0.7 compare_select_fusion.10
  74.7 11.4 %collective-permute-start.21 = (bf16[2,1,64,1536]{3,2,1,0:T(8,128)(2,1)}, bf16[2,1,64,1536]{3,2,1,0:T(8,128)(2,1)}, u32[]{:S(2)}, u32[]{:S(2)}) collective-permute-start(bf16[2,1,64,1536]{3,2,1,0:T(8,128)(2,1)} %collective-permute-done.19.rest_17_), channel_id=1, source_target_pairs={{0,4},{4,8},{8,12},{12,14},{14,10},{10,6},{6,2},{2,0},{1,5},{5,9},... | collective-permute-start | bytes 1179656 | tf_op jit(solution)/shard_map/ppermute | solution.py:67
  86.0 1.4 %collective-permute-start.11 = (bf16[2,1,64,1536]{3,2,0,1:T(8,128)(2,1)}, bf16[2,1,64,1536]{3,2,0,1:T(8,128)(2,1)}, u32[]{:S(2)}, u32[]{:S(2)}) collective-permute-start(bf16[2,1,64,1536]{3,2,0,1:T(8,128)(2,1)} %get-tuple-element.16), channel_id=1, source_target_pairs={{12,14},{13,15},{28,30},{29,31}} | collective-permute-start | bytes 1179656 | tf_op jit(solution)/shard_map/ppermute | solution.py:227
  87.5 1.4 %collective-permute-start.12 = (bf16[2,1,64,1536]{3,2,0,1:T(8,128)(2,1)}, bf16[2,1,64,1536]{3,2,0,1:T(8,128)(2,1)}, u32[]{:S(2)}, u32[]{:S(2)}) collective-permute-start(bf16[2,1,64,1536]{3,2,0,1:T(8,128)(2,1)} %get-tuple-element.17), channel_id=1, source_target_pairs={{2,0},{3,1},{18,16},{19,17}} | collective-permute-start | bytes 1179656 | tf_op jit(solution)/shard_map/ppermute | solution.py:228
  88.9 0.8 collective-permute-done.22.rest_20_
  89.7 7.7 %collective-permute-start.16 = (bf16[2,1,64,1536]{3,2,1,0:T(8,128)(2,1)S(1)}, bf16[2,1,64,1536]{3,2,1,0:T(8,128)(2,1)}, u32[]{:S(2)}, u32[]{:S(2)}) collective-permute-start(bf16[2,1,64,1536]{3,2,1,0:T(8,128)(2,1)S(1)} %collective-permute-done.10.rest_12_), channel_id=1, source_target_pairs={{0,4},{4,8},{8,12},{12,14},{14,10},{10,6},{6,2},{2,0},{1,5},{5,9},... | collective-permute-start | bytes 1179656 | tf_op jit(solution)/shard_map/ppermute | solution.py:62
  97.4 0.7 collective-permute-done.15.rest_13_
  98.1 0.1 add_bitcast_fusion
  98.2 0.1 copy.31
  98.3 0.1 reshape.421.table_ref
  98.4 6.9 %collective-permute-done.16.rest_14_ = bf16[2,1,64,1536]{3,2,1,0:T(8,128)(2,1)} collective-permute-done((bf16[2,1,64,1536]{3,2,1,0:T(8,128)(2,1)S(1)}, bf16[2,1,64,1536]{3,2,1,0:T(8,128)(2,1)}, u32[]{:S(2)}, u32[]{:S(2)}) %collective-permute-start.16) | collective-permute-done | bytes 393248 | tf_op jit(solution)/shard_map/ppermute | solution.py:62
  105.3 9.9 %collective-permute-done.23.rest_21_ = bf16[2,1,64,1536]{3,2,1,0:T(8,128)(2,1)} collective-permute-done((bf16[2,1,64,1536]{3,2,1,0:T(8,128)(2,1)}, bf16[2,1,64,1536]{3,2,1,0:T(8,128)(2,1)}, u32[]{:S(2)}, u32[]{:S(2)}) %collective-permute-start.23) | collective-permute-done | bytes 393248 | tf_op jit(solution)/shard_map/ppermute | solution.py:64
  115.2 14.8 %shard_map.100 = bf16[512,1536]{1,0:T(8,128)(2,1)} custom-call(s32[16]{0:T(128)S(1)} %reshape.421.table_ref, bf16[512,1536]{1,0:T(8,128)(2,1)} %bitcast.92, bf16[2,8,64,1536]{3,2,1,0:T(8,128)(2,1)} %copy-done.2, bf16[2,1,64,1536]{3,2,1,0:T(8,128)(2,1)S(1)} %collective-permute-done.rest_0_, bf16[2,1,64,1536]{3,2,1,0:T(8,128)(2,1)S(1)} %collective-permute-done.1.rest_1_, ...), custom_call_target="tpu_custom_call" | custom-call | flops 3221225472 | bytes 9437184 | tf_op jit(solution)/shard_map/pallas_call | solution.py:154
  (44 shorter events, 0.2 us)
Async XLA Ops:
  0.0 14.2 %collective-permute-start.3 = (s32[4]{0:T(128)}, s32[4]{0:T(128)S(1)}, u32[]{:S(2)}, u32[]{:S(2)}) collective-permute-start(s32[4]{0:T(128)} %bitcast.93), channel_id=1, source_target_pairs={{0,2},{2,4},{4,6},{6,8},{8,10},{10,12},{12,14},{1,3},{3,5},{5,7},{... | collective-permute-start | bytes 56 | tf_op jit(solution)/shard_map/ppermute | solution.py:34
  3.1 12.7 %collective-permute-start.2 = (s32[4]{0:T(128)}, s32[4]{0:T(128)S(1)}, u32[]{:S(2)}, u32[]{:S(2)}) collective-permute-start(s32[4]{0:T(128)} %bitcast.94), channel_id=1, source_target_pairs={{2,0},{4,2},{6,4},{8,6},{10,8},{12,10},{14,12},{3,1},{5,3},{7,5},{... | collective-permute-start | bytes 56 | tf_op jit(solution)/shard_map/ppermute | solution.py:34
  8.1 1.9 %copy-start.4 = (bf16[8,1,64,1536]{3,2,1,0:T(8,128)(2,1)S(1)}, bf16[8,1,64,1536]{3,2,1,0:T(8,128)(2,1)}, u32[]{:S(2)}) copy-start(bf16[8,1,64,1536]{3,2,1,0:T(8,128)(2,1)} %param.15) | copy-start | bytes 4718596
  10.6 2.6 %copy-start.2 = (bf16[2,8,64,1536]{3,2,1,0:T(8,128)(2,1)}, bf16[2,8,64,1536]{3,2,1,0:T(8,128)(2,1)S(1)}, u32[]{:S(2)}) copy-start(bf16[2,8,64,1536]{3,2,1,0:T(8,128)(2,1)S(1)} %maximum_bitcast_fusion.own_hbm) | copy-start | bytes 9437188
  11.6 13.5 %collective-permute-start.4 = (bf16[2,1,64,1536]{3,2,1,0:T(8,128)(2,1)}, bf16[2,1,64,1536]{3,2,1,0:T(8,128)(2,1)S(1)}, u32[]{:S(2)}, u32[]{:S(2)}) collective-permute-start(bf16[2,1,64,1536]{3,2,1,0:T(8,128)(2,1)} %get-tuple-element.27), channel_id=1, source_target_pairs={{0,4},{4,8},{8,12},{12,14},{14,10},{10,6},{6,2},{2,0},{1,5},{5,9},... | collective-permute-start | bytes 1179656 | tf_op jit(solution)/shard_map/ppermute | solution.py:67
  12.9 19.6 %collective-permute-start.13 = (bf16[2,1,64,1536]{3,2,1,0:T(8,128)(2,1)}, bf16[2,1,64,1536]{3,2,1,0:T(8,128)(2,1)S(1)}, u32[]{:S(2)}, u32[]{:S(2)}) collective-permute-start(bf16[2,1,64,1536]{3,2,1,0:T(8,128)(2,1)} %get-tuple-element.27), channel_id=1, source_target_pairs={{4,0},{8,4},{12,8},{14,12},{10,14},{6,10},{2,6},{0,2},{5,1},{9,5},... | collective-permute-start | bytes 1179656 | tf_op jit(solution)/shard_map/ppermute | solution.py:70
  13.1 17.7 %collective-permute-start.18 = (bf16[2,1,64,1536]{3,2,1,0:T(8,128)(2,1)S(1)}, bf16[2,1,64,1536]{3,2,1,0:T(8,128)(2,1)}, u32[]{:S(2)}, u32[]{:S(2)}) collective-permute-start(bf16[2,1,64,1536]{3,2,1,0:T(8,128)(2,1)S(1)} %get-tuple-element.26), channel_id=1, source_target_pairs={{4,0},{8,4},{12,8},{14,12},{10,14},{6,10},{2,6},{0,2},{5,1},{9,5},... | collective-permute-start | bytes 1179656 | tf_op jit(solution)/shard_map/ppermute | solution.py:70
  14.2 20.2 %collective-permute-start.17 = (bf16[2,1,64,1536]{3,2,1,0:T(8,128)(2,1)S(1)}, bf16[2,1,64,1536]{3,2,1,0:T(8,128)(2,1)}, u32[]{:S(2)}, u32[]{:S(2)}) collective-permute-start(bf16[2,1,64,1536]{3,2,1,0:T(8,128)(2,1)S(1)} %get-tuple-element.26), channel_id=1, source_target_pairs={{0,4},{4,8},{8,12},{12,14},{14,10},{10,6},{6,2},{2,0},{1,5},{5,9},... | collective-permute-start | bytes 1179656 | tf_op jit(solution)/shard_map/ppermute | solution.py:67
  15.9 22.8 %collective-permute-start = (bf16[2,1,64,1536]{3,2,1,0:T(8,128)(2,1)}, bf16[2,1,64,1536]{3,2,1,0:T(8,128)(2,1)S(1)}, u32[]{:S(2)}, u32[]{:S(2)}) collective-permute-start(bf16[2,1,64,1536]{3,2,1,0:T(8,128)(2,1)} %get-tuple-element.19), channel_id=1, source_target_pairs={{0,1},{2,3},{4,5},{6,7},{8,9},{10,11},{12,13},{14,15},{16,17},{18,... | collective-permute-start | bytes 1179656 | tf_op jit(solution)/shard_map/ppermute | solution.py:34
  23.6 1.3 copy-start.3
  25.1 16.3 %copy-start.5 = (s32[1,1,4]{2,1,0:T(1,128)S(1)}, s32[1,1,4]{2,1,0:T(1,128)}, u32[]{:S(2)}) copy-start(s32[1,1,4]{2,1,0:T(1,128)} %param.18) | copy-start | bytes 52
  25.1 16.3 %copy-start = (s32[8]{0:T(128)S(1)}, s32[8]{0:T(128)}, u32[]{:S(2)}) copy-start(s32[8]{0:T(128)} %constant.96.clone) | copy-start | bytes 100
  25.1 47.5 %copy-start.1 = (s32[7,2]{1,0:T(8,128)S(1)}, s32[7,2]{1,0:T(8,128)}, u32[]{:S(2)}) copy-start(s32[7,2]{1,0:T(8,128)} %constant.97.clone) | copy-start | bytes 172
  25.1 14.8 %collective-permute-start.1 = (bf16[2,1,64,1536]{3,2,1,0:T(8,128)(2,1)}, bf16[2,1,64,1536]{3,2,1,0:T(8,128)(2,1)S(1)}, u32[]{:S(2)}, u32[]{:S(2)}) collective-permute-start(bf16[2,1,64,1536]{3,2,1,0:T(8,128)(2,1)} %get-tuple-element.18), channel_id=1, source_target_pairs={{1,0},{3,2},{5,4},{7,6},{9,8},{11,10},{13,12},{15,14},{17,16},{19,... | collective-permute-start | bytes 1179656 | tf_op jit(solution)/shard_map/ppermute | solution.py:34
  30.8 9.2 %collective-permute-start.7 = (bf16[2,1,64,1536]{3,2,1,0:T(8,128)(2,1)S(1)}, bf16[2,1,64,1536]{3,2,1,0:T(8,128)(2,1)S(1)}, u32[]{:S(2)}, u32[]{:S(2)}) collective-permute-start(bf16[2,1,64,1536]{3,2,1,0:T(8,128)(2,1)S(1)} %collective-permute-done.4.rest_8_), channel_id=1, source_target_pairs={{0,4},{4,8},{8,12},{12,14},{14,10},{10,6},{6,2},{2,0},{1,5},{5,9},... | collective-permute-start | bytes 1179656 | tf_op jit(solution)/shard_map/ppermute | solution.py:67
  32.5 13.9 %collective-permute-start.5 = (bf16[2,1,64,1536]{3,2,0,1:T(8,128)(2,1)}, bf16[2,1,64,1536]{3,2,0,1:T(8,128)(2,1)S(1)}, u32[]{:S(2)}, u32[]{:S(2)}) collective-permute-start(bf16[2,1,64,1536]{3,2,0,1:T(8,128)(2,1)} %get-tuple-element.12), channel_id=1, source_target_pairs={{0,2},{2,4},{4,6},{6,8},{8,10},{10,12},{12,14},{1,3},{3,5},{5,7},{... | collective-permute-start | bytes 1179656 | tf_op jit(solution)/shard_map/ppermute | solution.py:34
  34.5 20.6 %collective-permute-start.6 = (bf16[2,1,64,1536]{3,2,0,1:T(8,128)(2,1)}, bf16[2,1,64,1536]{3,2,0,1:T(8,128)(2,1)S(1)}, u32[]{:S(2)}, u32[]{:S(2)}) collective-permute-start(bf16[2,1,64,1536]{3,2,0,1:T(8,128)(2,1)} %get-tuple-element.13), channel_id=1, source_target_pairs={{2,0},{4,2},{6,4},{8,6},{10,8},{12,10},{14,12},{3,1},{5,3},{7,5},{... | collective-permute-start | bytes 1179656 | tf_op jit(solution)/shard_map/ppermute | solution.py:34
  38.7 18.3 %collective-permute-start.20 = (bf16[2,1,64,1536]{3,2,1,0:T(8,128)(2,1)}, bf16[2,1,64,1536]{3,2,1,0:T(8,128)(2,1)}, u32[]{:S(2)}, u32[]{:S(2)}) collective-permute-start(bf16[2,1,64,1536]{3,2,1,0:T(8,128)(2,1)} %collective-permute-done.18.rest_16_), channel_id=1, source_target_pairs={{4,0},{8,4},{12,8},{14,12},{10,14},{6,10},{2,6},{0,2},{5,1},{9,5},... | collective-permute-start | bytes 1179656 | tf_op jit(solution)/shard_map/ppermute | solution.py:70
  39.9 22.2 %collective-permute-start.14 = (bf16[2,1,64,1536]{3,2,1,0:T(8,128)(2,1)S(1)}, bf16[2,1,64,1536]{3,2,1,0:T(8,128)(2,1)S(1)}, u32[]{:S(2)}, u32[]{:S(2)}) collective-permute-start(bf16[2,1,64,1536]{3,2,1,0:T(8,128)(2,1)S(1)} %collective-permute-done.13.rest_9_), channel_id=1, source_target_pairs={{4,0},{8,4},{12,8},{14,12},{10,14},{6,10},{2,6},{0,2},{5,1},{9,5},... | collective-permute-start | bytes 1179656 | tf_op jit(solution)/shard_map/ppermute | solution.py:70
  40.0 23.5 %collective-permute-start.10 = (bf16[2,1,64,1536]{3,2,1,0:T(8,128)(2,1)S(1)}, bf16[2,1,64,1536]{3,2,1,0:T(8,128)(2,1)S(1)}, u32[]{:S(2)}, u32[]{:S(2)}) collective-permute-start(bf16[2,1,64,1536]{3,2,1,0:T(8,128)(2,1)S(1)} %collective-permute-done.7.rest_10_), channel_id=1, source_target_pairs={{0,4},{4,8},{8,12},{12,14},{14,10},{10,6},{6,2},{2,0},{1,5},{5,9},... | collective-permute-start | bytes 1179656 | tf_op jit(solution)/shard_map/ppermute | solution.py:67
  46.4 28.2 %collective-permute-start.19 = (bf16[2,1,64,1536]{3,2,1,0:T(8,128)(2,1)}, bf16[2,1,64,1536]{3,2,1,0:T(8,128)(2,1)}, u32[]{:S(2)}, u32[]{:S(2)}) collective-permute-start(bf16[2,1,64,1536]{3,2,1,0:T(8,128)(2,1)} %collective-permute-done.17.rest_15_), channel_id=1, source_target_pairs={{0,4},{4,8},{8,12},{12,14},{14,10},{10,6},{6,2},{2,0},{1,5},{5,9},... | collective-permute-start | bytes 1179656 | tf_op jit(solution)/shard_map/ppermute | solution.py:67
  55.1 31.0 %collective-permute-start.8 = (bf16[2,1,64,1536]{3,2,0,1:T(8,128)(2,1)}, bf16[2,1,64,1536]{3,2,0,1:T(8,128)(2,1)}, u32[]{:S(2)}, u32[]{:S(2)}) collective-permute-start(bf16[2,1,64,1536]{3,2,0,1:T(8,128)(2,1)} %get-tuple-element.14), channel_id=1, source_target_pairs={{0,2},{2,4},{4,6},{6,8},{8,10},{10,12},{12,14},{1,3},{3,5},{5,7},{... | collective-permute-start | bytes 1179656 | tf_op jit(solution)/shard_map/ppermute | solution.py:34
  57.0 30.4 %collective-permute-start.9 = (bf16[2,1,64,1536]{3,2,0,1:T(8,128)(2,1)}, bf16[2,1,64,1536]{3,2,0,1:T(8,128)(2,1)}, u32[]{:S(2)}, u32[]{:S(2)}) collective-permute-start(bf16[2,1,64,1536]{3,2,0,1:T(8,128)(2,1)} %get-tuple-element.15), channel_id=1, source_target_pairs={{2,0},{4,2},{6,4},{8,6},{10,8},{12,10},{14,12},{3,1},{5,3},{7,5},{... | collective-permute-start | bytes 1179656 | tf_op jit(solution)/shard_map/ppermute | solution.py:34
  62.2 27.5 %collective-permute-start.22 = (bf16[2,1,64,1536]{3,2,1,0:T(8,128)(2,1)}, bf16[2,1,64,1536]{3,2,1,0:T(8,128)(2,1)}, u32[]{:S(2)}, u32[]{:S(2)}) collective-permute-start(bf16[2,1,64,1536]{3,2,1,0:T(8,128)(2,1)} %collective-permute-done.20.rest_18_), channel_id=1, source_target_pairs={{4,0},{8,4},{12,8},{14,12},{10,14},{6,10},{2,6},{0,2},{5,1},{9,5},... | collective-permute-start | bytes 1179656 | tf_op jit(solution)/shard_map/ppermute | solution.py:70
  63.5 34.7 %collective-permute-start.15 = (bf16[2,1,64,1536]{3,2,1,0:T(8,128)(2,1)S(1)}, bf16[2,1,64,1536]{3,2,1,0:T(8,128)(2,1)}, u32[]{:S(2)}, u32[]{:S(2)}) collective-permute-start(bf16[2,1,64,1536]{3,2,1,0:T(8,128)(2,1)S(1)} %collective-permute-done.14.rest_11_), channel_id=1, source_target_pairs={{4,0},{8,4},{12,8},{14,12},{10,14},{6,10},{2,6},{0,2},{5,1},{9,5},... | collective-permute-start | bytes 1179656 | tf_op jit(solution)/shard_map/ppermute | solution.py:70
  74.7 23.7 %collective-permute-start.21 = (bf16[2,1,64,1536]{3,2,1,0:T(8,128)(2,1)}, bf16[2,1,64,1536]{3,2,1,0:T(8,128)(2,1)}, u32[]{:S(2)}, u32[]{:S(2)}) collective-permute-start(bf16[2,1,64,1536]{3,2,1,0:T(8,128)(2,1)} %collective-permute-done.19.rest_17_), channel_id=1, source_target_pairs={{0,4},{4,8},{8,12},{12,14},{14,10},{10,6},{6,2},{2,0},{1,5},{5,9},... | collective-permute-start | bytes 1179656 | tf_op jit(solution)/shard_map/ppermute | solution.py:67
  86.0 12.3 %collective-permute-start.11 = (bf16[2,1,64,1536]{3,2,0,1:T(8,128)(2,1)}, bf16[2,1,64,1536]{3,2,0,1:T(8,128)(2,1)}, u32[]{:S(2)}, u32[]{:S(2)}) collective-permute-start(bf16[2,1,64,1536]{3,2,0,1:T(8,128)(2,1)} %get-tuple-element.16), channel_id=1, source_target_pairs={{12,14},{13,15},{28,30},{29,31}} | collective-permute-start | bytes 1179656 | tf_op jit(solution)/shard_map/ppermute | solution.py:227
  87.5 10.9 %collective-permute-start.12 = (bf16[2,1,64,1536]{3,2,0,1:T(8,128)(2,1)}, bf16[2,1,64,1536]{3,2,0,1:T(8,128)(2,1)}, u32[]{:S(2)}, u32[]{:S(2)}) collective-permute-start(bf16[2,1,64,1536]{3,2,0,1:T(8,128)(2,1)} %get-tuple-element.17), channel_id=1, source_target_pairs={{2,0},{3,1},{18,16},{19,17}} | collective-permute-start | bytes 1179656 | tf_op jit(solution)/shard_map/ppermute | solution.py:228
  89.7 15.6 %collective-permute-start.16 = (bf16[2,1,64,1536]{3,2,1,0:T(8,128)(2,1)S(1)}, bf16[2,1,64,1536]{3,2,1,0:T(8,128)(2,1)}, u32[]{:S(2)}, u32[]{:S(2)}) collective-permute-start(bf16[2,1,64,1536]{3,2,1,0:T(8,128)(2,1)S(1)} %collective-permute-done.10.rest_12_), channel_id=1, source_target_pairs={{0,4},{4,8},{8,12},{12,14},{14,10},{10,6},{6,2},{2,0},{1,5},{5,9},... | collective-permute-start | bytes 1179656 | tf_op jit(solution)/shard_map/ppermute | solution.py:62
  98.1 17.1 %collective-permute-start.23 = (bf16[2,1,64,1536]{3,2,1,0:T(8,128)(2,1)}, bf16[2,1,64,1536]{3,2,1,0:T(8,128)(2,1)}, u32[]{:S(2)}, u32[]{:S(2)}) collective-permute-start(bf16[2,1,64,1536]{3,2,1,0:T(8,128)(2,1)} %collective-permute-done.22.rest_20_), channel_id=1, source_target_pairs={{4,0},{8,4},{12,8},{14,12},{10,14},{6,10},{2,6},{0,2},{5,1},{9,5},... | collective-permute-start | bytes 1179656 | tf_op jit(solution)/shard_map/ppermute | solution.py:64

commit v18 on v17

--- a/solution.py
+++ b/solution.py
@@ -186,8 +186,13 @@
 
     stacked = jnp.stack([dequant(key_mant, key_exp), dequant(value_mant, value_exp)])[:, :, 0]
 
-    above = shift(stacked[:, tile_blocks - 1 :], "row", row_count, 1)
-    below = shift(stacked[:, :1], "row", row_count, -1)
+    if row_count == 2:
+        row_edge = jnp.where(lax.axis_index("row") == 0, tile_blocks - 1, 0)
+        edge = lax.dynamic_slice_in_dim(stacked, row_edge, 1, axis=1)
+        above = below = lax.ppermute(edge, "row", [(0, 1), (1, 0)])
+    else:
+        above = shift(stacked[:, tile_blocks - 1 :], "row", row_count, 1)
+        below = shift(stacked[:, :1], "row", row_count, -1)
 
     far_source = stacked[:, 0::4]
     dilated_entries = dilated_list[0, 0]

time: 131 us -> 132 us (level)
  the two profiles are of different devices: /device:TPU:19 before, /device:TPU:0 now
where the time goes in v18:
time: 132 us; the launch traced here: 131 us
  waiting for transfers between devices  49.9 us (38%)
  starting transfers between devices  41.5 us (31%)
  local copies, waits for them, and re-layouts  14 us (11%)
  Pallas kernels  13.7 us (10%)
  other arithmetic  11.7 us (9%)
    ppermute x6, waiting for transfers between devices, ring_gather(): behind = lax.ppermute(behind, 'col', backward)  33.9 us
    ppermute x6, starting transfers between devices, shift(): return lax.ppermute(x, axis, pairs)  17.4 us
    pallas_call x1, Pallas kernels, gather_attend(): pl.pallas_call(kernel, out_shape=jax.ShapeDtypeStruct((token_count, width...  13.7 us
    ppermute x6, starting transfers between devices, ring_gather(): behind = lax.ppermute(behind, 'col', backward)  13.2 us
    ppermute x6, waiting for transfers between devices, ring_gather(): ahead = lax.ppermute(ahead, 'col', forward)  5.95 us
    ppermute x6, starting transfers between devices, ring_gather(): ahead = lax.ppermute(ahead, 'col', forward)  5.65 us
    ppermute x1, waiting for transfers between devices, ring_gather(): arrays.append(lax.ppermute(behind, 'col', backward))  5.53 us
    ppermute x1, waiting for transfers between devices, ring_gather(): arrays.append(lax.ppermute(ahead, 'col', forward))  4.52 us
  transfers between devices with their start and end apart: 23, of which 8 were waited for; matrix products, arithmetic and copies ran while one was open for 18% of the time, Pallas kernels for 0%

profile of v18, /device:TPU:0, one launch (start us, length us, event | category | flops | bytes accessed | tf_op | source)
XLA Modules:
  0.0 131.3 jit_solution(15970308324365681935)
XLA Ops:
  0.0 4.9 %collective-permute-start.2 = (s32[4]{0:T(128)}, s32[4]{0:T(128)S(1)}, u32[]{:S(2)}, u32[]{:S(2)}) collective-permute-start(s32[4]{0:T(128)} %bitcast.97), channel_id=1, source_target_pairs={{0,2},{2,4},{4,6},{6,8},{8,10},{10,12},{12,14},{1,3},{3,5},{5,7},{... | collective-permute-start | bytes 56 | tf_op jit(solution)/shard_map/ppermute | solution.py:34
  4.9 1.3 collective-permute-start.1
  6.2 1.0 exponential_bitcast_fusion.1
  7.1 1.0 exponential_bitcast_fusion
  8.1 1.8 %fusion.1 = bf16[8,1,64,1536]{3,2,0,1:T(8,128)(2,1)S(1)} fusion(bf16[8,1,64,1536]{3,2,1,0:T(8,128)(2,1)} %param.15, f32[8,2,1536]{2,1,0:T(2,128)S(1)} %exponential_bitcast_fusion), kind=kLoop, calls=%fused_computation.10 | loop fusion | flops 2359296 | bytes 3244032 | tf_op jit(solution)/shard_map/convert_element_type | solution.py:24
  9.9 0.1 copy-done.5
  10.0 0.3 fusion.2
  10.3 0.0 copy-start.3
  10.3 0.3 fusion.own_hbm
  10.6 0.8 copy-done.3
  11.5 0.1 slice.29
  11.5 1.0 fusion.21
  12.6 2.6 %collective-permute-start.17 = (bf16[2,1,64,1536]{3,2,1,0:T(8,128)(2,1)}, bf16[2,1,64,1536]{3,2,1,0:T(8,128)(2,1)}, u32[]{:S(2)}, u32[]{:S(2)}) collective-permute-start(bf16[2,1,64,1536]{3,2,1,0:T(8,128)(2,1)} %get-tuple-element.24), channel_id=1, source_target_pairs={{4,0},{8,4},{12,8},{14,12},{10,14},{6,10},{2,6},{0,2},{5,1},{9,5},... | collective-permute-start | bytes 1179656 | tf_op jit(solution)/shard_map/ppermute | solution.py:70
  15.2 1.0 collective-permute-start.16
  16.2 1.1 collective-permute-start.12
  17.2 1.7 %fusion.4 = bf16[2,1,64,1536]{3,2,1,0:T(8,128)(2,1)} fusion(s32[]{:T(128)S(6)} %select_n.123, bf16[1,8,1,64,1536]{4,3,1,0,2:T(8,128)(2,1)S(1)} %bitcast.93, bf16[1,8,1,64,1536]{4,3,1,0,2:T(8,128)(2,1)} %bitcast.95), kind=kLoop, calls=%fused_computation.16 | loop fusion | flops 196608 | bytes 3538948 | tf_op jit(solution)/shard_map/dynamic_slice | solution.py:191
  18.9 1.0 collective-permute-start.3
  19.9 0.2 reduce-window.37
  20.1 0.0 collective-permute-start
  20.2 0.2 reduce-window.36
  20.4 0.1 select_reduce_fusion
  20.5 0.1 select_reduce_fusion.1
  20.6 2.5 %gather_fusion.4 = bf16[3,2,64,1536]{3,2,1,0:T(8,128)(2,1)S(1)} fusion(bf16[2,8,64,1536]{3,2,1,0:T(8,128)(2,1)} %copy-done.2, s32[1024]{0:T(1024)S(1)} %pad_clamp_fusion), kind=kCustom, calls=%fused_computation.1.clone | custom fusion | bytes 2359308 | tf_op jit(solution)/shard_map/jit(_take)/gather | solution.py:220
  23.2 3.6 %gather_fusion.3 = bf16[3,2,64,1536]{3,2,1,0:T(8,128)(2,1)} fusion(bf16[2,8,64,1536]{3,2,1,0:T(8,128)(2,1)} %copy-done.2, s32[1024]{0:T(1024)S(1)} %pad_clamp_fusion.1), kind=kCustom, calls=%fused_computation.clone | custom fusion | bytes 2359308 | tf_op jit(solution)/shard_map/jit(_take)/gather | solution.py:219
  26.7 0.2 select_bitcast_fusion
  26.9 1.1 copy-done.4
  28.0 0.2 select_bitcast_fusion.1
  28.2 1.0 fusion.19
  29.2 4.6 %collective-permute-done.3.rest_8_ = bf16[2,1,64,1536]{3,2,1,0:T(8,128)(2,1)S(1)} collective-permute-done((bf16[2,1,64,1536]{3,2,1,0:T(8,128)(2,1)}, bf16[2,1,64,1536]{3,2,1,0:T(8,128)(2,1)S(1)}, u32[]{:S(2)}, u32[]{:S(2)}) %collective-permute-start.3) | collective-permute-done | bytes 393248 | tf_op jit(solution)/shard_map/ppermute | solution.py:67
  33.8 1.2 collective-permute-start.6
  35.1 1.0 fusion.20
  36.1 2.7 %collective-permute-start.4 = (bf16[2,1,64,1536]{3,2,0,1:T(8,128)(2,1)}, bf16[2,1,64,1536]{3,2,0,1:T(8,128)(2,1)S(1)}, u32[]{:S(2)}, u32[]{:S(2)}) collective-permute-start(bf16[2,1,64,1536]{3,2,0,1:T(8,128)(2,1)} %get-tuple-element.12), channel_id=1, source_target_pairs={{0,2},{2,4},{4,6},{6,8},{8,10},{10,12},{12,14},{1,3},{3,5},{5,7},{... | collective-permute-start | bytes 1179656 | tf_op jit(solution)/shard_map/ppermute | solution.py:34
  38.9 2.5 %collective-permute-start.19 = (bf16[2,1,64,1536]{3,2,1,0:T(8,128)(2,1)}, bf16[2,1,64,1536]{3,2,1,0:T(8,128)(2,1)}, u32[]{:S(2)}, u32[]{:S(2)}) collective-permute-start(bf16[2,1,64,1536]{3,2,1,0:T(8,128)(2,1)} %collective-permute-done.17.rest_16_), channel_id=1, source_target_pairs={{4,0},{8,4},{12,8},{14,12},{10,14},{6,10},{2,6},{0,2},{5,1},{9,5},... | collective-permute-start | bytes 1179656 | tf_op jit(solution)/shard_map/ppermute | solution.py:70
  41.3 2.0 %collective-permute-start.13 = (bf16[2,1,64,1536]{3,2,1,0:T(8,128)(2,1)S(1)}, bf16[2,1,64,1536]{3,2,1,0:T(8,128)(2,1)S(1)}, u32[]{:S(2)}, u32[]{:S(2)}) collective-permute-start(bf16[2,1,64,1536]{3,2,1,0:T(8,128)(2,1)S(1)} %collective-permute-done.12.rest_9_), channel_id=1, source_target_pairs={{4,0},{8,4},{12,8},{14,12},{10,14},{6,10},{2,6},{0,2},{5,1},{9,5},... | collective-permute-start | bytes 1179656 | tf_op jit(solution)/shard_map/ppermute | solution.py:70
  43.3 1.3 %collective-permute-done.6.rest_10_ = bf16[2,1,64,1536]{3,2,1,0:T(8,128)(2,1)S(1)} collective-permute-done((bf16[2,1,64,1536]{3,2,1,0:T(8,128)(2,1)S(1)}, bf16[2,1,64,1536]{3,2,1,0:T(8,128)(2,1)S(1)}, u32[]{:S(2)}, u32[]{:S(2)}) %collective-permute-start.6) | collective-permute-done | bytes 393248 | tf_op jit(solution)/shard_map/ppermute | solution.py:67
  44.7 2.5 %collective-permute-start.9 = (bf16[2,1,64,1536]{3,2,1,0:T(8,128)(2,1)S(1)}, bf16[2,1,64,1536]{3,2,1,0:T(8,128)(2,1)S(1)}, u32[]{:S(2)}, u32[]{:S(2)}) collective-permute-start(bf16[2,1,64,1536]{3,2,1,0:T(8,128)(2,1)S(1)} %collective-permute-done.6.rest_10_), channel_id=1, source_target_pairs={{0,4},{4,8},{8,12},{12,14},{14,10},{10,6},{6,2},{2,0},{1,5},{5,9},... | collective-permute-start | bytes 1179656 | tf_op jit(solution)/shard_map/ppermute | solution.py:67
  47.2 0.6 dynamic_slice.8
  47.8 0.6 gather_fusion
  48.5 0.5 fusion.9
  49.0 12.2 %collective-permute-done.19.rest_18_ = bf16[2,1,64,1536]{3,2,1,0:T(8,128)(2,1)} collective-permute-done((bf16[2,1,64,1536]{3,2,1,0:T(8,128)(2,1)}, bf16[2,1,64,1536]{3,2,1,0:T(8,128)(2,1)}, u32[]{:S(2)}, u32[]{:S(2)}) %collective-permute-start.19) | collective-permute-done | bytes 393248 | tf_op jit(solution)/shard_map/ppermute | solution.py:70
  61.2 1.3 collective-permute-start.5
  62.5 5.9 %collective-permute-start.7 = (bf16[2,1,64,1536]{3,2,0,1:T(8,128)(2,1)}, bf16[2,1,64,1536]{3,2,0,1:T(8,128)(2,1)}, u32[]{:S(2)}, u32[]{:S(2)}) collective-permute-start(bf16[2,1,64,1536]{3,2,0,1:T(8,128)(2,1)} %get-tuple-element.14), channel_id=1, source_target_pairs={{0,2},{2,4},{4,6},{6,8},{8,10},{10,12},{12,14},{1,3},{3,5},{5,7},{... | collective-permute-start | bytes 1179656 | tf_op jit(solution)/shard_map/ppermute | solution.py:34
  68.4 2.4 %collective-permute-done.13.rest_11_ = bf16[2,1,64,1536]{3,2,1,0:T(8,128)(2,1)S(1)} collective-permute-done((bf16[2,1,64,1536]{3,2,1,0:T(8,128)(2,1)S(1)}, bf16[2,1,64,1536]{3,2,1,0:T(8,128)(2,1)S(1)}, u32[]{:S(2)}, u32[]{:S(2)}) %collective-permute-start.13) | collective-permute-done | bytes 393248 | tf_op jit(solution)/shard_map/ppermute | solution.py:70
  70.9 3.0 %collective-permute-start.21 = (bf16[2,1,64,1536]{3,2,1,0:T(8,128)(2,1)}, bf16[2,1,64,1536]{3,2,1,0:T(8,128)(2,1)}, u32[]{:S(2)}, u32[]{:S(2)}) collective-permute-start(bf16[2,1,64,1536]{3,2,1,0:T(8,128)(2,1)} %collective-permute-done.19.rest_18_), channel_id=1, source_target_pairs={{4,0},{8,4},{12,8},{14,12},{10,14},{6,10},{2,6},{0,2},{5,1},{9,5},... | collective-permute-start | bytes 1179656 | tf_op jit(solution)/shard_map/ppermute | solution.py:70
  73.8 2.0 %collective-permute-start.14 = (bf16[2,1,64,1536]{3,2,1,0:T(8,128)(2,1)S(1)}, bf16[2,1,64,1536]{3,2,1,0:T(8,128)(2,1)}, u32[]{:S(2)}, u32[]{:S(2)}) collective-permute-start(bf16[2,1,64,1536]{3,2,1,0:T(8,128)(2,1)S(1)} %collective-permute-done.13.rest_11_), channel_id=1, source_target_pairs={{4,0},{8,4},{12,8},{14,12},{10,14},{6,10},{2,6},{0,2},{5,1},{9,5},... | collective-permute-start | bytes 1179656 | tf_op jit(solution)/shard_map/ppermute | solution.py:70
  75.9 0.6 fusion.18
  76.5 1.4 %reduce-window.34 = s32[4,1]{0,1:T(1,128)} reduce-window(s32[4,1]{0,1:T(1,128)} %get-tuple-element.30, s32[]{:T(128)} %constant.103.clone), window={size=4x1 pad=3_0x0_0}, to_apply=%region_0.1 | reduce-window | flops 12 | bytes 36 | tf_op jit(solution)/shard_map/reduce-window.14
  77.9 1.3 %reduce-window.35 = s32[4,1]{0,1:T(1,128)} reduce-window(s32[4,1]{0,1:T(1,128)} %get-tuple-element.31, s32[]{:T(128)} %constant.103.clone), window={size=4x1 pad=3_0x0_0}, to_apply=%region_1.2 | reduce-window | flops 12 | bytes 36 | tf_op jit(solution)/shard_map/reduce-window.15
  79.2 0.6 gather_fusion.1
  79.8 0.6 gather_fusion.2
  80.5 0.1 pad_bitcast_fusion
  80.5 0.7 compare_select_fusion.10
  81.2 1.3 collective-permute-start.8
  82.5 16.7 %collective-permute-done.21.rest_20_ = bf16[2,1,64,1536]{3,2,1,0:T(8,128)(2,1)} collective-permute-done((bf16[2,1,64,1536]{3,2,1,0:T(8,128)(2,1)}, bf16[2,1,64,1536]{3,2,1,0:T(8,128)(2,1)}, u32[]{:S(2)}, u32[]{:S(2)}) %collective-permute-start.21) | collective-permute-done | bytes 393248 | tf_op jit(solution)/shard_map/ppermute | solution.py:70
  99.3 1.4 %collective-permute-start.10 = (bf16[2,1,64,1536]{3,2,0,1:T(8,128)(2,1)}, bf16[2,1,64,1536]{3,2,0,1:T(8,128)(2,1)}, u32[]{:S(2)}, u32[]{:S(2)}) collective-permute-start(bf16[2,1,64,1536]{3,2,0,1:T(8,128)(2,1)} %get-tuple-element.16), channel_id=1, source_target_pairs={{12,14},{13,15},{28,30},{29,31}} | collective-permute-start | bytes 1179656 | tf_op jit(solution)/shard_map/ppermute | solution.py:232
  100.7 1.3 collective-permute-start.11
  102.0 2.5 %collective-permute-done.14.rest_13_ = bf16[2,1,64,1536]{3,2,1,0:T(8,128)(2,1)} collective-permute-done((bf16[2,1,64,1536]{3,2,1,0:T(8,128)(2,1)S(1)}, bf16[2,1,64,1536]{3,2,1,0:T(8,128)(2,1)}, u32[]{:S(2)}, u32[]{:S(2)}) %collective-permute-start.14) | collective-permute-done | bytes 393248 | tf_op jit(solution)/shard_map/ppermute | solution.py:70
  104.5 2.6 %collective-permute-start.22 = (bf16[2,1,64,1536]{3,2,1,0:T(8,128)(2,1)}, bf16[2,1,64,1536]{3,2,1,0:T(8,128)(2,1)}, u32[]{:S(2)}, u32[]{:S(2)}) collective-permute-start(bf16[2,1,64,1536]{3,2,1,0:T(8,128)(2,1)} %collective-permute-done.21.rest_20_), channel_id=1, source_target_pairs={{4,0},{8,4},{12,8},{14,12},{10,14},{6,10},{2,6},{0,2},{5,1},{9,5},... | collective-permute-start | bytes 1179656 | tf_op jit(solution)/shard_map/ppermute | solution.py:64
  107.1 0.1 add_bitcast_fusion
  107.2 0.1 copy.31
  107.3 0.1 reshape.422.table_ref
  107.3 5.5 %collective-permute-done.22.rest_21_ = bf16[2,1,64,1536]{3,2,1,0:T(8,128)(2,1)} collective-permute-done((bf16[2,1,64,1536]{3,2,1,0:T(8,128)(2,1)}, bf16[2,1,64,1536]{3,2,1,0:T(8,128)(2,1)}, u32[]{:S(2)}, u32[]{:S(2)}) %collective-permute-start.22) | collective-permute-done | bytes 393248 | tf_op jit(solution)/shard_map/ppermute | solution.py:64
  112.9 4.5 %collective-permute-done.15.rest_14_ = bf16[2,1,64,1536]{3,2,1,0:T(8,128)(2,1)} collective-permute-done((bf16[2,1,64,1536]{3,2,1,0:T(8,128)(2,1)S(1)}, bf16[2,1,64,1536]{3,2,1,0:T(8,128)(2,1)}, u32[]{:S(2)}, u32[]{:S(2)}) %collective-permute-start.15) | collective-permute-done | bytes 393248 | tf_op jit(solution)/shard_map/ppermute | solution.py:62
  117.4 13.7 %shard_map.100 = bf16[512,1536]{1,0:T(8,128)(2,1)} custom-call(s32[16]{0:T(128)S(1)} %reshape.422.table_ref, bf16[512,1536]{1,0:T(8,128)(2,1)} %bitcast.96, bf16[2,8,64,1536]{3,2,1,0:T(8,128)(2,1)} %copy-done.2, bf16[2,1,64,1536]{3,2,1,0:T(8,128)(2,1)S(1)} %collective-permute-done.rest_0_.rest_1_, ...), custom_call_target="tpu_custom_call" | custom-call | flops 3221225472 | bytes 9437184 | tf_op jit(solution)/shard_map/pallas_call | solution.py:154
  (45 shorter events, 0.2 us)
Async XLA Ops:
  0.0 18.9 %collective-permute-start.2 = (s32[4]{0:T(128)}, s32[4]{0:T(128)S(1)}, u32[]{:S(2)}, u32[]{:S(2)}) collective-permute-start(s32[4]{0:T(128)} %bitcast.97), channel_id=1, source_target_pairs={{0,2},{2,4},{4,6},{6,8},{8,10},{10,12},{12,14},{1,3},{3,5},{5,7},{... | collective-permute-start | bytes 56 | tf_op jit(solution)/shard_map/ppermute | solution.py:34
  4.9 15.2 %collective-permute-start.1 = (s32[4]{0:T(128)}, s32[4]{0:T(128)S(1)}, u32[]{:S(2)}, u32[]{:S(2)}) collective-permute-start(s32[4]{0:T(128)} %bitcast.98), channel_id=1, source_target_pairs={{2,0},{4,2},{6,4},{8,6},{10,8},{12,10},{14,12},{3,1},{5,3},{7,5},{... | collective-permute-start | bytes 56 | tf_op jit(solution)/shard_map/ppermute | solution.py:34
  8.1 1.9 %copy-start.5 = (bf16[8,1,64,1536]{3,2,1,0:T(8,128)(2,1)S(1)}, bf16[8,1,64,1536]{3,2,1,0:T(8,128)(2,1)}, u32[]{:S(2)}) copy-start(bf16[8,1,64,1536]{3,2,1,0:T(8,128)(2,1)} %param.13) | copy-start | bytes 4718596
  10.3 1.1 copy-start.3
  11.5 4.7 %copy-start.2 = (bf16[2,8,64,1536]{3,2,1,0:T(8,128)(2,1)}, bf16[2,8,64,1536]{3,2,1,0:T(8,128)(2,1)S(1)}, u32[]{:S(2)}) copy-start(bf16[2,8,64,1536]{3,2,1,0:T(8,128)(2,1)S(1)} %fusion.own_hbm) | copy-start | bytes 9437188
  12.6 26.3 %collective-permute-start.17 = (bf16[2,1,64,1536]{3,2,1,0:T(8,128)(2,1)}, bf16[2,1,64,1536]{3,2,1,0:T(8,128)(2,1)}, u32[]{:S(2)}, u32[]{:S(2)}) collective-permute-start(bf16[2,1,64,1536]{3,2,1,0:T(8,128)(2,1)} %get-tuple-element.24), channel_id=1, source_target_pairs={{4,0},{8,4},{12,8},{14,12},{10,14},{6,10},{2,6},{0,2},{5,1},{9,5},... | collective-permute-start | bytes 1179656 | tf_op jit(solution)/shard_map/ppermute | solution.py:70
  15.2 26.1 %collective-permute-start.16 = (bf16[2,1,64,1536]{3,2,1,0:T(8,128)(2,1)}, bf16[2,1,64,1536]{3,2,1,0:T(8,128)(2,1)S(1)}, u32[]{:S(2)}, u32[]{:S(2)}) collective-permute-start(bf16[2,1,64,1536]{3,2,1,0:T(8,128)(2,1)} %get-tuple-element.24), channel_id=1, source_target_pairs={{0,4},{4,8},{8,12},{12,14},{14,10},{10,6},{6,2},{2,0},{1,5},{5,9},... | collective-permute-start | bytes 1179656 | tf_op jit(solution)/shard_map/ppermute | solution.py:67
  16.2 25.2 %collective-permute-start.12 = (bf16[2,1,64,1536]{3,2,1,0:T(8,128)(2,1)}, bf16[2,1,64,1536]{3,2,1,0:T(8,128)(2,1)S(1)}, u32[]{:S(2)}, u32[]{:S(2)}) collective-permute-start(bf16[2,1,64,1536]{3,2,1,0:T(8,128)(2,1)} %get-tuple-element.25), channel_id=1, source_target_pairs={{4,0},{8,4},{12,8},{14,12},{10,14},{6,10},{2,6},{0,2},{5,1},{9,5},... | collective-permute-start | bytes 1179656 | tf_op jit(solution)/shard_map/ppermute | solution.py:70
  18.9 14.9 %collective-permute-start.3 = (bf16[2,1,64,1536]{3,2,1,0:T(8,128)(2,1)}, bf16[2,1,64,1536]{3,2,1,0:T(8,128)(2,1)S(1)}, u32[]{:S(2)}, u32[]{:S(2)}) collective-permute-start(bf16[2,1,64,1536]{3,2,1,0:T(8,128)(2,1)} %get-tuple-element.25), channel_id=1, source_target_pairs={{0,4},{4,8},{8,12},{12,14},{14,10},{10,6},{6,2},{2,0},{1,5},{5,9},... | collective-permute-start | bytes 1179656 | tf_op jit(solution)/shard_map/ppermute | solution.py:67
  20.1 16.0 %collective-permute-start = (bf16[2,1,64,1536]{3,2,1,0:T(8,128)(2,1)}, bf16[2,1,64,1536]{3,2,1,0:T(8,128)(2,1)S(1)}, u32[]{:S(2)}, u32[]{:S(2)}) collective-permute-start(bf16[2,1,64,1536]{3,2,1,0:T(8,128)(2,1)} %fusion.4), channel_id=1, source_target_pairs={{0,1},{1,0},{2,3},{3,2},{4,5},{5,4},{6,7},{7,6},{8,9},{9,8},{10,11... | collective-permute-start | bytes 1179656 | tf_op jit(solution)/shard_map/ppermute | solution.py:192
  26.7 1.3 copy-start.4
  29.2 17.9 %copy-start.6 = (s32[1,1,4]{2,1,0:T(1,128)S(1)}, s32[1,1,4]{2,1,0:T(1,128)}, u32[]{:S(2)}) copy-start(s32[1,1,4]{2,1,0:T(1,128)} %param.18) | copy-start | bytes 52
  29.2 17.9 %copy-start = (s32[8]{0:T(128)S(1)}, s32[8]{0:T(128)}, u32[]{:S(2)}) copy-start(s32[8]{0:T(128)} %constant.101.clone) | copy-start | bytes 100
  29.2 19.2 %copy-start.7 = (s32[1,1,4]{2,1,0:T(1,128)S(1)}, s32[1,1,4]{2,1,0:T(1,128)}, u32[]{:S(2)}) copy-start(s32[1,1,4]{2,1,0:T(1,128)} %param.17) | copy-start | bytes 52
  29.2 50.0 %copy-start.1 = (s32[7,2]{1,0:T(8,128)S(1)}, s32[7,2]{1,0:T(8,128)}, u32[]{:S(2)}) copy-start(s32[7,2]{1,0:T(8,128)} %constant.102.clone) | copy-start | bytes 172
  33.8 10.8 %collective-permute-start.6 = (bf16[2,1,64,1536]{3,2,1,0:T(8,128)(2,1)S(1)}, bf16[2,1,64,1536]{3,2,1,0:T(8,128)(2,1)S(1)}, u32[]{:S(2)}, u32[]{:S(2)}) collective-permute-start(bf16[2,1,64,1536]{3,2,1,0:T(8,128)(2,1)S(1)} %collective-permute-done.3.rest_8_), channel_id=1, source_target_pairs={{0,4},{4,8},{8,12},{12,14},{14,10},{10,6},{6,2},{2,0},{1,5},{5,9},... | collective-permute-start | bytes 1179656 | tf_op jit(solution)/shard_map/ppermute | solution.py:67
  36.1 37.7 %collective-permute-start.4 = (bf16[2,1,64,1536]{3,2,0,1:T(8,128)(2,1)}, bf16[2,1,64,1536]{3,2,0,1:T(8,128)(2,1)S(1)}, u32[]{:S(2)}, u32[]{:S(2)}) collective-permute-start(bf16[2,1,64,1536]{3,2,0,1:T(8,128)(2,1)} %get-tuple-element.12), channel_id=1, source_target_pairs={{0,2},{2,4},{4,6},{6,8},{8,10},{10,12},{12,14},{1,3},{3,5},{5,7},{... | collective-permute-start | bytes 1179656 | tf_op jit(solution)/shard_map/ppermute | solution.py:34
  38.9 22.3 %collective-permute-start.19 = (bf16[2,1,64,1536]{3,2,1,0:T(8,128)(2,1)}, bf16[2,1,64,1536]{3,2,1,0:T(8,128)(2,1)}, u32[]{:S(2)}, u32[]{:S(2)}) collective-permute-start(bf16[2,1,64,1536]{3,2,1,0:T(8,128)(2,1)} %collective-permute-done.17.rest_16_), channel_id=1, source_target_pairs={{4,0},{8,4},{12,8},{14,12},{10,14},{6,10},{2,6},{0,2},{5,1},{9,5},... | collective-permute-start | bytes 1179656 | tf_op jit(solution)/shard_map/ppermute | solution.py:70
  41.3 21.2 %collective-permute-start.18 = (bf16[2,1,64,1536]{3,2,1,0:T(8,128)(2,1)S(1)}, bf16[2,1,64,1536]{3,2,1,0:T(8,128)(2,1)}, u32[]{:S(2)}, u32[]{:S(2)}) collective-permute-start(bf16[2,1,64,1536]{3,2,1,0:T(8,128)(2,1)S(1)} %collective-permute-done.16.rest_15_), channel_id=1, source_target_pairs={{0,4},{4,8},{8,12},{12,14},{14,10},{10,6},{6,2},{2,0},{1,5},{5,9},... | collective-permute-start | bytes 1179656 | tf_op jit(solution)/shard_map/ppermute | solution.py:67
  41.3 29.5 %collective-permute-start.13 = (bf16[2,1,64,1536]{3,2,1,0:T(8,128)(2,1)S(1)}, bf16[2,1,64,1536]{3,2,1,0:T(8,128)(2,1)S(1)}, u32[]{:S(2)}, u32[]{:S(2)}) collective-permute-start(bf16[2,1,64,1536]{3,2,1,0:T(8,128)(2,1)S(1)} %collective-permute-done.12.rest_9_), channel_id=1, source_target_pairs={{4,0},{8,4},{12,8},{14,12},{10,14},{6,10},{2,6},{0,2},{5,1},{9,5},... | collective-permute-start | bytes 1179656 | tf_op jit(solution)/shard_map/ppermute | solution.py:70
  44.7 29.2 %collective-permute-start.9 = (bf16[2,1,64,1536]{3,2,1,0:T(8,128)(2,1)S(1)}, bf16[2,1,64,1536]{3,2,1,0:T(8,128)(2,1)S(1)}, u32[]{:S(2)}, u32[]{:S(2)}) collective-permute-start(bf16[2,1,64,1536]{3,2,1,0:T(8,128)(2,1)S(1)} %collective-permute-done.6.rest_10_), channel_id=1, source_target_pairs={{0,4},{4,8},{8,12},{12,14},{14,10},{10,6},{6,2},{2,0},{1,5},{5,9},... | collective-permute-start | bytes 1179656 | tf_op jit(solution)/shard_map/ppermute | solution.py:67
  61.2 20.0 %collective-permute-start.5 = (bf16[2,1,64,1536]{3,2,0,1:T(8,128)(2,1)}, bf16[2,1,64,1536]{3,2,0,1:T(8,128)(2,1)S(1)}, u32[]{:S(2)}, u32[]{:S(2)}) collective-permute-start(bf16[2,1,64,1536]{3,2,0,1:T(8,128)(2,1)} %get-tuple-element.13), channel_id=1, source_target_pairs={{2,0},{4,2},{6,4},{8,6},{10,8},{12,10},{14,12},{3,1},{5,3},{7,5},{... | collective-permute-start | bytes 1179656 | tf_op jit(solution)/shard_map/ppermute | solution.py:34
  62.5 42.0 %collective-permute-start.7 = (bf16[2,1,64,1536]{3,2,0,1:T(8,128)(2,1)}, bf16[2,1,64,1536]{3,2,0,1:T(8,128)(2,1)}, u32[]{:S(2)}, u32[]{:S(2)}) collective-permute-start(bf16[2,1,64,1536]{3,2,0,1:T(8,128)(2,1)} %get-tuple-element.14), channel_id=1, source_target_pairs={{0,2},{2,4},{4,6},{6,8},{8,10},{10,12},{12,14},{1,3},{3,5},{5,7},{... | collective-permute-start | bytes 1179656 | tf_op jit(solution)/shard_map/ppermute | solution.py:34
  70.9 28.4 %collective-permute-start.21 = (bf16[2,1,64,1536]{3,2,1,0:T(8,128)(2,1)}, bf16[2,1,64,1536]{3,2,1,0:T(8,128)(2,1)}, u32[]{:S(2)}, u32[]{:S(2)}) collective-permute-start(bf16[2,1,64,1536]{3,2,1,0:T(8,128)(2,1)} %collective-permute-done.19.rest_18_), channel_id=1, source_target_pairs={{4,0},{8,4},{12,8},{14,12},{10,14},{6,10},{2,6},{0,2},{5,1},{9,5},... | collective-permute-start | bytes 1179656 | tf_op jit(solution)/shard_map/ppermute | solution.py:70
  73.8 26.8 %collective-permute-start.20 = (bf16[2,1,64,1536]{3,2,1,0:T(8,128)(2,1)}, bf16[2,1,64,1536]{3,2,1,0:T(8,128)(2,1)}, u32[]{:S(2)}, u32[]{:S(2)}) collective-permute-start(bf16[2,1,64,1536]{3,2,1,0:T(8,128)(2,1)} %collective-permute-done.18.rest_17_), channel_id=1, source_target_pairs={{0,4},{4,8},{8,12},{12,14},{14,10},{10,6},{6,2},{2,0},{1,5},{5,9},... | collective-permute-start | bytes 1179656 | tf_op jit(solution)/shard_map/ppermute | solution.py:67
  73.8 30.6 %collective-permute-start.14 = (bf16[2,1,64,1536]{3,2,1,0:T(8,128)(2,1)S(1)}, bf16[2,1,64,1536]{3,2,1,0:T(8,128)(2,1)}, u32[]{:S(2)}, u32[]{:S(2)}) collective-permute-start(bf16[2,1,64,1536]{3,2,1,0:T(8,128)(2,1)S(1)} %collective-permute-done.13.rest_11_), channel_id=1, source_target_pairs={{4,0},{8,4},{12,8},{14,12},{10,14},{6,10},{2,6},{0,2},{5,1},{9,5},... | collective-permute-start | bytes 1179656 | tf_op jit(solution)/shard_map/ppermute | solution.py:70
  81.2 26.1 %collective-permute-start.8 = (bf16[2,1,64,1536]{3,2,0,1:T(8,128)(2,1)}, bf16[2,1,64,1536]{3,2,0,1:T(8,128)(2,1)}, u32[]{:S(2)}, u32[]{:S(2)}) collective-permute-start(bf16[2,1,64,1536]{3,2,0,1:T(8,128)(2,1)} %get-tuple-element.15), channel_id=1, source_target_pairs={{2,0},{4,2},{6,4},{8,6},{10,8},{12,10},{14,12},{3,1},{5,3},{7,5},{... | collective-permute-start | bytes 1179656 | tf_op jit(solution)/shard_map/ppermute | solution.py:34
  99.3 18.1 %collective-permute-start.10 = (bf16[2,1,64,1536]{3,2,0,1:T(8,128)(2,1)}, bf16[2,1,64,1536]{3,2,0,1:T(8,128)(2,1)}, u32[]{:S(2)}, u32[]{:S(2)}) collective-permute-start(bf16[2,1,64,1536]{3,2,0,1:T(8,128)(2,1)} %get-tuple-element.16), channel_id=1, source_target_pairs={{12,14},{13,15},{28,30},{29,31}} | collective-permute-start | bytes 1179656 | tf_op jit(solution)/shard_map/ppermute | solution.py:232
  100.7 16.7 %collective-permute-start.11 = (bf16[2,1,64,1536]{3,2,0,1:T(8,128)(2,1)}, bf16[2,1,64,1536]{3,2,0,1:T(8,128)(2,1)}, u32[]{:S(2)}, u32[]{:S(2)}) collective-permute-start(bf16[2,1,64,1536]{3,2,0,1:T(8,128)(2,1)} %get-tuple-element.17), channel_id=1, source_target_pairs={{2,0},{3,1},{18,16},{19,17}} | collective-permute-start | bytes 1179656 | tf_op jit(solution)/shard_map/ppermute | solution.py:233
  104.5 12.9 %collective-permute-start.15 = (bf16[2,1,64,1536]{3,2,1,0:T(8,128)(2,1)S(1)}, bf16[2,1,64,1536]{3,2,1,0:T(8,128)(2,1)}, u32[]{:S(2)}, u32[]{:S(2)}) collective-permute-start(bf16[2,1,64,1536]{3,2,1,0:T(8,128)(2,1)S(1)} %collective-permute-done.9.rest_12_), channel_id=1, source_target_pairs={{0,4},{4,8},{8,12},{12,14},{14,10},{10,6},{6,2},{2,0},{1,5},{5,9},... | collective-permute-start | bytes 1179656 | tf_op jit(solution)/shard_map/ppermute | solution.py:62
  104.5 8.4 %collective-permute-start.22 = (bf16[2,1,64,1536]{3,2,1,0:T(8,128)(2,1)}, bf16[2,1,64,1536]{3,2,1,0:T(8,128)(2,1)}, u32[]{:S(2)}, u32[]{:S(2)}) collective-permute-start(bf16[2,1,64,1536]{3,2,1,0:T(8,128)(2,1)} %collective-permute-done.21.rest_20_), channel_id=1, source_target_pairs={{4,0},{8,4},{12,8},{14,12},{10,14},{6,10},{2,6},{0,2},{5,1},{9,5},... | collective-permute-start | bytes 1179656 | tf_op jit(solution)/shard_map/ppermute | solution.py:64

commit v19 on v17

--- a/solution.py
+++ b/solution.py
@@ -163,7 +163,7 @@
             pltpu.VMEM((blocks, block_length, width), jnp.bfloat16),
             pltpu.VMEM((blocks, block_length, width), jnp.bfloat16),
             pltpu.SemaphoreType.DMA((2, 2 + extra)),
-            pltpu.SemaphoreType.DMA((3 if heads % 3 == 0 else 1,)),
+            pltpu.SemaphoreType.DMA((6 if heads % 6 == 0 else 1,)),
         ],
         compiler_params=pltpu.CompilerParams(vmem_limit_bytes=48 * 1024 * 1024),
         cost_estimate=pl.CostEstimate(

time: 131 us -> 131 us (level)
  the two profiles are of different devices: /device:TPU:19 before, /device:TPU:25 now
where the time goes in v19:
time: 131 us; the launch traced here: 130 us
  waiting for transfers between devices  53.5 us (41%)
  starting transfers between devices  37 us (28%)
  Pallas kernels  15.2 us (12%)
  local copies, waits for them, and re-layouts  13.4 us (10%)
  other arithmetic  10.9 us (8%)
    ppermute x6, waiting for transfers between devices, ring_gather(): behind = lax.ppermute(behind, 'col', backward)  34.5 us
    ppermute x8, starting transfers between devices, shift(): return lax.ppermute(x, axis, pairs)  21.9 us
    pallas_call x1, Pallas kernels, gather_attend(): pl.pallas_call(kernel, out_shape=jax.ShapeDtypeStruct((token_count, width...  15.2 us
    ppermute x8, waiting for transfers between devices, shift(): return lax.ppermute(x, axis, pairs)  8.78 us
    ppermute x1, waiting for transfers between devices, ring_gather(): arrays.append(lax.ppermute(ahead, 'col', forward))  6.04 us
    ppermute x6, starting transfers between devices, ring_gather(): ahead = lax.ppermute(ahead, 'col', forward)  5.77 us
    ppermute x1, waiting for transfers between devices, ring_gather(): arrays.append(lax.ppermute(behind, 'col', backward))  4.18 us
    ppermute x1, starting transfers between devices, per_device(): cycle_sources.append(lax.ppermute(to_r, 'col', [(last - 1, last)]))  4.09 us
  transfers between devices with their start and end apart: 24, of which 9 were waited for; matrix products, arithmetic and copies ran while one was open for 18% of the time, Pallas kernels for 0%

profile of v19, /device:TPU:25, one launch (start us, length us, event | category | flops | bytes accessed | tf_op | source)
XLA Modules:
  0.0 130.4 jit_solution(14689858701347629144)
XLA Ops:
  0.0 3.1 %collective-permute-start.3 = (s32[4]{0:T(128)}, s32[4]{0:T(128)S(1)}, u32[]{:S(2)}, u32[]{:S(2)}) collective-permute-start(s32[4]{0:T(128)} %bitcast.93), channel_id=1, source_target_pairs={{0,2},{2,4},{4,6},{6,8},{8,10},{10,12},{12,14},{1,3},{3,5},{5,7},{... | collective-permute-start | bytes 56 | tf_op jit(solution)/shard_map/ppermute | solution.py:34
  3.1 3.0 %collective-permute-start.2 = (s32[4]{0:T(128)}, s32[4]{0:T(128)S(1)}, u32[]{:S(2)}, u32[]{:S(2)}) collective-permute-start(s32[4]{0:T(128)} %bitcast.94), channel_id=1, source_target_pairs={{2,0},{4,2},{6,4},{8,6},{10,8},{12,10},{14,12},{3,1},{5,3},{7,5},{... | collective-permute-start | bytes 56 | tf_op jit(solution)/shard_map/ppermute | solution.py:34
  6.2 1.0 exponential_bitcast_fusion.1
  7.2 1.0 exponential_bitcast_fusion
  8.1 1.8 %fusion.1 = bf16[8,1,64,1536]{3,2,0,1:T(8,128)(2,1)S(1)} fusion(bf16[8,1,64,1536]{3,2,1,0:T(8,128)(2,1)} %param.13, f32[8,2,1536]{2,1,0:T(2,128)S(1)} %exponential_bitcast_fusion.1), kind=kLoop, calls=%fused_computation.9 | loop fusion | flops 2359296 | bytes 3244032 | tf_op jit(solution)/shard_map/convert_element_type | solution.py:24
  10.0 0.1 copy-done.4
  10.0 0.3 fusion
  10.3 0.3 maximum_bitcast_fusion.own_hbm
  10.6 0.1 slice.37
  10.7 0.9 fusion.19
  11.6 0.3 collective-permute-start.4
  12.0 1.1 collective-permute-start.13
  13.1 0.2 collective-permute-start.18
  13.3 1.0 fusion.16
  14.2 1.3 collective-permute-start.17
  15.5 0.2 reduce-window.37
  15.7 0.1 select_reduce_fusion
  15.9 1.3 collective-permute-start
  17.2 0.2 reduce-window.36
  17.4 0.1 select_reduce_fusion.1
  17.5 2.5 %gather_fusion.4 = bf16[3,2,64,1536]{3,2,1,0:T(8,128)(2,1)S(1)} fusion(bf16[2,8,64,1536]{3,2,1,0:T(8,128)(2,1)} %copy-done.2, s32[1024]{0:T(1024)S(1)} %pad_clamp_fusion), kind=kCustom, calls=%fused_computation.1.clone | custom fusion | bytes 2359308 | tf_op jit(solution)/shard_map/jit(_take)/gather | solution.py:215
  20.1 3.6 %gather_fusion.3 = bf16[3,2,64,1536]{3,2,1,0:T(8,128)(2,1)} fusion(bf16[2,8,64,1536]{3,2,1,0:T(8,128)(2,1)} %copy-done.2, s32[1024]{0:T(1024)S(1)} %pad_clamp_fusion.1), kind=kCustom, calls=%fused_computation.clone | custom fusion | bytes 2359308 | tf_op jit(solution)/shard_map/jit(_take)/gather | solution.py:214
  23.6 0.2 select_bitcast_fusion
  23.8 1.1 copy-done.3
  24.9 0.2 select_bitcast_fusion.1
  25.1 0.0 copy-start
  25.1 0.0 copy-start.1
  25.1 4.4 %collective-permute-start.1 = (bf16[2,1,64,1536]{3,2,1,0:T(8,128)(2,1)}, bf16[2,1,64,1536]{3,2,1,0:T(8,128)(2,1)S(1)}, u32[]{:S(2)}, u32[]{:S(2)}) collective-permute-start(bf16[2,1,64,1536]{3,2,1,0:T(8,128)(2,1)} %get-tuple-element.18), channel_id=1, source_target_pairs={{1,0},{3,2},{5,4},{7,6},{9,8},{11,10},{13,12},{15,14},{17,16},{19,... | collective-permute-start | bytes 1179656 | tf_op jit(solution)/shard_map/ppermute | solution.py:34
  29.6 0.2 collective-permute-done.18.rest_16_
  29.8 0.2 collective-permute-start.7
  30.0 1.4 %fusion.17 = (bf16[2,1,64,1536]{3,2,0,1:T(8,128)(2,1)}, bf16[2,1,64,1536]{3,2,0,1:T(8,128)(2,1)}, bf16[2,1,64,1536]{3,2,0,1:T(8,128)(2,1)}, bf16[2,1,64,1536]{3,...) fusion(bf16[2,3,64,1536]{3,2,0,1:T(8,128)(2,1)S(1)} %select_bitcast_fusion, ...), kind=kLoop, calls=%fused_computation.73 | loop fusion | bytes 4718592 | tf_op jit(solution)/shard_map/slice | solution.py:220
  31.4 2.1 %collective-permute-start.5 = (bf16[2,1,64,1536]{3,2,0,1:T(8,128)(2,1)}, bf16[2,1,64,1536]{3,2,0,1:T(8,128)(2,1)S(1)}, u32[]{:S(2)}, u32[]{:S(2)}) collective-permute-start(bf16[2,1,64,1536]{3,2,0,1:T(8,128)(2,1)} %get-tuple-element.12), channel_id=1, source_target_pairs={{0,2},{2,4},{4,6},{6,8},{8,10},{10,12},{12,14},{1,3},{3,5},{5,7},{... | collective-permute-start | bytes 1179656 | tf_op jit(solution)/shard_map/ppermute | solution.py:34
  33.5 4.1 %collective-permute-start.6 = (bf16[2,1,64,1536]{3,2,0,1:T(8,128)(2,1)}, bf16[2,1,64,1536]{3,2,0,1:T(8,128)(2,1)S(1)}, u32[]{:S(2)}, u32[]{:S(2)}) collective-permute-start(bf16[2,1,64,1536]{3,2,0,1:T(8,128)(2,1)} %get-tuple-element.13), channel_id=1, source_target_pairs={{2,0},{4,2},{6,4},{8,6},{10,8},{12,10},{14,12},{3,1},{5,3},{7,5},{... | collective-permute-start | bytes 1179656 | tf_op jit(solution)/shard_map/ppermute | solution.py:34
  37.6 1.3 %collective-permute-start.20 = (bf16[2,1,64,1536]{3,2,1,0:T(8,128)(2,1)}, bf16[2,1,64,1536]{3,2,1,0:T(8,128)(2,1)}, u32[]{:S(2)}, u32[]{:S(2)}) collective-permute-start(bf16[2,1,64,1536]{3,2,1,0:T(8,128)(2,1)} %collective-permute-done.18.rest_16_), channel_id=1, source_target_pairs={{4,0},{8,4},{12,8},{14,12},{10,14},{6,10},{2,6},{0,2},{5,1},{9,5},... | collective-permute-start | bytes 1179656 | tf_op jit(solution)/shard_map/ppermute | solution.py:70
  39.0 1.1 collective-permute-start.14
  40.1 0.3 collective-permute-start.10
  40.5 0.7 dynamic_slice.3
  41.1 0.6 gather_fusion
  41.8 1.2 fusion.6
  43.0 1.5 %collective-permute-done.5 = bf16[2,1,64,1536]{3,2,0,1:T(8,128)(2,1)S(1)} collective-permute-done((bf16[2,1,64,1536]{3,2,0,1:T(8,128)(2,1)}, bf16[2,1,64,1536]{3,2,0,1:T(8,128)(2,1)S(1)}, u32[]{:S(2)}, u32[]{:S(2)}) %collective-permute-start.5) | collective-permute-done | bytes 393248 | tf_op jit(solution)/shard_map/ppermute | solution.py:34
  44.5 2.1 %collective-permute-start.19 = (bf16[2,1,64,1536]{3,2,1,0:T(8,128)(2,1)}, bf16[2,1,64,1536]{3,2,1,0:T(8,128)(2,1)}, u32[]{:S(2)}, u32[]{:S(2)}) collective-permute-start(bf16[2,1,64,1536]{3,2,1,0:T(8,128)(2,1)} %collective-permute-done.17.rest_15_), channel_id=1, source_target_pairs={{0,4},{4,8},{8,12},{12,14},{14,10},{10,6},{6,2},{2,0},{1,5},{5,9},... | collective-permute-start | bytes 1179656 | tf_op jit(solution)/shard_map/ppermute | solution.py:67
  46.6 7.3 %collective-permute-done.6 = bf16[2,1,64,1536]{3,2,0,1:T(8,128)(2,1)S(1)} collective-permute-done((bf16[2,1,64,1536]{3,2,0,1:T(8,128)(2,1)}, bf16[2,1,64,1536]{3,2,0,1:T(8,128)(2,1)S(1)}, u32[]{:S(2)}, u32[]{:S(2)}) %collective-permute-start.6) | collective-permute-done | bytes 393248 | tf_op jit(solution)/shard_map/ppermute | solution.py:34
  53.9 1.9 %collective-permute-start.8 = (bf16[2,1,64,1536]{3,2,0,1:T(8,128)(2,1)}, bf16[2,1,64,1536]{3,2,0,1:T(8,128)(2,1)}, u32[]{:S(2)}, u32[]{:S(2)}) collective-permute-start(bf16[2,1,64,1536]{3,2,0,1:T(8,128)(2,1)} %get-tuple-element.14), channel_id=1, source_target_pairs={{0,2},{2,4},{4,6},{6,8},{8,10},{10,12},{12,14},{1,3},{3,5},{5,7},{... | collective-permute-start | bytes 1179656 | tf_op jit(solution)/shard_map/ppermute | solution.py:34
  55.8 9.3 %collective-permute-done.20.rest_18_ = bf16[2,1,64,1536]{3,2,1,0:T(8,128)(2,1)} collective-permute-done((bf16[2,1,64,1536]{3,2,1,0:T(8,128)(2,1)}, bf16[2,1,64,1536]{3,2,1,0:T(8,128)(2,1)}, u32[]{:S(2)}, u32[]{:S(2)}) %collective-permute-start.20) | collective-permute-done | bytes 393248 | tf_op jit(solution)/shard_map/ppermute | solution.py:70
  65.0 1.9 %collective-permute-start.9 = (bf16[2,1,64,1536]{3,2,0,1:T(8,128)(2,1)}, bf16[2,1,64,1536]{3,2,0,1:T(8,128)(2,1)}, u32[]{:S(2)}, u32[]{:S(2)}) collective-permute-start(bf16[2,1,64,1536]{3,2,0,1:T(8,128)(2,1)} %get-tuple-element.15), channel_id=1, source_target_pairs={{2,0},{4,2},{6,4},{8,6},{10,8},{12,10},{14,12},{3,1},{5,3},{7,5},{... | collective-permute-start | bytes 1179656 | tf_op jit(solution)/shard_map/ppermute | solution.py:34
  67.0 12.2 %collective-permute-done.14.rest_11_ = bf16[2,1,64,1536]{3,2,1,0:T(8,128)(2,1)S(1)} collective-permute-done((bf16[2,1,64,1536]{3,2,1,0:T(8,128)(2,1)S(1)}, bf16[2,1,64,1536]{3,2,1,0:T(8,128)(2,1)S(1)}, u32[]{:S(2)}, u32[]{:S(2)}) %collective-permute-start.14) | collective-permute-done | bytes 393248 | tf_op jit(solution)/shard_map/ppermute | solution.py:70
  79.2 1.3 %fusion.15 = s32[4]{0:T(128)S(1)} fusion(s32[4]{0:T(128)S(1)} %gather_fusion, s32[]{:T(128)} %bitcast.5, s32[1,1,4]{2,1,0:T(1,128)} %param.18), kind=kLoop, calls=%fused_computation.68 | loop fusion | flops 140 | bytes 52 | tf_op jit(solution)/shard_map/concatenate | solution.py:240
  80.5 1.4 %reduce-window.34 = s32[4,1]{0,1:T(1,128)} reduce-window(s32[4,1]{0,1:T(1,128)} %get-tuple-element.32, s32[]{:T(128)} %constant.98.clone), window={size=4x1 pad=3_0x0_0}, to_apply=%region_0.1 | reduce-window | flops 12 | bytes 36 | tf_op jit(solution)/shard_map/reduce-window.14
  81.9 0.7 reduce-window.35
  82.7 0.6 gather_fusion.1
  83.3 0.6 gather_fusion.2
  83.9 0.1 pad_bitcast_fusion
  84.0 0.7 compare_select_fusion.10
  84.7 1.5 %collective-permute-start.21 = (bf16[2,1,64,1536]{3,2,1,0:T(8,128)(2,1)}, bf16[2,1,64,1536]{3,2,1,0:T(8,128)(2,1)}, u32[]{:S(2)}, u32[]{:S(2)}) collective-permute-start(bf16[2,1,64,1536]{3,2,1,0:T(8,128)(2,1)} %collective-permute-done.19.rest_17_), channel_id=1, source_target_pairs={{0,4},{4,8},{8,12},{12,14},{14,10},{10,6},{6,2},{2,0},{1,5},{5,9},... | collective-permute-start | bytes 1179656 | tf_op jit(solution)/shard_map/ppermute | solution.py:67
  86.2 4.1 %collective-permute-start.11 = (bf16[2,1,64,1536]{3,2,0,1:T(8,128)(2,1)}, bf16[2,1,64,1536]{3,2,0,1:T(8,128)(2,1)}, u32[]{:S(2)}, u32[]{:S(2)}) collective-permute-start(bf16[2,1,64,1536]{3,2,0,1:T(8,128)(2,1)} %get-tuple-element.16), channel_id=1, source_target_pairs={{12,14},{13,15},{28,30},{29,31}} | collective-permute-start | bytes 1179656 | tf_op jit(solution)/shard_map/ppermute | solution.py:227
  90.3 1.4 %collective-permute-start.12 = (bf16[2,1,64,1536]{3,2,0,1:T(8,128)(2,1)}, bf16[2,1,64,1536]{3,2,0,1:T(8,128)(2,1)}, u32[]{:S(2)}, u32[]{:S(2)}) collective-permute-start(bf16[2,1,64,1536]{3,2,0,1:T(8,128)(2,1)} %get-tuple-element.17), channel_id=1, source_target_pairs={{2,0},{3,1},{18,16},{19,17}} | collective-permute-start | bytes 1179656 | tf_op jit(solution)/shard_map/ppermute | solution.py:228
  91.7 4.4 %collective-permute-done.22.rest_20_ = bf16[2,1,64,1536]{3,2,1,0:T(8,128)(2,1)} collective-permute-done((bf16[2,1,64,1536]{3,2,1,0:T(8,128)(2,1)}, bf16[2,1,64,1536]{3,2,1,0:T(8,128)(2,1)}, u32[]{:S(2)}, u32[]{:S(2)}) %collective-permute-start.22) | collective-permute-done | bytes 393248 | tf_op jit(solution)/shard_map/ppermute | solution.py:70
  96.1 8.4 %collective-permute-done.15.rest_13_ = bf16[2,1,64,1536]{3,2,1,0:T(8,128)(2,1)} collective-permute-done((bf16[2,1,64,1536]{3,2,1,0:T(8,128)(2,1)S(1)}, bf16[2,1,64,1536]{3,2,1,0:T(8,128)(2,1)}, u32[]{:S(2)}, u32[]{:S(2)}) %collective-permute-start.15) | collective-permute-done | bytes 393248 | tf_op jit(solution)/shard_map/ppermute | solution.py:70
  104.5 0.1 add_bitcast_fusion
  104.6 0.1 copy.31
  104.7 0.1 reshape.421.table_ref
  104.8 6.0 %collective-permute-done.16.rest_14_ = bf16[2,1,64,1536]{3,2,1,0:T(8,128)(2,1)} collective-permute-done((bf16[2,1,64,1536]{3,2,1,0:T(8,128)(2,1)S(1)}, bf16[2,1,64,1536]{3,2,1,0:T(8,128)(2,1)}, u32[]{:S(2)}, u32[]{:S(2)}) %collective-permute-start.16) | collective-permute-done | bytes 393248 | tf_op jit(solution)/shard_map/ppermute | solution.py:62
  110.9 4.2 %collective-permute-done.23.rest_21_ = bf16[2,1,64,1536]{3,2,1,0:T(8,128)(2,1)} collective-permute-done((bf16[2,1,64,1536]{3,2,1,0:T(8,128)(2,1)}, bf16[2,1,64,1536]{3,2,1,0:T(8,128)(2,1)}, u32[]{:S(2)}, u32[]{:S(2)}) %collective-permute-start.23) | collective-permute-done | bytes 393248 | tf_op jit(solution)/shard_map/ppermute | solution.py:64
  115.0 15.2 %shard_map.100 = bf16[512,1536]{1,0:T(8,128)(2,1)} custom-call(s32[16]{0:T(128)S(1)} %reshape.421.table_ref, bf16[512,1536]{1,0:T(8,128)(2,1)} %bitcast.92, bf16[2,8,64,1536]{3,2,1,0:T(8,128)(2,1)} %copy-done.2, bf16[2,1,64,1536]{3,2,1,0:T(8,128)(2,1)S(1)} %collective-permute-done.rest_0_, bf16[2,1,64,1536]{3,2,1,0:T(8,128)(2,1)S(1)} %collective-permute-done.1.rest_1_, ...), custom_call_target="tpu_custom_call" | custom-call | flops 3221225472 | bytes 9437184 | tf_op jit(solution)/shard_map/pallas_call | solution.py:154
  (44 shorter events, 0.2 us)
Async XLA Ops:
  0.0 14.2 %collective-permute-start.3 = (s32[4]{0:T(128)}, s32[4]{0:T(128)S(1)}, u32[]{:S(2)}, u32[]{:S(2)}) collective-permute-start(s32[4]{0:T(128)} %bitcast.93), channel_id=1, source_target_pairs={{0,2},{2,4},{4,6},{6,8},{8,10},{10,12},{12,14},{1,3},{3,5},{5,7},{... | collective-permute-start | bytes 56 | tf_op jit(solution)/shard_map/ppermute | solution.py:34
  3.1 12.7 %collective-permute-start.2 = (s32[4]{0:T(128)}, s32[4]{0:T(128)S(1)}, u32[]{:S(2)}, u32[]{:S(2)}) collective-permute-start(s32[4]{0:T(128)} %bitcast.94), channel_id=1, source_target_pairs={{2,0},{4,2},{6,4},{8,6},{10,8},{12,10},{14,12},{3,1},{5,3},{7,5},{... | collective-permute-start | bytes 56 | tf_op jit(solution)/shard_map/ppermute | solution.py:34
  8.1 1.9 %copy-start.4 = (bf16[8,1,64,1536]{3,2,1,0:T(8,128)(2,1)S(1)}, bf16[8,1,64,1536]{3,2,1,0:T(8,128)(2,1)}, u32[]{:S(2)}) copy-start(bf16[8,1,64,1536]{3,2,1,0:T(8,128)(2,1)} %param.15) | copy-start | bytes 4718596
  10.6 2.6 %copy-start.2 = (bf16[2,8,64,1536]{3,2,1,0:T(8,128)(2,1)}, bf16[2,8,64,1536]{3,2,1,0:T(8,128)(2,1)S(1)}, u32[]{:S(2)}) copy-start(bf16[2,8,64,1536]{3,2,1,0:T(8,128)(2,1)S(1)} %maximum_bitcast_fusion.own_hbm) | copy-start | bytes 9437188
  11.6 13.5 %collective-permute-start.4 = (bf16[2,1,64,1536]{3,2,1,0:T(8,128)(2,1)}, bf16[2,1,64,1536]{3,2,1,0:T(8,128)(2,1)S(1)}, u32[]{:S(2)}, u32[]{:S(2)}) collective-permute-start(bf16[2,1,64,1536]{3,2,1,0:T(8,128)(2,1)} %get-tuple-element.27), channel_id=1, source_target_pairs={{0,4},{4,8},{8,12},{12,14},{14,10},{10,6},{6,2},{2,0},{1,5},{5,9},... | collective-permute-start | bytes 1179656 | tf_op jit(solution)/shard_map/ppermute | solution.py:67
  12.0 19.4 %collective-permute-start.13 = (bf16[2,1,64,1536]{3,2,1,0:T(8,128)(2,1)}, bf16[2,1,64,1536]{3,2,1,0:T(8,128)(2,1)S(1)}, u32[]{:S(2)}, u32[]{:S(2)}) collective-permute-start(bf16[2,1,64,1536]{3,2,1,0:T(8,128)(2,1)} %get-tuple-element.27), channel_id=1, source_target_pairs={{4,0},{8,4},{12,8},{14,12},{10,14},{6,10},{2,6},{0,2},{5,1},{9,5},... | collective-permute-start | bytes 1179656 | tf_op jit(solution)/shard_map/ppermute | solution.py:70
  13.1 16.7 %collective-permute-start.18 = (bf16[2,1,64,1536]{3,2,1,0:T(8,128)(2,1)S(1)}, bf16[2,1,64,1536]{3,2,1,0:T(8,128)(2,1)}, u32[]{:S(2)}, u32[]{:S(2)}) collective-permute-start(bf16[2,1,64,1536]{3,2,1,0:T(8,128)(2,1)S(1)} %get-tuple-element.26), channel_id=1, source_target_pairs={{4,0},{8,4},{12,8},{14,12},{10,14},{6,10},{2,6},{0,2},{5,1},{9,5},... | collective-permute-start | bytes 1179656 | tf_op jit(solution)/shard_map/ppermute | solution.py:70
  14.2 19.2 %collective-permute-start.17 = (bf16[2,1,64,1536]{3,2,1,0:T(8,128)(2,1)S(1)}, bf16[2,1,64,1536]{3,2,1,0:T(8,128)(2,1)}, u32[]{:S(2)}, u32[]{:S(2)}) collective-permute-start(bf16[2,1,64,1536]{3,2,1,0:T(8,128)(2,1)S(1)} %get-tuple-element.26), channel_id=1, source_target_pairs={{0,4},{4,8},{8,12},{12,14},{14,10},{10,6},{6,2},{2,0},{1,5},{5,9},... | collective-permute-start | bytes 1179656 | tf_op jit(solution)/shard_map/ppermute | solution.py:67
  15.9 21.7 %collective-permute-start = (bf16[2,1,64,1536]{3,2,1,0:T(8,128)(2,1)}, bf16[2,1,64,1536]{3,2,1,0:T(8,128)(2,1)S(1)}, u32[]{:S(2)}, u32[]{:S(2)}) collective-permute-start(bf16[2,1,64,1536]{3,2,1,0:T(8,128)(2,1)} %get-tuple-element.19), channel_id=1, source_target_pairs={{0,1},{2,3},{4,5},{6,7},{8,9},{10,11},{12,13},{14,15},{16,17},{18,... | collective-permute-start | bytes 1179656 | tf_op jit(solution)/shard_map/ppermute | solution.py:34
  23.6 1.3 copy-start.3
  25.1 15.3 %copy-start.5 = (s32[1,1,4]{2,1,0:T(1,128)S(1)}, s32[1,1,4]{2,1,0:T(1,128)}, u32[]{:S(2)}) copy-start(s32[1,1,4]{2,1,0:T(1,128)} %param.18) | copy-start | bytes 52
  25.1 15.3 %copy-start = (s32[8]{0:T(128)S(1)}, s32[8]{0:T(128)}, u32[]{:S(2)}) copy-start(s32[8]{0:T(128)} %constant.96.clone) | copy-start | bytes 100
  25.1 57.5 %copy-start.1 = (s32[7,2]{1,0:T(8,128)S(1)}, s32[7,2]{1,0:T(8,128)}, u32[]{:S(2)}) copy-start(s32[7,2]{1,0:T(8,128)} %constant.97.clone) | copy-start | bytes 172
  25.1 13.8 %collective-permute-start.1 = (bf16[2,1,64,1536]{3,2,1,0:T(8,128)(2,1)}, bf16[2,1,64,1536]{3,2,1,0:T(8,128)(2,1)S(1)}, u32[]{:S(2)}, u32[]{:S(2)}) collective-permute-start(bf16[2,1,64,1536]{3,2,1,0:T(8,128)(2,1)} %get-tuple-element.18), channel_id=1, source_target_pairs={{1,0},{3,2},{5,4},{7,6},{9,8},{11,10},{13,12},{15,14},{17,16},{19,... | collective-permute-start | bytes 1179656 | tf_op jit(solution)/shard_map/ppermute | solution.py:34
  29.8 10.3 %collective-permute-start.7 = (bf16[2,1,64,1536]{3,2,1,0:T(8,128)(2,1)S(1)}, bf16[2,1,64,1536]{3,2,1,0:T(8,128)(2,1)S(1)}, u32[]{:S(2)}, u32[]{:S(2)}) collective-permute-start(bf16[2,1,64,1536]{3,2,1,0:T(8,128)(2,1)S(1)} %collective-permute-done.4.rest_8_), channel_id=1, source_target_pairs={{0,4},{4,8},{8,12},{12,14},{14,10},{10,6},{6,2},{2,0},{1,5},{5,9},... | collective-permute-start | bytes 1179656 | tf_op jit(solution)/shard_map/ppermute | solution.py:67
  31.4 13.1 %collective-permute-start.5 = (bf16[2,1,64,1536]{3,2,0,1:T(8,128)(2,1)}, bf16[2,1,64,1536]{3,2,0,1:T(8,128)(2,1)S(1)}, u32[]{:S(2)}, u32[]{:S(2)}) collective-permute-start(bf16[2,1,64,1536]{3,2,0,1:T(8,128)(2,1)} %get-tuple-element.12), channel_id=1, source_target_pairs={{0,2},{2,4},{4,6},{6,8},{8,10},{10,12},{12,14},{1,3},{3,5},{5,7},{... | collective-permute-start | bytes 1179656 | tf_op jit(solution)/shard_map/ppermute | solution.py:34
  33.5 20.4 %collective-permute-start.6 = (bf16[2,1,64,1536]{3,2,0,1:T(8,128)(2,1)}, bf16[2,1,64,1536]{3,2,0,1:T(8,128)(2,1)S(1)}, u32[]{:S(2)}, u32[]{:S(2)}) collective-permute-start(bf16[2,1,64,1536]{3,2,0,1:T(8,128)(2,1)} %get-tuple-element.13), channel_id=1, source_target_pairs={{2,0},{4,2},{6,4},{8,6},{10,8},{12,10},{14,12},{3,1},{5,3},{7,5},{... | collective-permute-start | bytes 1179656 | tf_op jit(solution)/shard_map/ppermute | solution.py:34
  37.6 27.4 %collective-permute-start.20 = (bf16[2,1,64,1536]{3,2,1,0:T(8,128)(2,1)}, bf16[2,1,64,1536]{3,2,1,0:T(8,128)(2,1)}, u32[]{:S(2)}, u32[]{:S(2)}) collective-permute-start(bf16[2,1,64,1536]{3,2,1,0:T(8,128)(2,1)} %collective-permute-done.18.rest_16_), channel_id=1, source_target_pairs={{4,0},{8,4},{12,8},{14,12},{10,14},{6,10},{2,6},{0,2},{5,1},{9,5},... | collective-permute-start | bytes 1179656 | tf_op jit(solution)/shard_map/ppermute | solution.py:70
  39.0 40.2 %collective-permute-start.14 = (bf16[2,1,64,1536]{3,2,1,0:T(8,128)(2,1)S(1)}, bf16[2,1,64,1536]{3,2,1,0:T(8,128)(2,1)S(1)}, u32[]{:S(2)}, u32[]{:S(2)}) collective-permute-start(bf16[2,1,64,1536]{3,2,1,0:T(8,128)(2,1)S(1)} %collective-permute-done.13.rest_9_), channel_id=1, source_target_pairs={{4,0},{8,4},{12,8},{14,12},{10,14},{6,10},{2,6},{0,2},{5,1},{9,5},... | collective-permute-start | bytes 1179656 | tf_op jit(solution)/shard_map/ppermute | solution.py:70
  40.1 39.1 %collective-permute-start.10 = (bf16[2,1,64,1536]{3,2,1,0:T(8,128)(2,1)S(1)}, bf16[2,1,64,1536]{3,2,1,0:T(8,128)(2,1)S(1)}, u32[]{:S(2)}, u32[]{:S(2)}) collective-permute-start(bf16[2,1,64,1536]{3,2,1,0:T(8,128)(2,1)S(1)} %collective-permute-done.7.rest_10_), channel_id=1, source_target_pairs={{0,4},{4,8},{8,12},{12,14},{14,10},{10,6},{6,2},{2,0},{1,5},{5,9},... | collective-permute-start | bytes 1179656 | tf_op jit(solution)/shard_map/ppermute | solution.py:67
  44.5 40.2 %collective-permute-start.19 = (bf16[2,1,64,1536]{3,2,1,0:T(8,128)(2,1)}, bf16[2,1,64,1536]{3,2,1,0:T(8,128)(2,1)}, u32[]{:S(2)}, u32[]{:S(2)}) collective-permute-start(bf16[2,1,64,1536]{3,2,1,0:T(8,128)(2,1)} %collective-permute-done.17.rest_15_), channel_id=1, source_target_pairs={{0,4},{4,8},{8,12},{12,14},{14,10},{10,6},{6,2},{2,0},{1,5},{5,9},... | collective-permute-start | bytes 1179656 | tf_op jit(solution)/shard_map/ppermute | solution.py:67
  53.9 32.4 %collective-permute-start.8 = (bf16[2,1,64,1536]{3,2,0,1:T(8,128)(2,1)}, bf16[2,1,64,1536]{3,2,0,1:T(8,128)(2,1)}, u32[]{:S(2)}, u32[]{:S(2)}) collective-permute-start(bf16[2,1,64,1536]{3,2,0,1:T(8,128)(2,1)} %get-tuple-element.14), channel_id=1, source_target_pairs={{0,2},{2,4},{4,6},{6,8},{8,10},{10,12},{12,14},{1,3},{3,5},{5,7},{... | collective-permute-start | bytes 1179656 | tf_op jit(solution)/shard_map/ppermute | solution.py:34
  65.0 25.3 %collective-permute-start.9 = (bf16[2,1,64,1536]{3,2,0,1:T(8,128)(2,1)}, bf16[2,1,64,1536]{3,2,0,1:T(8,128)(2,1)}, u32[]{:S(2)}, u32[]{:S(2)}) collective-permute-start(bf16[2,1,64,1536]{3,2,0,1:T(8,128)(2,1)} %get-tuple-element.15), channel_id=1, source_target_pairs={{2,0},{4,2},{6,4},{8,6},{10,8},{12,10},{14,12},{3,1},{5,3},{7,5},{... | collective-permute-start | bytes 1179656 | tf_op jit(solution)/shard_map/ppermute | solution.py:34
  79.1 17.0 %collective-permute-start.22 = (bf16[2,1,64,1536]{3,2,1,0:T(8,128)(2,1)}, bf16[2,1,64,1536]{3,2,1,0:T(8,128)(2,1)}, u32[]{:S(2)}, u32[]{:S(2)}) collective-permute-start(bf16[2,1,64,1536]{3,2,1,0:T(8,128)(2,1)} %collective-permute-done.20.rest_18_), channel_id=1, source_target_pairs={{4,0},{8,4},{12,8},{14,12},{10,14},{6,10},{2,6},{0,2},{5,1},{9,5},... | collective-permute-start | bytes 1179656 | tf_op jit(solution)/shard_map/ppermute | solution.py:70
  79.1 25.4 %collective-permute-start.15 = (bf16[2,1,64,1536]{3,2,1,0:T(8,128)(2,1)S(1)}, bf16[2,1,64,1536]{3,2,1,0:T(8,128)(2,1)}, u32[]{:S(2)}, u32[]{:S(2)}) collective-permute-start(bf16[2,1,64,1536]{3,2,1,0:T(8,128)(2,1)S(1)} %collective-permute-done.14.rest_11_), channel_id=1, source_target_pairs={{4,0},{8,4},{12,8},{14,12},{10,14},{6,10},{2,6},{0,2},{5,1},{9,5},... | collective-permute-start | bytes 1179656 | tf_op jit(solution)/shard_map/ppermute | solution.py:70
  84.7 20.1 %collective-permute-start.21 = (bf16[2,1,64,1536]{3,2,1,0:T(8,128)(2,1)}, bf16[2,1,64,1536]{3,2,1,0:T(8,128)(2,1)}, u32[]{:S(2)}, u32[]{:S(2)}) collective-permute-start(bf16[2,1,64,1536]{3,2,1,0:T(8,128)(2,1)} %collective-permute-done.19.rest_17_), channel_id=1, source_target_pairs={{0,4},{4,8},{8,12},{12,14},{14,10},{10,6},{6,2},{2,0},{1,5},{5,9},... | collective-permute-start | bytes 1179656 | tf_op jit(solution)/shard_map/ppermute | solution.py:67
  86.2 18.6 %collective-permute-start.11 = (bf16[2,1,64,1536]{3,2,0,1:T(8,128)(2,1)}, bf16[2,1,64,1536]{3,2,0,1:T(8,128)(2,1)}, u32[]{:S(2)}, u32[]{:S(2)}) collective-permute-start(bf16[2,1,64,1536]{3,2,0,1:T(8,128)(2,1)} %get-tuple-element.16), channel_id=1, source_target_pairs={{12,14},{13,15},{28,30},{29,31}} | collective-permute-start | bytes 1179656 | tf_op jit(solution)/shard_map/ppermute | solution.py:227
  90.3 14.5 %collective-permute-start.12 = (bf16[2,1,64,1536]{3,2,0,1:T(8,128)(2,1)}, bf16[2,1,64,1536]{3,2,0,1:T(8,128)(2,1)}, u32[]{:S(2)}, u32[]{:S(2)}) collective-permute-start(bf16[2,1,64,1536]{3,2,0,1:T(8,128)(2,1)} %get-tuple-element.17), channel_id=1, source_target_pairs={{2,0},{3,1},{18,16},{19,17}} | collective-permute-start | bytes 1179656 | tf_op jit(solution)/shard_map/ppermute | solution.py:228
  96.1 14.8 %collective-permute-start.16 = (bf16[2,1,64,1536]{3,2,1,0:T(8,128)(2,1)S(1)}, bf16[2,1,64,1536]{3,2,1,0:T(8,128)(2,1)}, u32[]{:S(2)}, u32[]{:S(2)}) collective-permute-start(bf16[2,1,64,1536]{3,2,1,0:T(8,128)(2,1)S(1)} %collective-permute-done.10.rest_12_), channel_id=1, source_target_pairs={{0,4},{4,8},{8,12},{12,14},{14,10},{10,6},{6,2},{2,0},{1,5},{5,9},... | collective-permute-start | bytes 1179656 | tf_op jit(solution)/shard_map/ppermute | solution.py:62
  104.5 10.5 %collective-permute-start.23 = (bf16[2,1,64,1536]{3,2,1,0:T(8,128)(2,1)}, bf16[2,1,64,1536]{3,2,1,0:T(8,128)(2,1)}, u32[]{:S(2)}, u32[]{:S(2)}) collective-permute-start(bf16[2,1,64,1536]{3,2,1,0:T(8,128)(2,1)} %collective-permute-done.22.rest_20_), channel_id=1, source_target_pairs={{4,0},{8,4},{12,8},{14,12},{10,14},{6,10},{2,6},{0,2},{5,1},{9,5},... | collective-permute-start | bytes 1179656 | tf_op jit(solution)/shard_map/ppermute | solution.py:64

commit v20 on v17

--- a/solution.py
+++ b/solution.py
@@ -218,7 +218,7 @@
     for slot in range(edge_cap):
         to_r = right_payload[:, slot : slot + 1]
         to_l = left_payload[:, slot : slot + 1]
-        later = far_sources[min(2 * slot, len(far_sources) - 1)]
+        later = far_sources[min(2 * min(slot, 1), len(far_sources) - 1)]
         to_r, to_l, _ = lax.optimization_barrier((to_r, to_l, later))
         if slot < main_cap:
             cycle_sources.append(shift(to_r, "col", col_count, 1))

time: 131 us -> 132 us (level)
  the two profiles are of different devices: /device:TPU:19 before, /device:TPU:18 now
where the time goes in v20:
time: 132 us; the launch traced here: 131 us
  starting transfers between devices  50.3 us (38%)
  waiting for transfers between devices  42.9 us (32%)
  Pallas kernels  14.3 us (11%)
  local copies, waits for them, and re-layouts  13.5 us (10%)
  other arithmetic  10 us (8%)
    ppermute x6, starting transfers between devices, ring_gather(): ahead = lax.ppermute(ahead, 'col', forward)  23 us
    ppermute x6, waiting for transfers between devices, ring_gather(): behind = lax.ppermute(behind, 'col', backward)  22.4 us
    ppermute x8, starting transfers between devices, shift(): return lax.ppermute(x, axis, pairs)  20 us
    pallas_call x1, Pallas kernels, gather_attend(): pl.pallas_call(kernel, out_shape=jax.ShapeDtypeStruct((token_count, width...  14.3 us
    ppermute x8, waiting for transfers between devices, shift(): return lax.ppermute(x, axis, pairs)  13.1 us
    ppermute x1, waiting for transfers between devices, ring_gather(): arrays.append(lax.ppermute(behind, 'col', backward))  7.28 us
    gather x1, local copies, waits for them, and re-layouts, per_device(): right_payload = jnp.take(stacked, to_right, axis=1)  3.56 us
    another operation x4, other arithmetic  3.02 us
  transfers between devices with their start and end apart: 24, of which 9 were waited for; matrix products, arithmetic and copies ran while one was open for 17% of the time, Pallas kernels for 0%

profile of v20, /device:TPU:18, one launch (start us, length us, event | category | flops | bytes accessed | tf_op | source)
XLA Modules:
  0.0 131.5 jit_solution(16692077170039148665)
XLA Ops:
  0.0 3.4 %collective-permute-start.3 = (s32[4]{0:T(128)}, s32[4]{0:T(128)S(1)}, u32[]{:S(2)}, u32[]{:S(2)}) collective-permute-start(s32[4]{0:T(128)} %bitcast.94), channel_id=1, source_target_pairs={{0,2},{2,4},{4,6},{6,8},{8,10},{10,12},{12,14},{1,3},{3,5},{5,7},{... | collective-permute-start | bytes 56 | tf_op jit(solution)/shard_map/ppermute | solution.py:34
  3.4 3.3 %collective-permute-start.2 = (s32[4]{0:T(128)}, s32[4]{0:T(128)S(1)}, u32[]{:S(2)}, u32[]{:S(2)}) collective-permute-start(s32[4]{0:T(128)} %bitcast.95), channel_id=1, source_target_pairs={{2,0},{4,2},{6,4},{8,6},{10,8},{12,10},{14,12},{3,1},{5,3},{7,5},{... | collective-permute-start | bytes 56 | tf_op jit(solution)/shard_map/ppermute | solution.py:34
  6.8 1.0 exponential_bitcast_fusion.1
  7.7 1.0 exponential_bitcast_fusion
  8.7 1.8 %fusion.1 = bf16[8,1,64,1536]{3,2,0,1:T(8,128)(2,1)S(1)} fusion(bf16[8,1,64,1536]{3,2,1,0:T(8,128)(2,1)} %param.13, f32[8,2,1536]{2,1,0:T(2,128)S(1)} %exponential_bitcast_fusion.1), kind=kLoop, calls=%fused_computation.9 | loop fusion | flops 2359296 | bytes 3244032 | tf_op jit(solution)/shard_map/convert_element_type | solution.py:24
  10.5 0.1 copy-done.4
  10.6 0.3 fusion
  10.9 0.3 maximum_bitcast_fusion.own_hbm
  11.3 1.1 fusion.19
  12.4 1.6 %collective-permute-start.4 = (bf16[2,1,64,1536]{3,2,1,0:T(8,128)(2,1)}, bf16[2,1,64,1536]{3,2,1,0:T(8,128)(2,1)S(1)}, u32[]{:S(2)}, u32[]{:S(2)}) collective-permute-start(bf16[2,1,64,1536]{3,2,1,0:T(8,128)(2,1)} %get-tuple-element.27), channel_id=1, source_target_pairs={{0,4},{4,8},{8,12},{12,14},{14,10},{10,6},{6,2},{2,0},{1,5},{5,9},... | collective-permute-start | bytes 1179656 | tf_op jit(solution)/shard_map/ppermute | solution.py:67
  13.9 0.4 collective-permute-start.12
  14.4 0.4 collective-permute-start.18
  14.8 0.9 fusion.16
  15.8 1.6 %collective-permute-start.17 = (bf16[2,1,64,1536]{3,2,1,0:T(8,128)(2,1)}, bf16[2,1,64,1536]{3,2,1,0:T(8,128)(2,1)}, u32[]{:S(2)}, u32[]{:S(2)}) collective-permute-start(bf16[2,1,64,1536]{3,2,1,0:T(8,128)(2,1)} %get-tuple-element.26), channel_id=1, source_target_pairs={{0,4},{4,8},{8,12},{12,14},{14,10},{10,6},{6,2},{2,0},{1,5},{5,9},... | collective-permute-start | bytes 1179656 | tf_op jit(solution)/shard_map/ppermute | solution.py:67
  17.3 0.2 reduce-window.37
  17.5 0.1 select_reduce_fusion
  17.7 1.3 collective-permute-start
  19.0 0.2 reduce-window.36
  19.2 0.1 select_reduce_fusion.1
  19.4 2.5 %gather_fusion.4 = bf16[3,2,64,1536]{3,2,1,0:T(8,128)(2,1)S(1)} fusion(bf16[2,8,64,1536]{3,2,1,0:T(8,128)(2,1)} %copy-done.2, s32[1024]{0:T(1024)S(1)} %pad_clamp_fusion), kind=kCustom, calls=%fused_computation.1.clone | custom fusion | bytes 2359308 | tf_op jit(solution)/shard_map/jit(_take)/gather | solution.py:215
  21.9 3.6 %gather_fusion.3 = bf16[3,2,64,1536]{3,2,1,0:T(8,128)(2,1)} fusion(bf16[2,8,64,1536]{3,2,1,0:T(8,128)(2,1)} %copy-done.2, s32[1024]{0:T(1024)S(1)} %pad_clamp_fusion.1), kind=kCustom, calls=%fused_computation.clone | custom fusion | bytes 2359308 | tf_op jit(solution)/shard_map/jit(_take)/gather | solution.py:214
  25.5 0.2 select_bitcast_fusion
  25.6 1.1 copy-done.3
  26.7 0.2 select_bitcast_fusion.1
  27.0 1.4 %collective-permute-start.1 = (bf16[2,1,64,1536]{3,2,1,0:T(8,128)(2,1)}, bf16[2,1,64,1536]{3,2,1,0:T(8,128)(2,1)S(1)}, u32[]{:S(2)}, u32[]{:S(2)}) collective-permute-start(bf16[2,1,64,1536]{3,2,1,0:T(8,128)(2,1)} %get-tuple-element.18), channel_id=1, source_target_pairs={{1,0},{3,2},{5,4},{7,6},{9,8},{11,10},{13,12},{15,14},{17,16},{19,... | collective-permute-start | bytes 1179656 | tf_op jit(solution)/shard_map/ppermute | solution.py:34
  28.4 4.3 %collective-permute-done.18.rest_16_ = bf16[2,1,64,1536]{3,2,1,0:T(8,128)(2,1)} collective-permute-done((bf16[2,1,64,1536]{3,2,1,0:T(8,128)(2,1)}, bf16[2,1,64,1536]{3,2,1,0:T(8,128)(2,1)}, u32[]{:S(2)}, u32[]{:S(2)}) %collective-permute-start.18) | collective-permute-done | bytes 393248 | tf_op jit(solution)/shard_map/ppermute | solution.py:70
  32.7 0.6 collective-permute-start.7
  33.3 1.4 %fusion.17 = (bf16[2,1,64,1536]{3,2,0,1:T(8,128)(2,1)}, bf16[2,1,64,1536]{3,2,0,1:T(8,128)(2,1)}, bf16[2,1,64,1536]{3,2,0,1:T(8,128)(2,1)}, bf16[2,1,64,1536]{3,...) fusion(bf16[2,3,64,1536]{3,2,0,1:T(8,128)(2,1)S(1)} %select_bitcast_fusion, ...), kind=kLoop, calls=%fused_computation.73 | loop fusion | bytes 4718592 | tf_op jit(solution)/shard_map/slice | solution.py:220
  34.7 1.9 %collective-permute-start.5 = (bf16[2,1,64,1536]{3,2,0,1:T(8,128)(2,1)}, bf16[2,1,64,1536]{3,2,0,1:T(8,128)(2,1)S(1)}, u32[]{:S(2)}, u32[]{:S(2)}) collective-permute-start(bf16[2,1,64,1536]{3,2,0,1:T(8,128)(2,1)} %get-tuple-element.12), channel_id=1, source_target_pairs={{0,2},{2,4},{4,6},{6,8},{8,10},{10,12},{12,14},{1,3},{3,5},{5,7},{... | collective-permute-start | bytes 1179656 | tf_op jit(solution)/shard_map/ppermute | solution.py:34
  36.7 4.8 %collective-permute-start.6 = (bf16[2,1,64,1536]{3,2,0,1:T(8,128)(2,1)}, bf16[2,1,64,1536]{3,2,0,1:T(8,128)(2,1)S(1)}, u32[]{:S(2)}, u32[]{:S(2)}) collective-permute-start(bf16[2,1,64,1536]{3,2,0,1:T(8,128)(2,1)} %get-tuple-element.13), channel_id=1, source_target_pairs={{2,0},{4,2},{6,4},{8,6},{10,8},{12,10},{14,12},{3,1},{5,3},{7,5},{... | collective-permute-start | bytes 1179656 | tf_op jit(solution)/shard_map/ppermute | solution.py:34
  41.5 1.5 %collective-permute-start.20 = (bf16[2,1,64,1536]{3,2,1,0:T(8,128)(2,1)}, bf16[2,1,64,1536]{3,2,1,0:T(8,128)(2,1)}, u32[]{:S(2)}, u32[]{:S(2)}) collective-permute-start(bf16[2,1,64,1536]{3,2,1,0:T(8,128)(2,1)} %collective-permute-done.18.rest_16_), channel_id=1, source_target_pairs={{4,0},{8,4},{12,8},{14,12},{10,14},{6,10},{2,6},{0,2},{5,1},{9,5},... | collective-permute-start | bytes 1179656 | tf_op jit(solution)/shard_map/ppermute | solution.py:70
  43.0 0.1 collective-permute-start.13
  43.0 2.0 %collective-permute-start.19 = (bf16[2,1,64,1536]{3,2,1,0:T(8,128)(2,1)}, bf16[2,1,64,1536]{3,2,1,0:T(8,128)(2,1)}, u32[]{:S(2)}, u32[]{:S(2)}) collective-permute-start(bf16[2,1,64,1536]{3,2,1,0:T(8,128)(2,1)} %collective-permute-done.17.rest_15_), channel_id=1, source_target_pairs={{0,4},{4,8},{8,12},{12,14},{14,10},{10,6},{6,2},{2,0},{1,5},{5,9},... | collective-permute-start | bytes 1179656 | tf_op jit(solution)/shard_map/ppermute | solution.py:67
  45.0 0.6 dynamic_slice.3
  45.6 0.6 gather_fusion
  46.3 0.6 fusion.6
  46.9 5.1 %collective-permute-done.5 = bf16[2,1,64,1536]{3,2,0,1:T(8,128)(2,1)S(1)} collective-permute-done((bf16[2,1,64,1536]{3,2,0,1:T(8,128)(2,1)}, bf16[2,1,64,1536]{3,2,0,1:T(8,128)(2,1)S(1)}, u32[]{:S(2)}, u32[]{:S(2)}) %collective-permute-start.5) | collective-permute-done | bytes 393248 | tf_op jit(solution)/shard_map/ppermute | solution.py:34
  52.0 0.7 collective-permute-start.10
  52.7 2.3 %collective-permute-done.6 = bf16[2,1,64,1536]{3,2,0,1:T(8,128)(2,1)S(1)} collective-permute-done((bf16[2,1,64,1536]{3,2,0,1:T(8,128)(2,1)}, bf16[2,1,64,1536]{3,2,0,1:T(8,128)(2,1)S(1)}, u32[]{:S(2)}, u32[]{:S(2)}) %collective-permute-start.6) | collective-permute-done | bytes 393248 | tf_op jit(solution)/shard_map/ppermute | solution.py:34
  55.0 1.4 %collective-permute-start.11 = (bf16[2,1,64,1536]{3,2,0,1:T(8,128)(2,1)}, bf16[2,1,64,1536]{3,2,0,1:T(8,128)(2,1)}, u32[]{:S(2)}, u32[]{:S(2)}) collective-permute-start(bf16[2,1,64,1536]{3,2,0,1:T(8,128)(2,1)} %get-tuple-element.17), channel_id=1, source_target_pairs={{2,0},{3,1},{18,16},{19,17}} | collective-permute-start | bytes 1179656 | tf_op jit(solution)/shard_map/ppermute | solution.py:228
  56.4 4.3 %collective-permute-done.20.rest_18_ = bf16[2,1,64,1536]{3,2,1,0:T(8,128)(2,1)} collective-permute-done((bf16[2,1,64,1536]{3,2,1,0:T(8,128)(2,1)}, bf16[2,1,64,1536]{3,2,1,0:T(8,128)(2,1)}, u32[]{:S(2)}, u32[]{:S(2)}) %collective-permute-start.20) | collective-permute-done | bytes 393248 | tf_op jit(solution)/shard_map/ppermute | solution.py:70
  60.7 1.9 %collective-permute-start.8 = (bf16[2,1,64,1536]{3,2,0,1:T(8,128)(2,1)}, bf16[2,1,64,1536]{3,2,0,1:T(8,128)(2,1)}, u32[]{:S(2)}, u32[]{:S(2)}) collective-permute-start(bf16[2,1,64,1536]{3,2,0,1:T(8,128)(2,1)} %get-tuple-element.14), channel_id=1, source_target_pairs={{0,2},{2,4},{4,6},{6,8},{8,10},{10,12},{12,14},{1,3},{3,5},{5,7},{... | collective-permute-start | bytes 1179656 | tf_op jit(solution)/shard_map/ppermute | solution.py:34
  62.6 2.9 %collective-permute-done.13.rest_11_ = bf16[2,1,64,1536]{3,2,1,0:T(8,128)(2,1)S(1)} collective-permute-done((bf16[2,1,64,1536]{3,2,1,0:T(8,128)(2,1)S(1)}, bf16[2,1,64,1536]{3,2,1,0:T(8,128)(2,1)S(1)}, u32[]{:S(2)}, u32[]{:S(2)}) %collective-permute-start.13) | collective-permute-done | bytes 393248 | tf_op jit(solution)/shard_map/ppermute | solution.py:70
  65.5 15.2 %collective-permute-start.14 = (bf16[2,1,64,1536]{3,2,1,0:T(8,128)(2,1)S(1)}, bf16[2,1,64,1536]{3,2,1,0:T(8,128)(2,1)}, u32[]{:S(2)}, u32[]{:S(2)}) collective-permute-start(bf16[2,1,64,1536]{3,2,1,0:T(8,128)(2,1)S(1)} %collective-permute-done.7.rest_10_), channel_id=1, source_target_pairs={{0,4},{4,8},{8,12},{12,14},{14,10},{10,6},{6,2},{2,0},{1,5},{5,9},... | collective-permute-start | bytes 1179656 | tf_op jit(solution)/shard_map/ppermute | solution.py:67
  80.7 0.6 fusion.15
  81.3 1.3 reduce-window.34
  82.6 1.4 %reduce-window.35 = s32[4,1]{0,1:T(1,128)} reduce-window(s32[4,1]{0,1:T(1,128)} %get-tuple-element.33, s32[]{:T(128)} %constant.98.clone), window={size=4x1 pad=3_0x0_0}, to_apply=%region_1.2 | reduce-window | flops 12 | bytes 36 | tf_op jit(solution)/shard_map/reduce-window.15
  84.0 0.6 gather_fusion.1
  84.6 0.6 gather_fusion.2
  85.3 0.1 pad_bitcast_fusion
  85.3 0.7 compare_select_fusion.10
  86.0 1.9 %collective-permute-start.9 = (bf16[2,1,64,1536]{3,2,0,1:T(8,128)(2,1)}, bf16[2,1,64,1536]{3,2,0,1:T(8,128)(2,1)}, u32[]{:S(2)}, u32[]{:S(2)}) collective-permute-start(bf16[2,1,64,1536]{3,2,0,1:T(8,128)(2,1)} %get-tuple-element.15), channel_id=1, source_target_pairs={{2,0},{4,2},{6,4},{8,6},{10,8},{12,10},{14,12},{3,1},{5,3},{7,5},{... | collective-permute-start | bytes 1179656 | tf_op jit(solution)/shard_map/ppermute | solution.py:34
  87.9 0.1 collective-permute-start.15
  88.0 2.1 %collective-permute-start.21 = (bf16[2,1,64,1536]{3,2,1,0:T(8,128)(2,1)}, bf16[2,1,64,1536]{3,2,1,0:T(8,128)(2,1)}, u32[]{:S(2)}, u32[]{:S(2)}) collective-permute-start(bf16[2,1,64,1536]{3,2,1,0:T(8,128)(2,1)} %collective-permute-done.19.rest_17_), channel_id=1, source_target_pairs={{0,4},{4,8},{8,12},{12,14},{14,10},{10,6},{6,2},{2,0},{1,5},{5,9},... | collective-permute-start | bytes 1179656 | tf_op jit(solution)/shard_map/ppermute | solution.py:67
  90.1 2.7 %collective-permute-start.16 = (bf16[2,1,64,1536]{3,2,1,0:T(8,128)(2,1)}, bf16[2,1,64,1536]{3,2,1,0:T(8,128)(2,1)}, u32[]{:S(2)}, u32[]{:S(2)}) collective-permute-start(bf16[2,1,64,1536]{3,2,1,0:T(8,128)(2,1)} %collective-permute-done.14.rest_12_), channel_id=1, source_target_pairs={{0,4},{4,8},{8,12},{12,14},{14,10},{10,6},{6,2},{2,0},{1,5},{5,9},... | collective-permute-start | bytes 1179656 | tf_op jit(solution)/shard_map/ppermute | solution.py:62
  92.8 0.1 collective-permute-done.22.rest_20_
  92.9 0.1 collective-permute-start.23
  93.0 0.1 add_bitcast_fusion
  93.1 0.1 copy.31
  93.2 0.1 reshape.421.table_ref
  93.2 5.7 %collective-permute-done.9 = bf16[2,1,64,1536]{3,2,0,1:T(8,128)(2,1)} collective-permute-done((bf16[2,1,64,1536]{3,2,0,1:T(8,128)(2,1)}, bf16[2,1,64,1536]{3,2,0,1:T(8,128)(2,1)}, u32[]{:S(2)}, u32[]{:S(2)}) %collective-permute-start.9) | collective-permute-done | bytes 393248 | tf_op jit(solution)/shard_map/ppermute | solution.py:34
  99.0 10.8 %collective-permute-done.15.rest_13_ = bf16[2,1,64,1536]{3,2,1,0:T(8,128)(2,1)} collective-permute-done((bf16[2,1,64,1536]{3,2,1,0:T(8,128)(2,1)S(1)}, bf16[2,1,64,1536]{3,2,1,0:T(8,128)(2,1)}, u32[]{:S(2)}, u32[]{:S(2)}) %collective-permute-start.15) | collective-permute-done | bytes 393248 | tf_op jit(solution)/shard_map/ppermute | solution.py:70
  109.8 7.3 %collective-permute-done.23.rest_21_ = bf16[2,1,64,1536]{3,2,1,0:T(8,128)(2,1)} collective-permute-done((bf16[2,1,64,1536]{3,2,1,0:T(8,128)(2,1)}, bf16[2,1,64,1536]{3,2,1,0:T(8,128)(2,1)}, u32[]{:S(2)}, u32[]{:S(2)}) %collective-permute-start.23) | collective-permute-done | bytes 393248 | tf_op jit(solution)/shard_map/ppermute | solution.py:64
  117.0 14.3 %shard_map.100 = bf16[512,1536]{1,0:T(8,128)(2,1)} custom-call(s32[16]{0:T(128)S(1)} %reshape.421.table_ref, bf16[512,1536]{1,0:T(8,128)(2,1)} %bitcast.93, bf16[2,8,64,1536]{3,2,1,0:T(8,128)(2,1)} %copy-done.2, bf16[2,1,64,1536]{3,2,1,0:T(8,128)(2,1)S(1)} %collective-permute-done.rest_0_, bf16[2,1,64,1536]{3,2,1,0:T(8,128)(2,1)S(1)} %collective-permute-done.1.rest_1_, ...), custom_call_target="tpu_custom_call" | custom-call | flops 3221225472 | bytes 9437184 | tf_op jit(solution)/shard_map/pallas_call | solution.py:154
  (46 shorter events, 0.2 us)
Async XLA Ops:
  0.0 15.8 %collective-permute-start.3 = (s32[4]{0:T(128)}, s32[4]{0:T(128)S(1)}, u32[]{:S(2)}, u32[]{:S(2)}) collective-permute-start(s32[4]{0:T(128)} %bitcast.94), channel_id=1, source_target_pairs={{0,2},{2,4},{4,6},{6,8},{8,10},{10,12},{12,14},{1,3},{3,5},{5,7},{... | collective-permute-start | bytes 56 | tf_op jit(solution)/shard_map/ppermute | solution.py:34
  3.4 14.2 %collective-permute-start.2 = (s32[4]{0:T(128)}, s32[4]{0:T(128)S(1)}, u32[]{:S(2)}, u32[]{:S(2)}) collective-permute-start(s32[4]{0:T(128)} %bitcast.95), channel_id=1, source_target_pairs={{2,0},{4,2},{6,4},{8,6},{10,8},{12,10},{14,12},{3,1},{5,3},{7,5},{... | collective-permute-start | bytes 56 | tf_op jit(solution)/shard_map/ppermute | solution.py:34
  8.7 1.9 %copy-start.4 = (bf16[8,1,64,1536]{3,2,1,0:T(8,128)(2,1)S(1)}, bf16[8,1,64,1536]{3,2,1,0:T(8,128)(2,1)}, u32[]{:S(2)}) copy-start(bf16[8,1,64,1536]{3,2,1,0:T(8,128)(2,1)} %param.15) | copy-start | bytes 4718596
  11.2 3.6 %copy-start.2 = (bf16[2,8,64,1536]{3,2,1,0:T(8,128)(2,1)}, bf16[2,8,64,1536]{3,2,1,0:T(8,128)(2,1)S(1)}, u32[]{:S(2)}) copy-start(bf16[2,8,64,1536]{3,2,1,0:T(8,128)(2,1)S(1)} %maximum_bitcast_fusion.own_hbm) | copy-start | bytes 9437188
  12.4 14.5 %collective-permute-start.4 = (bf16[2,1,64,1536]{3,2,1,0:T(8,128)(2,1)}, bf16[2,1,64,1536]{3,2,1,0:T(8,128)(2,1)S(1)}, u32[]{:S(2)}, u32[]{:S(2)}) collective-permute-start(bf16[2,1,64,1536]{3,2,1,0:T(8,128)(2,1)} %get-tuple-element.27), channel_id=1, source_target_pairs={{0,4},{4,8},{8,12},{12,14},{14,10},{10,6},{6,2},{2,0},{1,5},{5,9},... | collective-permute-start | bytes 1179656 | tf_op jit(solution)/shard_map/ppermute | solution.py:67
  13.9 20.8 %collective-permute-start.12 = (bf16[2,1,64,1536]{3,2,1,0:T(8,128)(2,1)}, bf16[2,1,64,1536]{3,2,1,0:T(8,128)(2,1)S(1)}, u32[]{:S(2)}, u32[]{:S(2)}) collective-permute-start(bf16[2,1,64,1536]{3,2,1,0:T(8,128)(2,1)} %get-tuple-element.27), channel_id=1, source_target_pairs={{4,0},{8,4},{12,8},{14,12},{10,14},{6,10},{2,6},{0,2},{5,1},{9,5},... | collective-permute-start | bytes 1179656 | tf_op jit(solution)/shard_map/ppermute | solution.py:70
  14.4 18.3 %collective-permute-start.18 = (bf16[2,1,64,1536]{3,2,1,0:T(8,128)(2,1)}, bf16[2,1,64,1536]{3,2,1,0:T(8,128)(2,1)}, u32[]{:S(2)}, u32[]{:S(2)}) collective-permute-start(bf16[2,1,64,1536]{3,2,1,0:T(8,128)(2,1)} %get-tuple-element.26), channel_id=1, source_target_pairs={{4,0},{8,4},{12,8},{14,12},{10,14},{6,10},{2,6},{0,2},{5,1},{9,5},... | collective-permute-start | bytes 1179656 | tf_op jit(solution)/shard_map/ppermute | solution.py:70
  15.8 20.9 %collective-permute-start.17 = (bf16[2,1,64,1536]{3,2,1,0:T(8,128)(2,1)}, bf16[2,1,64,1536]{3,2,1,0:T(8,128)(2,1)}, u32[]{:S(2)}, u32[]{:S(2)}) collective-permute-start(bf16[2,1,64,1536]{3,2,1,0:T(8,128)(2,1)} %get-tuple-element.26), channel_id=1, source_target_pairs={{0,4},{4,8},{8,12},{12,14},{14,10},{10,6},{6,2},{2,0},{1,5},{5,9},... | collective-permute-start | bytes 1179656 | tf_op jit(solution)/shard_map/ppermute | solution.py:67
  17.7 23.8 %collective-permute-start = (bf16[2,1,64,1536]{3,2,1,0:T(8,128)(2,1)}, bf16[2,1,64,1536]{3,2,1,0:T(8,128)(2,1)S(1)}, u32[]{:S(2)}, u32[]{:S(2)}) collective-permute-start(bf16[2,1,64,1536]{3,2,1,0:T(8,128)(2,1)} %get-tuple-element.19), channel_id=1, source_target_pairs={{0,1},{2,3},{4,5},{6,7},{8,9},{10,11},{12,13},{14,15},{16,17},{18,... | collective-permute-start | bytes 1179656 | tf_op jit(solution)/shard_map/ppermute | solution.py:34
  25.4 1.3 copy-start.3
  26.9 18.1 %copy-start.5 = (s32[1,1,4]{2,1,0:T(1,128)S(1)}, s32[1,1,4]{2,1,0:T(1,128)}, u32[]{:S(2)}) copy-start(s32[1,1,4]{2,1,0:T(1,128)} %param.18) | copy-start | bytes 52
  26.9 18.1 %copy-start = (s32[8]{0:T(128)S(1)}, s32[8]{0:T(128)}, u32[]{:S(2)}) copy-start(s32[8]{0:T(128)} %constant.96.clone) | copy-start | bytes 100
  26.9 19.4 %copy-start.6 = (s32[1,1,4]{2,1,0:T(1,128)S(1)}, s32[1,1,4]{2,1,0:T(1,128)}, u32[]{:S(2)}) copy-start(s32[1,1,4]{2,1,0:T(1,128)} %param.17) | copy-start | bytes 52
  26.9 57.0 %copy-start.1 = (s32[7,2]{1,0:T(8,128)S(1)}, s32[7,2]{1,0:T(8,128)}, u32[]{:S(2)}) copy-start(s32[7,2]{1,0:T(8,128)} %constant.97.clone) | copy-start | bytes 172
  27.0 16.0 %collective-permute-start.1 = (bf16[2,1,64,1536]{3,2,1,0:T(8,128)(2,1)}, bf16[2,1,64,1536]{3,2,1,0:T(8,128)(2,1)S(1)}, u32[]{:S(2)}, u32[]{:S(2)}) collective-permute-start(bf16[2,1,64,1536]{3,2,1,0:T(8,128)(2,1)} %get-tuple-element.18), channel_id=1, source_target_pairs={{1,0},{3,2},{5,4},{7,6},{9,8},{11,10},{13,12},{15,14},{17,16},{19,... | collective-permute-start | bytes 1179656 | tf_op jit(solution)/shard_map/ppermute | solution.py:34
  32.7 10.3 %collective-permute-start.7 = (bf16[2,1,64,1536]{3,2,1,0:T(8,128)(2,1)S(1)}, bf16[2,1,64,1536]{3,2,1,0:T(8,128)(2,1)S(1)}, u32[]{:S(2)}, u32[]{:S(2)}) collective-permute-start(bf16[2,1,64,1536]{3,2,1,0:T(8,128)(2,1)S(1)} %collective-permute-done.4.rest_8_), channel_id=1, source_target_pairs={{0,4},{4,8},{8,12},{12,14},{14,10},{10,6},{6,2},{2,0},{1,5},{5,9},... | collective-permute-start | bytes 1179656 | tf_op jit(solution)/shard_map/ppermute | solution.py:67
  34.7 17.2 %collective-permute-start.5 = (bf16[2,1,64,1536]{3,2,0,1:T(8,128)(2,1)}, bf16[2,1,64,1536]{3,2,0,1:T(8,128)(2,1)S(1)}, u32[]{:S(2)}, u32[]{:S(2)}) collective-permute-start(bf16[2,1,64,1536]{3,2,0,1:T(8,128)(2,1)} %get-tuple-element.12), channel_id=1, source_target_pairs={{0,2},{2,4},{4,6},{6,8},{8,10},{10,12},{12,14},{1,3},{3,5},{5,7},{... | collective-permute-start | bytes 1179656 | tf_op jit(solution)/shard_map/ppermute | solution.py:34
  36.7 18.3 %collective-permute-start.6 = (bf16[2,1,64,1536]{3,2,0,1:T(8,128)(2,1)}, bf16[2,1,64,1536]{3,2,0,1:T(8,128)(2,1)S(1)}, u32[]{:S(2)}, u32[]{:S(2)}) collective-permute-start(bf16[2,1,64,1536]{3,2,0,1:T(8,128)(2,1)} %get-tuple-element.13), channel_id=1, source_target_pairs={{2,0},{4,2},{6,4},{8,6},{10,8},{12,10},{14,12},{3,1},{5,3},{7,5},{... | collective-permute-start | bytes 1179656 | tf_op jit(solution)/shard_map/ppermute | solution.py:34
  41.5 19.2 %collective-permute-start.20 = (bf16[2,1,64,1536]{3,2,1,0:T(8,128)(2,1)}, bf16[2,1,64,1536]{3,2,1,0:T(8,128)(2,1)}, u32[]{:S(2)}, u32[]{:S(2)}) collective-permute-start(bf16[2,1,64,1536]{3,2,1,0:T(8,128)(2,1)} %collective-permute-done.18.rest_16_), channel_id=1, source_target_pairs={{4,0},{8,4},{12,8},{14,12},{10,14},{6,10},{2,6},{0,2},{5,1},{9,5},... | collective-permute-start | bytes 1179656 | tf_op jit(solution)/shard_map/ppermute | solution.py:70
  43.0 22.6 %collective-permute-start.13 = (bf16[2,1,64,1536]{3,2,1,0:T(8,128)(2,1)S(1)}, bf16[2,1,64,1536]{3,2,1,0:T(8,128)(2,1)S(1)}, u32[]{:S(2)}, u32[]{:S(2)}) collective-permute-start(bf16[2,1,64,1536]{3,2,1,0:T(8,128)(2,1)S(1)} %collective-permute-done.12.rest_9_), channel_id=1, source_target_pairs={{4,0},{8,4},{12,8},{14,12},{10,14},{6,10},{2,6},{0,2},{5,1},{9,5},... | collective-permute-start | bytes 1179656 | tf_op jit(solution)/shard_map/ppermute | solution.py:70
  43.0 37.7 %collective-permute-start.19 = (bf16[2,1,64,1536]{3,2,1,0:T(8,128)(2,1)}, bf16[2,1,64,1536]{3,2,1,0:T(8,128)(2,1)}, u32[]{:S(2)}, u32[]{:S(2)}) collective-permute-start(bf16[2,1,64,1536]{3,2,1,0:T(8,128)(2,1)} %collective-permute-done.17.rest_15_), channel_id=1, source_target_pairs={{0,4},{4,8},{8,12},{12,14},{14,10},{10,6},{6,2},{2,0},{1,5},{5,9},... | collective-permute-start | bytes 1179656 | tf_op jit(solution)/shard_map/ppermute | solution.py:67
  52.0 34.0 %collective-permute-start.10 = (bf16[2,1,64,1536]{3,2,0,1:T(8,128)(2,1)}, bf16[2,1,64,1536]{3,2,0,1:T(8,128)(2,1)S(1)}, u32[]{:S(2)}, u32[]{:S(2)}) collective-permute-start(bf16[2,1,64,1536]{3,2,0,1:T(8,128)(2,1)} %get-tuple-element.16), channel_id=1, source_target_pairs={{12,14},{13,15},{28,30},{29,31}} | collective-permute-start | bytes 1179656 | tf_op jit(solution)/shard_map/ppermute | solution.py:227
  55.0 33.0 %collective-permute-start.11 = (bf16[2,1,64,1536]{3,2,0,1:T(8,128)(2,1)}, bf16[2,1,64,1536]{3,2,0,1:T(8,128)(2,1)}, u32[]{:S(2)}, u32[]{:S(2)}) collective-permute-start(bf16[2,1,64,1536]{3,2,0,1:T(8,128)(2,1)} %get-tuple-element.17), channel_id=1, source_target_pairs={{2,0},{3,1},{18,16},{19,17}} | collective-permute-start | bytes 1179656 | tf_op jit(solution)/shard_map/ppermute | solution.py:228
  60.7 27.3 %collective-permute-start.8 = (bf16[2,1,64,1536]{3,2,0,1:T(8,128)(2,1)}, bf16[2,1,64,1536]{3,2,0,1:T(8,128)(2,1)}, u32[]{:S(2)}, u32[]{:S(2)}) collective-permute-start(bf16[2,1,64,1536]{3,2,0,1:T(8,128)(2,1)} %get-tuple-element.14), channel_id=1, source_target_pairs={{0,2},{2,4},{4,6},{6,8},{8,10},{10,12},{12,14},{1,3},{3,5},{5,7},{... | collective-permute-start | bytes 1179656 | tf_op jit(solution)/shard_map/ppermute | solution.py:34
  65.5 24.6 %collective-permute-start.14 = (bf16[2,1,64,1536]{3,2,1,0:T(8,128)(2,1)S(1)}, bf16[2,1,64,1536]{3,2,1,0:T(8,128)(2,1)}, u32[]{:S(2)}, u32[]{:S(2)}) collective-permute-start(bf16[2,1,64,1536]{3,2,1,0:T(8,128)(2,1)S(1)} %collective-permute-done.7.rest_10_), channel_id=1, source_target_pairs={{0,4},{4,8},{8,12},{12,14},{14,10},{10,6},{6,2},{2,0},{1,5},{5,9},... | collective-permute-start | bytes 1179656 | tf_op jit(solution)/shard_map/ppermute | solution.py:67
  80.7 12.2 %collective-permute-start.22 = (bf16[2,1,64,1536]{3,2,1,0:T(8,128)(2,1)}, bf16[2,1,64,1536]{3,2,1,0:T(8,128)(2,1)}, u32[]{:S(2)}, u32[]{:S(2)}) collective-permute-start(bf16[2,1,64,1536]{3,2,1,0:T(8,128)(2,1)} %collective-permute-done.20.rest_18_), channel_id=1, source_target_pairs={{4,0},{8,4},{12,8},{14,12},{10,14},{6,10},{2,6},{0,2},{5,1},{9,5},... | collective-permute-start | bytes 1179656 | tf_op jit(solution)/shard_map/ppermute | solution.py:70
  86.0 13.0 %collective-permute-start.9 = (bf16[2,1,64,1536]{3,2,0,1:T(8,128)(2,1)}, bf16[2,1,64,1536]{3,2,0,1:T(8,128)(2,1)}, u32[]{:S(2)}, u32[]{:S(2)}) collective-permute-start(bf16[2,1,64,1536]{3,2,0,1:T(8,128)(2,1)} %get-tuple-element.15), channel_id=1, source_target_pairs={{2,0},{4,2},{6,4},{8,6},{10,8},{12,10},{14,12},{3,1},{5,3},{7,5},{... | collective-permute-start | bytes 1179656 | tf_op jit(solution)/shard_map/ppermute | solution.py:34
  87.9 21.8 %collective-permute-start.15 = (bf16[2,1,64,1536]{3,2,1,0:T(8,128)(2,1)S(1)}, bf16[2,1,64,1536]{3,2,1,0:T(8,128)(2,1)}, u32[]{:S(2)}, u32[]{:S(2)}) collective-permute-start(bf16[2,1,64,1536]{3,2,1,0:T(8,128)(2,1)S(1)} %collective-permute-done.13.rest_11_), channel_id=1, source_target_pairs={{4,0},{8,4},{12,8},{14,12},{10,14},{6,10},{2,6},{0,2},{5,1},{9,5},... | collective-permute-start | bytes 1179656 | tf_op jit(solution)/shard_map/ppermute | solution.py:70
  88.0 21.7 %collective-permute-start.21 = (bf16[2,1,64,1536]{3,2,1,0:T(8,128)(2,1)}, bf16[2,1,64,1536]{3,2,1,0:T(8,128)(2,1)}, u32[]{:S(2)}, u32[]{:S(2)}) collective-permute-start(bf16[2,1,64,1536]{3,2,1,0:T(8,128)(2,1)} %collective-permute-done.19.rest_17_), channel_id=1, source_target_pairs={{0,4},{4,8},{8,12},{12,14},{14,10},{10,6},{6,2},{2,0},{1,5},{5,9},... | collective-permute-start | bytes 1179656 | tf_op jit(solution)/shard_map/ppermute | solution.py:67
  90.1 19.7 %collective-permute-start.16 = (bf16[2,1,64,1536]{3,2,1,0:T(8,128)(2,1)}, bf16[2,1,64,1536]{3,2,1,0:T(8,128)(2,1)}, u32[]{:S(2)}, u32[]{:S(2)}) collective-permute-start(bf16[2,1,64,1536]{3,2,1,0:T(8,128)(2,1)} %collective-permute-done.14.rest_12_), channel_id=1, source_target_pairs={{0,4},{4,8},{8,12},{12,14},{14,10},{10,6},{6,2},{2,0},{1,5},{5,9},... | collective-permute-start | bytes 1179656 | tf_op jit(solution)/shard_map/ppermute | solution.py:62
  92.9 24.1 %collective-permute-start.23 = (bf16[2,1,64,1536]{3,2,1,0:T(8,128)(2,1)}, bf16[2,1,64,1536]{3,2,1,0:T(8,128)(2,1)}, u32[]{:S(2)}, u32[]{:S(2)}) collective-permute-start(bf16[2,1,64,1536]{3,2,1,0:T(8,128)(2,1)} %collective-permute-done.22.rest_20_), channel_id=1, source_target_pairs={{4,0},{8,4},{12,8},{14,12},{10,14},{6,10},{2,6},{0,2},{5,1},{9,5},... | collective-permute-start | bytes 1179656 | tf_op jit(solution)/shard_map/ppermute | solution.py:64
